TPU v7x, 512 devices: a whole 4x8x8 slice. The times are simulated.
512 devices in a mesh: lat: 8 (over y_lo, core), lon: 64 (over x, y_hi, z).
Axes of the slice: x: 4, y: 8 (y_hi: 2, y_lo: 4; y = y_hi * 4 + y_lo), z: 8, core: 2. Of those that a mesh axis runs over, the one named last changes fastest.
Arguments:
- fields: bfloat16 [512, 1024, 256], P('lat', 'lon'), may hold values from -16 to 16
- kernel: bfloat16 [3, 3, 256, 256], replicated, may hold values from -0.125 to 0.125
- norm_gain: float32 [256], replicated, may hold values from 0.5 to 1.5
- norm_shift: float32 [256], replicated, may hold values from -3 to 3
- cotangent: bfloat16 [512, 1024, 256], P('lat', 'lon'), may hold values from -6 to 6
Outputs:
- block_out: bfloat16 [512, 1024, 256], P('lat', 'lon')
- grad_fields: bfloat16 [512, 1024, 256], P('lat', 'lon')
- grad_kernel: float32 [2304, 256], P('lon', 'lat')
- grad_gain: float32 [256], replicated
- grad_shift: float32 [256], replicated
All inputs are finite; a program needn't handle non-finite values.
Results may differ from a plain program's by a relative error of at most 0.004.
Values may be sent and summed in bfloat16 or wider, within the bound.
No kernel may reach another device: no remote copies, remote signals or barrier semaphores. Data moves between devices by JAX's collectives and lax.ppermute only.
A program may use at most 64 MiB of HBM per device.

v0:
```python
import jax
import jax.numpy as jnp
from jax import lax
from jax.sharding import PartitionSpec as P

G = 32


def with_halo(shard, sides, width, wrap):
    for axis, dim in sides:
        peers, length = (lax.axis_size(axis), shard.shape[dim])
        up = [(i, (i + 1) % peers) for i in range(peers if wrap else peers - 1)]
        down = [(j, i) for i, j in up]
        last = lax.slice_in_dim(shard, length - width, length, axis=dim)
        initial = lax.slice_in_dim(shard, 0, width, axis=dim)
        before = lax.ppermute(last, axis, up)
        after = lax.ppermute(initial, axis, down)
        shard = jnp.concatenate([before, shard, after], axis=dim)
    return shard


def passed_along(block, axis, distance):
    devices = range(lax.axis_size(axis))
    route = [((i - distance) % len(devices), i) for i in devices]
    return lax.ppermute(block, axis, route)


def extend(field):
    halfway = lax.axis_size("lon") // 2
    widened = with_halo(field, (("lon", 1),), 1, True)
    banded = with_halo(widened, (("lat", 0),), 1, False)
    distant = passed_along(jnp.stack([widened[0], widened[-1]]), "lon", halfway)
    return (banded, distant)


def local(fields, kernel, norm_gain, norm_shift, cotangent):
    height, breadth, channels = fields.shape
    north = lax.axis_index("lat") == 0
    south = lax.axis_index("lat") == lax.axis_size("lat") - 1
    banded, distant = extend(fields)
    merged = banded.at[0].set(jnp.where(north, distant[0], banded[0]))
    merged = merged.at[-1].set(jnp.where(south, distant[1], merged[-1]))
    patches = jnp.concatenate(
        [
            merged[tap_row : tap_row + height, tap_col : tap_col + breadth].reshape(-1, channels)
            for tap_row in range(3)
            for tap_col in range(3)
        ],
        1,
    )
    conv_out = jnp.dot(
        patches, kernel.reshape(9 * channels, channels), preferred_element_type=jnp.float32
    )
    count = height * breadth * lax.axis_size("lat") * lax.axis_size("lon") * (channels // G)
    first, second = lax.psum(
        (jnp.sum(conv_out, 0), jnp.sum(conv_out * conv_out, 0)), ("lat", "lon")
    )
    mean = first.reshape(G, -1).sum(1) / count
    var = second.reshape(G, -1).sum(1) / count - mean * mean
    rstd = lax.rsqrt(var + 1e-05)
    mean_ch = jnp.repeat(mean, channels // G)
    rstd_ch = jnp.repeat(rstd, channels // G)
    ghat = (conv_out - mean_ch) * rstd_ch
    pre = ghat * norm_gain + norm_shift
    sigma = jax.nn.sigmoid(pre)
    block_out = (
        (fields.reshape(-1, channels).astype(jnp.float32) + pre * sigma)
        .astype(jnp.bfloat16)
        .reshape(height, breadth, channels)
    )
    upstream = cotangent.astype(jnp.float32).reshape(-1, channels)
    dpre = upstream * (sigma * (1.0 + pre * (1.0 - sigma)))
    grad_gain, grad_shift = lax.psum((jnp.sum(dpre * ghat, 0), jnp.sum(dpre, 0)), ("lat", "lon"))
    mean_a = (norm_gain * grad_shift).reshape(G, -1).sum(1) / count
    mean_b = (norm_gain * grad_gain).reshape(G, -1).sum(1) / count
    dconv = (
        (
            dpre * norm_gain
            - jnp.repeat(mean_a, channels // G)
            - ghat * jnp.repeat(mean_b, channels // G)
        )
        * rstd_ch
    ).astype(jnp.bfloat16)
    grad_banded, grad_distant = extend(dconv.reshape(height, breadth, channels))
    grad_patches = jnp.concatenate(
        [
            grad_banded[
                2 - tap_row : 2 - tap_row + height, 2 - tap_col : 2 - tap_col + breadth
            ].reshape(-1, channels)
            for tap_row in range(3)
            for tap_col in range(3)
        ],
        1,
    )
    flipped = jnp.concatenate(
        [kernel[tap_row, tap_col].T for tap_row in range(3) for tap_col in range(3)], 0
    )
    back = jnp.dot(grad_patches, flipped, preferred_element_type=jnp.float32).reshape(
        height, breadth, channels
    )
    upper_term = jnp.zeros((breadth, channels), jnp.float32)
    lower_term = jnp.zeros((breadth, channels), jnp.float32)
    for tap_col in range(3):
        upper_term = upper_term + jnp.dot(
            grad_distant[0, 2 - tap_col : 2 - tap_col + breadth],
            kernel[0, tap_col].T,
            preferred_element_type=jnp.float32,
        )
        lower_term = lower_term + jnp.dot(
            grad_distant[1, 2 - tap_col : 2 - tap_col + breadth],
            kernel[2, tap_col].T,
            preferred_element_type=jnp.float32,
        )
    back = back.at[0].add(jnp.where(north, upper_term, 0.0))
    back = back.at[-1].add(jnp.where(south, lower_term, 0.0))
    grad_fields = (upstream.reshape(height, breadth, channels) + back).astype(jnp.bfloat16)
    term_full = lax.dot_general(
        patches, dconv, (((0,), (0,)), ((), ())), preferred_element_type=jnp.float32
    )
    owned_cols = lax.psum_scatter(term_full, "lat", scatter_dimension=1, tiled=True)
    grad_kernel = lax.psum_scatter(owned_cols, "lon", scatter_dimension=0, tiled=True)
    return (block_out, grad_fields, grad_kernel, grad_gain, grad_shift)


def solution(mesh):
    in_specs = (P("lat", "lon", None), P(), P(), P(), P("lat", "lon", None))
    out_specs = (P("lat", "lon", None), P("lat", "lon", None), P("lon", "lat"), P(), P())
    return jax.shard_map(local, mesh=mesh, in_specs=in_specs, out_specs=out_specs, check_vma=False)
```

profile of v0, /device:TPU:16, one launch (start us, length us, event | category | flops | bytes accessed | tf_op | source)
XLA Modules:
  0.0 1089.5 jit_solution(14591799681026607741)
XLA Ops:
  7.2 1.2 fusion.35
  8.4 4.3 collective-permute-start
  12.7 14.2 %collective-permute-start.1 = (bf16[64,1,256]{2,1,0:T(2,128)(2,1)S(1)}, bf16[64,1,256]{2,1,0:T(2,128)(2,1)S(1)}, u32[]{:S(2)}, u32[]{:S(2)}) collective-permute-start(bf16[64,1,256]{2,1,0:T(2,128)(2,1)S(1)} %get-tuple-element.89), channel_id=1, source_target_pairs={{1,0},{2,1},{3,2},{4,3},{5,4},{6,5},{7,6},{8,7},{9,8},{10,9},{11,1... | collective-permute-start | bytes 98312 | tf_op jit(solution)/shard_map/ppermute | solution.py:17
  26.9 1.6 bitcast_dynamic-update-slice_fusion.8
  28.6 1.6 bitcast_dynamic-update-slice_fusion.7
  30.1 1.6 bitcast_dynamic-update-slice_fusion.6
  31.7 1.6 bitcast_dynamic-update-slice_fusion.5
  33.3 1.6 bitcast_dynamic-update-slice_fusion.4
  34.9 1.9 collective-permute-start.2
  36.8 3.6 collective-permute-start.3
  40.5 2.7 collective-permute-start.4
  43.7 4.0 collective-permute-done.4
  48.6 1.6 copy-done.2
  50.3 1.4 fusion.30
  51.8 93.0 %all-reduce.2 = (f32[32,8]{1,0:T(8,128)S(1)}, f32[32,8]{1,0:T(8,128)S(1)}) all-reduce(f32[32,8]{1,0:T(8,128)S(1)} %reshape.224, f32[32,8]{1,0:T(8,128)S(1)} %reshape.223), channel_id=1, replica_groups=mesh['lat'=8,'lon'=64] {'lat','lon'}, use_global_device_ids=true, to_apply=%region_4.5 | all-reduce | flops 512 | bytes 4096 | tf_op jit(solution)/shard_map/psum | solution.py:55
  146.1 94.4 %all-reduce.1 = (f32[256]{0:T(256)S(1)}, f32[256]{0:T(256)S(1)}) all-reduce(f32[256]{0:T(256)S(1)} %get-tuple-element.54, f32[256]{0:T(256)S(1)} %get-tuple-element.53), channel_id=1, replica_groups=mesh['lat'=8,'lon'=64] {'lat','lon'}, use_global_device_ids=true, to_apply=%region_10.11 | all-reduce | flops 512 | bytes 4096 | tf_op jit(solution)/shard_map/psum | solution.py:73
  241.3 1.6 multiply_convert_fusion
  242.9 5.2 fusion.38
  248.2 1.2 copy-done.3
  250.7 0.7 bitcast_dynamic-update-slice_fusion.1
  251.6 3.2 collective-permute-start.5
  254.8 10.7 collective-permute-start.6
  266.2 1.3 dynamic-slice.32
  268.2 1.9 collective-permute-done.6
  270.1 1.9 collective-permute-start.8
  272.0 3.6 collective-permute-start.7
  275.7 2.1 collective-permute-start.9
  279.0 0.8 fusion.32
  280.2 2.7 fusion.37
  284.4 1.0 add_convert_fusion
  285.4 795.8 %all-reduce.5.cloned.1.call-done = f32[2304,32]{0,1:T(8,128)} async-done(((f32[2304,32]{0,1:T(8,128)}), f32[2304,32]{0,1:T(8,128)}) %all-reduce.5.cloned.1.call-update) | async-done | bytes 294928
  1081.3 1.4 constant_dynamic-slice_fusion
  (89 shorter events, 8.8 us)
Async XLA Ops:
  7.2 27.7 %copy-start = (bf16[64,16,256]{2,1,0:T(8,128)(2,1)S(1)}, bf16[64,16,256]{2,1,0:T(8,128)(2,1)}, u32[]{:S(2)}) copy-start(bf16[64,16,256]{2,1,0:T(8,128)(2,1)} %param.13) | copy-start | bytes 1572868
  7.2 277.1 %reduce-scatter.3.cloned.1.call-start = ((), (), s32[]{:S(2)}) async-start(), calls=%async_computation.1 | async-start | bytes 2654208 | tf_op jit(solution)/shard_map/reduce_scatter | solution.py:120
  8.4 26.4 %collective-permute-start = (bf16[64,1,256]{2,1,0:T(2,128)(2,1)S(1)}, bf16[64,1,256]{2,1,0:T(2,128)(2,1)S(1)}, u32[]{:S(2)}, u32[]{:S(2)}) collective-permute-start(bf16[64,1,256]{2,1,0:T(2,128)(2,1)S(1)} %get-tuple-element.88), channel_id=1, source_target_pairs={{0,1},{1,2},{2,3},{3,4},{4,5},{5,6},{6,7},{7,8},{8,9},{9,10},{10,1... | collective-permute-start | bytes 98312 | tf_op jit(solution)/shard_map/ppermute | solution.py:16
  12.7 22.2 %collective-permute-start.1 = (bf16[64,1,256]{2,1,0:T(2,128)(2,1)S(1)}, bf16[64,1,256]{2,1,0:T(2,128)(2,1)S(1)}, u32[]{:S(2)}, u32[]{:S(2)}) collective-permute-start(bf16[64,1,256]{2,1,0:T(2,128)(2,1)S(1)} %get-tuple-element.89), channel_id=1, source_target_pairs={{1,0},{2,1},{3,2},{4,3},{5,4},{6,5},{7,6},{8,7},{9,8},{10,9},{11,1... | collective-permute-start | bytes 98312 | tf_op jit(solution)/shard_map/ppermute | solution.py:17
  34.9 8.3 collective-permute-start.2
  36.8 6.4 collective-permute-start.3
  40.5 7.2 collective-permute-start.4
  48.5 1.8 copy-start.2
  48.6 3.0 copy-start.4
  50.3 95.2 %copy-start.1 = (bf16[64,16,256]{2,1,0:T(8,128)(2,1)S(1)}, bf16[64,16,256]{2,1,0:T(8,128)(2,1)}, u32[]{:S(2)}) copy-start(bf16[64,16,256]{2,1,0:T(8,128)(2,1)} %param.17) | copy-start | bytes 1572868
  50.3 95.2 %copy-start.5 = (f32[256]{0:T(256)S(1)}, f32[256]{0:T(256)}, u32[]{:S(2)}) copy-start(f32[256]{0:T(256)} %param.15) | copy-start | bytes 3076
  50.3 95.2 %copy-start.6 = (f32[256]{0:T(256)S(1)}, f32[256]{0:T(256)}, u32[]{:S(2)}) copy-start(f32[256]{0:T(256)} %param.16) | copy-start | bytes 3076
  240.5 2.4 copy-start.7
  240.5 2.4 copy-start.8
  248.1 1.3 copy-start.3
  248.1 833.1 %all-reduce.5.cloned.1.call-start = ((), (), s32[]{:S(2)}) async-start(), calls=%async_computation.2 | async-start | bytes 589824
  251.6 16.6 %collective-permute-start.5 = (bf16[64,1,256]{2,1,0:T(2,128)(2,1)S(1)}, bf16[64,1,256]{2,1,0:T(2,128)(2,1)S(1)}, u32[]{:S(2)}, u32[]{:S(2)}) collective-permute-start(bf16[64,1,256]{2,1,0:T(2,128)(2,1)S(1)} %get-tuple-element.86), channel_id=1, source_target_pairs={{0,1},{1,2},{2,3},{3,4},{4,5},{5,6},{6,7},{7,8},{8,9},{9,10},{10,1... | collective-permute-start | bytes 98312 | tf_op jit(solution)/shard_map/ppermute | solution.py:16
  254.8 15.3 %collective-permute-start.6 = (bf16[64,1,256]{2,1,0:T(2,128)(2,1)S(1)}, bf16[64,1,256]{2,1,0:T(2,128)(2,1)S(1)}, u32[]{:S(2)}, u32[]{:S(2)}) collective-permute-start(bf16[64,1,256]{2,1,0:T(2,128)(2,1)S(1)} %get-tuple-element.87), channel_id=1, source_target_pairs={{1,0},{2,1},{3,2},{4,3},{5,4},{6,5},{7,6},{8,7},{9,8},{10,9},{11,1... | collective-permute-start | bytes 98312 | tf_op jit(solution)/shard_map/ppermute | solution.py:17
  270.1 8.2 collective-permute-start.8
  272.0 6.3 collective-permute-start.7
  275.7 7.3 collective-permute-start.9
Sparse Core Ops, SparseCore 0:
  248.2 35.9 reduce-scatter.2
  287.2 794.0 all-reduce.4
where the time goes:
time: 1090 us
  waiting for transfers between devices  802 us (74%)
  blocking collectives  187 us (17%)
  starting transfers between devices  48.5 us (4%)
  local copies, waits for them, and re-layouts  20.5 us (2%)
  between operations  15.2 us (1%)
    unnamed x3, waiting for transfers between devices  796 us
    psum x1, blocking collectives, local(): lax.psum((jnp.sum(dpre * ghat, 0), jnp.sum(dpre, 0)), ('lat', 'lon'))  94.4 us
    psum x1, blocking collectives, local(): lax.psum((jnp.sum(conv_out, 0), jnp.sum(conv_out * conv_out, 0)), ('lat',...  93 us
    ppermute x4, starting transfers between devices, with_halo(): after = lax.ppermute(initial, axis, down)  32.3 us
  transfers between devices with their start and end apart: 12, of which 4 were waited for; matrix products, arithmetic and copies ran while one was open for 2% of the time, Pallas kernels for 0%

commit v1 on v0

--- a/solution.py
+++ b/solution.py
@@ -33,6 +33,41 @@
     return (banded, distant)
 
 
+def exchange(block, axis, bit):
+    peers = lax.axis_size(axis)
+    return lax.ppermute(block, axis, [(i, i ^ (1 << bit)) for i in range(peers)])
+
+
+def butterfly_order():
+    lat_bits = (lax.axis_size("lat") - 1).bit_length()
+    lon_bits = (lax.axis_size("lon") - 1).bit_length()
+    order = [("lat", b) for b in range(lat_bits)] + [("lon", b) for b in range(lon_bits)]
+    return order
+
+
+def butterfly_sum(value):
+    for axis, bit in butterfly_order():
+        value = value + exchange(value, axis, bit)
+    return value
+
+
+def halving_sum(blocks):
+    lat_n, lon_n = blocks.shape[0], blocks.shape[1]
+    lat_bits, lon_bits = (lat_n - 1).bit_length(), (lon_n - 1).bit_length()
+    tail = blocks.shape[2:]
+    split = blocks.reshape((2,) * lat_bits + (2,) * lon_bits + tail)
+    dims = {("lat", b): lat_bits - 1 - b for b in range(lat_bits)}
+    dims.update({("lon", b): lat_bits + lon_bits - 1 - b for b in range(lon_bits)})
+    for axis, bit in butterfly_order():
+        dim = dims[(axis, bit)]
+        mine = (lax.axis_index(axis) >> bit) & 1
+        keep = lax.dynamic_index_in_dim(split, mine, dim, keepdims=False)
+        send = lax.dynamic_index_in_dim(split, 1 - mine, dim, keepdims=False)
+        split = keep + exchange(send, axis, bit)
+        dims = {k: (d - 1 if d > dim else d) for k, d in dims.items() if k != (axis, bit)}
+    return split.reshape(tail)
+
+
 def local(fields, kernel, norm_gain, norm_shift, cotangent):
     height, breadth, channels = fields.shape
     north = lax.axis_index("lat") == 0
@@ -52,11 +87,12 @@
         patches, kernel.reshape(9 * channels, channels), preferred_element_type=jnp.float32
     )
     count = height * breadth * lax.axis_size("lat") * lax.axis_size("lon") * (channels // G)
-    first, second = lax.psum(
-        (jnp.sum(conv_out, 0), jnp.sum(conv_out * conv_out, 0)), ("lat", "lon")
+    local_stats = jnp.concatenate(
+        [jnp.sum(conv_out, 0).reshape(G, -1).sum(1), jnp.sum(conv_out * conv_out, 0).reshape(G, -1).sum(1)]
     )
-    mean = first.reshape(G, -1).sum(1) / count
-    var = second.reshape(G, -1).sum(1) / count - mean * mean
+    stats = butterfly_sum(local_stats)
+    mean = stats[:G] / count
+    var = stats[G:] / count - mean * mean
     rstd = lax.rsqrt(var + 1e-05)
     mean_ch = jnp.repeat(mean, channels // G)
     rstd_ch = jnp.repeat(rstd, channels // G)
@@ -70,7 +106,8 @@
     )
     upstream = cotangent.astype(jnp.float32).reshape(-1, channels)
     dpre = upstream * (sigma * (1.0 + pre * (1.0 - sigma)))
-    grad_gain, grad_shift = lax.psum((jnp.sum(dpre * ghat, 0), jnp.sum(dpre, 0)), ("lat", "lon"))
+    grad_sums = butterfly_sum(jnp.concatenate([jnp.sum(dpre * ghat, 0), jnp.sum(dpre, 0)]))
+    grad_gain, grad_shift = grad_sums[:channels], grad_sums[channels:]
     mean_a = (norm_gain * grad_shift).reshape(G, -1).sum(1) / count
     mean_b = (norm_gain * grad_gain).reshape(G, -1).sum(1) / count
     dconv = (
@@ -114,11 +151,14 @@
     back = back.at[0].add(jnp.where(north, upper_term, 0.0))
     back = back.at[-1].add(jnp.where(south, lower_term, 0.0))
     grad_fields = (upstream.reshape(height, breadth, channels) + back).astype(jnp.bfloat16)
-    term_full = lax.dot_general(
-        patches, dconv, (((0,), (0,)), ((), ())), preferred_element_type=jnp.float32
+    lat_n, lon_n = lax.axis_size("lat"), lax.axis_size("lon")
+    blocks = jnp.einsum(
+        "njr,nio->ijro",
+        patches.reshape(-1, lon_n, 9 * channels // lon_n),
+        dconv.reshape(-1, lat_n, channels // lat_n),
+        preferred_element_type=jnp.float32,
     )
-    owned_cols = lax.psum_scatter(term_full, "lat", scatter_dimension=1, tiled=True)
-    grad_kernel = lax.psum_scatter(owned_cols, "lon", scatter_dimension=0, tiled=True)
+    grad_kernel = halving_sum(blocks)
     return (block_out, grad_fields, grad_kernel, grad_gain, grad_shift)
 
 

time: 1090 us -> 413 us (0.38)
  the two profiles are of different devices: /device:TPU:16 before, /device:TPU:6 now
where the time goes in v1:
time: 413 us; the launch traced here: 411 us
  waiting for transfers between devices  170 us (41%)
  starting transfers between devices  146 us (35%)
  local copies, waits for them, and re-layouts  60.1 us (15%)
  matrix products  21.8 us (5%)
  other arithmetic  11 us (3%)
    ppermute x27, waiting for transfers between devices, exchange(): return lax.ppermute(block, axis, [(i, i ^ 1 << bit) for i in range(peers)])  165 us
    ppermute x27, starting transfers between devices, exchange(): return lax.ppermute(block, axis, [(i, i ^ 1 << bit) for i in range(peers)])  99.4 us
    ppermute x4, starting transfers between devices, with_halo(): after = lax.ppermute(initial, axis, down)  27.7 us
    unnamed x45, local copies, waits for them, and re-layouts  25.4 us
    dot_general x1, matrix products, local(): jnp.einsum('njr,nio->ijro', patches.reshape(-1, lon_n, 9 * channels // lo...  15.6 us
    ppermute x4, starting transfers between devices, with_halo(): before = lax.ppermute(last, axis, up)  10.6 us
    transpose x1, local copies, waits for them, and re-layouts, local(): jnp.einsum('njr,nio->ijro', patches.reshape(-1, lon_n, 9 * channels // lo...  8.86 us
    ppermute x2, starting transfers between devices, passed_along(): return lax.ppermute(block, axis, route)  8.31 us
  transfers between devices with their start and end apart: 37, of which 26 were waited for; matrix products, arithmetic and copies ran while one was open for 8% of the time, Pallas kernels for 0%

profile of v1, /device:TPU:6, one launch (start us, length us, event | category | flops | bytes accessed | tf_op | source)
XLA Modules:
  0.0 410.6 jit_solution(13379505080357673606)
XLA Ops:
  1.8 4.3 %collective-permute-start = (bf16[64,1,256]{2,1,0:T(2,128)(2,1)S(1)}, bf16[64,1,256]{2,1,0:T(2,128)(2,1)S(1)}, u32[]{:S(2)}, u32[]{:S(2)}) collective-permute-start(bf16[64,1,256]{2,1,0:T(2,128)(2,1)S(1)} %get-tuple-element.88), channel_id=1, source_target_pairs={{0,1},{1,2},{2,3},{3,4},{4,5},{5,6},{6,7},{7,8},{8,9},{9,10},{10,1... | collective-permute-start | bytes 98312 | tf_op jit(solution)/shard_map/ppermute | solution.py:16
  6.1 14.1 %collective-permute-start.1 = (bf16[64,1,256]{2,1,0:T(2,128)(2,1)S(1)}, bf16[64,1,256]{2,1,0:T(2,128)(2,1)S(1)}, u32[]{:S(2)}, u32[]{:S(2)}) collective-permute-start(bf16[64,1,256]{2,1,0:T(2,128)(2,1)S(1)} %get-tuple-element.89), channel_id=1, source_target_pairs={{1,0},{2,1},{3,2},{4,3},{5,4},{6,5},{7,6},{8,7},{9,8},{10,9},{11,1... | collective-permute-start | bytes 98312 | tf_op jit(solution)/shard_map/ppermute | solution.py:17
  54.1 3.8 fusion.37
  61.5 4.7 %collective-permute-start.6 = (f32[64]{0:T(128)S(1)}, f32[64]{0:T(128)S(1)}, u32[]{:S(2)}, u32[]{:S(2)}) collective-permute-start(f32[64]{0:T(128)S(1)} %fusion.51), channel_id=1, source_target_pairs={{0,128},{64,192},{128,0},{192,64},{256,384},{320,448},{384,256},{4... | collective-permute-start | bytes 776 | tf_op jit(solution)/shard_map/ppermute | solution.py:38
  67.8 4.0 collective-permute-start.7
  76.0 3.5 collective-permute-done.8
  81.5 4.4 %collective-permute-done.9 = f32[64]{0:T(128)S(1)} collective-permute-done((f32[64]{0:T(128)S(1)}, f32[64]{0:T(128)S(1)}, u32[]{:S(2)}, u32[]{:S(2)}) %collective-permute-start.9) | collective-permute-done | bytes 288 | tf_op jit(solution)/shard_map/ppermute | solution.py:38
  85.9 5.4 %collective-permute-start.10 = (f32[64]{0:T(128)S(1)}, f32[64]{0:T(128)S(1)}, u32[]{:S(2)}, u32[]{:S(2)}) collective-permute-start(f32[64]{0:T(128)S(1)} %add.216), channel_id=1, source_target_pairs={{0,4},{1,5},{2,6},{3,7},{4,0},{5,1},{6,2},{7,3},{8,12},{9,13},{10,... | collective-permute-start | bytes 776 | tf_op jit(solution)/shard_map/ppermute | solution.py:38
  91.3 3.9 collective-permute-done.10
  95.2 6.6 %collective-permute-start.11 = (f32[64]{0:T(128)S(1)}, f32[64]{0:T(128)S(1)}, u32[]{:S(2)}, u32[]{:S(2)}) collective-permute-start(f32[64]{0:T(128)S(1)} %add.217), channel_id=1, source_target_pairs={{0,8},{1,9},{2,10},{3,11},{4,12},{5,13},{6,14},{7,15},{8,0},{9,1},... | collective-permute-start | bytes 776 | tf_op jit(solution)/shard_map/ppermute | solution.py:38
  110.0 4.6 %collective-permute-start.13 = (f32[64]{0:T(128)S(1)}, f32[64]{0:T(128)S(1)}, u32[]{:S(2)}, u32[]{:S(2)}) collective-permute-start(f32[64]{0:T(128)S(1)} %add.219), channel_id=1, source_target_pairs={{0,32},{1,33},{2,34},{3,35},{4,36},{5,37},{6,38},{7,39},{8,40},{9,... | collective-permute-start | bytes 776 | tf_op jit(solution)/shard_map/ppermute | solution.py:38
  121.5 3.9 collective-permute-start.15
  127.0 3.9 collective-permute-start.16
  138.8 3.6 collective-permute-start.18
  145.2 6.7 %collective-permute-start.19 = (f32[512]{0:T(512)S(1)}, f32[512]{0:T(512)S(1)}, u32[]{:S(2)}, u32[]{:S(2)}) collective-permute-start(f32[512]{0:T(512)S(1)} %add.232), channel_id=1, source_target_pairs={{0,4},{1,5},{2,6},{3,7},{4,0},{5,1},{6,2},{7,3},{8,12},{9,13},{10,... | collective-permute-start | bytes 6152 | tf_op jit(solution)/shard_map/ppermute | solution.py:38
  154.6 6.7 %collective-permute-start.20 = (f32[512]{0:T(512)S(1)}, f32[512]{0:T(512)S(1)}, u32[]{:S(2)}, u32[]{:S(2)}) collective-permute-start(f32[512]{0:T(512)S(1)} %add.233), channel_id=1, source_target_pairs={{0,8},{1,9},{2,10},{3,11},{4,12},{5,13},{6,14},{7,15},{8,0},{9,1},... | collective-permute-start | bytes 6152 | tf_op jit(solution)/shard_map/ppermute | solution.py:38
  169.4 4.8 %collective-permute-start.22 = (f32[512]{0:T(512)S(1)}, f32[512]{0:T(512)S(1)}, u32[]{:S(2)}, u32[]{:S(2)}) collective-permute-start(f32[512]{0:T(512)S(1)} %add.235), channel_id=1, source_target_pairs={{0,32},{1,33},{2,34},{3,35},{4,36},{5,37},{6,38},{7,39},{8,40},{9,... | collective-permute-start | bytes 6152 | tf_op jit(solution)/shard_map/ppermute | solution.py:38
  174.3 7.2 %reshape.250 = bf16[1024,64,36]{0,2,1:T(8,128)(2,1)} reshape(bf16[1024,2304]{0,1:T(8,128)(2,1)} %constant_dynamic-update-slice_fusion) | data formatting | bytes 9437184 | tf_op jit(solution)/shard_map/reshape | solution.py:157
  184.7 15.6 %fusion.3 = f32[8,64,36,32]{1,3,2,0:T(8,128)} fusion(bf16[1024,8,32,1]{0,2,3,1:T(8,128)(2,1)S(1)} %bitcast.191, bf16[1024,64,36]{0,2,1:T(8,128)(2,1)} %reshape.250), kind=kOutput, calls=%fused_computation.5 | convolution fusion | flops 1207959552 | bytes 7602176 | tf_op jit(solution)/shard_map/njr,nio->ijro/dot_general | solution.py:155
  200.3 8.9 %copy.34 = f32[8,64,36,32]{2,3,1,0:T(8,128)} copy(f32[8,64,36,32]{1,3,2,0:T(8,128)} %fusion.3) | data formatting | bytes 4718592 | tf_op jit(solution)/shard_map/njr,nio->ijro/transpose | solution.py:155
  211.3 10.8 %collective-permute-start.24 = (bf16[64,1,256]{2,1,0:T(2,128)(2,1)S(1)}, bf16[64,1,256]{2,1,0:T(2,128)(2,1)S(1)}, u32[]{:S(2)}, u32[]{:S(2)}) collective-permute-start(bf16[64,1,256]{2,1,0:T(2,128)(2,1)S(1)} %get-tuple-element.87), channel_id=1, source_target_pairs={{1,0},{2,1},{3,2},{4,3},{5,4},{6,5},{7,6},{8,7},{9,8},{10,9},{11,1... | collective-permute-start | bytes 98312 | tf_op jit(solution)/shard_map/ppermute | solution.py:17
  231.3 5.3 %collective-permute-start.27 = (bf16[2,18,256]{2,1,0:T(8,128)(2,1)S(1)}, bf16[2,18,256]{2,1,0:T(8,128)(2,1)S(1)}, u32[]{:S(2)}, u32[]{:S(2)}) collective-permute-start(bf16[2,18,256]{2,1,0:T(8,128)(2,1)S(1)} %pad_maximum_fusion.5), channel_id=1, source_target_pairs={{32,0},{33,1},{34,2},{35,3},{36,4},{37,5},{38,6},{39,7},{40,8},{41... | collective-permute-start | bytes 55304 | tf_op jit(solution)/shard_map/ppermute | solution.py:25
  241.8 3.9 collective-permute-start.29
  245.9 45.6 %collective-permute-done.29 = f32[2,2,2,2,2,2,2,36,32]{7,8,6,5,4,3,2,1,0:T(8,128)S(1)} collective-permute-done((f32[2,2,2,2,2,2,2,36,32]{7,8,6,5,4,3,2,1,0:T(8,128)S(1)}, f32[2,2,2,2,2,2,2,36,32]{7,8,6,5,4,3,2,1,0:T(8,128)S(1)}, u32[]{:S(2)}, u32[]{:S(2)}) %collective-permute-start.29) | collective-permute-done | bytes 589856 | tf_op jit(solution)/shard_map/ppermute | solution.py:38
  292.1 5.1 %collective-permute-start.30 = (f32[2,2,2,2,2,2,36,32]{6,7,5,4,3,2,1,0:T(8,128)S(1)}, f32[2,2,2,2,2,2,36,32]{6,7,5,4,3,2,1,0:T(8,128)S(1)}, u32[]{:S(2)}, u32[]{:S(2)}) collective-permute-start(f32[2,2,2,2,2,2,36,32]{6,7,5,4,3,2,1,0:T(8,128)S(1)} %dynamic-slice_bitcast_fusion.2), channel_id=1, source_target_pairs={{0,256},{64,320},{128,384},{192,448},{256,0},{320,64},{384,128},{4... | collective-permute-start | bytes 884744 | tf_op jit(solution)/shard_map/ppermute | solution.py:38
  300.0 43.1 %collective-permute-done.30 = f32[2,2,2,2,2,2,36,32]{6,7,5,4,3,2,1,0:T(8,128)S(1)} collective-permute-done((f32[2,2,2,2,2,2,36,32]{6,7,5,4,3,2,1,0:T(8,128)S(1)}, f32[2,2,2,2,2,2,36,32]{6,7,5,4,3,2,1,0:T(8,128)S(1)}, u32[]{:S(2)}, u32[]{:S(2)}) %collective-permute-start.30) | collective-permute-done | bytes 294944 | tf_op jit(solution)/shard_map/ppermute | solution.py:38
  345.4 13.3 %collective-permute-done.31 = f32[2,2,2,2,2,36,32]{5,6,4,3,2,1,0:T(8,128)S(1)} collective-permute-done((f32[2,2,2,2,2,36,32]{5,6,4,3,2,1,0:T(8,128)S(1)}, f32[2,2,2,2,2,36,32]{5,6,4,3,2,1,0:T(8,128)S(1)}, u32[]{:S(2)}, u32[]{:S(2)}) %collective-permute-start.31) | collective-permute-done | bytes 147488 | tf_op jit(solution)/shard_map/ppermute | solution.py:38
  360.9 13.3 %collective-permute-done.32 = f32[2,2,2,2,36,32]{4,5,3,2,1,0:T(8,128)S(1)} collective-permute-done((f32[2,2,2,2,36,32]{4,5,3,2,1,0:T(8,128)S(1)}, f32[2,2,2,2,36,32]{4,5,3,2,1,0:T(8,128)S(1)}, u32[]{:S(2)}, u32[]{:S(2)}) %collective-permute-start.32) | collective-permute-done | bytes 73760 | tf_op jit(solution)/shard_map/ppermute | solution.py:38
  374.3 3.8 collective-permute-start.33
  378.3 8.1 %collective-permute-done.33 = f32[2,2,2,36,32]{3,4,2,1,0:T(8,128)S(1)} collective-permute-done((f32[2,2,2,36,32]{3,4,2,1,0:T(8,128)S(1)}, f32[2,2,2,36,32]{3,4,2,1,0:T(8,128)S(1)}, u32[]{:S(2)}, u32[]{:S(2)}) %collective-permute-start.33) | collective-permute-done | bytes 36896 | tf_op jit(solution)/shard_map/ppermute | solution.py:38
  386.4 5.1 %collective-permute-start.34 = (f32[2,2,36,32]{2,3,1,0:T(8,128)S(1)}, f32[2,2,36,32]{2,3,1,0:T(8,128)S(1)}, u32[]{:S(2)}, u32[]{:S(2)}) collective-permute-start(f32[2,2,36,32]{2,3,1,0:T(8,128)S(1)} %dynamic-slice_bitcast_fusion.6), channel_id=1, source_target_pairs={{0,8},{1,9},{2,10},{3,11},{4,12},{5,13},{6,14},{7,15},{8,0},{9,1},... | collective-permute-start | bytes 55304 | tf_op jit(solution)/shard_map/ppermute | solution.py:38
  391.7 5.3 %collective-permute-done.34 = f32[2,2,36,32]{2,3,1,0:T(8,128)S(1)} collective-permute-done((f32[2,2,36,32]{2,3,1,0:T(8,128)S(1)}, f32[2,2,36,32]{2,3,1,0:T(8,128)S(1)}, u32[]{:S(2)}, u32[]{:S(2)}) %collective-permute-start.34) | collective-permute-done | bytes 18464 | tf_op jit(solution)/shard_map/ppermute | solution.py:38
  (186 shorter events, 125.8 us)
Async XLA Ops:
  1.8 20.0 %collective-permute-start = (bf16[64,1,256]{2,1,0:T(2,128)(2,1)S(1)}, bf16[64,1,256]{2,1,0:T(2,128)(2,1)S(1)}, u32[]{:S(2)}, u32[]{:S(2)}) collective-permute-start(bf16[64,1,256]{2,1,0:T(2,128)(2,1)S(1)} %get-tuple-element.88), channel_id=1, source_target_pairs={{0,1},{1,2},{2,3},{3,4},{4,5},{5,6},{6,7},{7,8},{8,9},{9,10},{10,1... | collective-permute-start | bytes 98312 | tf_op jit(solution)/shard_map/ppermute | solution.py:16
  6.1 16.9 %collective-permute-start.1 = (bf16[64,1,256]{2,1,0:T(2,128)(2,1)S(1)}, bf16[64,1,256]{2,1,0:T(2,128)(2,1)S(1)}, u32[]{:S(2)}, u32[]{:S(2)}) collective-permute-start(bf16[64,1,256]{2,1,0:T(2,128)(2,1)S(1)} %get-tuple-element.89), channel_id=1, source_target_pairs={{1,0},{2,1},{3,2},{4,3},{5,4},{6,5},{7,6},{8,7},{9,8},{10,9},{11,1... | collective-permute-start | bytes 98312 | tf_op jit(solution)/shard_map/ppermute | solution.py:17
  23.7 5.7 %collective-permute-start.2 = (bf16[1,18,256]{2,1,0:T(8,128)(2,1)S(1)}, bf16[1,18,256]{2,1,0:T(8,128)(2,1)S(1)}, u32[]{:S(2)}, u32[]{:S(2)}) collective-permute-start(bf16[1,18,256]{2,1,0:T(8,128)(2,1)S(1)} %get-tuple-element.82), channel_id=1, source_target_pairs={{0,64},{64,128},{128,192},{192,256},{256,320},{320,384},{384,448},... | collective-permute-start | bytes 27656 | tf_op jit(solution)/shard_map/ppermute | solution.py:16
  26.3 7.2 %collective-permute-start.4 = (bf16[2,18,256]{2,1,0:T(8,128)(2,1)S(1)}, bf16[2,18,256]{2,1,0:T(8,128)(2,1)S(1)}, u32[]{:S(2)}, u32[]{:S(2)}) collective-permute-start(bf16[2,18,256]{2,1,0:T(8,128)(2,1)S(1)} %pad_maximum_fusion.4), channel_id=1, source_target_pairs={{32,0},{33,1},{34,2},{35,3},{36,4},{37,5},{38,6},{39,7},{40,8},{41... | collective-permute-start | bytes 55304 | tf_op jit(solution)/shard_map/ppermute | solution.py:25
  61.5 6.3 %collective-permute-start.6 = (f32[64]{0:T(128)S(1)}, f32[64]{0:T(128)S(1)}, u32[]{:S(2)}, u32[]{:S(2)}) collective-permute-start(f32[64]{0:T(128)S(1)} %fusion.51), channel_id=1, source_target_pairs={{0,128},{64,192},{128,0},{192,64},{256,384},{320,448},{384,256},{4... | collective-permute-start | bytes 776 | tf_op jit(solution)/shard_map/ppermute | solution.py:38
  67.8 6.3 %collective-permute-start.7 = (f32[64]{0:T(128)S(1)}, f32[64]{0:T(128)S(1)}, u32[]{:S(2)}, u32[]{:S(2)}) collective-permute-start(f32[64]{0:T(128)S(1)} %add.213), channel_id=1, source_target_pairs={{0,256},{64,320},{128,384},{192,448},{256,0},{320,64},{384,128},{4... | collective-permute-start | bytes 776 | tf_op jit(solution)/shard_map/ppermute | solution.py:38
  79.5 6.3 %collective-permute-start.9 = (f32[64]{0:T(128)S(1)}, f32[64]{0:T(128)S(1)}, u32[]{:S(2)}, u32[]{:S(2)}) collective-permute-start(f32[64]{0:T(128)S(1)} %add.215), channel_id=1, source_target_pairs={{0,2},{1,3},{2,0},{3,1},{4,6},{5,7},{6,4},{7,5},{8,10},{9,11},{10,... | collective-permute-start | bytes 776 | tf_op jit(solution)/shard_map/ppermute | solution.py:38
  85.9 9.3 %collective-permute-start.10 = (f32[64]{0:T(128)S(1)}, f32[64]{0:T(128)S(1)}, u32[]{:S(2)}, u32[]{:S(2)}) collective-permute-start(f32[64]{0:T(128)S(1)} %add.216), channel_id=1, source_target_pairs={{0,4},{1,5},{2,6},{3,7},{4,0},{5,1},{6,2},{7,3},{8,12},{9,13},{10,... | collective-permute-start | bytes 776 | tf_op jit(solution)/shard_map/ppermute | solution.py:38
  95.2 9.3 %collective-permute-start.11 = (f32[64]{0:T(128)S(1)}, f32[64]{0:T(128)S(1)}, u32[]{:S(2)}, u32[]{:S(2)}) collective-permute-start(f32[64]{0:T(128)S(1)} %add.217), channel_id=1, source_target_pairs={{0,8},{1,9},{2,10},{3,11},{4,12},{5,13},{6,14},{7,15},{8,0},{9,1},... | collective-permute-start | bytes 776 | tf_op jit(solution)/shard_map/ppermute | solution.py:38
  110.0 6.9 %collective-permute-start.13 = (f32[64]{0:T(128)S(1)}, f32[64]{0:T(128)S(1)}, u32[]{:S(2)}, u32[]{:S(2)}) collective-permute-start(f32[64]{0:T(128)S(1)} %add.219), channel_id=1, source_target_pairs={{0,32},{1,33},{2,34},{3,35},{4,36},{5,37},{6,38},{7,39},{8,40},{9,... | collective-permute-start | bytes 776 | tf_op jit(solution)/shard_map/ppermute | solution.py:38
  121.5 5.5 %collective-permute-start.15 = (f32[512]{0:T(512)S(1)}, f32[512]{0:T(512)S(1)}, u32[]{:S(2)}, u32[]{:S(2)}) collective-permute-start(f32[512]{0:T(512)S(1)} %fusion.35), channel_id=1, source_target_pairs={{0,128},{64,192},{128,0},{192,64},{256,384},{320,448},{384,256},{4... | collective-permute-start | bytes 6152 | tf_op jit(solution)/shard_map/ppermute | solution.py:38
  127.0 6.4 %collective-permute-start.16 = (f32[512]{0:T(512)S(1)}, f32[512]{0:T(512)S(1)}, u32[]{:S(2)}, u32[]{:S(2)}) collective-permute-start(f32[512]{0:T(512)S(1)} %add.229), channel_id=1, source_target_pairs={{0,256},{64,320},{128,384},{192,448},{256,0},{320,64},{384,128},{4... | collective-permute-start | bytes 6152 | tf_op jit(solution)/shard_map/ppermute | solution.py:38
  133.4 5.5 %collective-permute-start.17 = (f32[512]{0:T(512)S(1)}, f32[512]{0:T(512)S(1)}, u32[]{:S(2)}, u32[]{:S(2)}) collective-permute-start(f32[512]{0:T(512)S(1)} %add.230), channel_id=1, source_target_pairs={{0,1},{1,0},{2,3},{3,2},{4,5},{5,4},{6,7},{7,6},{8,9},{9,8},{10,11... | collective-permute-start | bytes 6152 | tf_op jit(solution)/shard_map/ppermute | solution.py:38
  138.8 6.4 %collective-permute-start.18 = (f32[512]{0:T(512)S(1)}, f32[512]{0:T(512)S(1)}, u32[]{:S(2)}, u32[]{:S(2)}) collective-permute-start(f32[512]{0:T(512)S(1)} %add.231), channel_id=1, source_target_pairs={{0,2},{1,3},{2,0},{3,1},{4,6},{5,7},{6,4},{7,5},{8,10},{9,11},{10,... | collective-permute-start | bytes 6152 | tf_op jit(solution)/shard_map/ppermute | solution.py:38
  145.2 9.4 %collective-permute-start.19 = (f32[512]{0:T(512)S(1)}, f32[512]{0:T(512)S(1)}, u32[]{:S(2)}, u32[]{:S(2)}) collective-permute-start(f32[512]{0:T(512)S(1)} %add.232), channel_id=1, source_target_pairs={{0,4},{1,5},{2,6},{3,7},{4,0},{5,1},{6,2},{7,3},{8,12},{9,13},{10,... | collective-permute-start | bytes 6152 | tf_op jit(solution)/shard_map/ppermute | solution.py:38
  154.6 9.4 %collective-permute-start.20 = (f32[512]{0:T(512)S(1)}, f32[512]{0:T(512)S(1)}, u32[]{:S(2)}, u32[]{:S(2)}) collective-permute-start(f32[512]{0:T(512)S(1)} %add.233), channel_id=1, source_target_pairs={{0,8},{1,9},{2,10},{3,11},{4,12},{5,13},{6,14},{7,15},{8,0},{9,1},... | collective-permute-start | bytes 6152 | tf_op jit(solution)/shard_map/ppermute | solution.py:38
  164.0 5.5 %collective-permute-start.21 = (f32[512]{0:T(512)S(1)}, f32[512]{0:T(512)S(1)}, u32[]{:S(2)}, u32[]{:S(2)}) collective-permute-start(f32[512]{0:T(512)S(1)} %add.234), channel_id=1, source_target_pairs={{0,16},{1,17},{2,18},{3,19},{4,20},{5,21},{6,22},{7,23},{8,24},{9,... | collective-permute-start | bytes 6152 | tf_op jit(solution)/shard_map/ppermute | solution.py:38
  169.4 12.1 %collective-permute-start.22 = (f32[512]{0:T(512)S(1)}, f32[512]{0:T(512)S(1)}, u32[]{:S(2)}, u32[]{:S(2)}) collective-permute-start(f32[512]{0:T(512)S(1)} %add.235), channel_id=1, source_target_pairs={{0,32},{1,33},{2,34},{3,35},{4,36},{5,37},{6,38},{7,39},{8,40},{9,... | collective-permute-start | bytes 6152 | tf_op jit(solution)/shard_map/ppermute | solution.py:38
  209.3 17.3 %collective-permute-start.23 = (bf16[64,1,256]{2,1,0:T(2,128)(2,1)S(1)}, bf16[64,1,256]{2,1,0:T(2,128)(2,1)S(1)}, u32[]{:S(2)}, u32[]{:S(2)}) collective-permute-start(bf16[64,1,256]{2,1,0:T(2,128)(2,1)S(1)} %get-tuple-element.86), channel_id=1, source_target_pairs={{0,1},{1,2},{2,3},{3,4},{4,5},{5,6},{6,7},{7,8},{8,9},{9,10},{10,1... | collective-permute-start | bytes 98312 | tf_op jit(solution)/shard_map/ppermute | solution.py:16
  211.3 15.4 %collective-permute-start.24 = (bf16[64,1,256]{2,1,0:T(2,128)(2,1)S(1)}, bf16[64,1,256]{2,1,0:T(2,128)(2,1)S(1)}, u32[]{:S(2)}, u32[]{:S(2)}) collective-permute-start(bf16[64,1,256]{2,1,0:T(2,128)(2,1)S(1)} %get-tuple-element.87), channel_id=1, source_target_pairs={{1,0},{2,1},{3,2},{4,3},{5,4},{6,5},{7,6},{8,7},{9,8},{10,9},{11,1... | collective-permute-start | bytes 98312 | tf_op jit(solution)/shard_map/ppermute | solution.py:17
  224.7 14.1 %collective-permute-start.28 = (f32[2,2,2,2,2,2,2,2,36,32]{8,9,7,6,5,4,3,2,1,0:T(8,128)S(1)}, f32[2,2,2,2,2,2,2,2,36,32]{8,9,7,6,5,4,3,2,1,0:T(8,128)S(1)}, u32[]{:S(2)}, u32[]{:S(2)}) collective-permute-start(f32[2,2,2,2,2,2,2,2,36,32]{8,9,7,6,5,4,3,2,1,0:T(8,128)S(1)} %dynamic-slice_bitcast_fusion), channel_id=1, source_target_pairs={{0,64},{64,0},{128,192},{192,128},{256,320},{320,256},{384,448},{4... | collective-permute-start | bytes 3538952 | tf_op jit(solution)/shard_map/ppermute | solution.py:38
  226.7 10.4 %collective-permute-start.25 = (bf16[1,18,256]{2,1,0:T(8,128)(2,1)S(1)}, bf16[1,18,256]{2,1,0:T(8,128)(2,1)S(1)}, u32[]{:S(2)}, u32[]{:S(2)}) collective-permute-start(bf16[1,18,256]{2,1,0:T(8,128)(2,1)S(1)} %get-tuple-element.81), channel_id=1, source_target_pairs={{64,0},{128,64},{192,128},{256,192},{320,256},{384,320},{448,384},... | collective-permute-start | bytes 27656 | tf_op jit(solution)/shard_map/ppermute | solution.py:17
  228.3 8.8 %collective-permute-start.26 = (bf16[1,18,256]{2,1,0:T(8,128)(2,1)S(1)}, bf16[1,18,256]{2,1,0:T(8,128)(2,1)S(1)}, u32[]{:S(2)}, u32[]{:S(2)}) collective-permute-start(bf16[1,18,256]{2,1,0:T(8,128)(2,1)S(1)} %get-tuple-element.80), channel_id=1, source_target_pairs={{0,64},{64,128},{128,192},{192,256},{256,320},{320,384},{384,448},... | collective-permute-start | bytes 27656 | tf_op jit(solution)/shard_map/ppermute | solution.py:16
  231.3 67.4 %collective-permute-start.27 = (bf16[2,18,256]{2,1,0:T(8,128)(2,1)S(1)}, bf16[2,18,256]{2,1,0:T(8,128)(2,1)S(1)}, u32[]{:S(2)}, u32[]{:S(2)}) collective-permute-start(bf16[2,18,256]{2,1,0:T(8,128)(2,1)S(1)} %pad_maximum_fusion.5), channel_id=1, source_target_pairs={{32,0},{33,1},{34,2},{35,3},{36,4},{37,5},{38,6},{39,7},{40,8},{41... | collective-permute-start | bytes 55304 | tf_op jit(solution)/shard_map/ppermute | solution.py:25
  241.8 49.7 %collective-permute-start.29 = (f32[2,2,2,2,2,2,2,36,32]{7,8,6,5,4,3,2,1,0:T(8,128)S(1)}, f32[2,2,2,2,2,2,2,36,32]{7,8,6,5,4,3,2,1,0:T(8,128)S(1)}, u32[]{:S(2)}, u32[]{:S(2)}) collective-permute-start(f32[2,2,2,2,2,2,2,36,32]{7,8,6,5,4,3,2,1,0:T(8,128)S(1)} %dynamic-slice_bitcast_fusion.1), channel_id=1, source_target_pairs={{0,128},{64,192},{128,0},{192,64},{256,384},{320,448},{384,256},{4... | collective-permute-start | bytes 1769480 | tf_op jit(solution)/shard_map/ppermute | solution.py:38
  292.1 51.0 %collective-permute-start.30 = (f32[2,2,2,2,2,2,36,32]{6,7,5,4,3,2,1,0:T(8,128)S(1)}, f32[2,2,2,2,2,2,36,32]{6,7,5,4,3,2,1,0:T(8,128)S(1)}, u32[]{:S(2)}, u32[]{:S(2)}) collective-permute-start(f32[2,2,2,2,2,2,36,32]{6,7,5,4,3,2,1,0:T(8,128)S(1)} %dynamic-slice_bitcast_fusion.2), channel_id=1, source_target_pairs={{0,256},{64,320},{128,384},{192,448},{256,0},{320,64},{384,128},{4... | collective-permute-start | bytes 884744 | tf_op jit(solution)/shard_map/ppermute | solution.py:38
  343.4 15.3 %collective-permute-start.31 = (f32[2,2,2,2,2,36,32]{5,6,4,3,2,1,0:T(8,128)S(1)}, f32[2,2,2,2,2,36,32]{5,6,4,3,2,1,0:T(8,128)S(1)}, u32[]{:S(2)}, u32[]{:S(2)}) collective-permute-start(f32[2,2,2,2,2,36,32]{5,6,4,3,2,1,0:T(8,128)S(1)} %dynamic-slice_bitcast_fusion.3), channel_id=1, source_target_pairs={{0,1},{1,0},{2,3},{3,2},{4,5},{5,4},{6,7},{7,6},{8,9},{9,8},{10,11... | collective-permute-start | bytes 442376 | tf_op jit(solution)/shard_map/ppermute | solution.py:38
  358.8 15.3 %collective-permute-start.32 = (f32[2,2,2,2,36,32]{4,5,3,2,1,0:T(8,128)S(1)}, f32[2,2,2,2,36,32]{4,5,3,2,1,0:T(8,128)S(1)}, u32[]{:S(2)}, u32[]{:S(2)}) collective-permute-start(f32[2,2,2,2,36,32]{4,5,3,2,1,0:T(8,128)S(1)} %dynamic-slice_bitcast_fusion.4), channel_id=1, source_target_pairs={{0,2},{1,3},{2,0},{3,1},{4,6},{5,7},{6,4},{7,5},{8,10},{9,11},{10,... | collective-permute-start | bytes 221192 | tf_op jit(solution)/shard_map/ppermute | solution.py:38
  374.3 12.1 %collective-permute-start.33 = (f32[2,2,2,36,32]{3,4,2,1,0:T(8,128)S(1)}, f32[2,2,2,36,32]{3,4,2,1,0:T(8,128)S(1)}, u32[]{:S(2)}, u32[]{:S(2)}) collective-permute-start(f32[2,2,2,36,32]{3,4,2,1,0:T(8,128)S(1)} %dynamic-slice_bitcast_fusion.5), channel_id=1, source_target_pairs={{0,4},{1,5},{2,6},{3,7},{4,0},{5,1},{6,2},{7,3},{8,12},{9,13},{10,... | collective-permute-start | bytes 110600 | tf_op jit(solution)/shard_map/ppermute | solution.py:38
  386.4 10.6 %collective-permute-start.34 = (f32[2,2,36,32]{2,3,1,0:T(8,128)S(1)}, f32[2,2,36,32]{2,3,1,0:T(8,128)S(1)}, u32[]{:S(2)}, u32[]{:S(2)}) collective-permute-start(f32[2,2,36,32]{2,3,1,0:T(8,128)S(1)} %dynamic-slice_bitcast_fusion.6), channel_id=1, source_target_pairs={{0,8},{1,9},{2,10},{3,11},{4,12},{5,13},{6,14},{7,15},{8,0},{9,1},... | collective-permute-start | bytes 55304 | tf_op jit(solution)/shard_map/ppermute | solution.py:38
  397.1 5.8 %collective-permute-start.35 = (f32[2,36,32]{1,2,0:T(8,128)S(1)}, f32[2,36,32]{1,2,0:T(8,128)S(1)}, u32[]{:S(2)}, u32[]{:S(2)}) collective-permute-start(f32[2,36,32]{1,2,0:T(8,128)S(1)} %dynamic-slice_bitcast_fusion.7), channel_id=1, source_target_pairs={{0,16},{1,17},{2,18},{3,19},{4,20},{5,21},{6,22},{7,23},{8,24},{9,... | collective-permute-start | bytes 27656 | tf_op jit(solution)/shard_map/ppermute | solution.py:38
  402.9 7.1 %collective-permute-start.36 = (f32[36,32]{0,1:T(8,128)S(1)}, f32[36,32]{0,1:T(8,128)S(1)}, u32[]{:S(2)}, u32[]{:S(2)}) collective-permute-start(f32[36,32]{0,1:T(8,128)S(1)} %dynamic-slice_bitcast_fusion.8), channel_id=1, source_target_pairs={{0,32},{1,33},{2,34},{3,35},{4,36},{5,37},{6,38},{7,39},{8,40},{9,... | collective-permute-start | bytes 13832 | tf_op jit(solution)/shard_map/ppermute | solution.py:38
  (15 other events, 248.1 us)

commit v2 on v1

--- a/solution.py
+++ b/solution.py
@@ -51,21 +51,35 @@
     return value
 
 
-def halving_sum(blocks):
-    lat_n, lon_n = blocks.shape[0], blocks.shape[1]
-    lat_bits, lon_bits = (lat_n - 1).bit_length(), (lon_n - 1).bit_length()
-    tail = blocks.shape[2:]
-    split = blocks.reshape((2,) * lat_bits + (2,) * lon_bits + tail)
-    dims = {("lat", b): lat_bits - 1 - b for b in range(lat_bits)}
-    dims.update({("lon", b): lat_bits + lon_bits - 1 - b for b in range(lon_bits)})
-    for axis, bit in butterfly_order():
-        dim = dims[(axis, bit)]
-        mine = (lax.axis_index(axis) >> bit) & 1
+def halving_sum(term):
+    lon_n = term.shape[0]
+    lon_bits = (lon_n - 1).bit_length()
+    lat_bits = (lax.axis_size("lat") - 1).bit_length()
+    split = term.reshape((2,) * lon_bits + term.shape[1:])
+    dims = {b: lon_bits - 1 - b for b in range(lon_bits)}
+
+    def row_round(split, bit, dims):
+        dim = dims[bit]
+        mine = (lax.axis_index("lon") >> bit) & 1
         keep = lax.dynamic_index_in_dim(split, mine, dim, keepdims=False)
         send = lax.dynamic_index_in_dim(split, 1 - mine, dim, keepdims=False)
-        split = keep + exchange(send, axis, bit)
-        dims = {k: (d - 1 if d > dim else d) for k, d in dims.items() if k != (axis, bit)}
-    return split.reshape(tail)
+        dims = {k: (d - 1 if d > dim else d) for k, d in dims.items() if k != bit}
+        return keep + exchange(send, "lon", bit), dims
+
+    def col_round(split, bit):
+        half = split.shape[-1] // 2
+        mine = (lax.axis_index("lat") >> bit) & 1
+        keep = lax.dynamic_slice_in_dim(split, mine * half, half, axis=split.ndim - 1)
+        send = lax.dynamic_slice_in_dim(split, (1 - mine) * half, half, axis=split.ndim - 1)
+        return keep + exchange(send, "lat", bit)
+
+    split = col_round(split, 0)
+    row_order = [0, 4, 1, 5, 2, 3] if lon_bits == 6 else list(range(lon_bits))
+    for bit in row_order:
+        split, dims = row_round(split, bit, dims)
+    for bit in range(1, lat_bits):
+        split = col_round(split, bit)
+    return split
 
 
 def local(fields, kernel, norm_gain, norm_shift, cotangent):
@@ -152,10 +166,13 @@
     back = back.at[-1].add(jnp.where(south, lower_term, 0.0))
     grad_fields = (upstream.reshape(height, breadth, channels) + back).astype(jnp.bfloat16)
     lat_n, lon_n = lax.axis_size("lat"), lax.axis_size("lon")
+    lat_bits = (lat_n - 1).bit_length()
+    lat_major = dconv.reshape((-1,) + (2,) * lat_bits + (channels // lat_n,))
+    lat_major = lat_major.transpose((0,) + tuple(range(lat_bits, 0, -1)) + (lat_bits + 1,))
     blocks = jnp.einsum(
-        "njr,nio->ijro",
+        "njr,nc->jrc",
         patches.reshape(-1, lon_n, 9 * channels // lon_n),
-        dconv.reshape(-1, lat_n, channels // lat_n),
+        lat_major.reshape(-1, channels),
         preferred_element_type=jnp.float32,
     )
     grad_kernel = halving_sum(blocks)

time: 413 us -> 302 us (0.73)
  waiting for transfers between devices: 170 us -> 94.7 us
  local copies, waits for them, and re-layouts: 60.1 us -> 42 us
  matrix products: 21.8 us -> 10.3 us
  starting transfers between devices: 146 us -> 141 us
    ppermute x27, waiting for transfers between devices: 165 us -> 89.4 us  [exchange(): return lax.ppermute(block, axis, [(i, i ^ 1 << bit) for i in range(peers)])]
    dot_general x1, matrix products: 15.6 us -> 4.13 us  [local(): jnp.einsum('njr,nc->jrc', patches.reshape(-1, lon_n, 9 * channels // lon_...]
    transpose x1, local copies, waits for them, and re-layouts: 8.86 us -> 0.04 us  [local(): lat_major.transpose((0,) + tuple(range(lat_bits, 0, -1)) + (lat_bits + 1,))]
    unnamed x45, local copies, waits for them, and re-layouts: 25.4 us -> 17.6 us
    ppermute x27, starting transfers between devices: 99.4 us -> 94.2 us  [exchange(): return lax.ppermute(block, axis, [(i, i ^ 1 << bit) for i in range(peers)])]
  transfers between devices with their start and end apart: 37 -> 37, of which waited for: 26 -> 28; matrix products, arithmetic and copies ran while one was open for 8% -> 9% of each run, Pallas kernels for 0% -> 0%
where the time goes in v2:
time: 302 us; the launch traced here: 298 us
  starting transfers between devices  141 us (47%)
  waiting for transfers between devices  94.7 us (31%)
  local copies, waits for them, and re-layouts  42 us (14%)
  matrix products  10.3 us (3%)
  other arithmetic  9.22 us (3%)
    ppermute x27, starting transfers between devices, exchange(): return lax.ppermute(block, axis, [(i, i ^ 1 << bit) for i in range(peers)])  94.2 us
    ppermute x27, waiting for transfers between devices, exchange(): return lax.ppermute(block, axis, [(i, i ^ 1 << bit) for i in range(peers)])  89.4 us
    ppermute x4, starting transfers between devices, with_halo(): after = lax.ppermute(initial, axis, down)  27.7 us
    unnamed x45, local copies, waits for them, and re-layouts  17.6 us
    ppermute x4, starting transfers between devices, with_halo(): before = lax.ppermute(last, axis, up)  10.5 us
    reshape x9, local copies, waits for them, and re-layouts, local(): merged[tap_row:tap_row + height, tap_col:tap_col + breadth]  8.96 us
    ppermute x2, starting transfers between devices, passed_along(): return lax.ppermute(block, axis, route)  8.09 us
    reshape x1, local copies, waits for them, and re-layouts, local(): patches.reshape(-1, lon_n, 9 * channels // lon_n)  7.23 us
  transfers between devices with their start and end apart: 37, of which 28 were waited for; matrix products, arithmetic and copies ran while one was open for 9% of the time, Pallas kernels for 0%

profile of v2, /device:TPU:6, one launch (start us, length us, event | category | flops | bytes accessed | tf_op | source)
XLA Modules:
  0.0 298.2 jit_solution(17281953640369013997)
XLA Ops:
  1.8 4.3 %collective-permute-start = (bf16[64,1,256]{2,1,0:T(2,128)(2,1)S(1)}, bf16[64,1,256]{2,1,0:T(2,128)(2,1)S(1)}, u32[]{:S(2)}, u32[]{:S(2)}) collective-permute-start(bf16[64,1,256]{2,1,0:T(2,128)(2,1)S(1)} %get-tuple-element.105), channel_id=1, source_target_pairs={{0,1},{1,2},{2,3},{3,4},{4,5},{5,6},{6,7},{7,8},{8,9},{9,10},{10,1... | collective-permute-start | bytes 98312 | tf_op jit(solution)/shard_map/ppermute | solution.py:16
  6.1 14.1 %collective-permute-start.1 = (bf16[64,1,256]{2,1,0:T(2,128)(2,1)S(1)}, bf16[64,1,256]{2,1,0:T(2,128)(2,1)S(1)}, u32[]{:S(2)}, u32[]{:S(2)}) collective-permute-start(bf16[64,1,256]{2,1,0:T(2,128)(2,1)S(1)} %get-tuple-element.106), channel_id=1, source_target_pairs={{1,0},{2,1},{3,2},{4,3},{5,4},{6,5},{7,6},{8,7},{9,8},{10,9},{11,1... | collective-permute-start | bytes 98312 | tf_op jit(solution)/shard_map/ppermute | solution.py:17
  26.3 3.0 %collective-permute-start.4 = (bf16[2,18,256]{2,1,0:T(8,128)(2,1)S(1)}, bf16[2,18,256]{2,1,0:T(8,128)(2,1)S(1)}, u32[]{:S(2)}, u32[]{:S(2)}) collective-permute-start(bf16[2,18,256]{2,1,0:T(8,128)(2,1)S(1)} %pad_maximum_fusion.4), channel_id=1, source_target_pairs={{32,0},{33,1},{34,2},{35,3},{36,4},{37,5},{38,6},{39,7},{40,8},{41... | collective-permute-start | bytes 55304 | tf_op jit(solution)/shard_map/ppermute | solution.py:25
  54.9 3.8 %fusion.31 = (f32[256]{0:T(256)S(1)}, f32[256]{0:T(256)S(1)}, f32[1024,256]{1,0:T(8,128)S(1)}) fusion(bf16[1024,2304]{0,1:T(8,128)(2,1)} %constant_dynamic-update-slice_fusion, bf16[2304,256]{1,0:T(8,128)(2,1)S(1)} %bitcast.158), kind=kOutput, calls=%fused_computation.122 | convolution fusion | flops 1208745472 | bytes 6948864 | tf_op jit(solution)/shard_map/dot_general | solution.py:100
  62.3 4.7 %collective-permute-start.6 = (f32[64]{0:T(128)S(1)}, f32[64]{0:T(128)S(1)}, u32[]{:S(2)}, u32[]{:S(2)}) collective-permute-start(f32[64]{0:T(128)S(1)} %fusion.47), channel_id=1, source_target_pairs={{0,128},{64,192},{128,0},{192,64},{256,384},{320,448},{384,256},{4... | collective-permute-start | bytes 776 | tf_op jit(solution)/shard_map/ppermute | solution.py:38
  68.5 4.0 %collective-permute-start.7 = (f32[64]{0:T(128)S(1)}, f32[64]{0:T(128)S(1)}, u32[]{:S(2)}, u32[]{:S(2)}) collective-permute-start(f32[64]{0:T(128)S(1)} %add.207), channel_id=1, source_target_pairs={{0,256},{64,320},{128,384},{192,448},{256,0},{320,64},{384,128},{4... | collective-permute-start | bytes 776 | tf_op jit(solution)/shard_map/ppermute | solution.py:38
  76.8 3.5 %collective-permute-done.8 = f32[64]{0:T(128)S(1)} collective-permute-done((f32[64]{0:T(128)S(1)}, f32[64]{0:T(128)S(1)}, u32[]{:S(2)}, u32[]{:S(2)}) %collective-permute-start.8) | collective-permute-done | bytes 288 | tf_op jit(solution)/shard_map/ppermute | solution.py:38
  82.2 4.4 %collective-permute-done.9 = f32[64]{0:T(128)S(1)} collective-permute-done((f32[64]{0:T(128)S(1)}, f32[64]{0:T(128)S(1)}, u32[]{:S(2)}, u32[]{:S(2)}) %collective-permute-start.9) | collective-permute-done | bytes 288 | tf_op jit(solution)/shard_map/ppermute | solution.py:38
  86.6 5.4 %collective-permute-start.10 = (f32[64]{0:T(128)S(1)}, f32[64]{0:T(128)S(1)}, u32[]{:S(2)}, u32[]{:S(2)}) collective-permute-start(f32[64]{0:T(128)S(1)} %add.210), channel_id=1, source_target_pairs={{0,4},{1,5},{2,6},{3,7},{4,0},{5,1},{6,2},{7,3},{8,12},{9,13},{10,... | collective-permute-start | bytes 776 | tf_op jit(solution)/shard_map/ppermute | solution.py:38
  92.1 3.9 %collective-permute-done.10 = f32[64]{0:T(128)S(1)} collective-permute-done((f32[64]{0:T(128)S(1)}, f32[64]{0:T(128)S(1)}, u32[]{:S(2)}, u32[]{:S(2)}) %collective-permute-start.10) | collective-permute-done | bytes 288 | tf_op jit(solution)/shard_map/ppermute | solution.py:38
  95.9 6.6 %collective-permute-start.11 = (f32[64]{0:T(128)S(1)}, f32[64]{0:T(128)S(1)}, u32[]{:S(2)}, u32[]{:S(2)}) collective-permute-start(f32[64]{0:T(128)S(1)} %add.211), channel_id=1, source_target_pairs={{0,8},{1,9},{2,10},{3,11},{4,12},{5,13},{6,14},{7,15},{8,0},{9,1},... | collective-permute-start | bytes 776 | tf_op jit(solution)/shard_map/ppermute | solution.py:38
  110.7 4.5 %collective-permute-start.13 = (f32[64]{0:T(128)S(1)}, f32[64]{0:T(128)S(1)}, u32[]{:S(2)}, u32[]{:S(2)}) collective-permute-start(f32[64]{0:T(128)S(1)} %add.213), channel_id=1, source_target_pairs={{0,32},{1,33},{2,34},{3,35},{4,36},{5,37},{6,38},{7,39},{8,40},{9,... | collective-permute-start | bytes 776 | tf_op jit(solution)/shard_map/ppermute | solution.py:38
  121.8 3.9 %collective-permute-start.15 = (f32[512]{0:T(512)S(1)}, f32[512]{0:T(512)S(1)}, u32[]{:S(2)}, u32[]{:S(2)}) collective-permute-start(f32[512]{0:T(512)S(1)} %fusion.29), channel_id=1, source_target_pairs={{0,128},{64,192},{128,0},{192,64},{256,384},{320,448},{384,256},{4... | collective-permute-start | bytes 6152 | tf_op jit(solution)/shard_map/ppermute | solution.py:38
  127.2 4.0 %collective-permute-start.16 = (f32[512]{0:T(512)S(1)}, f32[512]{0:T(512)S(1)}, u32[]{:S(2)}, u32[]{:S(2)}) collective-permute-start(f32[512]{0:T(512)S(1)} %add.223), channel_id=1, source_target_pairs={{0,256},{64,320},{128,384},{192,448},{256,0},{320,64},{384,128},{4... | collective-permute-start | bytes 6152 | tf_op jit(solution)/shard_map/ppermute | solution.py:38
  139.1 3.6 %collective-permute-start.18 = (f32[512]{0:T(512)S(1)}, f32[512]{0:T(512)S(1)}, u32[]{:S(2)}, u32[]{:S(2)}) collective-permute-start(f32[512]{0:T(512)S(1)} %add.225), channel_id=1, source_target_pairs={{0,2},{1,3},{2,0},{3,1},{4,6},{5,7},{6,4},{7,5},{8,10},{9,11},{10,... | collective-permute-start | bytes 6152 | tf_op jit(solution)/shard_map/ppermute | solution.py:38
  145.4 6.6 %collective-permute-start.19 = (f32[512]{0:T(512)S(1)}, f32[512]{0:T(512)S(1)}, u32[]{:S(2)}, u32[]{:S(2)}) collective-permute-start(f32[512]{0:T(512)S(1)} %add.226), channel_id=1, source_target_pairs={{0,4},{1,5},{2,6},{3,7},{4,0},{5,1},{6,2},{7,3},{8,12},{9,13},{10,... | collective-permute-start | bytes 6152 | tf_op jit(solution)/shard_map/ppermute | solution.py:38
  154.8 6.6 %collective-permute-start.20 = (f32[512]{0:T(512)S(1)}, f32[512]{0:T(512)S(1)}, u32[]{:S(2)}, u32[]{:S(2)}) collective-permute-start(f32[512]{0:T(512)S(1)} %add.227), channel_id=1, source_target_pairs={{0,8},{1,9},{2,10},{3,11},{4,12},{5,13},{6,14},{7,15},{8,0},{9,1},... | collective-permute-start | bytes 6152 | tf_op jit(solution)/shard_map/ppermute | solution.py:38
  169.7 4.5 %collective-permute-start.22 = (f32[512]{0:T(512)S(1)}, f32[512]{0:T(512)S(1)}, u32[]{:S(2)}, u32[]{:S(2)}) collective-permute-start(f32[512]{0:T(512)S(1)} %add.229), channel_id=1, source_target_pairs={{0,32},{1,33},{2,34},{3,35},{4,36},{5,37},{6,38},{7,39},{8,40},{9,... | collective-permute-start | bytes 6152 | tf_op jit(solution)/shard_map/ppermute | solution.py:38
  174.2 7.2 %reshape.251 = bf16[1024,64,36]{0,2,1:T(8,128)(2,1)} reshape(bf16[1024,2304]{0,1:T(8,128)(2,1)} %constant_dynamic-update-slice_fusion) | data formatting | bytes 9437184 | tf_op jit(solution)/shard_map/reshape | solution.py:174
  186.8 11.0 %collective-permute-start.24 = (bf16[64,1,256]{2,1,0:T(2,128)(2,1)S(1)}, bf16[64,1,256]{2,1,0:T(2,128)(2,1)S(1)}, u32[]{:S(2)}, u32[]{:S(2)}) collective-permute-start(bf16[64,1,256]{2,1,0:T(2,128)(2,1)S(1)} %get-tuple-element.104), channel_id=1, source_target_pairs={{1,0},{2,1},{3,2},{4,3},{5,4},{6,5},{7,6},{8,7},{9,8},{10,9},{11,1... | collective-permute-start | bytes 98312 | tf_op jit(solution)/shard_map/ppermute | solution.py:17
  197.8 4.1 %fusion.40 = f32[2,2,2,2,2,2,36,256]{7,6,5,4,3,2,1,0:T(8,128)S(1)} fusion(bf16[2,2,2,2,2,2,36,1024]{7,6,5,4,3,2,1,0:T(8,128)(2,1)} %bitcast.157, bf16[1024,256,1,1,1,1,1,1]{0,1,7,6,5,4,3,2:T(8,128)(2,1)S(1)} %bitcast.179), kind=kOutput, calls=%fused_computation.131 | convolution fusion | flops 1207959552 | bytes 7602176 | tf_op jit(solution)/shard_map/njr,nc->jrc/dot_general | solution.py:172
  209.0 5.1 %collective-permute-start.27 = (bf16[2,18,256]{2,1,0:T(8,128)(2,1)S(1)}, bf16[2,18,256]{2,1,0:T(8,128)(2,1)S(1)}, u32[]{:S(2)}, u32[]{:S(2)}) collective-permute-start(bf16[2,18,256]{2,1,0:T(8,128)(2,1)S(1)} %pad_maximum_fusion.5), channel_id=1, source_target_pairs={{32,0},{33,1},{34,2},{35,3},{36,4},{37,5},{38,6},{39,7},{40,8},{41... | collective-permute-start | bytes 55304 | tf_op jit(solution)/shard_map/ppermute | solution.py:25
  219.1 15.6 %collective-permute-done.29 = f32[2,2,2,2,2,36,128]{6,4,5,3,2,1,0:T(2,128)S(1)} collective-permute-done((f32[2,2,2,2,2,36,128]{6,4,5,3,2,1,0:T(2,128)S(1)}, f32[2,2,2,2,2,36,128]{6,4,5,3,2,1,0:T(2,128)S(1)}, u32[]{:S(2)}, u32[]{:S(2)}) %collective-permute-start.29) | collective-permute-done | bytes 589856 | tf_op jit(solution)/shard_map/ppermute | solution.py:38
  239.9 6.2 %collective-permute-done.30 = f32[2,2,2,2,36,128]{5,3,4,2,1,0:T(2,128)S(1)} collective-permute-done((f32[2,2,2,2,36,128]{5,3,4,2,1,0:T(2,128)S(1)}, f32[2,2,2,2,36,128]{5,3,4,2,1,0:T(2,128)S(1)}, u32[]{:S(2)}, u32[]{:S(2)}) %collective-permute-start.30) | collective-permute-done | bytes 294944 | tf_op jit(solution)/shard_map/ppermute | solution.py:38
  248.7 8.8 %collective-permute-done.31 = f32[2,2,2,36,128]{4,2,3,1,0:T(2,128)S(1)} collective-permute-done((f32[2,2,2,36,128]{4,2,3,1,0:T(2,128)S(1)}, f32[2,2,2,36,128]{4,2,3,1,0:T(2,128)S(1)}, u32[]{:S(2)}, u32[]{:S(2)}) %collective-permute-start.31) | collective-permute-done | bytes 147488 | tf_op jit(solution)/shard_map/ppermute | solution.py:38
  257.6 3.8 %collective-permute-start.32 = (f32[2,2,36,128]{3,1,2,0:T(2,128)S(1)}, f32[2,2,36,128]{3,1,2,0:T(2,128)S(1)}, u32[]{:S(2)}, u32[]{:S(2)}) collective-permute-start(f32[2,2,36,128]{3,1,2,0:T(2,128)S(1)} %dynamic-slice_bitcast_fusion.1), channel_id=1, source_target_pairs={{0,32},{1,33},{2,34},{3,35},{4,36},{5,37},{6,38},{7,39},{8,40},{9,... | collective-permute-start | bytes 221192 | tf_op jit(solution)/shard_map/ppermute | solution.py:38
  261.7 3.7 %collective-permute-done.32 = f32[2,2,36,128]{3,1,2,0:T(2,128)S(1)} collective-permute-done((f32[2,2,36,128]{3,1,2,0:T(2,128)S(1)}, f32[2,2,36,128]{3,1,2,0:T(2,128)S(1)}, u32[]{:S(2)}, u32[]{:S(2)}) %collective-permute-start.32) | collective-permute-done | bytes 73760 | tf_op jit(solution)/shard_map/ppermute | solution.py:38
  267.6 7.7 %collective-permute-done.33 = f32[2,36,128]{2,0,1:T(2,128)S(1)} collective-permute-done((f32[2,36,128]{2,0,1:T(2,128)S(1)}, f32[2,36,128]{2,0,1:T(2,128)S(1)}, u32[]{:S(2)}, u32[]{:S(2)}) %collective-permute-start.33) | collective-permute-done | bytes 36896 | tf_op jit(solution)/shard_map/ppermute | solution.py:38
  275.4 3.7 %collective-permute-start.34 = (f32[36,128]{1,0:T(8,128)S(1)}, f32[36,128]{1,0:T(8,128)S(1)}, u32[]{:S(2)}, u32[]{:S(2)}) collective-permute-start(f32[36,128]{1,0:T(8,128)S(1)} %bitcast.183), channel_id=1, source_target_pairs={{0,8},{1,9},{2,10},{3,11},{4,12},{5,13},{6,14},{7,15},{8,0},{9,1},... | collective-permute-start | bytes 55304 | tf_op jit(solution)/shard_map/ppermute | solution.py:38
  279.3 5.7 %collective-permute-done.34 = f32[36,128]{1,0:T(8,128)S(1)} collective-permute-done((f32[36,128]{1,0:T(8,128)S(1)}, f32[36,128]{1,0:T(8,128)S(1)}, u32[]{:S(2)}, u32[]{:S(2)}) %collective-permute-start.34) | collective-permute-done | bytes 18464 | tf_op jit(solution)/shard_map/ppermute | solution.py:38
  285.1 3.9 %collective-permute-start.35 = (f32[36,64]{1,0:T(8,128)S(1)}, f32[36,64]{1,0:T(8,128)S(1)}, u32[]{:S(2)}, u32[]{:S(2)}) collective-permute-start(f32[36,64]{1,0:T(8,128)S(1)} %constant_dynamic-slice_fusion.1), channel_id=1, source_target_pairs={{0,128},{64,192},{128,0},{192,64},{256,384},{320,448},{384,256},{4... | collective-permute-start | bytes 27656 | tf_op jit(solution)/shard_map/ppermute | solution.py:38
  290.9 3.0 %collective-permute-start.36 = (f32[36,32]{1,0:T(8,128)S(1)}, f32[36,32]{1,0:T(8,128)S(1)}, u32[]{:S(2)}, u32[]{:S(2)}) collective-permute-start(f32[36,32]{1,0:T(8,128)S(1)} %constant_dynamic-slice_fusion), channel_id=1, source_target_pairs={{0,256},{64,320},{128,384},{192,448},{256,0},{320,64},{384,128},{4... | collective-permute-start | bytes 13832 | tf_op jit(solution)/shard_map/ppermute | solution.py:38
  (189 shorter events, 115.6 us)
Async XLA Ops:
  1.8 20.0 %collective-permute-start = (bf16[64,1,256]{2,1,0:T(2,128)(2,1)S(1)}, bf16[64,1,256]{2,1,0:T(2,128)(2,1)S(1)}, u32[]{:S(2)}, u32[]{:S(2)}) collective-permute-start(bf16[64,1,256]{2,1,0:T(2,128)(2,1)S(1)} %get-tuple-element.105), channel_id=1, source_target_pairs={{0,1},{1,2},{2,3},{3,4},{4,5},{5,6},{6,7},{7,8},{8,9},{9,10},{10,1... | collective-permute-start | bytes 98312 | tf_op jit(solution)/shard_map/ppermute | solution.py:16
  6.1 16.9 %collective-permute-start.1 = (bf16[64,1,256]{2,1,0:T(2,128)(2,1)S(1)}, bf16[64,1,256]{2,1,0:T(2,128)(2,1)S(1)}, u32[]{:S(2)}, u32[]{:S(2)}) collective-permute-start(bf16[64,1,256]{2,1,0:T(2,128)(2,1)S(1)} %get-tuple-element.106), channel_id=1, source_target_pairs={{1,0},{2,1},{3,2},{4,3},{5,4},{6,5},{7,6},{8,7},{9,8},{10,9},{11,1... | collective-permute-start | bytes 98312 | tf_op jit(solution)/shard_map/ppermute | solution.py:17
  23.7 5.7 %collective-permute-start.2 = (bf16[1,18,256]{2,1,0:T(8,128)(2,1)S(1)}, bf16[1,18,256]{2,1,0:T(8,128)(2,1)S(1)}, u32[]{:S(2)}, u32[]{:S(2)}) collective-permute-start(bf16[1,18,256]{2,1,0:T(8,128)(2,1)S(1)} %get-tuple-element.99), channel_id=1, source_target_pairs={{0,64},{64,128},{128,192},{192,256},{256,320},{320,384},{384,448},... | collective-permute-start | bytes 27656 | tf_op jit(solution)/shard_map/ppermute | solution.py:16
  26.3 7.2 %collective-permute-start.4 = (bf16[2,18,256]{2,1,0:T(8,128)(2,1)S(1)}, bf16[2,18,256]{2,1,0:T(8,128)(2,1)S(1)}, u32[]{:S(2)}, u32[]{:S(2)}) collective-permute-start(bf16[2,18,256]{2,1,0:T(8,128)(2,1)S(1)} %pad_maximum_fusion.4), channel_id=1, source_target_pairs={{32,0},{33,1},{34,2},{35,3},{36,4},{37,5},{38,6},{39,7},{40,8},{41... | collective-permute-start | bytes 55304 | tf_op jit(solution)/shard_map/ppermute | solution.py:25
  62.3 6.3 %collective-permute-start.6 = (f32[64]{0:T(128)S(1)}, f32[64]{0:T(128)S(1)}, u32[]{:S(2)}, u32[]{:S(2)}) collective-permute-start(f32[64]{0:T(128)S(1)} %fusion.47), channel_id=1, source_target_pairs={{0,128},{64,192},{128,0},{192,64},{256,384},{320,448},{384,256},{4... | collective-permute-start | bytes 776 | tf_op jit(solution)/shard_map/ppermute | solution.py:38
  68.5 6.3 %collective-permute-start.7 = (f32[64]{0:T(128)S(1)}, f32[64]{0:T(128)S(1)}, u32[]{:S(2)}, u32[]{:S(2)}) collective-permute-start(f32[64]{0:T(128)S(1)} %add.207), channel_id=1, source_target_pairs={{0,256},{64,320},{128,384},{192,448},{256,0},{320,64},{384,128},{4... | collective-permute-start | bytes 776 | tf_op jit(solution)/shard_map/ppermute | solution.py:38
  80.3 6.3 %collective-permute-start.9 = (f32[64]{0:T(128)S(1)}, f32[64]{0:T(128)S(1)}, u32[]{:S(2)}, u32[]{:S(2)}) collective-permute-start(f32[64]{0:T(128)S(1)} %add.209), channel_id=1, source_target_pairs={{0,2},{1,3},{2,0},{3,1},{4,6},{5,7},{6,4},{7,5},{8,10},{9,11},{10,... | collective-permute-start | bytes 776 | tf_op jit(solution)/shard_map/ppermute | solution.py:38
  86.6 9.3 %collective-permute-start.10 = (f32[64]{0:T(128)S(1)}, f32[64]{0:T(128)S(1)}, u32[]{:S(2)}, u32[]{:S(2)}) collective-permute-start(f32[64]{0:T(128)S(1)} %add.210), channel_id=1, source_target_pairs={{0,4},{1,5},{2,6},{3,7},{4,0},{5,1},{6,2},{7,3},{8,12},{9,13},{10,... | collective-permute-start | bytes 776 | tf_op jit(solution)/shard_map/ppermute | solution.py:38
  95.9 9.3 %collective-permute-start.11 = (f32[64]{0:T(128)S(1)}, f32[64]{0:T(128)S(1)}, u32[]{:S(2)}, u32[]{:S(2)}) collective-permute-start(f32[64]{0:T(128)S(1)} %add.211), channel_id=1, source_target_pairs={{0,8},{1,9},{2,10},{3,11},{4,12},{5,13},{6,14},{7,15},{8,0},{9,1},... | collective-permute-start | bytes 776 | tf_op jit(solution)/shard_map/ppermute | solution.py:38
  110.7 6.9 %collective-permute-start.13 = (f32[64]{0:T(128)S(1)}, f32[64]{0:T(128)S(1)}, u32[]{:S(2)}, u32[]{:S(2)}) collective-permute-start(f32[64]{0:T(128)S(1)} %add.213), channel_id=1, source_target_pairs={{0,32},{1,33},{2,34},{3,35},{4,36},{5,37},{6,38},{7,39},{8,40},{9,... | collective-permute-start | bytes 776 | tf_op jit(solution)/shard_map/ppermute | solution.py:38
  121.8 5.5 %collective-permute-start.15 = (f32[512]{0:T(512)S(1)}, f32[512]{0:T(512)S(1)}, u32[]{:S(2)}, u32[]{:S(2)}) collective-permute-start(f32[512]{0:T(512)S(1)} %fusion.29), channel_id=1, source_target_pairs={{0,128},{64,192},{128,0},{192,64},{256,384},{320,448},{384,256},{4... | collective-permute-start | bytes 6152 | tf_op jit(solution)/shard_map/ppermute | solution.py:38
  127.2 6.4 %collective-permute-start.16 = (f32[512]{0:T(512)S(1)}, f32[512]{0:T(512)S(1)}, u32[]{:S(2)}, u32[]{:S(2)}) collective-permute-start(f32[512]{0:T(512)S(1)} %add.223), channel_id=1, source_target_pairs={{0,256},{64,320},{128,384},{192,448},{256,0},{320,64},{384,128},{4... | collective-permute-start | bytes 6152 | tf_op jit(solution)/shard_map/ppermute | solution.py:38
  133.6 5.5 %collective-permute-start.17 = (f32[512]{0:T(512)S(1)}, f32[512]{0:T(512)S(1)}, u32[]{:S(2)}, u32[]{:S(2)}) collective-permute-start(f32[512]{0:T(512)S(1)} %add.224), channel_id=1, source_target_pairs={{0,1},{1,0},{2,3},{3,2},{4,5},{5,4},{6,7},{7,6},{8,9},{9,8},{10,11... | collective-permute-start | bytes 6152 | tf_op jit(solution)/shard_map/ppermute | solution.py:38
  139.1 6.4 %collective-permute-start.18 = (f32[512]{0:T(512)S(1)}, f32[512]{0:T(512)S(1)}, u32[]{:S(2)}, u32[]{:S(2)}) collective-permute-start(f32[512]{0:T(512)S(1)} %add.225), channel_id=1, source_target_pairs={{0,2},{1,3},{2,0},{3,1},{4,6},{5,7},{6,4},{7,5},{8,10},{9,11},{10,... | collective-permute-start | bytes 6152 | tf_op jit(solution)/shard_map/ppermute | solution.py:38
  145.4 9.4 %collective-permute-start.19 = (f32[512]{0:T(512)S(1)}, f32[512]{0:T(512)S(1)}, u32[]{:S(2)}, u32[]{:S(2)}) collective-permute-start(f32[512]{0:T(512)S(1)} %add.226), channel_id=1, source_target_pairs={{0,4},{1,5},{2,6},{3,7},{4,0},{5,1},{6,2},{7,3},{8,12},{9,13},{10,... | collective-permute-start | bytes 6152 | tf_op jit(solution)/shard_map/ppermute | solution.py:38
  154.8 9.4 %collective-permute-start.20 = (f32[512]{0:T(512)S(1)}, f32[512]{0:T(512)S(1)}, u32[]{:S(2)}, u32[]{:S(2)}) collective-permute-start(f32[512]{0:T(512)S(1)} %add.227), channel_id=1, source_target_pairs={{0,8},{1,9},{2,10},{3,11},{4,12},{5,13},{6,14},{7,15},{8,0},{9,1},... | collective-permute-start | bytes 6152 | tf_op jit(solution)/shard_map/ppermute | solution.py:38
  164.2 5.5 %collective-permute-start.21 = (f32[512]{0:T(512)S(1)}, f32[512]{0:T(512)S(1)}, u32[]{:S(2)}, u32[]{:S(2)}) collective-permute-start(f32[512]{0:T(512)S(1)} %add.228), channel_id=1, source_target_pairs={{0,16},{1,17},{2,18},{3,19},{4,20},{5,21},{6,22},{7,23},{8,24},{9,... | collective-permute-start | bytes 6152 | tf_op jit(solution)/shard_map/ppermute | solution.py:38
  169.7 11.8 %collective-permute-start.22 = (f32[512]{0:T(512)S(1)}, f32[512]{0:T(512)S(1)}, u32[]{:S(2)}, u32[]{:S(2)}) collective-permute-start(f32[512]{0:T(512)S(1)} %add.229), channel_id=1, source_target_pairs={{0,32},{1,33},{2,34},{3,35},{4,36},{5,37},{6,38},{7,39},{8,40},{9,... | collective-permute-start | bytes 6152 | tf_op jit(solution)/shard_map/ppermute | solution.py:38
  184.8 19.8 %collective-permute-start.23 = (bf16[64,1,256]{2,1,0:T(2,128)(2,1)S(1)}, bf16[64,1,256]{2,1,0:T(2,128)(2,1)S(1)}, u32[]{:S(2)}, u32[]{:S(2)}) collective-permute-start(bf16[64,1,256]{2,1,0:T(2,128)(2,1)S(1)} %get-tuple-element.103), channel_id=1, source_target_pairs={{0,1},{1,2},{2,3},{3,4},{4,5},{5,6},{6,7},{7,8},{8,9},{9,10},{10,1... | collective-permute-start | bytes 98312 | tf_op jit(solution)/shard_map/ppermute | solution.py:16
  186.8 17.8 %collective-permute-start.24 = (bf16[64,1,256]{2,1,0:T(2,128)(2,1)S(1)}, bf16[64,1,256]{2,1,0:T(2,128)(2,1)S(1)}, u32[]{:S(2)}, u32[]{:S(2)}) collective-permute-start(bf16[64,1,256]{2,1,0:T(2,128)(2,1)S(1)} %get-tuple-element.104), channel_id=1, source_target_pairs={{1,0},{2,1},{3,2},{4,3},{5,4},{6,5},{7,6},{8,7},{9,8},{10,9},{11,1... | collective-permute-start | bytes 98312 | tf_op jit(solution)/shard_map/ppermute | solution.py:17
  202.7 13.6 %collective-permute-start.28 = (f32[2,2,2,2,2,2,36,128]{7,5,6,4,3,2,1,0:T(2,128)S(1)}, f32[2,2,2,2,2,2,36,128]{7,5,6,4,3,2,1,0:T(2,128)S(1)}, u32[]{:S(2)}, u32[]{:S(2)}) collective-permute-start(f32[2,2,2,2,2,2,36,128]{7,5,6,4,3,2,1,0:T(2,128)S(1)} %copy.86), channel_id=1, source_target_pairs={{0,64},{64,0},{128,192},{192,128},{256,320},{320,256},{384,448},{4... | collective-permute-start | bytes 3538952 | tf_op jit(solution)/shard_map/ppermute | solution.py:38
  204.6 9.9 %collective-permute-start.25 = (bf16[1,18,256]{2,1,0:T(8,128)(2,1)S(1)}, bf16[1,18,256]{2,1,0:T(8,128)(2,1)S(1)}, u32[]{:S(2)}, u32[]{:S(2)}) collective-permute-start(bf16[1,18,256]{2,1,0:T(8,128)(2,1)S(1)} %get-tuple-element.98), channel_id=1, source_target_pairs={{64,0},{128,64},{192,128},{256,192},{320,256},{384,320},{448,384},... | collective-permute-start | bytes 27656 | tf_op jit(solution)/shard_map/ppermute | solution.py:17
  205.9 8.6 %collective-permute-start.26 = (bf16[1,18,256]{2,1,0:T(8,128)(2,1)S(1)}, bf16[1,18,256]{2,1,0:T(8,128)(2,1)S(1)}, u32[]{:S(2)}, u32[]{:S(2)}) collective-permute-start(bf16[1,18,256]{2,1,0:T(8,128)(2,1)S(1)} %get-tuple-element.97), channel_id=1, source_target_pairs={{0,64},{64,128},{128,192},{192,256},{256,320},{320,384},{384,448},... | collective-permute-start | bytes 27656 | tf_op jit(solution)/shard_map/ppermute | solution.py:16
  209.0 29.6 %collective-permute-start.27 = (bf16[2,18,256]{2,1,0:T(8,128)(2,1)S(1)}, bf16[2,18,256]{2,1,0:T(8,128)(2,1)S(1)}, u32[]{:S(2)}, u32[]{:S(2)}) collective-permute-start(bf16[2,18,256]{2,1,0:T(8,128)(2,1)S(1)} %pad_maximum_fusion.5), channel_id=1, source_target_pairs={{32,0},{33,1},{34,2},{35,3},{36,4},{37,5},{38,6},{39,7},{40,8},{41... | collective-permute-start | bytes 55304 | tf_op jit(solution)/shard_map/ppermute | solution.py:25
  216.9 17.7 %collective-permute-start.29 = (f32[2,2,2,2,2,36,128]{6,4,5,3,2,1,0:T(2,128)S(1)}, f32[2,2,2,2,2,36,128]{6,4,5,3,2,1,0:T(2,128)S(1)}, u32[]{:S(2)}, u32[]{:S(2)}) collective-permute-start(f32[2,2,2,2,2,36,128]{6,4,5,3,2,1,0:T(2,128)S(1)} %bitcast.178), channel_id=1, source_target_pairs={{0,1},{1,0},{2,3},{3,2},{4,5},{5,4},{6,7},{7,6},{8,9},{9,8},{10,11... | collective-permute-start | bytes 1769480 | tf_op jit(solution)/shard_map/ppermute | solution.py:38
  235.1 11.0 %collective-permute-start.30 = (f32[2,2,2,2,36,128]{5,3,4,2,1,0:T(2,128)S(1)}, f32[2,2,2,2,36,128]{5,3,4,2,1,0:T(2,128)S(1)}, u32[]{:S(2)}, u32[]{:S(2)}) collective-permute-start(f32[2,2,2,2,36,128]{5,3,4,2,1,0:T(2,128)S(1)} %dynamic-slice_bitcast_fusion), channel_id=1, source_target_pairs={{0,16},{1,17},{2,18},{3,19},{4,20},{5,21},{6,22},{7,23},{8,24},{9,... | collective-permute-start | bytes 884744 | tf_op jit(solution)/shard_map/ppermute | solution.py:38
  246.6 10.9 %collective-permute-start.31 = (f32[2,2,2,36,128]{4,2,3,1,0:T(2,128)S(1)}, f32[2,2,2,36,128]{4,2,3,1,0:T(2,128)S(1)}, u32[]{:S(2)}, u32[]{:S(2)}) collective-permute-start(f32[2,2,2,36,128]{4,2,3,1,0:T(2,128)S(1)} %bitcast.181), channel_id=1, source_target_pairs={{0,2},{1,3},{2,0},{3,1},{4,6},{5,7},{6,4},{7,5},{8,10},{9,11},{10,... | collective-permute-start | bytes 442376 | tf_op jit(solution)/shard_map/ppermute | solution.py:38
  257.6 7.8 %collective-permute-start.32 = (f32[2,2,36,128]{3,1,2,0:T(2,128)S(1)}, f32[2,2,36,128]{3,1,2,0:T(2,128)S(1)}, u32[]{:S(2)}, u32[]{:S(2)}) collective-permute-start(f32[2,2,36,128]{3,1,2,0:T(2,128)S(1)} %dynamic-slice_bitcast_fusion.1), channel_id=1, source_target_pairs={{0,32},{1,33},{2,34},{3,35},{4,36},{5,37},{6,38},{7,39},{8,40},{9,... | collective-permute-start | bytes 221192 | tf_op jit(solution)/shard_map/ppermute | solution.py:38
  265.5 9.8 %collective-permute-start.33 = (f32[2,36,128]{2,0,1:T(2,128)S(1)}, f32[2,36,128]{2,0,1:T(2,128)S(1)}, u32[]{:S(2)}, u32[]{:S(2)}) collective-permute-start(f32[2,36,128]{2,0,1:T(2,128)S(1)} %bitcast.182), channel_id=1, source_target_pairs={{0,4},{1,5},{2,6},{3,7},{4,0},{5,1},{6,2},{7,3},{8,12},{9,13},{10,... | collective-permute-start | bytes 110600 | tf_op jit(solution)/shard_map/ppermute | solution.py:38
  275.4 9.6 %collective-permute-start.34 = (f32[36,128]{1,0:T(8,128)S(1)}, f32[36,128]{1,0:T(8,128)S(1)}, u32[]{:S(2)}, u32[]{:S(2)}) collective-permute-start(f32[36,128]{1,0:T(8,128)S(1)} %bitcast.183), channel_id=1, source_target_pairs={{0,8},{1,9},{2,10},{3,11},{4,12},{5,13},{6,14},{7,15},{8,0},{9,1},... | collective-permute-start | bytes 55304 | tf_op jit(solution)/shard_map/ppermute | solution.py:38
  285.1 5.7 %collective-permute-start.35 = (f32[36,64]{1,0:T(8,128)S(1)}, f32[36,64]{1,0:T(8,128)S(1)}, u32[]{:S(2)}, u32[]{:S(2)}) collective-permute-start(f32[36,64]{1,0:T(8,128)S(1)} %constant_dynamic-slice_fusion.1), channel_id=1, source_target_pairs={{0,128},{64,192},{128,0},{192,64},{256,384},{320,448},{384,256},{4... | collective-permute-start | bytes 27656 | tf_op jit(solution)/shard_map/ppermute | solution.py:38
  290.9 6.6 %collective-permute-start.36 = (f32[36,32]{1,0:T(8,128)S(1)}, f32[36,32]{1,0:T(8,128)S(1)}, u32[]{:S(2)}, u32[]{:S(2)}) collective-permute-start(f32[36,32]{1,0:T(8,128)S(1)} %constant_dynamic-slice_fusion), channel_id=1, source_target_pairs={{0,256},{64,320},{128,384},{192,448},{256,0},{320,64},{384,128},{4... | collective-permute-start | bytes 13832 | tf_op jit(solution)/shard_map/ppermute | solution.py:38
  (14 other events, 250.0 us)

commit v3 on v2

--- a/solution.py
+++ b/solution.py
@@ -82,6 +82,17 @@
     return split
 
 
+def conv_valid(field, weights):
+    return lax.conv_general_dilated(
+        field[None],
+        weights,
+        (1, 1),
+        "VALID",
+        dimension_numbers=("NHWC", "HWIO", "NHWC"),
+        preferred_element_type=jnp.float32,
+    )[0]
+
+
 def local(fields, kernel, norm_gain, norm_shift, cotangent):
     height, breadth, channels = fields.shape
     north = lax.axis_index("lat") == 0
@@ -89,17 +100,7 @@
     banded, distant = extend(fields)
     merged = banded.at[0].set(jnp.where(north, distant[0], banded[0]))
     merged = merged.at[-1].set(jnp.where(south, distant[1], merged[-1]))
-    patches = jnp.concatenate(
-        [
-            merged[tap_row : tap_row + height, tap_col : tap_col + breadth].reshape(-1, channels)
-            for tap_row in range(3)
-            for tap_col in range(3)
-        ],
-        1,
-    )
-    conv_out = jnp.dot(
-        patches, kernel.reshape(9 * channels, channels), preferred_element_type=jnp.float32
-    )
+    conv_out = conv_valid(merged, kernel).reshape(-1, channels)
     count = height * breadth * lax.axis_size("lat") * lax.axis_size("lon") * (channels // G)
     local_stats = jnp.concatenate(
         [jnp.sum(conv_out, 0).reshape(G, -1).sum(1), jnp.sum(conv_out * conv_out, 0).reshape(G, -1).sum(1)]
@@ -133,22 +134,8 @@
         * rstd_ch
     ).astype(jnp.bfloat16)
     grad_banded, grad_distant = extend(dconv.reshape(height, breadth, channels))
-    grad_patches = jnp.concatenate(
-        [
-            grad_banded[
-                2 - tap_row : 2 - tap_row + height, 2 - tap_col : 2 - tap_col + breadth
-            ].reshape(-1, channels)
-            for tap_row in range(3)
-            for tap_col in range(3)
-        ],
-        1,
-    )
-    flipped = jnp.concatenate(
-        [kernel[tap_row, tap_col].T for tap_row in range(3) for tap_col in range(3)], 0
-    )
-    back = jnp.dot(grad_patches, flipped, preferred_element_type=jnp.float32).reshape(
-        height, breadth, channels
-    )
+    flipped = jnp.swapaxes(kernel[::-1, ::-1], 2, 3)
+    back = conv_valid(grad_banded, flipped)
     upper_term = jnp.zeros((breadth, channels), jnp.float32)
     lower_term = jnp.zeros((breadth, channels), jnp.float32)
     for tap_col in range(3):
@@ -169,12 +156,15 @@
     lat_bits = (lat_n - 1).bit_length()
     lat_major = dconv.reshape((-1,) + (2,) * lat_bits + (channels // lat_n,))
     lat_major = lat_major.transpose((0,) + tuple(range(lat_bits, 0, -1)) + (lat_bits + 1,))
-    blocks = jnp.einsum(
-        "njr,nc->jrc",
-        patches.reshape(-1, lon_n, 9 * channels // lon_n),
-        lat_major.reshape(-1, channels),
+    term = lax.conv_general_dilated(
+        merged[None],
+        lat_major.reshape(height, breadth, 1, channels),
+        (1, 1),
+        "VALID",
+        dimension_numbers=("CHWN", "HWIO", "HWNC"),
         preferred_element_type=jnp.float32,
     )
+    blocks = term.reshape(lon_n, 9 * channels // lon_n, channels)
     grad_kernel = halving_sum(blocks)
     return (block_out, grad_fields, grad_kernel, grad_gain, grad_shift)
 

time: 302 us -> 300 us (level)
  waiting for transfers between devices: 94.7 us -> 83.9 us
  matrix products: 10.3 us -> 14.3 us
    conv_general_dilated x0 -> x3, matrix products: none -> 13.4 us  [the longest x1 9.27 us: local(): lax.conv_general_dilated(merged[None], lat_major.reshape(height, breadth,...]
    ppermute x27, waiting for transfers between devices: 89.4 us -> 76.4 us  [exchange(): return lax.ppermute(block, axis, [(i, i ^ 1 << bit) for i in range(peers)])]
    another operation x0 -> x3, local copies, waits for them, and re-layouts: none -> 12.4 us  [the longest x2 10 us: local(): conv_out = conv_valid(merged, kernel).reshape(-1, channels)]
    unnamed x45 -> x59, local copies, waits for them, and re-layouts: 17.6 us -> 7.35 us
    dot_general x3 -> x0, matrix products: 9.38 us -> none  [the longest x1 4.13 us: local(): jnp.einsum('njr,nc->jrc', patches.reshape(-1, lon_n, 9 * channels // lon_...]
    reshape x10 -> x3, local copies, waits for them, and re-layouts: 16.2 us -> 12.5 us  [the longest x2 10.2 us: local(): upstream = cotangent.astype(jnp.float32).reshape(-1, channels)]
  transfers between devices with their start and end apart: 37 -> 37, of which waited for: 28 -> 30; matrix products, arithmetic and copies ran while one was open for 9% -> 11% of each run, Pallas kernels for 0% -> 0%
where the time goes in v3:
time: 300 us; the launch traced here: 297 us
  starting transfers between devices  143 us (48%)
  waiting for transfers between devices  83.9 us (28%)
  local copies, waits for them, and re-layouts  42.9 us (14%)
  matrix products  14.3 us (5%)
  other arithmetic  11 us (4%)
    ppermute x27, starting transfers between devices, exchange(): return lax.ppermute(block, axis, [(i, i ^ 1 << bit) for i in range(peers)])  96.4 us
    ppermute x27, waiting for transfers between devices, exchange(): return lax.ppermute(block, axis, [(i, i ^ 1 << bit) for i in range(peers)])  76.4 us
    ppermute x4, starting transfers between devices, with_halo(): after = lax.ppermute(initial, axis, down)  28.1 us
    ppermute x4, starting transfers between devices, with_halo(): before = lax.ppermute(last, axis, up)  10.8 us
    reshape x2, local copies, waits for them, and re-layouts, local(): upstream = cotangent.astype(jnp.float32).reshape(-1, channels)  10.2 us
    another operation x2, local copies, waits for them, and re-layouts, local(): conv_out = conv_valid(merged, kernel).reshape(-1, channels)  10 us
    conv_general_dilated x1, matrix products, local(): lax.conv_general_dilated(merged[None], lat_major.reshape(height, breadth,...  9.27 us
    ppermute x2, starting transfers between devices, passed_along(): return lax.ppermute(block, axis, route)  7.95 us
  transfers between devices with their start and end apart: 37, of which 30 were waited for; matrix products, arithmetic and copies ran while one was open for 11% of the time, Pallas kernels for 0%

profile of v3, /device:TPU:6, one launch (start us, length us, event | category | flops | bytes accessed | tf_op | source)
XLA Modules:
  0.0 297.1 jit_solution(12043626514236143722)
XLA Ops:
  1.8 4.3 %collective-permute-start = (bf16[64,1,256]{2,1,0:T(2,128)(2,1)S(1)}, bf16[64,1,256]{2,1,0:T(2,128)(2,1)S(1)}, u32[]{:S(2)}, u32[]{:S(2)}) collective-permute-start(bf16[64,1,256]{2,1,0:T(2,128)(2,1)S(1)} %get-tuple-element.91), channel_id=1, source_target_pairs={{0,1},{1,2},{2,3},{3,4},{4,5},{5,6},{6,7},{7,8},{8,9},{9,10},{10,1... | collective-permute-start | bytes 98312 | tf_op jit(solution)/shard_map/ppermute | solution.py:16
  6.1 14.1 %collective-permute-start.1 = (bf16[64,1,256]{2,1,0:T(2,128)(2,1)S(1)}, bf16[64,1,256]{2,1,0:T(2,128)(2,1)S(1)}, u32[]{:S(2)}, u32[]{:S(2)}) collective-permute-start(bf16[64,1,256]{2,1,0:T(2,128)(2,1)S(1)} %get-tuple-element.92), channel_id=1, source_target_pairs={{1,0},{2,1},{3,2},{4,3},{5,4},{6,5},{7,6},{8,7},{9,8},{10,9},{11,1... | collective-permute-start | bytes 98312 | tf_op jit(solution)/shard_map/ppermute | solution.py:17
  41.6 4.7 %collective-permute-start.6 = (f32[64]{0:T(128)S(1)}, f32[64]{0:T(128)S(1)}, u32[]{:S(2)}, u32[]{:S(2)}) collective-permute-start(f32[64]{0:T(128)S(1)} %fusion.64), channel_id=1, source_target_pairs={{0,128},{64,192},{128,0},{192,64},{256,384},{320,448},{384,256},{4... | collective-permute-start | bytes 776 | tf_op jit(solution)/shard_map/ppermute | solution.py:38
  47.9 4.0 %collective-permute-start.7 = (f32[64]{0:T(128)S(1)}, f32[64]{0:T(128)S(1)}, u32[]{:S(2)}, u32[]{:S(2)}) collective-permute-start(f32[64]{0:T(128)S(1)} %add.237), channel_id=1, source_target_pairs={{0,256},{64,320},{128,384},{192,448},{256,0},{320,64},{384,128},{4... | collective-permute-start | bytes 776 | tf_op jit(solution)/shard_map/ppermute | solution.py:38
  56.1 3.5 %collective-permute-done.8 = f32[64]{0:T(128)S(1)} collective-permute-done((f32[64]{0:T(128)S(1)}, f32[64]{0:T(128)S(1)}, u32[]{:S(2)}, u32[]{:S(2)}) %collective-permute-start.8) | collective-permute-done | bytes 288 | tf_op jit(solution)/shard_map/ppermute | solution.py:38
  61.6 4.4 %collective-permute-done.9 = f32[64]{0:T(128)S(1)} collective-permute-done((f32[64]{0:T(128)S(1)}, f32[64]{0:T(128)S(1)}, u32[]{:S(2)}, u32[]{:S(2)}) %collective-permute-start.9) | collective-permute-done | bytes 288 | tf_op jit(solution)/shard_map/ppermute | solution.py:38
  66.0 5.4 %collective-permute-start.10 = (f32[64]{0:T(128)S(1)}, f32[64]{0:T(128)S(1)}, u32[]{:S(2)}, u32[]{:S(2)}) collective-permute-start(f32[64]{0:T(128)S(1)} %add.240), channel_id=1, source_target_pairs={{0,4},{1,5},{2,6},{3,7},{4,0},{5,1},{6,2},{7,3},{8,12},{9,13},{10,... | collective-permute-start | bytes 776 | tf_op jit(solution)/shard_map/ppermute | solution.py:38
  71.4 3.9 %collective-permute-done.10 = f32[64]{0:T(128)S(1)} collective-permute-done((f32[64]{0:T(128)S(1)}, f32[64]{0:T(128)S(1)}, u32[]{:S(2)}, u32[]{:S(2)}) %collective-permute-start.10) | collective-permute-done | bytes 288 | tf_op jit(solution)/shard_map/ppermute | solution.py:38
  75.3 6.6 %collective-permute-start.11 = (f32[64]{0:T(128)S(1)}, f32[64]{0:T(128)S(1)}, u32[]{:S(2)}, u32[]{:S(2)}) collective-permute-start(f32[64]{0:T(128)S(1)} %add.241), channel_id=1, source_target_pairs={{0,8},{1,9},{2,10},{3,11},{4,12},{5,13},{6,14},{7,15},{8,0},{9,1},... | collective-permute-start | bytes 776 | tf_op jit(solution)/shard_map/ppermute | solution.py:38
  90.1 4.5 %collective-permute-start.13 = (f32[64]{0:T(128)S(1)}, f32[64]{0:T(128)S(1)}, u32[]{:S(2)}, u32[]{:S(2)}) collective-permute-start(f32[64]{0:T(128)S(1)} %add.243), channel_id=1, source_target_pairs={{0,32},{1,33},{2,34},{3,35},{4,36},{5,37},{6,38},{7,39},{8,40},{9,... | collective-permute-start | bytes 776 | tf_op jit(solution)/shard_map/ppermute | solution.py:38
  101.4 3.9 %collective-permute-start.15 = (f32[512]{0:T(512)S(1)}, f32[512]{0:T(512)S(1)}, u32[]{:S(2)}, u32[]{:S(2)}) collective-permute-start(f32[512]{0:T(512)S(1)} %fusion.55), channel_id=1, source_target_pairs={{0,128},{64,192},{128,0},{192,64},{256,384},{320,448},{384,256},{4... | collective-permute-start | bytes 6152 | tf_op jit(solution)/shard_map/ppermute | solution.py:38
  106.9 4.0 %collective-permute-start.16 = (f32[512]{0:T(512)S(1)}, f32[512]{0:T(512)S(1)}, u32[]{:S(2)}, u32[]{:S(2)}) collective-permute-start(f32[512]{0:T(512)S(1)} %add.253), channel_id=1, source_target_pairs={{0,256},{64,320},{128,384},{192,448},{256,0},{320,64},{384,128},{4... | collective-permute-start | bytes 6152 | tf_op jit(solution)/shard_map/ppermute | solution.py:38
  118.7 3.6 %collective-permute-start.18 = (f32[512]{0:T(512)S(1)}, f32[512]{0:T(512)S(1)}, u32[]{:S(2)}, u32[]{:S(2)}) collective-permute-start(f32[512]{0:T(512)S(1)} %add.255), channel_id=1, source_target_pairs={{0,2},{1,3},{2,0},{3,1},{4,6},{5,7},{6,4},{7,5},{8,10},{9,11},{10,... | collective-permute-start | bytes 6152 | tf_op jit(solution)/shard_map/ppermute | solution.py:38
  125.1 6.6 %collective-permute-start.19 = (f32[512]{0:T(512)S(1)}, f32[512]{0:T(512)S(1)}, u32[]{:S(2)}, u32[]{:S(2)}) collective-permute-start(f32[512]{0:T(512)S(1)} %add.256), channel_id=1, source_target_pairs={{0,4},{1,5},{2,6},{3,7},{4,0},{5,1},{6,2},{7,3},{8,12},{9,13},{10,... | collective-permute-start | bytes 6152 | tf_op jit(solution)/shard_map/ppermute | solution.py:38
  134.4 6.6 %collective-permute-start.20 = (f32[512]{0:T(512)S(1)}, f32[512]{0:T(512)S(1)}, u32[]{:S(2)}, u32[]{:S(2)}) collective-permute-start(f32[512]{0:T(512)S(1)} %add.257), channel_id=1, source_target_pairs={{0,8},{1,9},{2,10},{3,11},{4,12},{5,13},{6,14},{7,15},{8,0},{9,1},... | collective-permute-start | bytes 6152 | tf_op jit(solution)/shard_map/ppermute | solution.py:38
  146.5 5.0 %reshape.344 = f32[1024,2,2,2,32]{4,3,2,1,0:T(2,128)} reshape(bf16[64,16,256]{2,1,0:T(8,128)(2,1)S(1)} %copy-done.4) | data formatting | bytes 1572864 | tf_op jit(solution)/shard_map/reshape | solution.py:122
  151.6 5.2 %copy.123 = f32[1024,2,2,2,32]{0,4,3,2,1:T(8,128)S(1)} copy(f32[1024,2,2,2,32]{4,3,2,1,0:T(2,128)} %reshape.344) | data formatting | bytes 2097152 | tf_op jit(solution)/shard_map/reshape | solution.py:122
  157.4 4.9 %reshape_squeeze.6 = f32[1024,2,2,2,32]{4,3,2,1,0:T(2,128)} reshape(f32[64,1,16,256]{3,2,0,1:T(8,128)S(1)} %copy.138) | data formatting | bytes 2097152 | tf_op jit(solution)/shard_map/reshape;squeeze | solution.py:103
  162.3 5.2 %copy.122 = f32[1024,2,2,2,32]{0,4,3,2,1:T(8,128)S(1)} copy(f32[1024,2,2,2,32]{4,3,2,1,0:T(2,128)} %reshape_squeeze.6) | data formatting | bytes 2097152 | tf_op jit(solution)/shard_map/reshape;squeeze | solution.py:103
  167.7 6.0 %collective-permute-start.22 = (f32[512]{0:T(512)S(1)}, f32[512]{0:T(512)S(1)}, u32[]{:S(2)}, u32[]{:S(2)}) collective-permute-start(f32[512]{0:T(512)S(1)} %add.259), channel_id=1, source_target_pairs={{0,32},{1,33},{2,34},{3,35},{4,36},{5,37},{6,38},{7,39},{8,40},{9,... | collective-permute-start | bytes 6152 | tf_op jit(solution)/shard_map/ppermute | solution.py:38
  182.4 9.3 %fusion.14 = f32[3,3,256,256]{3,2,1,0:T(8,128)} fusion(bf16[64,16,1,256]{3,2,1,0:T(2,128)(2,1)} %reshape.381, bf16[1,66,18,256]{3,2,1,0:T(8,128)(2,1)S(1)} %copy-done.8), kind=kOutput, calls=%fused_computation.18 | convolution fusion | flops 1207959552 | bytes 3491840 | tf_op jit(solution)/shard_map/conv_general_dilated | solution.py:159
  207.2 3.9 %collective-permute-start.23 = (bf16[64,1,256]{2,1,0:T(2,128)(2,1)S(1)}, bf16[64,1,256]{2,1,0:T(2,128)(2,1)S(1)}, u32[]{:S(2)}, u32[]{:S(2)}) collective-permute-start(bf16[64,1,256]{2,1,0:T(2,128)(2,1)S(1)} %get-tuple-element.89), channel_id=1, source_target_pairs={{0,1},{1,2},{2,3},{3,4},{4,5},{5,6},{6,7},{7,8},{8,9},{9,10},{10,1... | collective-permute-start | bytes 98312 | tf_op jit(solution)/shard_map/ppermute | solution.py:16
  211.1 11.4 %collective-permute-start.24 = (bf16[64,1,256]{2,1,0:T(2,128)(2,1)S(1)}, bf16[64,1,256]{2,1,0:T(2,128)(2,1)S(1)}, u32[]{:S(2)}, u32[]{:S(2)}) collective-permute-start(bf16[64,1,256]{2,1,0:T(2,128)(2,1)S(1)} %get-tuple-element.90), channel_id=1, source_target_pairs={{1,0},{2,1},{3,2},{4,3},{5,4},{6,5},{7,6},{8,7},{9,8},{10,9},{11,1... | collective-permute-start | bytes 98312 | tf_op jit(solution)/shard_map/ppermute | solution.py:17
  227.4 4.9 %collective-permute-start.27 = (bf16[2,18,256]{2,1,0:T(8,128)(2,1)S(1)}, bf16[2,18,256]{2,1,0:T(8,128)(2,1)S(1)}, u32[]{:S(2)}, u32[]{:S(2)}) collective-permute-start(bf16[2,18,256]{2,1,0:T(8,128)(2,1)S(1)} %pad_maximum_fusion.2), channel_id=1, source_target_pairs={{32,0},{33,1},{34,2},{35,3},{36,4},{37,5},{38,6},{39,7},{40,8},{41... | collective-permute-start | bytes 55304 | tf_op jit(solution)/shard_map/ppermute | solution.py:25
  240.0 3.4 %collective-permute-done.30 = f32[2,2,2,2,36,128]{5,3,4,2,1,0:T(2,128)S(1)} collective-permute-done((f32[2,2,2,2,36,128]{5,3,4,2,1,0:T(2,128)S(1)}, f32[2,2,2,2,36,128]{5,3,4,2,1,0:T(2,128)S(1)}, u32[]{:S(2)}, u32[]{:S(2)}) %collective-permute-start.30) | collective-permute-done | bytes 294944 | tf_op jit(solution)/shard_map/ppermute | solution.py:38
  246.0 10.4 %collective-permute-done.31 = f32[2,2,2,36,128]{4,2,3,1,0:T(2,128)S(1)} collective-permute-done((f32[2,2,2,36,128]{4,2,3,1,0:T(2,128)S(1)}, f32[2,2,2,36,128]{4,2,3,1,0:T(2,128)S(1)}, u32[]{:S(2)}, u32[]{:S(2)}) %collective-permute-start.31) | collective-permute-done | bytes 147488 | tf_op jit(solution)/shard_map/ppermute | solution.py:38
  256.5 4.3 %collective-permute-start.32 = (f32[2,2,36,128]{3,1,2,0:T(2,128)S(1)}, f32[2,2,36,128]{3,1,2,0:T(2,128)S(1)}, u32[]{:S(2)}, u32[]{:S(2)}) collective-permute-start(f32[2,2,36,128]{3,1,2,0:T(2,128)S(1)} %dynamic-slice_bitcast_fusion.1), channel_id=1, source_target_pairs={{0,32},{1,33},{2,34},{3,35},{4,36},{5,37},{6,38},{7,39},{8,40},{9,... | collective-permute-start | bytes 221192 | tf_op jit(solution)/shard_map/ppermute | solution.py:38
  261.0 3.2 %collective-permute-done.32 = f32[2,2,36,128]{3,1,2,0:T(2,128)S(1)} collective-permute-done((f32[2,2,36,128]{3,1,2,0:T(2,128)S(1)}, f32[2,2,36,128]{3,1,2,0:T(2,128)S(1)}, u32[]{:S(2)}, u32[]{:S(2)}) %collective-permute-start.32) | collective-permute-done | bytes 73760 | tf_op jit(solution)/shard_map/ppermute | solution.py:38
  266.5 7.7 %collective-permute-done.33 = f32[2,36,128]{2,0,1:T(2,128)S(1)} collective-permute-done((f32[2,36,128]{2,0,1:T(2,128)S(1)}, f32[2,36,128]{2,0,1:T(2,128)S(1)}, u32[]{:S(2)}, u32[]{:S(2)}) %collective-permute-start.33) | collective-permute-done | bytes 36896 | tf_op jit(solution)/shard_map/ppermute | solution.py:38
  274.2 4.3 %collective-permute-start.34 = (f32[36,128]{1,0:T(8,128)S(1)}, f32[36,128]{1,0:T(8,128)S(1)}, u32[]{:S(2)}, u32[]{:S(2)}) collective-permute-start(f32[36,128]{1,0:T(8,128)S(1)} %bitcast.141), channel_id=1, source_target_pairs={{0,8},{1,9},{2,10},{3,11},{4,12},{5,13},{6,14},{7,15},{8,0},{9,1},... | collective-permute-start | bytes 55304 | tf_op jit(solution)/shard_map/ppermute | solution.py:38
  278.7 5.1 %collective-permute-done.34 = f32[36,128]{1,0:T(8,128)S(1)} collective-permute-done((f32[36,128]{1,0:T(8,128)S(1)}, f32[36,128]{1,0:T(8,128)S(1)}, u32[]{:S(2)}, u32[]{:S(2)}) %collective-permute-start.34) | collective-permute-done | bytes 18464 | tf_op jit(solution)/shard_map/ppermute | solution.py:38
  283.9 3.4 %collective-permute-start.35 = (f32[36,64]{1,0:T(8,128)S(1)}, f32[36,64]{1,0:T(8,128)S(1)}, u32[]{:S(2)}, u32[]{:S(2)}) collective-permute-start(f32[36,64]{1,0:T(8,128)S(1)} %constant_dynamic-slice_fusion.1), channel_id=1, source_target_pairs={{0,128},{64,192},{128,0},{192,64},{256,384},{320,448},{384,256},{4... | collective-permute-start | bytes 27656 | tf_op jit(solution)/shard_map/ppermute | solution.py:38
  (222 shorter events, 117.7 us)
Async XLA Ops:
  1.8 20.0 %collective-permute-start = (bf16[64,1,256]{2,1,0:T(2,128)(2,1)S(1)}, bf16[64,1,256]{2,1,0:T(2,128)(2,1)S(1)}, u32[]{:S(2)}, u32[]{:S(2)}) collective-permute-start(bf16[64,1,256]{2,1,0:T(2,128)(2,1)S(1)} %get-tuple-element.91), channel_id=1, source_target_pairs={{0,1},{1,2},{2,3},{3,4},{4,5},{5,6},{6,7},{7,8},{8,9},{9,10},{10,1... | collective-permute-start | bytes 98312 | tf_op jit(solution)/shard_map/ppermute | solution.py:16
  6.1 16.9 %collective-permute-start.1 = (bf16[64,1,256]{2,1,0:T(2,128)(2,1)S(1)}, bf16[64,1,256]{2,1,0:T(2,128)(2,1)S(1)}, u32[]{:S(2)}, u32[]{:S(2)}) collective-permute-start(bf16[64,1,256]{2,1,0:T(2,128)(2,1)S(1)} %get-tuple-element.92), channel_id=1, source_target_pairs={{1,0},{2,1},{3,2},{4,3},{5,4},{6,5},{7,6},{8,7},{9,8},{10,9},{11,1... | collective-permute-start | bytes 98312 | tf_op jit(solution)/shard_map/ppermute | solution.py:17
  23.7 5.7 %collective-permute-start.2 = (bf16[1,18,256]{2,1,0:T(8,128)(2,1)S(1)}, bf16[1,18,256]{2,1,0:T(8,128)(2,1)S(1)}, u32[]{:S(2)}, u32[]{:S(2)}) collective-permute-start(bf16[1,18,256]{2,1,0:T(8,128)(2,1)S(1)} %get-tuple-element.87), channel_id=1, source_target_pairs={{0,64},{64,128},{128,192},{192,256},{256,320},{320,384},{384,448},... | collective-permute-start | bytes 27656 | tf_op jit(solution)/shard_map/ppermute | solution.py:16
  26.3 7.2 %collective-permute-start.4 = (bf16[2,18,256]{2,1,0:T(8,128)(2,1)S(1)}, bf16[2,18,256]{2,1,0:T(8,128)(2,1)S(1)}, u32[]{:S(2)}, u32[]{:S(2)}) collective-permute-start(bf16[2,18,256]{2,1,0:T(8,128)(2,1)S(1)} %pad_maximum_fusion.1), channel_id=1, source_target_pairs={{32,0},{33,1},{34,2},{35,3},{36,4},{37,5},{38,6},{39,7},{40,8},{41... | collective-permute-start | bytes 55304 | tf_op jit(solution)/shard_map/ppermute | solution.py:25
  41.6 6.3 %collective-permute-start.6 = (f32[64]{0:T(128)S(1)}, f32[64]{0:T(128)S(1)}, u32[]{:S(2)}, u32[]{:S(2)}) collective-permute-start(f32[64]{0:T(128)S(1)} %fusion.64), channel_id=1, source_target_pairs={{0,128},{64,192},{128,0},{192,64},{256,384},{320,448},{384,256},{4... | collective-permute-start | bytes 776 | tf_op jit(solution)/shard_map/ppermute | solution.py:38
  47.9 6.3 %collective-permute-start.7 = (f32[64]{0:T(128)S(1)}, f32[64]{0:T(128)S(1)}, u32[]{:S(2)}, u32[]{:S(2)}) collective-permute-start(f32[64]{0:T(128)S(1)} %add.237), channel_id=1, source_target_pairs={{0,256},{64,320},{128,384},{192,448},{256,0},{320,64},{384,128},{4... | collective-permute-start | bytes 776 | tf_op jit(solution)/shard_map/ppermute | solution.py:38
  54.2 5.4 %collective-permute-start.8 = (f32[64]{0:T(128)S(1)}, f32[64]{0:T(128)S(1)}, u32[]{:S(2)}, u32[]{:S(2)}) collective-permute-start(f32[64]{0:T(128)S(1)} %add.238), channel_id=1, source_target_pairs={{0,1},{1,0},{2,3},{3,2},{4,5},{5,4},{6,7},{7,6},{8,9},{9,8},{10,11... | collective-permute-start | bytes 776 | tf_op jit(solution)/shard_map/ppermute | solution.py:38
  59.6 6.3 %collective-permute-start.9 = (f32[64]{0:T(128)S(1)}, f32[64]{0:T(128)S(1)}, u32[]{:S(2)}, u32[]{:S(2)}) collective-permute-start(f32[64]{0:T(128)S(1)} %add.239), channel_id=1, source_target_pairs={{0,2},{1,3},{2,0},{3,1},{4,6},{5,7},{6,4},{7,5},{8,10},{9,11},{10,... | collective-permute-start | bytes 776 | tf_op jit(solution)/shard_map/ppermute | solution.py:38
  66.0 9.3 %collective-permute-start.10 = (f32[64]{0:T(128)S(1)}, f32[64]{0:T(128)S(1)}, u32[]{:S(2)}, u32[]{:S(2)}) collective-permute-start(f32[64]{0:T(128)S(1)} %add.240), channel_id=1, source_target_pairs={{0,4},{1,5},{2,6},{3,7},{4,0},{5,1},{6,2},{7,3},{8,12},{9,13},{10,... | collective-permute-start | bytes 776 | tf_op jit(solution)/shard_map/ppermute | solution.py:38
  75.3 9.3 %collective-permute-start.11 = (f32[64]{0:T(128)S(1)}, f32[64]{0:T(128)S(1)}, u32[]{:S(2)}, u32[]{:S(2)}) collective-permute-start(f32[64]{0:T(128)S(1)} %add.241), channel_id=1, source_target_pairs={{0,8},{1,9},{2,10},{3,11},{4,12},{5,13},{6,14},{7,15},{8,0},{9,1},... | collective-permute-start | bytes 776 | tf_op jit(solution)/shard_map/ppermute | solution.py:38
  90.1 6.9 %collective-permute-start.13 = (f32[64]{0:T(128)S(1)}, f32[64]{0:T(128)S(1)}, u32[]{:S(2)}, u32[]{:S(2)}) collective-permute-start(f32[64]{0:T(128)S(1)} %add.243), channel_id=1, source_target_pairs={{0,32},{1,33},{2,34},{3,35},{4,36},{5,37},{6,38},{7,39},{8,40},{9,... | collective-permute-start | bytes 776 | tf_op jit(solution)/shard_map/ppermute | solution.py:38
  101.4 5.5 %collective-permute-start.15 = (f32[512]{0:T(512)S(1)}, f32[512]{0:T(512)S(1)}, u32[]{:S(2)}, u32[]{:S(2)}) collective-permute-start(f32[512]{0:T(512)S(1)} %fusion.55), channel_id=1, source_target_pairs={{0,128},{64,192},{128,0},{192,64},{256,384},{320,448},{384,256},{4... | collective-permute-start | bytes 6152 | tf_op jit(solution)/shard_map/ppermute | solution.py:38
  106.9 6.4 %collective-permute-start.16 = (f32[512]{0:T(512)S(1)}, f32[512]{0:T(512)S(1)}, u32[]{:S(2)}, u32[]{:S(2)}) collective-permute-start(f32[512]{0:T(512)S(1)} %add.253), channel_id=1, source_target_pairs={{0,256},{64,320},{128,384},{192,448},{256,0},{320,64},{384,128},{4... | collective-permute-start | bytes 6152 | tf_op jit(solution)/shard_map/ppermute | solution.py:38
  113.2 5.5 %collective-permute-start.17 = (f32[512]{0:T(512)S(1)}, f32[512]{0:T(512)S(1)}, u32[]{:S(2)}, u32[]{:S(2)}) collective-permute-start(f32[512]{0:T(512)S(1)} %add.254), channel_id=1, source_target_pairs={{0,1},{1,0},{2,3},{3,2},{4,5},{5,4},{6,7},{7,6},{8,9},{9,8},{10,11... | collective-permute-start | bytes 6152 | tf_op jit(solution)/shard_map/ppermute | solution.py:38
  118.7 6.4 %collective-permute-start.18 = (f32[512]{0:T(512)S(1)}, f32[512]{0:T(512)S(1)}, u32[]{:S(2)}, u32[]{:S(2)}) collective-permute-start(f32[512]{0:T(512)S(1)} %add.255), channel_id=1, source_target_pairs={{0,2},{1,3},{2,0},{3,1},{4,6},{5,7},{6,4},{7,5},{8,10},{9,11},{10,... | collective-permute-start | bytes 6152 | tf_op jit(solution)/shard_map/ppermute | solution.py:38
  125.1 9.4 %collective-permute-start.19 = (f32[512]{0:T(512)S(1)}, f32[512]{0:T(512)S(1)}, u32[]{:S(2)}, u32[]{:S(2)}) collective-permute-start(f32[512]{0:T(512)S(1)} %add.256), channel_id=1, source_target_pairs={{0,4},{1,5},{2,6},{3,7},{4,0},{5,1},{6,2},{7,3},{8,12},{9,13},{10,... | collective-permute-start | bytes 6152 | tf_op jit(solution)/shard_map/ppermute | solution.py:38
  134.4 9.4 %collective-permute-start.20 = (f32[512]{0:T(512)S(1)}, f32[512]{0:T(512)S(1)}, u32[]{:S(2)}, u32[]{:S(2)}) collective-permute-start(f32[512]{0:T(512)S(1)} %add.257), channel_id=1, source_target_pairs={{0,8},{1,9},{2,10},{3,11},{4,12},{5,13},{6,14},{7,15},{8,0},{9,1},... | collective-permute-start | bytes 6152 | tf_op jit(solution)/shard_map/ppermute | solution.py:38
  143.8 23.8 %collective-permute-start.21 = (f32[512]{0:T(512)S(1)}, f32[512]{0:T(512)S(1)}, u32[]{:S(2)}, u32[]{:S(2)}) collective-permute-start(f32[512]{0:T(512)S(1)} %add.258), channel_id=1, source_target_pairs={{0,16},{1,17},{2,18},{3,19},{4,20},{5,21},{6,22},{7,23},{8,24},{9,... | collective-permute-start | bytes 6152 | tf_op jit(solution)/shard_map/ppermute | solution.py:38
  167.7 7.4 %collective-permute-start.22 = (f32[512]{0:T(512)S(1)}, f32[512]{0:T(512)S(1)}, u32[]{:S(2)}, u32[]{:S(2)}) collective-permute-start(f32[512]{0:T(512)S(1)} %add.259), channel_id=1, source_target_pairs={{0,32},{1,33},{2,34},{3,35},{4,36},{5,37},{6,38},{7,39},{8,40},{9,... | collective-permute-start | bytes 6152 | tf_op jit(solution)/shard_map/ppermute | solution.py:38
  205.2 28.2 %collective-permute-start.29 = (f32[2,2,2,2,2,36,128]{6,4,5,3,2,1,0:T(2,128)}, f32[2,2,2,2,2,36,128]{6,4,5,3,2,1,0:T(2,128)S(1)}, u32[]{:S(2)}, u32[]{:S(2)}) collective-permute-start(f32[2,2,2,2,2,36,128]{6,4,5,3,2,1,0:T(2,128)} %bitcast.127), channel_id=1, source_target_pairs={{0,1},{1,0},{2,3},{3,2},{4,5},{5,4},{6,7},{7,6},{8,9},{9,8},{10,11... | collective-permute-start | bytes 1769480 | tf_op jit(solution)/shard_map/ppermute | solution.py:38
  207.2 15.8 %collective-permute-start.23 = (bf16[64,1,256]{2,1,0:T(2,128)(2,1)S(1)}, bf16[64,1,256]{2,1,0:T(2,128)(2,1)S(1)}, u32[]{:S(2)}, u32[]{:S(2)}) collective-permute-start(bf16[64,1,256]{2,1,0:T(2,128)(2,1)S(1)} %get-tuple-element.89), channel_id=1, source_target_pairs={{0,1},{1,2},{2,3},{3,4},{4,5},{5,6},{6,7},{7,8},{8,9},{9,10},{10,1... | collective-permute-start | bytes 98312 | tf_op jit(solution)/shard_map/ppermute | solution.py:16
  211.1 13.6 %collective-permute-start.24 = (bf16[64,1,256]{2,1,0:T(2,128)(2,1)S(1)}, bf16[64,1,256]{2,1,0:T(2,128)(2,1)S(1)}, u32[]{:S(2)}, u32[]{:S(2)}) collective-permute-start(bf16[64,1,256]{2,1,0:T(2,128)(2,1)S(1)} %get-tuple-element.90), channel_id=1, source_target_pairs={{1,0},{2,1},{3,2},{4,3},{5,4},{6,5},{7,6},{8,7},{9,8},{10,9},{11,1... | collective-permute-start | bytes 98312 | tf_op jit(solution)/shard_map/ppermute | solution.py:17
  224.7 7.5 %collective-permute-start.25 = (bf16[1,18,256]{2,1,0:T(8,128)(2,1)S(1)}, bf16[1,18,256]{2,1,0:T(8,128)(2,1)S(1)}, u32[]{:S(2)}, u32[]{:S(2)}) collective-permute-start(bf16[1,18,256]{2,1,0:T(8,128)(2,1)S(1)} %get-tuple-element.85), channel_id=1, source_target_pairs={{0,64},{64,128},{128,192},{192,256},{256,320},{320,384},{384,448},... | collective-permute-start | bytes 27656 | tf_op jit(solution)/shard_map/ppermute | solution.py:16
  226.0 6.2 %collective-permute-start.26 = (bf16[1,18,256]{2,1,0:T(8,128)(2,1)S(1)}, bf16[1,18,256]{2,1,0:T(8,128)(2,1)S(1)}, u32[]{:S(2)}, u32[]{:S(2)}) collective-permute-start(bf16[1,18,256]{2,1,0:T(8,128)(2,1)S(1)} %get-tuple-element.86), channel_id=1, source_target_pairs={{64,0},{128,64},{192,128},{256,192},{320,256},{384,320},{448,384},... | collective-permute-start | bytes 27656 | tf_op jit(solution)/shard_map/ppermute | solution.py:17
  227.4 12.5 %collective-permute-start.27 = (bf16[2,18,256]{2,1,0:T(8,128)(2,1)S(1)}, bf16[2,18,256]{2,1,0:T(8,128)(2,1)S(1)}, u32[]{:S(2)}, u32[]{:S(2)}) collective-permute-start(bf16[2,18,256]{2,1,0:T(8,128)(2,1)S(1)} %pad_maximum_fusion.2), channel_id=1, source_target_pairs={{32,0},{33,1},{34,2},{35,3},{36,4},{37,5},{38,6},{39,7},{40,8},{41... | collective-permute-start | bytes 55304 | tf_op jit(solution)/shard_map/ppermute | solution.py:25
  233.8 9.6 %collective-permute-start.30 = (f32[2,2,2,2,36,128]{5,3,4,2,1,0:T(2,128)S(1)}, f32[2,2,2,2,36,128]{5,3,4,2,1,0:T(2,128)S(1)}, u32[]{:S(2)}, u32[]{:S(2)}) collective-permute-start(f32[2,2,2,2,36,128]{5,3,4,2,1,0:T(2,128)S(1)} %dynamic-slice_bitcast_fusion), channel_id=1, source_target_pairs={{0,16},{1,17},{2,18},{3,19},{4,20},{5,21},{6,22},{7,23},{8,24},{9,... | collective-permute-start | bytes 884744 | tf_op jit(solution)/shard_map/ppermute | solution.py:38
  243.9 12.4 %collective-permute-start.31 = (f32[2,2,2,36,128]{4,2,3,1,0:T(2,128)S(1)}, f32[2,2,2,36,128]{4,2,3,1,0:T(2,128)S(1)}, u32[]{:S(2)}, u32[]{:S(2)}) collective-permute-start(f32[2,2,2,36,128]{4,2,3,1,0:T(2,128)S(1)} %bitcast.138), channel_id=1, source_target_pairs={{0,2},{1,3},{2,0},{3,1},{4,6},{5,7},{6,4},{7,5},{8,10},{9,11},{10,... | collective-permute-start | bytes 442376 | tf_op jit(solution)/shard_map/ppermute | solution.py:38
  256.5 7.8 %collective-permute-start.32 = (f32[2,2,36,128]{3,1,2,0:T(2,128)S(1)}, f32[2,2,36,128]{3,1,2,0:T(2,128)S(1)}, u32[]{:S(2)}, u32[]{:S(2)}) collective-permute-start(f32[2,2,36,128]{3,1,2,0:T(2,128)S(1)} %dynamic-slice_bitcast_fusion.1), channel_id=1, source_target_pairs={{0,32},{1,33},{2,34},{3,35},{4,36},{5,37},{6,38},{7,39},{8,40},{9,... | collective-permute-start | bytes 221192 | tf_op jit(solution)/shard_map/ppermute | solution.py:38
  264.4 9.8 %collective-permute-start.33 = (f32[2,36,128]{2,0,1:T(2,128)S(1)}, f32[2,36,128]{2,0,1:T(2,128)S(1)}, u32[]{:S(2)}, u32[]{:S(2)}) collective-permute-start(f32[2,36,128]{2,0,1:T(2,128)S(1)} %bitcast.140), channel_id=1, source_target_pairs={{0,4},{1,5},{2,6},{3,7},{4,0},{5,1},{6,2},{7,3},{8,12},{9,13},{10,... | collective-permute-start | bytes 110600 | tf_op jit(solution)/shard_map/ppermute | solution.py:38
  274.2 9.6 %collective-permute-start.34 = (f32[36,128]{1,0:T(8,128)S(1)}, f32[36,128]{1,0:T(8,128)S(1)}, u32[]{:S(2)}, u32[]{:S(2)}) collective-permute-start(f32[36,128]{1,0:T(8,128)S(1)} %bitcast.141), channel_id=1, source_target_pairs={{0,8},{1,9},{2,10},{3,11},{4,12},{5,13},{6,14},{7,15},{8,0},{9,1},... | collective-permute-start | bytes 55304 | tf_op jit(solution)/shard_map/ppermute | solution.py:38
  283.9 5.7 %collective-permute-start.35 = (f32[36,64]{1,0:T(8,128)S(1)}, f32[36,64]{1,0:T(8,128)S(1)}, u32[]{:S(2)}, u32[]{:S(2)}) collective-permute-start(f32[36,64]{1,0:T(8,128)S(1)} %constant_dynamic-slice_fusion.1), channel_id=1, source_target_pairs={{0,128},{64,192},{128,0},{192,64},{256,384},{320,448},{384,256},{4... | collective-permute-start | bytes 27656 | tf_op jit(solution)/shard_map/ppermute | solution.py:38
  289.7 6.6 %collective-permute-start.36 = (f32[36,32]{1,0:T(8,128)S(1)}, f32[36,32]{1,0:T(8,128)S(1)}, u32[]{:S(2)}, u32[]{:S(2)}) collective-permute-start(f32[36,32]{1,0:T(8,128)S(1)} %constant_dynamic-slice_fusion), channel_id=1, source_target_pairs={{0,256},{64,320},{128,384},{192,448},{256,0},{320,64},{384,128},{4... | collective-permute-start | bytes 13832 | tf_op jit(solution)/shard_map/ppermute | solution.py:38
  (32 other events, 251.3 us)

commit v4 on v3

--- a/solution.py
+++ b/solution.py
@@ -51,35 +51,14 @@
     return value
 
 
-def halving_sum(term):
-    lon_n = term.shape[0]
-    lon_bits = (lon_n - 1).bit_length()
-    lat_bits = (lax.axis_size("lat") - 1).bit_length()
-    split = term.reshape((2,) * lon_bits + term.shape[1:])
-    dims = {b: lon_bits - 1 - b for b in range(lon_bits)}
-
-    def row_round(split, bit, dims):
-        dim = dims[bit]
+def lon_halving_sum(rows):
+    for bit in reversed(range((lax.axis_size("lon") - 1).bit_length())):
+        half = rows.shape[1] // 2
         mine = (lax.axis_index("lon") >> bit) & 1
-        keep = lax.dynamic_index_in_dim(split, mine, dim, keepdims=False)
-        send = lax.dynamic_index_in_dim(split, 1 - mine, dim, keepdims=False)
-        dims = {k: (d - 1 if d > dim else d) for k, d in dims.items() if k != bit}
-        return keep + exchange(send, "lon", bit), dims
-
-    def col_round(split, bit):
-        half = split.shape[-1] // 2
-        mine = (lax.axis_index("lat") >> bit) & 1
-        keep = lax.dynamic_slice_in_dim(split, mine * half, half, axis=split.ndim - 1)
-        send = lax.dynamic_slice_in_dim(split, (1 - mine) * half, half, axis=split.ndim - 1)
-        return keep + exchange(send, "lat", bit)
-
-    split = col_round(split, 0)
-    row_order = [0, 4, 1, 5, 2, 3] if lon_bits == 6 else list(range(lon_bits))
-    for bit in row_order:
-        split, dims = row_round(split, bit, dims)
-    for bit in range(1, lat_bits):
-        split = col_round(split, bit)
-    return split
+        keep = lax.dynamic_slice_in_dim(rows, mine * half, half, axis=1)
+        send = lax.dynamic_slice_in_dim(rows, (1 - mine) * half, half, axis=1)
+        rows = keep + exchange(send, "lon", bit)
+    return rows
 
 
 def conv_valid(field, weights):
@@ -121,19 +100,27 @@
     )
     upstream = cotangent.astype(jnp.float32).reshape(-1, channels)
     dpre = upstream * (sigma * (1.0 + pre * (1.0 - sigma)))
+    pair_banded, pair_distant = extend(
+        jnp.concatenate([dpre, ghat], 1).reshape(height, breadth, 2 * channels)
+    )
     grad_sums = butterfly_sum(jnp.concatenate([jnp.sum(dpre * ghat, 0), jnp.sum(dpre, 0)]))
     grad_gain, grad_shift = grad_sums[:channels], grad_sums[channels:]
     mean_a = (norm_gain * grad_shift).reshape(G, -1).sum(1) / count
     mean_b = (norm_gain * grad_gain).reshape(G, -1).sum(1) / count
-    dconv = (
-        (
-            dpre * norm_gain
-            - jnp.repeat(mean_a, channels // G)
-            - ghat * jnp.repeat(mean_b, channels // G)
-        )
-        * rstd_ch
-    ).astype(jnp.bfloat16)
-    grad_banded, grad_distant = extend(dconv.reshape(height, breadth, channels))
+
+    def normalized_grad(pair):
+        return (
+            (
+                pair[..., :channels] * norm_gain
+                - jnp.repeat(mean_a, channels // G)
+                - pair[..., channels:] * jnp.repeat(mean_b, channels // G)
+            )
+            * rstd_ch
+        ).astype(jnp.bfloat16)
+
+    grad_banded = normalized_grad(pair_banded)
+    grad_distant = normalized_grad(pair_distant)
+    dconv = grad_banded[1:-1, 1:-1]
     flipped = jnp.swapaxes(kernel[::-1, ::-1], 2, 3)
     back = conv_valid(grad_banded, flipped)
     upper_term = jnp.zeros((breadth, channels), jnp.float32)
@@ -152,20 +139,16 @@
     back = back.at[0].add(jnp.where(north, upper_term, 0.0))
     back = back.at[-1].add(jnp.where(south, lower_term, 0.0))
     grad_fields = (upstream.reshape(height, breadth, channels) + back).astype(jnp.bfloat16)
-    lat_n, lon_n = lax.axis_size("lat"), lax.axis_size("lon")
-    lat_bits = (lat_n - 1).bit_length()
-    lat_major = dconv.reshape((-1,) + (2,) * lat_bits + (channels // lat_n,))
-    lat_major = lat_major.transpose((0,) + tuple(range(lat_bits, 0, -1)) + (lat_bits + 1,))
     term = lax.conv_general_dilated(
         merged[None],
-        lat_major.reshape(height, breadth, 1, channels),
+        dconv.reshape(height, breadth, 1, channels),
         (1, 1),
         "VALID",
-        dimension_numbers=("CHWN", "HWIO", "HWNC"),
+        dimension_numbers=("CHWN", "HWIO", "CHWN"),
         preferred_element_type=jnp.float32,
-    )
-    blocks = term.reshape(lon_n, 9 * channels // lon_n, channels)
-    grad_kernel = halving_sum(blocks)
+    ).reshape(channels, 9 * channels)
+    owned_cols = lax.psum_scatter(term, "lat", scatter_dimension=0, tiled=True)
+    grad_kernel = lon_halving_sum(owned_cols).T
     return (block_out, grad_fields, grad_kernel, grad_gain, grad_shift)
 
 

time: 300 us -> 301 us (level)
  local copies, waits for them, and re-layouts: 42.9 us -> 13.3 us
  waiting for transfers between devices: 83.9 us -> 103 us
  between operations: 1.77 us -> 15 us
    reduce_scatter x0 -> x1, waiting for transfers between devices: none -> 32.8 us  [local(): owned_cols = lax.psum_scatter(term, 'lat', scatter_dimension=0, tiled=True)]
    ppermute x27 -> x24, waiting for transfers between devices: 76.4 us -> 59.4 us  [exchange(): return lax.ppermute(block, axis, [(i, i ^ 1 << bit) for i in range(peers)])]
    another operation x3 -> x0, local copies, waits for them, and re-layouts: 12.4 us -> none  [the longest x2 10 us: local(): conv_out = conv_valid(merged, kernel).reshape(-1, channels)]
    reshape x3 -> x2, local copies, waits for them, and re-layouts: 12.5 us -> 2.2 us  [the longest x1 1.98 us: local(): term = lax.conv_general_dilated(merged[None], dconv.reshape(height, bread...]
    ppermute x4, waiting for transfers between devices: 2.93 us -> 6.94 us  [with_halo(): after = lax.ppermute(initial, axis, down)]
    ppermute x27 -> x24, starting transfers between devices: 96.4 us -> 98.6 us  [exchange(): return lax.ppermute(block, axis, [(i, i ^ 1 << bit) for i in range(peers)])]
    unnamed x59 -> x52, local copies, waits for them, and re-layouts: 7.35 us -> 5.7 us
  transfers between devices with their start and end apart: 37 -> 35, of which waited for: 30 -> 30; matrix products, arithmetic and copies ran while one was open for 11% -> 4% of each run, Pallas kernels for 0% -> 0%
where the time goes in v4:
time: 301 us; the launch traced here: 300 us
  starting transfers between devices  144 us (48%)
  waiting for transfers between devices  103 us (34%)
  between operations  15 us (5%)
  local copies, waits for them, and re-layouts  13.3 us (4%)
  other arithmetic  12.7 us (4%)
  matrix products  11.8 us (4%)
    ppermute x24, starting transfers between devices, exchange(): return lax.ppermute(block, axis, [(i, i ^ 1 << bit) for i in range(peers)])  98.6 us
    ppermute x24, waiting for transfers between devices, exchange(): return lax.ppermute(block, axis, [(i, i ^ 1 << bit) for i in range(peers)])  59.4 us
    reduce_scatter x1, waiting for transfers between devices, local(): owned_cols = lax.psum_scatter(term, 'lat', scatter_dimension=0, tiled=True)  32.8 us
    ppermute x4, starting transfers between devices, with_halo(): after = lax.ppermute(initial, axis, down)  27.7 us
    ppermute x4, starting transfers between devices, with_halo(): before = lax.ppermute(last, axis, up)  8.78 us
    ppermute x2, starting transfers between devices, passed_along(): return lax.ppermute(block, axis, route)  8.61 us
    ppermute x4, waiting for transfers between devices, with_halo(): after = lax.ppermute(initial, axis, down)  6.94 us
    conv_general_dilated x1, matrix products, local(): lax.conv_general_dilated(merged[None], dconv.reshape(height, breadth, 1,...  6.68 us
  transfers between devices with their start and end apart: 35, of which 30 were waited for; matrix products, arithmetic and copies ran while one was open for 4% of the time, Pallas kernels for 0%

profile of v4, /device:TPU:6, one launch (start us, length us, event | category | flops | bytes accessed | tf_op | source)
XLA Modules:
  0.0 300.0 jit_solution(15730891260478190373)
XLA Ops:
  8.4 4.3 %collective-permute-start = (bf16[64,1,256]{2,1,0:T(2,128)(2,1)S(1)}, bf16[64,1,256]{2,1,0:T(2,128)(2,1)S(1)}, u32[]{:S(2)}, u32[]{:S(2)}) collective-permute-start(bf16[64,1,256]{2,1,0:T(2,128)(2,1)S(1)} %get-tuple-element.69), channel_id=1, source_target_pairs={{0,1},{1,2},{2,3},{3,4},{4,5},{5,6},{6,7},{7,8},{8,9},{9,10},{10,1... | collective-permute-start | bytes 98312 | tf_op jit(solution)/shard_map/ppermute | solution.py:16
  12.6 14.1 %collective-permute-start.1 = (bf16[64,1,256]{2,1,0:T(2,128)(2,1)S(1)}, bf16[64,1,256]{2,1,0:T(2,128)(2,1)S(1)}, u32[]{:S(2)}, u32[]{:S(2)}) collective-permute-start(bf16[64,1,256]{2,1,0:T(2,128)(2,1)S(1)} %get-tuple-element.70), channel_id=1, source_target_pairs={{1,0},{2,1},{3,2},{4,3},{5,4},{6,5},{7,6},{8,7},{9,8},{10,9},{11,1... | collective-permute-start | bytes 98312 | tf_op jit(solution)/shard_map/ppermute | solution.py:17
  32.9 3.0 %collective-permute-start.4 = (bf16[2,18,256]{2,1,0:T(8,128)(2,1)S(1)}, bf16[2,18,256]{2,1,0:T(8,128)(2,1)S(1)}, u32[]{:S(2)}, u32[]{:S(2)}) collective-permute-start(bf16[2,18,256]{2,1,0:T(8,128)(2,1)S(1)} %pad_maximum_fusion.9), channel_id=1, source_target_pairs={{32,0},{33,1},{34,2},{35,3},{36,4},{37,5},{38,6},{39,7},{40,8},{41... | collective-permute-start | bytes 55304 | tf_op jit(solution)/shard_map/ppermute | solution.py:25
  48.2 4.7 %collective-permute-start.6 = (f32[64]{0:T(128)S(1)}, f32[64]{0:T(128)S(1)}, u32[]{:S(2)}, u32[]{:S(2)}) collective-permute-start(f32[64]{0:T(128)S(1)} %fusion.69), channel_id=1, source_target_pairs={{0,128},{64,192},{128,0},{192,64},{256,384},{320,448},{384,256},{4... | collective-permute-start | bytes 776 | tf_op jit(solution)/shard_map/ppermute | solution.py:38
  54.5 4.0 %collective-permute-start.7 = (f32[64]{0:T(128)S(1)}, f32[64]{0:T(128)S(1)}, u32[]{:S(2)}, u32[]{:S(2)}) collective-permute-start(f32[64]{0:T(128)S(1)} %add.182), channel_id=1, source_target_pairs={{0,256},{64,320},{128,384},{192,448},{256,0},{320,64},{384,128},{4... | collective-permute-start | bytes 776 | tf_op jit(solution)/shard_map/ppermute | solution.py:38
  62.7 3.5 %collective-permute-done.8 = f32[64]{0:T(128)S(1)} collective-permute-done((f32[64]{0:T(128)S(1)}, f32[64]{0:T(128)S(1)}, u32[]{:S(2)}, u32[]{:S(2)}) %collective-permute-start.8) | collective-permute-done | bytes 288 | tf_op jit(solution)/shard_map/ppermute | solution.py:38
  68.1 4.4 %collective-permute-done.9 = f32[64]{0:T(128)S(1)} collective-permute-done((f32[64]{0:T(128)S(1)}, f32[64]{0:T(128)S(1)}, u32[]{:S(2)}, u32[]{:S(2)}) %collective-permute-start.9) | collective-permute-done | bytes 288 | tf_op jit(solution)/shard_map/ppermute | solution.py:38
  72.5 5.4 %collective-permute-start.10 = (f32[64]{0:T(128)S(1)}, f32[64]{0:T(128)S(1)}, u32[]{:S(2)}, u32[]{:S(2)}) collective-permute-start(f32[64]{0:T(128)S(1)} %add.185), channel_id=1, source_target_pairs={{0,4},{1,5},{2,6},{3,7},{4,0},{5,1},{6,2},{7,3},{8,12},{9,13},{10,... | collective-permute-start | bytes 776 | tf_op jit(solution)/shard_map/ppermute | solution.py:38
  78.0 3.9 %collective-permute-done.10 = f32[64]{0:T(128)S(1)} collective-permute-done((f32[64]{0:T(128)S(1)}, f32[64]{0:T(128)S(1)}, u32[]{:S(2)}, u32[]{:S(2)}) %collective-permute-start.10) | collective-permute-done | bytes 288 | tf_op jit(solution)/shard_map/ppermute | solution.py:38
  81.9 6.6 %collective-permute-start.11 = (f32[64]{0:T(128)S(1)}, f32[64]{0:T(128)S(1)}, u32[]{:S(2)}, u32[]{:S(2)}) collective-permute-start(f32[64]{0:T(128)S(1)} %add.186), channel_id=1, source_target_pairs={{0,8},{1,9},{2,10},{3,11},{4,12},{5,13},{6,14},{7,15},{8,0},{9,1},... | collective-permute-start | bytes 776 | tf_op jit(solution)/shard_map/ppermute | solution.py:38
  96.6 4.5 %collective-permute-start.13 = (f32[64]{0:T(128)S(1)}, f32[64]{0:T(128)S(1)}, u32[]{:S(2)}, u32[]{:S(2)}) collective-permute-start(f32[64]{0:T(128)S(1)} %add.188), channel_id=1, source_target_pairs={{0,32},{1,33},{2,34},{3,35},{4,36},{5,37},{6,38},{7,39},{8,40},{9,... | collective-permute-start | bytes 776 | tf_op jit(solution)/shard_map/ppermute | solution.py:38
  109.0 3.9 %collective-permute-start.19 = (f32[512]{0:T(512)S(1)}, f32[512]{0:T(512)S(1)}, u32[]{:S(2)}, u32[]{:S(2)}) collective-permute-start(f32[512]{0:T(512)S(1)} %fusion.61), channel_id=1, source_target_pairs={{0,128},{64,192},{128,0},{192,64},{256,384},{320,448},{384,256},{4... | collective-permute-start | bytes 6152 | tf_op jit(solution)/shard_map/ppermute | solution.py:38
  114.5 4.0 %collective-permute-start.20 = (f32[512]{0:T(512)S(1)}, f32[512]{0:T(512)S(1)}, u32[]{:S(2)}, u32[]{:S(2)}) collective-permute-start(f32[512]{0:T(512)S(1)} %add.198), channel_id=1, source_target_pairs={{0,256},{64,320},{128,384},{192,448},{256,0},{320,64},{384,128},{4... | collective-permute-start | bytes 6152 | tf_op jit(solution)/shard_map/ppermute | solution.py:38
  126.3 3.6 %collective-permute-start.22 = (f32[512]{0:T(512)S(1)}, f32[512]{0:T(512)S(1)}, u32[]{:S(2)}, u32[]{:S(2)}) collective-permute-start(f32[512]{0:T(512)S(1)} %add.200), channel_id=1, source_target_pairs={{0,2},{1,3},{2,0},{3,1},{4,6},{5,7},{6,4},{7,5},{8,10},{9,11},{10,... | collective-permute-start | bytes 6152 | tf_op jit(solution)/shard_map/ppermute | solution.py:38
  132.7 6.6 %collective-permute-start.23 = (f32[512]{0:T(512)S(1)}, f32[512]{0:T(512)S(1)}, u32[]{:S(2)}, u32[]{:S(2)}) collective-permute-start(f32[512]{0:T(512)S(1)} %add.201), channel_id=1, source_target_pairs={{0,4},{1,5},{2,6},{3,7},{4,0},{5,1},{6,2},{7,3},{8,12},{9,13},{10,... | collective-permute-start | bytes 6152 | tf_op jit(solution)/shard_map/ppermute | solution.py:38
  142.1 6.6 %collective-permute-start.24 = (f32[512]{0:T(512)S(1)}, f32[512]{0:T(512)S(1)}, u32[]{:S(2)}, u32[]{:S(2)}) collective-permute-start(f32[512]{0:T(512)S(1)} %add.202), channel_id=1, source_target_pairs={{0,8},{1,9},{2,10},{3,11},{4,12},{5,13},{6,14},{7,15},{8,0},{9,1},... | collective-permute-start | bytes 6152 | tf_op jit(solution)/shard_map/ppermute | solution.py:38
  156.9 4.5 %collective-permute-start.26 = (f32[512]{0:T(512)S(1)}, f32[512]{0:T(512)S(1)}, u32[]{:S(2)}, u32[]{:S(2)}) collective-permute-start(f32[512]{0:T(512)S(1)} %add.204), channel_id=1, source_target_pairs={{0,32},{1,33},{2,34},{3,35},{4,36},{5,37},{6,38},{7,39},{8,40},{9,... | collective-permute-start | bytes 6152 | tf_op jit(solution)/shard_map/ppermute | solution.py:38
  163.6 10.8 %collective-permute-start.15 = (f32[64,1,512]{2,1,0:T(1,128)S(1)}, f32[64,1,512]{2,1,0:T(1,128)S(1)}, u32[]{:S(2)}, u32[]{:S(2)}) collective-permute-start(f32[64,1,512]{2,1,0:T(1,128)S(1)} %get-tuple-element.66), channel_id=1, source_target_pairs={{1,0},{2,1},{3,2},{4,3},{5,4},{6,5},{7,6},{8,7},{9,8},{10,9},{11,1... | collective-permute-start | bytes 393224 | tf_op jit(solution)/shard_map/ppermute | solution.py:17
  180.7 3.8 %collective-permute-done.17 = f32[1,18,512]{2,1,0:T(8,128)S(1)} collective-permute-done((f32[1,18,512]{2,1,0:T(8,128)S(1)}, f32[1,18,512]{2,1,0:T(8,128)S(1)}, u32[]{:S(2)}, u32[]{:S(2)}) %collective-permute-start.17) | collective-permute-done | bytes 36896 | tf_op jit(solution)/shard_map/ppermute | solution.py:17
  187.0 6.7 %fusion.18 = f32[256,3,3,256]{0,3,2,1:T(8,128)S(1)} fusion(bf16[1,66,18,256]{3,2,1,0:T(8,128)(2,1)S(1)} %copy-done.4, bf16[64,16,1,256]{3,1,0,2:T(8,128)(2,1)S(1)} %slice_bitcast_fusion), kind=kOutput, calls=%fused_computation.26 | convolution fusion | flops 1207959552 | bytes 3491840 | tf_op jit(solution)/shard_map/conv_general_dilated | solution.py:142
  196.3 2.9 add_convert_fusion
  199.2 5.6 %collective-permute-start.27 = (f32[2,18,512]{2,1,0:T(8,128)S(1)}, f32[2,18,512]{2,1,0:T(8,128)S(1)}, u32[]{:S(2)}, u32[]{:S(2)}) collective-permute-start(f32[2,18,512]{2,1,0:T(8,128)S(1)} %pad_maximum_fusion.4), channel_id=1, source_target_pairs={{32,0},{33,1},{34,2},{35,3},{36,4},{37,5},{38,6},{39,7},{40,8},{41... | collective-permute-start | bytes 221192 | tf_op jit(solution)/shard_map/ppermute | solution.py:25
  210.3 32.8 %reduce-scatter.2.cloned.1.call-done = f32[32,2304]{1,0:T(8,128)} async-done(((f32[256,2304]{1,0:T(8,128)}), f32[32,2304]{1,0:T(8,128)}) %reduce-scatter.2.cloned.1.call-update) | async-done | bytes 294928 | tf_op jit(solution)/shard_map/reduce_scatter | solution.py:150
  244.0 3.4 %collective-permute-start.28 = (f32[32,1152]{1,0:T(8,128)S(1)}, f32[32,1152]{1,0:T(8,128)S(1)}, u32[]{:S(2)}, u32[]{:S(2)}) collective-permute-start(f32[32,1152]{1,0:T(8,128)S(1)} %constant_dynamic-slice_fusion.5), channel_id=1, source_target_pairs={{0,32},{1,33},{2,34},{3,35},{4,36},{5,37},{6,38},{7,39},{8,40},{9,... | collective-permute-start | bytes 442376 | tf_op jit(solution)/shard_map/ppermute | solution.py:38
  247.5 5.0 %collective-permute-done.28 = f32[32,1152]{1,0:T(8,128)S(1)} collective-permute-done((f32[32,1152]{1,0:T(8,128)S(1)}, f32[32,1152]{1,0:T(8,128)S(1)}, u32[]{:S(2)}, u32[]{:S(2)}) %collective-permute-start.28) | collective-permute-done | bytes 147488 | tf_op jit(solution)/shard_map/ppermute | solution.py:38
  253.6 2.9 collective-permute-start.29
  256.6 3.3 %collective-permute-done.29 = f32[32,576]{1,0:T(8,128)S(1)} collective-permute-done((f32[32,576]{1,0:T(8,128)S(1)}, f32[32,576]{1,0:T(8,128)S(1)}, u32[]{:S(2)}, u32[]{:S(2)}) %collective-permute-start.29) | collective-permute-done | bytes 73760 | tf_op jit(solution)/shard_map/ppermute | solution.py:38
  260.1 6.1 %collective-permute-start.30 = (f32[32,288]{1,0:T(8,128)S(1)}, f32[32,288]{1,0:T(8,128)S(1)}, u32[]{:S(2)}, u32[]{:S(2)}) collective-permute-start(f32[32,288]{1,0:T(8,128)S(1)} %constant_dynamic-slice_fusion.3), channel_id=1, source_target_pairs={{0,8},{1,9},{2,10},{3,11},{4,12},{5,13},{6,14},{7,15},{8,0},{9,1},... | collective-permute-start | bytes 110600 | tf_op jit(solution)/shard_map/ppermute | solution.py:38
  266.3 3.7 %collective-permute-done.30 = f32[32,288]{1,0:T(8,128)S(1)} collective-permute-done((f32[32,288]{1,0:T(8,128)S(1)}, f32[32,288]{1,0:T(8,128)S(1)}, u32[]{:S(2)}, u32[]{:S(2)}) %collective-permute-start.30) | collective-permute-done | bytes 36896 | tf_op jit(solution)/shard_map/ppermute | solution.py:38
  270.1 8.0 %collective-permute-start.31 = (f32[32,144]{1,0:T(8,128)S(1)}, f32[32,144]{1,0:T(8,128)S(1)}, u32[]{:S(2)}, u32[]{:S(2)}) collective-permute-start(f32[32,144]{1,0:T(8,128)S(1)} %constant_dynamic-slice_fusion.2), channel_id=1, source_target_pairs={{0,4},{1,5},{2,6},{3,7},{4,0},{5,1},{6,2},{7,3},{8,12},{9,13},{10,... | collective-permute-start | bytes 55304 | tf_op jit(solution)/shard_map/ppermute | solution.py:38
  280.1 4.7 %collective-permute-start.32 = (f32[32,72]{1,0:T(8,128)S(1)}, f32[32,72]{1,0:T(8,128)S(1)}, u32[]{:S(2)}, u32[]{:S(2)}) collective-permute-start(f32[32,72]{1,0:T(8,128)S(1)} %constant_dynamic-slice_fusion.1), channel_id=1, source_target_pairs={{0,2},{1,3},{2,0},{3,1},{4,6},{5,7},{6,4},{7,5},{8,10},{9,11},{10,... | collective-permute-start | bytes 27656 | tf_op jit(solution)/shard_map/ppermute | solution.py:38
  286.8 3.6 %collective-permute-start.33 = (f32[32,36]{1,0:T(8,128)S(1)}, f32[32,36]{1,0:T(8,128)S(1)}, u32[]{:S(2)}, u32[]{:S(2)}) collective-permute-start(f32[32,36]{1,0:T(8,128)S(1)} %constant_dynamic-slice_fusion), channel_id=1, source_target_pairs={{0,1},{1,0},{2,3},{3,2},{4,5},{5,4},{6,7},{7,6},{8,9},{9,8},{10,11... | collective-permute-start | bytes 13832 | tf_op jit(solution)/shard_map/ppermute | solution.py:38
  (183 shorter events, 94.3 us)
Async XLA Ops:
  7.2 235.9 %reduce-scatter.2.cloned.1.call-start = ((), (), s32[]{:S(2)}) async-start(), calls=%async_computation.1 | async-start | bytes 2654208 | tf_op jit(solution)/shard_map/reduce_scatter | solution.py:150
  8.4 20.0 %collective-permute-start = (bf16[64,1,256]{2,1,0:T(2,128)(2,1)S(1)}, bf16[64,1,256]{2,1,0:T(2,128)(2,1)S(1)}, u32[]{:S(2)}, u32[]{:S(2)}) collective-permute-start(bf16[64,1,256]{2,1,0:T(2,128)(2,1)S(1)} %get-tuple-element.69), channel_id=1, source_target_pairs={{0,1},{1,2},{2,3},{3,4},{4,5},{5,6},{6,7},{7,8},{8,9},{9,10},{10,1... | collective-permute-start | bytes 98312 | tf_op jit(solution)/shard_map/ppermute | solution.py:16
  12.6 16.9 %collective-permute-start.1 = (bf16[64,1,256]{2,1,0:T(2,128)(2,1)S(1)}, bf16[64,1,256]{2,1,0:T(2,128)(2,1)S(1)}, u32[]{:S(2)}, u32[]{:S(2)}) collective-permute-start(bf16[64,1,256]{2,1,0:T(2,128)(2,1)S(1)} %get-tuple-element.70), channel_id=1, source_target_pairs={{1,0},{2,1},{3,2},{4,3},{5,4},{6,5},{7,6},{8,7},{9,8},{10,9},{11,1... | collective-permute-start | bytes 98312 | tf_op jit(solution)/shard_map/ppermute | solution.py:17
  30.2 5.7 %collective-permute-start.2 = (bf16[1,18,256]{2,1,0:T(8,128)(2,1)S(1)}, bf16[1,18,256]{2,1,0:T(8,128)(2,1)S(1)}, u32[]{:S(2)}, u32[]{:S(2)}) collective-permute-start(bf16[1,18,256]{2,1,0:T(8,128)(2,1)S(1)} %get-tuple-element.67), channel_id=1, source_target_pairs={{0,64},{64,128},{128,192},{192,256},{256,320},{320,384},{384,448},... | collective-permute-start | bytes 27656 | tf_op jit(solution)/shard_map/ppermute | solution.py:16
  31.5 4.4 %collective-permute-start.3 = (bf16[1,18,256]{2,1,0:T(8,128)(2,1)S(1)}, bf16[1,18,256]{2,1,0:T(8,128)(2,1)S(1)}, u32[]{:S(2)}, u32[]{:S(2)}) collective-permute-start(bf16[1,18,256]{2,1,0:T(8,128)(2,1)S(1)} %get-tuple-element.68), channel_id=1, source_target_pairs={{64,0},{128,64},{192,128},{256,192},{320,256},{384,320},{448,384},... | collective-permute-start | bytes 27656 | tf_op jit(solution)/shard_map/ppermute | solution.py:17
  32.9 7.2 %collective-permute-start.4 = (bf16[2,18,256]{2,1,0:T(8,128)(2,1)S(1)}, bf16[2,18,256]{2,1,0:T(8,128)(2,1)S(1)}, u32[]{:S(2)}, u32[]{:S(2)}) collective-permute-start(bf16[2,18,256]{2,1,0:T(8,128)(2,1)S(1)} %pad_maximum_fusion.9), channel_id=1, source_target_pairs={{32,0},{33,1},{34,2},{35,3},{36,4},{37,5},{38,6},{39,7},{40,8},{41... | collective-permute-start | bytes 55304 | tf_op jit(solution)/shard_map/ppermute | solution.py:25
  48.2 6.3 %collective-permute-start.6 = (f32[64]{0:T(128)S(1)}, f32[64]{0:T(128)S(1)}, u32[]{:S(2)}, u32[]{:S(2)}) collective-permute-start(f32[64]{0:T(128)S(1)} %fusion.69), channel_id=1, source_target_pairs={{0,128},{64,192},{128,0},{192,64},{256,384},{320,448},{384,256},{4... | collective-permute-start | bytes 776 | tf_op jit(solution)/shard_map/ppermute | solution.py:38
  54.5 6.3 %collective-permute-start.7 = (f32[64]{0:T(128)S(1)}, f32[64]{0:T(128)S(1)}, u32[]{:S(2)}, u32[]{:S(2)}) collective-permute-start(f32[64]{0:T(128)S(1)} %add.182), channel_id=1, source_target_pairs={{0,256},{64,320},{128,384},{192,448},{256,0},{320,64},{384,128},{4... | collective-permute-start | bytes 776 | tf_op jit(solution)/shard_map/ppermute | solution.py:38
  60.8 5.4 %collective-permute-start.8 = (f32[64]{0:T(128)S(1)}, f32[64]{0:T(128)S(1)}, u32[]{:S(2)}, u32[]{:S(2)}) collective-permute-start(f32[64]{0:T(128)S(1)} %add.183), channel_id=1, source_target_pairs={{0,1},{1,0},{2,3},{3,2},{4,5},{5,4},{6,7},{7,6},{8,9},{9,8},{10,11... | collective-permute-start | bytes 776 | tf_op jit(solution)/shard_map/ppermute | solution.py:38
  66.2 6.3 %collective-permute-start.9 = (f32[64]{0:T(128)S(1)}, f32[64]{0:T(128)S(1)}, u32[]{:S(2)}, u32[]{:S(2)}) collective-permute-start(f32[64]{0:T(128)S(1)} %add.184), channel_id=1, source_target_pairs={{0,2},{1,3},{2,0},{3,1},{4,6},{5,7},{6,4},{7,5},{8,10},{9,11},{10,... | collective-permute-start | bytes 776 | tf_op jit(solution)/shard_map/ppermute | solution.py:38
  72.5 9.3 %collective-permute-start.10 = (f32[64]{0:T(128)S(1)}, f32[64]{0:T(128)S(1)}, u32[]{:S(2)}, u32[]{:S(2)}) collective-permute-start(f32[64]{0:T(128)S(1)} %add.185), channel_id=1, source_target_pairs={{0,4},{1,5},{2,6},{3,7},{4,0},{5,1},{6,2},{7,3},{8,12},{9,13},{10,... | collective-permute-start | bytes 776 | tf_op jit(solution)/shard_map/ppermute | solution.py:38
  81.9 9.3 %collective-permute-start.11 = (f32[64]{0:T(128)S(1)}, f32[64]{0:T(128)S(1)}, u32[]{:S(2)}, u32[]{:S(2)}) collective-permute-start(f32[64]{0:T(128)S(1)} %add.186), channel_id=1, source_target_pairs={{0,8},{1,9},{2,10},{3,11},{4,12},{5,13},{6,14},{7,15},{8,0},{9,1},... | collective-permute-start | bytes 776 | tf_op jit(solution)/shard_map/ppermute | solution.py:38
  91.2 5.4 %collective-permute-start.12 = (f32[64]{0:T(128)S(1)}, f32[64]{0:T(128)S(1)}, u32[]{:S(2)}, u32[]{:S(2)}) collective-permute-start(f32[64]{0:T(128)S(1)} %add.187), channel_id=1, source_target_pairs={{0,16},{1,17},{2,18},{3,19},{4,20},{5,21},{6,22},{7,23},{8,24},{9,... | collective-permute-start | bytes 776 | tf_op jit(solution)/shard_map/ppermute | solution.py:38
  96.6 6.9 %collective-permute-start.13 = (f32[64]{0:T(128)S(1)}, f32[64]{0:T(128)S(1)}, u32[]{:S(2)}, u32[]{:S(2)}) collective-permute-start(f32[64]{0:T(128)S(1)} %add.188), channel_id=1, source_target_pairs={{0,32},{1,33},{2,34},{3,35},{4,36},{5,37},{6,38},{7,39},{8,40},{9,... | collective-permute-start | bytes 776 | tf_op jit(solution)/shard_map/ppermute | solution.py:38
  109.0 5.5 %collective-permute-start.19 = (f32[512]{0:T(512)S(1)}, f32[512]{0:T(512)S(1)}, u32[]{:S(2)}, u32[]{:S(2)}) collective-permute-start(f32[512]{0:T(512)S(1)} %fusion.61), channel_id=1, source_target_pairs={{0,128},{64,192},{128,0},{192,64},{256,384},{320,448},{384,256},{4... | collective-permute-start | bytes 6152 | tf_op jit(solution)/shard_map/ppermute | solution.py:38
  114.5 6.4 %collective-permute-start.20 = (f32[512]{0:T(512)S(1)}, f32[512]{0:T(512)S(1)}, u32[]{:S(2)}, u32[]{:S(2)}) collective-permute-start(f32[512]{0:T(512)S(1)} %add.198), channel_id=1, source_target_pairs={{0,256},{64,320},{128,384},{192,448},{256,0},{320,64},{384,128},{4... | collective-permute-start | bytes 6152 | tf_op jit(solution)/shard_map/ppermute | solution.py:38
  120.8 5.5 %collective-permute-start.21 = (f32[512]{0:T(512)S(1)}, f32[512]{0:T(512)S(1)}, u32[]{:S(2)}, u32[]{:S(2)}) collective-permute-start(f32[512]{0:T(512)S(1)} %add.199), channel_id=1, source_target_pairs={{0,1},{1,0},{2,3},{3,2},{4,5},{5,4},{6,7},{7,6},{8,9},{9,8},{10,11... | collective-permute-start | bytes 6152 | tf_op jit(solution)/shard_map/ppermute | solution.py:38
  126.3 6.4 %collective-permute-start.22 = (f32[512]{0:T(512)S(1)}, f32[512]{0:T(512)S(1)}, u32[]{:S(2)}, u32[]{:S(2)}) collective-permute-start(f32[512]{0:T(512)S(1)} %add.200), channel_id=1, source_target_pairs={{0,2},{1,3},{2,0},{3,1},{4,6},{5,7},{6,4},{7,5},{8,10},{9,11},{10,... | collective-permute-start | bytes 6152 | tf_op jit(solution)/shard_map/ppermute | solution.py:38
  132.7 9.4 %collective-permute-start.23 = (f32[512]{0:T(512)S(1)}, f32[512]{0:T(512)S(1)}, u32[]{:S(2)}, u32[]{:S(2)}) collective-permute-start(f32[512]{0:T(512)S(1)} %add.201), channel_id=1, source_target_pairs={{0,4},{1,5},{2,6},{3,7},{4,0},{5,1},{6,2},{7,3},{8,12},{9,13},{10,... | collective-permute-start | bytes 6152 | tf_op jit(solution)/shard_map/ppermute | solution.py:38
  142.1 9.4 %collective-permute-start.24 = (f32[512]{0:T(512)S(1)}, f32[512]{0:T(512)S(1)}, u32[]{:S(2)}, u32[]{:S(2)}) collective-permute-start(f32[512]{0:T(512)S(1)} %add.202), channel_id=1, source_target_pairs={{0,8},{1,9},{2,10},{3,11},{4,12},{5,13},{6,14},{7,15},{8,0},{9,1},... | collective-permute-start | bytes 6152 | tf_op jit(solution)/shard_map/ppermute | solution.py:38
  151.4 5.5 %collective-permute-start.25 = (f32[512]{0:T(512)S(1)}, f32[512]{0:T(512)S(1)}, u32[]{:S(2)}, u32[]{:S(2)}) collective-permute-start(f32[512]{0:T(512)S(1)} %add.203), channel_id=1, source_target_pairs={{0,16},{1,17},{2,18},{3,19},{4,20},{5,21},{6,22},{7,23},{8,24},{9,... | collective-permute-start | bytes 6152 | tf_op jit(solution)/shard_map/ppermute | solution.py:38
  156.9 17.5 %collective-permute-start.26 = (f32[512]{0:T(512)S(1)}, f32[512]{0:T(512)S(1)}, u32[]{:S(2)}, u32[]{:S(2)}) collective-permute-start(f32[512]{0:T(512)S(1)} %add.204), channel_id=1, source_target_pairs={{0,32},{1,33},{2,34},{3,35},{4,36},{5,37},{6,38},{7,39},{8,40},{9,... | collective-permute-start | bytes 6152 | tf_op jit(solution)/shard_map/ppermute | solution.py:38
  161.7 13.9 %collective-permute-start.14 = (f32[64,1,512]{2,1,0:T(1,128)S(1)}, f32[64,1,512]{2,1,0:T(1,128)S(1)}, u32[]{:S(2)}, u32[]{:S(2)}) collective-permute-start(f32[64,1,512]{2,1,0:T(1,128)S(1)} %get-tuple-element.65), channel_id=1, source_target_pairs={{0,1},{1,2},{2,3},{3,4},{4,5},{5,6},{6,7},{7,8},{8,9},{9,10},{10,1... | collective-permute-start | bytes 393224 | tf_op jit(solution)/shard_map/ppermute | solution.py:16
  163.6 13.9 %collective-permute-start.15 = (f32[64,1,512]{2,1,0:T(1,128)S(1)}, f32[64,1,512]{2,1,0:T(1,128)S(1)}, u32[]{:S(2)}, u32[]{:S(2)}) collective-permute-start(f32[64,1,512]{2,1,0:T(1,128)S(1)} %get-tuple-element.66), channel_id=1, source_target_pairs={{1,0},{2,1},{3,2},{4,3},{5,4},{6,5},{7,6},{8,7},{9,8},{10,9},{11,1... | collective-permute-start | bytes 393224 | tf_op jit(solution)/shard_map/ppermute | solution.py:17
  178.8 5.7 %collective-permute-start.17 = (f32[1,18,512]{2,1,0:T(8,128)S(1)}, f32[1,18,512]{2,1,0:T(8,128)S(1)}, u32[]{:S(2)}, u32[]{:S(2)}) collective-permute-start(f32[1,18,512]{2,1,0:T(8,128)S(1)} %get-tuple-element.64), channel_id=1, source_target_pairs={{64,0},{128,64},{192,128},{256,192},{320,256},{384,320},{448,384},... | collective-permute-start | bytes 110600 | tf_op jit(solution)/shard_map/ppermute | solution.py:17
  199.2 10.8 %collective-permute-start.27 = (f32[2,18,512]{2,1,0:T(8,128)S(1)}, f32[2,18,512]{2,1,0:T(8,128)S(1)}, u32[]{:S(2)}, u32[]{:S(2)}) collective-permute-start(f32[2,18,512]{2,1,0:T(8,128)S(1)} %pad_maximum_fusion.4), channel_id=1, source_target_pairs={{32,0},{33,1},{34,2},{35,3},{36,4},{37,5},{38,6},{39,7},{40,8},{41... | collective-permute-start | bytes 221192 | tf_op jit(solution)/shard_map/ppermute | solution.py:25
  244.0 8.5 %collective-permute-start.28 = (f32[32,1152]{1,0:T(8,128)S(1)}, f32[32,1152]{1,0:T(8,128)S(1)}, u32[]{:S(2)}, u32[]{:S(2)}) collective-permute-start(f32[32,1152]{1,0:T(8,128)S(1)} %constant_dynamic-slice_fusion.5), channel_id=1, source_target_pairs={{0,32},{1,33},{2,34},{3,35},{4,36},{5,37},{6,38},{7,39},{8,40},{9,... | collective-permute-start | bytes 442376 | tf_op jit(solution)/shard_map/ppermute | solution.py:38
  253.6 6.3 %collective-permute-start.29 = (f32[32,576]{1,0:T(8,128)S(1)}, f32[32,576]{1,0:T(8,128)S(1)}, u32[]{:S(2)}, u32[]{:S(2)}) collective-permute-start(f32[32,576]{1,0:T(8,128)S(1)} %constant_dynamic-slice_fusion.4), channel_id=1, source_target_pairs={{0,16},{1,17},{2,18},{3,19},{4,20},{5,21},{6,22},{7,23},{8,24},{9,... | collective-permute-start | bytes 221192 | tf_op jit(solution)/shard_map/ppermute | solution.py:38
  260.1 9.9 %collective-permute-start.30 = (f32[32,288]{1,0:T(8,128)S(1)}, f32[32,288]{1,0:T(8,128)S(1)}, u32[]{:S(2)}, u32[]{:S(2)}) collective-permute-start(f32[32,288]{1,0:T(8,128)S(1)} %constant_dynamic-slice_fusion.3), channel_id=1, source_target_pairs={{0,8},{1,9},{2,10},{3,11},{4,12},{5,13},{6,14},{7,15},{8,0},{9,1},... | collective-permute-start | bytes 110600 | tf_op jit(solution)/shard_map/ppermute | solution.py:38
  270.1 9.8 %collective-permute-start.31 = (f32[32,144]{1,0:T(8,128)S(1)}, f32[32,144]{1,0:T(8,128)S(1)}, u32[]{:S(2)}, u32[]{:S(2)}) collective-permute-start(f32[32,144]{1,0:T(8,128)S(1)} %constant_dynamic-slice_fusion.2), channel_id=1, source_target_pairs={{0,4},{1,5},{2,6},{3,7},{4,0},{5,1},{6,2},{7,3},{8,12},{9,13},{10,... | collective-permute-start | bytes 55304 | tf_op jit(solution)/shard_map/ppermute | solution.py:38
  280.1 6.5 %collective-permute-start.32 = (f32[32,72]{1,0:T(8,128)S(1)}, f32[32,72]{1,0:T(8,128)S(1)}, u32[]{:S(2)}, u32[]{:S(2)}) collective-permute-start(f32[32,72]{1,0:T(8,128)S(1)} %constant_dynamic-slice_fusion.1), channel_id=1, source_target_pairs={{0,2},{1,3},{2,0},{3,1},{4,6},{5,7},{6,4},{7,5},{8,10},{9,11},{10,... | collective-permute-start | bytes 27656 | tf_op jit(solution)/shard_map/ppermute | solution.py:38
  286.8 5.6 %collective-permute-start.33 = (f32[32,36]{1,0:T(8,128)S(1)}, f32[32,36]{1,0:T(8,128)S(1)}, u32[]{:S(2)}, u32[]{:S(2)}) collective-permute-start(f32[32,36]{1,0:T(8,128)S(1)} %constant_dynamic-slice_fusion), channel_id=1, source_target_pairs={{0,1},{1,0},{2,3},{3,2},{4,5},{5,4},{6,7},{7,6},{8,9},{9,8},{10,11... | collective-permute-start | bytes 13832 | tf_op jit(solution)/shard_map/ppermute | solution.py:38
  (27 other events, 332.3 us)
Sparse Core Ops, SparseCore 0:
  195.8 47.2 reduce-scatter.1

commit v5 on v4

--- a/solution.py
+++ b/solution.py
@@ -100,27 +100,29 @@
     )
     upstream = cotangent.astype(jnp.float32).reshape(-1, channels)
     dpre = upstream * (sigma * (1.0 + pre * (1.0 - sigma)))
-    pair_banded, pair_distant = extend(
-        jnp.concatenate([dpre, ghat], 1).reshape(height, breadth, 2 * channels)
-    )
     grad_sums = butterfly_sum(jnp.concatenate([jnp.sum(dpre * ghat, 0), jnp.sum(dpre, 0)]))
     grad_gain, grad_shift = grad_sums[:channels], grad_sums[channels:]
     mean_a = (norm_gain * grad_shift).reshape(G, -1).sum(1) / count
     mean_b = (norm_gain * grad_gain).reshape(G, -1).sum(1) / count
-
-    def normalized_grad(pair):
-        return (
-            (
-                pair[..., :channels] * norm_gain
-                - jnp.repeat(mean_a, channels // G)
-                - pair[..., channels:] * jnp.repeat(mean_b, channels // G)
-            )
-            * rstd_ch
-        ).astype(jnp.bfloat16)
-
-    grad_banded = normalized_grad(pair_banded)
-    grad_distant = normalized_grad(pair_distant)
-    dconv = grad_banded[1:-1, 1:-1]
+    dconv = (
+        (
+            dpre * norm_gain
+            - jnp.repeat(mean_a, channels // G)
+            - ghat * jnp.repeat(mean_b, channels // G)
+        )
+        * rstd_ch
+    ).astype(jnp.bfloat16)
+    dconv = dconv.reshape(height, breadth, channels)
+    term = lax.conv_general_dilated(
+        merged[None],
+        dconv.reshape(height, breadth, 1, channels),
+        (1, 1),
+        "VALID",
+        dimension_numbers=("CHWN", "HWIO", "CHWN"),
+        preferred_element_type=jnp.float32,
+    ).reshape(channels, 9 * channels)
+    owned_cols = lax.psum_scatter(term, "lat", scatter_dimension=0, tiled=True)
+    grad_banded, grad_distant = extend(dconv)
     flipped = jnp.swapaxes(kernel[::-1, ::-1], 2, 3)
     back = conv_valid(grad_banded, flipped)
     upper_term = jnp.zeros((breadth, channels), jnp.float32)
@@ -139,15 +141,6 @@
     back = back.at[0].add(jnp.where(north, upper_term, 0.0))
     back = back.at[-1].add(jnp.where(south, lower_term, 0.0))
     grad_fields = (upstream.reshape(height, breadth, channels) + back).astype(jnp.bfloat16)
-    term = lax.conv_general_dilated(
-        merged[None],
-        dconv.reshape(height, breadth, 1, channels),
-        (1, 1),
-        "VALID",
-        dimension_numbers=("CHWN", "HWIO", "CHWN"),
-        preferred_element_type=jnp.float32,
-    ).reshape(channels, 9 * channels)
-    owned_cols = lax.psum_scatter(term, "lat", scatter_dimension=0, tiled=True)
     grad_kernel = lon_halving_sum(owned_cols).T
     return (block_out, grad_fields, grad_kernel, grad_gain, grad_shift)
 

time: 301 us -> 282 us (0.937)
  waiting for transfers between devices: 103 us -> 92.4 us
  starting transfers between devices: 144 us -> 138 us
    reduce_scatter x1, waiting for transfers between devices: 32.8 us -> 17 us  [local(): owned_cols = lax.psum_scatter(term, 'lat', scatter_dimension=0, tiled=True)]
    ppermute x24, waiting for transfers between devices: 59.4 us -> 66.5 us  [exchange(): return lax.ppermute(block, axis, [(i, i ^ 1 << bit) for i in range(peers)])]
    ppermute x24, starting transfers between devices: 98.6 us -> 93.7 us  [exchange(): return lax.ppermute(block, axis, [(i, i ^ 1 << bit) for i in range(peers)])]
    ppermute x4, waiting for transfers between devices: 6.94 us -> 3.88 us  [with_halo(): after = lax.ppermute(initial, axis, down)]
  transfers between devices with their start and end apart: 35 -> 35, of which waited for: 30 -> 31; matrix products, arithmetic and copies ran while one was open for 4% -> 3% of each run, Pallas kernels for 0% -> 0%
where the time goes in v5:
time: 282 us; the launch traced here: 280 us
  starting transfers between devices  138 us (49%)
  waiting for transfers between devices  92.4 us (33%)
  between operations  14.8 us (5%)
  matrix products  13.1 us (5%)
  local copies, waits for them, and re-layouts  12.2 us (4%)
  other arithmetic  9.79 us (3%)
    ppermute x24, starting transfers between devices, exchange(): return lax.ppermute(block, axis, [(i, i ^ 1 << bit) for i in range(peers)])  93.7 us
    ppermute x24, waiting for transfers between devices, exchange(): return lax.ppermute(block, axis, [(i, i ^ 1 << bit) for i in range(peers)])  66.5 us
    ppermute x4, starting transfers between devices, with_halo(): after = lax.ppermute(initial, axis, down)  28.4 us
    reduce_scatter x1, waiting for transfers between devices, local(): owned_cols = lax.psum_scatter(term, 'lat', scatter_dimension=0, tiled=True)  17 us
    ppermute x4, starting transfers between devices, with_halo(): before = lax.ppermute(last, axis, up)  9.54 us
    conv_general_dilated x1, matrix products, local(): lax.conv_general_dilated(merged[None], dconv.reshape(height, breadth, 1,...  7.97 us
    ppermute x2, starting transfers between devices, passed_along(): return lax.ppermute(block, axis, route)  6.26 us
  transfers between devices with their start and end apart: 35, of which 31 were waited for; matrix products, arithmetic and copies ran while one was open for 3% of the time, Pallas kernels for 0%

profile of v5, /device:TPU:6, one launch (start us, length us, event | category | flops | bytes accessed | tf_op | source)
XLA Modules:
  0.0 280.3 jit_solution(89763551643658857)
XLA Ops:
  8.4 4.3 %collective-permute-start = (bf16[64,1,256]{2,1,0:T(2,128)(2,1)S(1)}, bf16[64,1,256]{2,1,0:T(2,128)(2,1)S(1)}, u32[]{:S(2)}, u32[]{:S(2)}) collective-permute-start(bf16[64,1,256]{2,1,0:T(2,128)(2,1)S(1)} %get-tuple-element.69), channel_id=1, source_target_pairs={{0,1},{1,2},{2,3},{3,4},{4,5},{5,6},{6,7},{7,8},{8,9},{9,10},{10,1... | collective-permute-start | bytes 98312 | tf_op jit(solution)/shard_map/ppermute | solution.py:16
  12.6 14.1 %collective-permute-start.1 = (bf16[64,1,256]{2,1,0:T(2,128)(2,1)S(1)}, bf16[64,1,256]{2,1,0:T(2,128)(2,1)S(1)}, u32[]{:S(2)}, u32[]{:S(2)}) collective-permute-start(bf16[64,1,256]{2,1,0:T(2,128)(2,1)S(1)} %get-tuple-element.70), channel_id=1, source_target_pairs={{1,0},{2,1},{3,2},{4,3},{5,4},{6,5},{7,6},{8,7},{9,8},{10,9},{11,1... | collective-permute-start | bytes 98312 | tf_op jit(solution)/shard_map/ppermute | solution.py:17
  32.9 3.0 %collective-permute-start.4 = (bf16[2,18,256]{2,1,0:T(8,128)(2,1)S(1)}, bf16[2,18,256]{2,1,0:T(8,128)(2,1)S(1)}, u32[]{:S(2)}, u32[]{:S(2)}) collective-permute-start(bf16[2,18,256]{2,1,0:T(8,128)(2,1)S(1)} %pad_maximum_fusion.1), channel_id=1, source_target_pairs={{32,0},{33,1},{34,2},{35,3},{36,4},{37,5},{38,6},{39,7},{40,8},{41... | collective-permute-start | bytes 55304 | tf_op jit(solution)/shard_map/ppermute | solution.py:25
  47.4 4.7 %collective-permute-start.6 = (f32[64]{0:T(128)S(1)}, f32[64]{0:T(128)S(1)}, u32[]{:S(2)}, u32[]{:S(2)}) collective-permute-start(f32[64]{0:T(128)S(1)} %fusion.65), channel_id=1, source_target_pairs={{0,128},{64,192},{128,0},{192,64},{256,384},{320,448},{384,256},{4... | collective-permute-start | bytes 776 | tf_op jit(solution)/shard_map/ppermute | solution.py:38
  53.7 4.0 %collective-permute-start.7 = (f32[64]{0:T(128)S(1)}, f32[64]{0:T(128)S(1)}, u32[]{:S(2)}, u32[]{:S(2)}) collective-permute-start(f32[64]{0:T(128)S(1)} %add.188), channel_id=1, source_target_pairs={{0,256},{64,320},{128,384},{192,448},{256,0},{320,64},{384,128},{4... | collective-permute-start | bytes 776 | tf_op jit(solution)/shard_map/ppermute | solution.py:38
  61.9 3.5 %collective-permute-done.8 = f32[64]{0:T(128)S(1)} collective-permute-done((f32[64]{0:T(128)S(1)}, f32[64]{0:T(128)S(1)}, u32[]{:S(2)}, u32[]{:S(2)}) %collective-permute-start.8) | collective-permute-done | bytes 288 | tf_op jit(solution)/shard_map/ppermute | solution.py:38
  67.3 4.4 %collective-permute-done.9 = f32[64]{0:T(128)S(1)} collective-permute-done((f32[64]{0:T(128)S(1)}, f32[64]{0:T(128)S(1)}, u32[]{:S(2)}, u32[]{:S(2)}) %collective-permute-start.9) | collective-permute-done | bytes 288 | tf_op jit(solution)/shard_map/ppermute | solution.py:38
  71.7 5.4 %collective-permute-start.10 = (f32[64]{0:T(128)S(1)}, f32[64]{0:T(128)S(1)}, u32[]{:S(2)}, u32[]{:S(2)}) collective-permute-start(f32[64]{0:T(128)S(1)} %add.191), channel_id=1, source_target_pairs={{0,4},{1,5},{2,6},{3,7},{4,0},{5,1},{6,2},{7,3},{8,12},{9,13},{10,... | collective-permute-start | bytes 776 | tf_op jit(solution)/shard_map/ppermute | solution.py:38
  77.2 3.9 %collective-permute-done.10 = f32[64]{0:T(128)S(1)} collective-permute-done((f32[64]{0:T(128)S(1)}, f32[64]{0:T(128)S(1)}, u32[]{:S(2)}, u32[]{:S(2)}) %collective-permute-start.10) | collective-permute-done | bytes 288 | tf_op jit(solution)/shard_map/ppermute | solution.py:38
  81.1 6.6 %collective-permute-start.11 = (f32[64]{0:T(128)S(1)}, f32[64]{0:T(128)S(1)}, u32[]{:S(2)}, u32[]{:S(2)}) collective-permute-start(f32[64]{0:T(128)S(1)} %add.192), channel_id=1, source_target_pairs={{0,8},{1,9},{2,10},{3,11},{4,12},{5,13},{6,14},{7,15},{8,0},{9,1},... | collective-permute-start | bytes 776 | tf_op jit(solution)/shard_map/ppermute | solution.py:38
  95.8 4.5 %collective-permute-start.13 = (f32[64]{0:T(128)S(1)}, f32[64]{0:T(128)S(1)}, u32[]{:S(2)}, u32[]{:S(2)}) collective-permute-start(f32[64]{0:T(128)S(1)} %add.194), channel_id=1, source_target_pairs={{0,32},{1,33},{2,34},{3,35},{4,36},{5,37},{6,38},{7,39},{8,40},{9,... | collective-permute-start | bytes 776 | tf_op jit(solution)/shard_map/ppermute | solution.py:38
  107.1 3.9 %collective-permute-start.15 = (f32[512]{0:T(512)S(1)}, f32[512]{0:T(512)S(1)}, u32[]{:S(2)}, u32[]{:S(2)}) collective-permute-start(f32[512]{0:T(512)S(1)} %fusion.57), channel_id=1, source_target_pairs={{0,128},{64,192},{128,0},{192,64},{256,384},{320,448},{384,256},{4... | collective-permute-start | bytes 6152 | tf_op jit(solution)/shard_map/ppermute | solution.py:38
  112.6 4.0 %collective-permute-start.16 = (f32[512]{0:T(512)S(1)}, f32[512]{0:T(512)S(1)}, u32[]{:S(2)}, u32[]{:S(2)}) collective-permute-start(f32[512]{0:T(512)S(1)} %add.204), channel_id=1, source_target_pairs={{0,256},{64,320},{128,384},{192,448},{256,0},{320,64},{384,128},{4... | collective-permute-start | bytes 6152 | tf_op jit(solution)/shard_map/ppermute | solution.py:38
  121.7 2.8 collective-permute-done.17
  124.5 3.6 %collective-permute-start.18 = (f32[512]{0:T(512)S(1)}, f32[512]{0:T(512)S(1)}, u32[]{:S(2)}, u32[]{:S(2)}) collective-permute-start(f32[512]{0:T(512)S(1)} %add.206), channel_id=1, source_target_pairs={{0,2},{1,3},{2,0},{3,1},{4,6},{5,7},{6,4},{7,5},{8,10},{9,11},{10,... | collective-permute-start | bytes 6152 | tf_op jit(solution)/shard_map/ppermute | solution.py:38
  130.8 6.6 %collective-permute-start.19 = (f32[512]{0:T(512)S(1)}, f32[512]{0:T(512)S(1)}, u32[]{:S(2)}, u32[]{:S(2)}) collective-permute-start(f32[512]{0:T(512)S(1)} %add.207), channel_id=1, source_target_pairs={{0,4},{1,5},{2,6},{3,7},{4,0},{5,1},{6,2},{7,3},{8,12},{9,13},{10,... | collective-permute-start | bytes 6152 | tf_op jit(solution)/shard_map/ppermute | solution.py:38
  140.2 6.6 %collective-permute-start.20 = (f32[512]{0:T(512)S(1)}, f32[512]{0:T(512)S(1)}, u32[]{:S(2)}, u32[]{:S(2)}) collective-permute-start(f32[512]{0:T(512)S(1)} %add.208), channel_id=1, source_target_pairs={{0,8},{1,9},{2,10},{3,11},{4,12},{5,13},{6,14},{7,15},{8,0},{9,1},... | collective-permute-start | bytes 6152 | tf_op jit(solution)/shard_map/ppermute | solution.py:38
  152.2 2.8 %collective-permute-done.21 = f32[512]{0:T(512)S(1)} collective-permute-done((f32[512]{0:T(512)S(1)}, f32[512]{0:T(512)S(1)}, u32[]{:S(2)}, u32[]{:S(2)}) %collective-permute-start.21) | collective-permute-done | bytes 2080 | tf_op jit(solution)/shard_map/ppermute | solution.py:38
  155.1 4.7 %collective-permute-start.22 = (f32[512]{0:T(512)S(1)}, f32[512]{0:T(512)S(1)}, u32[]{:S(2)}, u32[]{:S(2)}) collective-permute-start(f32[512]{0:T(512)S(1)} %add.210), channel_id=1, source_target_pairs={{0,32},{1,33},{2,34},{3,35},{4,36},{5,37},{6,38},{7,39},{8,40},{9,... | collective-permute-start | bytes 6152 | tf_op jit(solution)/shard_map/ppermute | solution.py:38
  165.2 8.0 %fusion.14 = f32[256,3,3,256]{0,3,2,1:T(8,128)} fusion(bf16[1,66,18,256]{3,2,1,0:T(8,128)(2,1)S(1)} %fusion.49, bf16[64,16,1,256]{3,1,0,2:T(8,128)(2,1)S(1)} %bitcast.100), kind=kOutput, calls=%fused_computation.19 | convolution fusion | flops 1207959552 | bytes 3491840 | tf_op jit(solution)/shard_map/conv_general_dilated | solution.py:116
  173.2 3.1 %copy.27 = f32[256,2304]{1,0:T(8,128)} copy(f32[256,2304]{0,1:T(8,128)} %bitcast.108) | data formatting | bytes 4718592 | tf_op jit(solution)/shard_map/reshape | solution.py:123
  179.1 11.7 %collective-permute-start.24 = (bf16[64,1,256]{2,1,0:T(2,128)(2,1)S(1)}, bf16[64,1,256]{2,1,0:T(2,128)(2,1)S(1)}, u32[]{:S(2)}, u32[]{:S(2)}) collective-permute-start(bf16[64,1,256]{2,1,0:T(2,128)(2,1)S(1)} %get-tuple-element.68), channel_id=1, source_target_pairs={{1,0},{2,1},{3,2},{4,3},{5,4},{6,5},{7,6},{8,7},{9,8},{10,9},{11,1... | collective-permute-start | bytes 98312 | tf_op jit(solution)/shard_map/ppermute | solution.py:17
  196.6 3.2 %collective-permute-start.27 = (bf16[2,18,256]{2,1,0:T(8,128)(2,1)S(1)}, bf16[2,18,256]{2,1,0:T(8,128)(2,1)S(1)}, u32[]{:S(2)}, u32[]{:S(2)}) collective-permute-start(bf16[2,18,256]{2,1,0:T(8,128)(2,1)S(1)} %pad_maximum_fusion.2), channel_id=1, source_target_pairs={{32,0},{33,1},{34,2},{35,3},{36,4},{37,5},{38,6},{39,7},{40,8},{41... | collective-permute-start | bytes 55304 | tf_op jit(solution)/shard_map/ppermute | solution.py:25
  206.6 17.0 %reduce-scatter.2.cloned.1.call-done = f32[32,2304]{1,0:T(8,128)} async-done(((f32[256,2304]{1,0:T(8,128)}), f32[32,2304]{1,0:T(8,128)}) %reduce-scatter.2.cloned.1.call-update) | async-done | bytes 294928 | tf_op jit(solution)/shard_map/reduce_scatter | solution.py:124
  224.4 2.8 %collective-permute-start.28 = (f32[32,1152]{1,0:T(8,128)S(1)}, f32[32,1152]{1,0:T(8,128)S(1)}, u32[]{:S(2)}, u32[]{:S(2)}) collective-permute-start(f32[32,1152]{1,0:T(8,128)S(1)} %constant_dynamic-slice_fusion.5), channel_id=1, source_target_pairs={{0,32},{1,33},{2,34},{3,35},{4,36},{5,37},{6,38},{7,39},{8,40},{9,... | collective-permute-start | bytes 442376 | tf_op jit(solution)/shard_map/ppermute | solution.py:38
  227.4 5.6 %collective-permute-done.28 = f32[32,1152]{1,0:T(8,128)S(1)} collective-permute-done((f32[32,1152]{1,0:T(8,128)S(1)}, f32[32,1152]{1,0:T(8,128)S(1)}, u32[]{:S(2)}, u32[]{:S(2)}) %collective-permute-start.28) | collective-permute-done | bytes 147488 | tf_op jit(solution)/shard_map/ppermute | solution.py:38
  236.9 3.5 %collective-permute-done.29 = f32[32,576]{1,0:T(8,128)S(1)} collective-permute-done((f32[32,576]{1,0:T(8,128)S(1)}, f32[32,576]{1,0:T(8,128)S(1)}, u32[]{:S(2)}, u32[]{:S(2)}) %collective-permute-start.29) | collective-permute-done | bytes 73760 | tf_op jit(solution)/shard_map/ppermute | solution.py:38
  240.5 4.9 %collective-permute-start.30 = (f32[32,288]{1,0:T(8,128)S(1)}, f32[32,288]{1,0:T(8,128)S(1)}, u32[]{:S(2)}, u32[]{:S(2)}) collective-permute-start(f32[32,288]{1,0:T(8,128)S(1)} %constant_dynamic-slice_fusion.3), channel_id=1, source_target_pairs={{0,8},{1,9},{2,10},{3,11},{4,12},{5,13},{6,14},{7,15},{8,0},{9,1},... | collective-permute-start | bytes 110600 | tf_op jit(solution)/shard_map/ppermute | solution.py:38
  245.6 4.8 %collective-permute-done.30 = f32[32,288]{1,0:T(8,128)S(1)} collective-permute-done((f32[32,288]{1,0:T(8,128)S(1)}, f32[32,288]{1,0:T(8,128)S(1)}, u32[]{:S(2)}, u32[]{:S(2)}) %collective-permute-start.30) | collective-permute-done | bytes 36896 | tf_op jit(solution)/shard_map/ppermute | solution.py:38
  250.6 6.9 %collective-permute-start.31 = (f32[32,144]{1,0:T(8,128)S(1)}, f32[32,144]{1,0:T(8,128)S(1)}, u32[]{:S(2)}, u32[]{:S(2)}) collective-permute-start(f32[32,144]{1,0:T(8,128)S(1)} %constant_dynamic-slice_fusion.2), channel_id=1, source_target_pairs={{0,4},{1,5},{2,6},{3,7},{4,0},{5,1},{6,2},{7,3},{8,12},{9,13},{10,... | collective-permute-start | bytes 55304 | tf_op jit(solution)/shard_map/ppermute | solution.py:38
  260.4 3.5 %collective-permute-start.32 = (f32[32,72]{1,0:T(8,128)S(1)}, f32[32,72]{1,0:T(8,128)S(1)}, u32[]{:S(2)}, u32[]{:S(2)}) collective-permute-start(f32[32,72]{1,0:T(8,128)S(1)} %constant_dynamic-slice_fusion.1), channel_id=1, source_target_pairs={{0,2},{1,3},{2,0},{3,1},{4,6},{5,7},{6,4},{7,5},{8,10},{9,11},{10,... | collective-permute-start | bytes 27656 | tf_op jit(solution)/shard_map/ppermute | solution.py:38
  264.1 2.9 %collective-permute-done.32 = f32[32,72]{1,0:T(8,128)S(1)} collective-permute-done((f32[32,72]{1,0:T(8,128)S(1)}, f32[32,72]{1,0:T(8,128)S(1)}, u32[]{:S(2)}, u32[]{:S(2)}) %collective-permute-start.32) | collective-permute-done | bytes 9248 | tf_op jit(solution)/shard_map/ppermute | solution.py:38
  (152 shorter events, 94.3 us)
Async XLA Ops:
  7.2 216.3 %reduce-scatter.2.cloned.1.call-start = ((), (), s32[]{:S(2)}) async-start(), calls=%async_computation.1 | async-start | bytes 2654208 | tf_op jit(solution)/shard_map/reduce_scatter | solution.py:124
  8.4 20.0 %collective-permute-start = (bf16[64,1,256]{2,1,0:T(2,128)(2,1)S(1)}, bf16[64,1,256]{2,1,0:T(2,128)(2,1)S(1)}, u32[]{:S(2)}, u32[]{:S(2)}) collective-permute-start(bf16[64,1,256]{2,1,0:T(2,128)(2,1)S(1)} %get-tuple-element.69), channel_id=1, source_target_pairs={{0,1},{1,2},{2,3},{3,4},{4,5},{5,6},{6,7},{7,8},{8,9},{9,10},{10,1... | collective-permute-start | bytes 98312 | tf_op jit(solution)/shard_map/ppermute | solution.py:16
  12.6 16.9 %collective-permute-start.1 = (bf16[64,1,256]{2,1,0:T(2,128)(2,1)S(1)}, bf16[64,1,256]{2,1,0:T(2,128)(2,1)S(1)}, u32[]{:S(2)}, u32[]{:S(2)}) collective-permute-start(bf16[64,1,256]{2,1,0:T(2,128)(2,1)S(1)} %get-tuple-element.70), channel_id=1, source_target_pairs={{1,0},{2,1},{3,2},{4,3},{5,4},{6,5},{7,6},{8,7},{9,8},{10,9},{11,1... | collective-permute-start | bytes 98312 | tf_op jit(solution)/shard_map/ppermute | solution.py:17
  30.2 5.7 %collective-permute-start.2 = (bf16[1,18,256]{2,1,0:T(8,128)(2,1)S(1)}, bf16[1,18,256]{2,1,0:T(8,128)(2,1)S(1)}, u32[]{:S(2)}, u32[]{:S(2)}) collective-permute-start(bf16[1,18,256]{2,1,0:T(8,128)(2,1)S(1)} %get-tuple-element.65), channel_id=1, source_target_pairs={{0,64},{64,128},{128,192},{192,256},{256,320},{320,384},{384,448},... | collective-permute-start | bytes 27656 | tf_op jit(solution)/shard_map/ppermute | solution.py:16
  32.9 7.2 %collective-permute-start.4 = (bf16[2,18,256]{2,1,0:T(8,128)(2,1)S(1)}, bf16[2,18,256]{2,1,0:T(8,128)(2,1)S(1)}, u32[]{:S(2)}, u32[]{:S(2)}) collective-permute-start(bf16[2,18,256]{2,1,0:T(8,128)(2,1)S(1)} %pad_maximum_fusion.1), channel_id=1, source_target_pairs={{32,0},{33,1},{34,2},{35,3},{36,4},{37,5},{38,6},{39,7},{40,8},{41... | collective-permute-start | bytes 55304 | tf_op jit(solution)/shard_map/ppermute | solution.py:25
  47.4 6.3 %collective-permute-start.6 = (f32[64]{0:T(128)S(1)}, f32[64]{0:T(128)S(1)}, u32[]{:S(2)}, u32[]{:S(2)}) collective-permute-start(f32[64]{0:T(128)S(1)} %fusion.65), channel_id=1, source_target_pairs={{0,128},{64,192},{128,0},{192,64},{256,384},{320,448},{384,256},{4... | collective-permute-start | bytes 776 | tf_op jit(solution)/shard_map/ppermute | solution.py:38
  53.7 6.3 %collective-permute-start.7 = (f32[64]{0:T(128)S(1)}, f32[64]{0:T(128)S(1)}, u32[]{:S(2)}, u32[]{:S(2)}) collective-permute-start(f32[64]{0:T(128)S(1)} %add.188), channel_id=1, source_target_pairs={{0,256},{64,320},{128,384},{192,448},{256,0},{320,64},{384,128},{4... | collective-permute-start | bytes 776 | tf_op jit(solution)/shard_map/ppermute | solution.py:38
  60.0 5.4 %collective-permute-start.8 = (f32[64]{0:T(128)S(1)}, f32[64]{0:T(128)S(1)}, u32[]{:S(2)}, u32[]{:S(2)}) collective-permute-start(f32[64]{0:T(128)S(1)} %add.189), channel_id=1, source_target_pairs={{0,1},{1,0},{2,3},{3,2},{4,5},{5,4},{6,7},{7,6},{8,9},{9,8},{10,11... | collective-permute-start | bytes 776 | tf_op jit(solution)/shard_map/ppermute | solution.py:38
  65.4 6.3 %collective-permute-start.9 = (f32[64]{0:T(128)S(1)}, f32[64]{0:T(128)S(1)}, u32[]{:S(2)}, u32[]{:S(2)}) collective-permute-start(f32[64]{0:T(128)S(1)} %add.190), channel_id=1, source_target_pairs={{0,2},{1,3},{2,0},{3,1},{4,6},{5,7},{6,4},{7,5},{8,10},{9,11},{10,... | collective-permute-start | bytes 776 | tf_op jit(solution)/shard_map/ppermute | solution.py:38
  71.7 9.3 %collective-permute-start.10 = (f32[64]{0:T(128)S(1)}, f32[64]{0:T(128)S(1)}, u32[]{:S(2)}, u32[]{:S(2)}) collective-permute-start(f32[64]{0:T(128)S(1)} %add.191), channel_id=1, source_target_pairs={{0,4},{1,5},{2,6},{3,7},{4,0},{5,1},{6,2},{7,3},{8,12},{9,13},{10,... | collective-permute-start | bytes 776 | tf_op jit(solution)/shard_map/ppermute | solution.py:38
  81.1 9.3 %collective-permute-start.11 = (f32[64]{0:T(128)S(1)}, f32[64]{0:T(128)S(1)}, u32[]{:S(2)}, u32[]{:S(2)}) collective-permute-start(f32[64]{0:T(128)S(1)} %add.192), channel_id=1, source_target_pairs={{0,8},{1,9},{2,10},{3,11},{4,12},{5,13},{6,14},{7,15},{8,0},{9,1},... | collective-permute-start | bytes 776 | tf_op jit(solution)/shard_map/ppermute | solution.py:38
  90.4 5.4 %collective-permute-start.12 = (f32[64]{0:T(128)S(1)}, f32[64]{0:T(128)S(1)}, u32[]{:S(2)}, u32[]{:S(2)}) collective-permute-start(f32[64]{0:T(128)S(1)} %add.193), channel_id=1, source_target_pairs={{0,16},{1,17},{2,18},{3,19},{4,20},{5,21},{6,22},{7,23},{8,24},{9,... | collective-permute-start | bytes 776 | tf_op jit(solution)/shard_map/ppermute | solution.py:38
  95.8 6.9 %collective-permute-start.13 = (f32[64]{0:T(128)S(1)}, f32[64]{0:T(128)S(1)}, u32[]{:S(2)}, u32[]{:S(2)}) collective-permute-start(f32[64]{0:T(128)S(1)} %add.194), channel_id=1, source_target_pairs={{0,32},{1,33},{2,34},{3,35},{4,36},{5,37},{6,38},{7,39},{8,40},{9,... | collective-permute-start | bytes 776 | tf_op jit(solution)/shard_map/ppermute | solution.py:38
  107.1 5.5 %collective-permute-start.15 = (f32[512]{0:T(512)S(1)}, f32[512]{0:T(512)S(1)}, u32[]{:S(2)}, u32[]{:S(2)}) collective-permute-start(f32[512]{0:T(512)S(1)} %fusion.57), channel_id=1, source_target_pairs={{0,128},{64,192},{128,0},{192,64},{256,384},{320,448},{384,256},{4... | collective-permute-start | bytes 6152 | tf_op jit(solution)/shard_map/ppermute | solution.py:38
  112.6 6.4 %collective-permute-start.16 = (f32[512]{0:T(512)S(1)}, f32[512]{0:T(512)S(1)}, u32[]{:S(2)}, u32[]{:S(2)}) collective-permute-start(f32[512]{0:T(512)S(1)} %add.204), channel_id=1, source_target_pairs={{0,256},{64,320},{128,384},{192,448},{256,0},{320,64},{384,128},{4... | collective-permute-start | bytes 6152 | tf_op jit(solution)/shard_map/ppermute | solution.py:38
  119.0 5.5 %collective-permute-start.17 = (f32[512]{0:T(512)S(1)}, f32[512]{0:T(512)S(1)}, u32[]{:S(2)}, u32[]{:S(2)}) collective-permute-start(f32[512]{0:T(512)S(1)} %add.205), channel_id=1, source_target_pairs={{0,1},{1,0},{2,3},{3,2},{4,5},{5,4},{6,7},{7,6},{8,9},{9,8},{10,11... | collective-permute-start | bytes 6152 | tf_op jit(solution)/shard_map/ppermute | solution.py:38
  124.5 6.4 %collective-permute-start.18 = (f32[512]{0:T(512)S(1)}, f32[512]{0:T(512)S(1)}, u32[]{:S(2)}, u32[]{:S(2)}) collective-permute-start(f32[512]{0:T(512)S(1)} %add.206), channel_id=1, source_target_pairs={{0,2},{1,3},{2,0},{3,1},{4,6},{5,7},{6,4},{7,5},{8,10},{9,11},{10,... | collective-permute-start | bytes 6152 | tf_op jit(solution)/shard_map/ppermute | solution.py:38
  130.8 9.4 %collective-permute-start.19 = (f32[512]{0:T(512)S(1)}, f32[512]{0:T(512)S(1)}, u32[]{:S(2)}, u32[]{:S(2)}) collective-permute-start(f32[512]{0:T(512)S(1)} %add.207), channel_id=1, source_target_pairs={{0,4},{1,5},{2,6},{3,7},{4,0},{5,1},{6,2},{7,3},{8,12},{9,13},{10,... | collective-permute-start | bytes 6152 | tf_op jit(solution)/shard_map/ppermute | solution.py:38
  140.2 9.4 %collective-permute-start.20 = (f32[512]{0:T(512)S(1)}, f32[512]{0:T(512)S(1)}, u32[]{:S(2)}, u32[]{:S(2)}) collective-permute-start(f32[512]{0:T(512)S(1)} %add.208), channel_id=1, source_target_pairs={{0,8},{1,9},{2,10},{3,11},{4,12},{5,13},{6,14},{7,15},{8,0},{9,1},... | collective-permute-start | bytes 6152 | tf_op jit(solution)/shard_map/ppermute | solution.py:38
  149.6 5.5 %collective-permute-start.21 = (f32[512]{0:T(512)S(1)}, f32[512]{0:T(512)S(1)}, u32[]{:S(2)}, u32[]{:S(2)}) collective-permute-start(f32[512]{0:T(512)S(1)} %add.209), channel_id=1, source_target_pairs={{0,16},{1,17},{2,18},{3,19},{4,20},{5,21},{6,22},{7,23},{8,24},{9,... | collective-permute-start | bytes 6152 | tf_op jit(solution)/shard_map/ppermute | solution.py:38
  155.1 7.0 %collective-permute-start.22 = (f32[512]{0:T(512)S(1)}, f32[512]{0:T(512)S(1)}, u32[]{:S(2)}, u32[]{:S(2)}) collective-permute-start(f32[512]{0:T(512)S(1)} %add.210), channel_id=1, source_target_pairs={{0,32},{1,33},{2,34},{3,35},{4,36},{5,37},{6,38},{7,39},{8,40},{9,... | collective-permute-start | bytes 6152 | tf_op jit(solution)/shard_map/ppermute | solution.py:38
  176.4 15.3 %collective-permute-start.23 = (bf16[64,1,256]{2,1,0:T(2,128)(2,1)S(1)}, bf16[64,1,256]{2,1,0:T(2,128)(2,1)S(1)}, u32[]{:S(2)}, u32[]{:S(2)}) collective-permute-start(bf16[64,1,256]{2,1,0:T(2,128)(2,1)S(1)} %get-tuple-element.67), channel_id=1, source_target_pairs={{0,1},{1,2},{2,3},{3,4},{4,5},{5,6},{6,7},{7,8},{8,9},{9,10},{10,1... | collective-permute-start | bytes 98312 | tf_op jit(solution)/shard_map/ppermute | solution.py:16
  179.1 14.8 %collective-permute-start.24 = (bf16[64,1,256]{2,1,0:T(2,128)(2,1)S(1)}, bf16[64,1,256]{2,1,0:T(2,128)(2,1)S(1)}, u32[]{:S(2)}, u32[]{:S(2)}) collective-permute-start(bf16[64,1,256]{2,1,0:T(2,128)(2,1)S(1)} %get-tuple-element.68), channel_id=1, source_target_pairs={{1,0},{2,1},{3,2},{4,3},{5,4},{6,5},{7,6},{8,7},{9,8},{10,9},{11,1... | collective-permute-start | bytes 98312 | tf_op jit(solution)/shard_map/ppermute | solution.py:17
  193.9 5.8 %collective-permute-start.25 = (bf16[1,18,256]{2,1,0:T(8,128)(2,1)S(1)}, bf16[1,18,256]{2,1,0:T(8,128)(2,1)S(1)}, u32[]{:S(2)}, u32[]{:S(2)}) collective-permute-start(bf16[1,18,256]{2,1,0:T(8,128)(2,1)S(1)} %get-tuple-element.63), channel_id=1, source_target_pairs={{0,64},{64,128},{128,192},{192,256},{256,320},{320,384},{384,448},... | collective-permute-start | bytes 27656 | tf_op jit(solution)/shard_map/ppermute | solution.py:16
  195.2 5.0 %collective-permute-start.26 = (bf16[1,18,256]{2,1,0:T(8,128)(2,1)S(1)}, bf16[1,18,256]{2,1,0:T(8,128)(2,1)S(1)}, u32[]{:S(2)}, u32[]{:S(2)}) collective-permute-start(bf16[1,18,256]{2,1,0:T(8,128)(2,1)S(1)} %get-tuple-element.64), channel_id=1, source_target_pairs={{64,0},{128,64},{192,128},{256,192},{320,256},{384,320},{448,384},... | collective-permute-start | bytes 27656 | tf_op jit(solution)/shard_map/ppermute | solution.py:17
  196.6 9.8 %collective-permute-start.27 = (bf16[2,18,256]{2,1,0:T(8,128)(2,1)S(1)}, bf16[2,18,256]{2,1,0:T(8,128)(2,1)S(1)}, u32[]{:S(2)}, u32[]{:S(2)}) collective-permute-start(bf16[2,18,256]{2,1,0:T(8,128)(2,1)S(1)} %pad_maximum_fusion.2), channel_id=1, source_target_pairs={{32,0},{33,1},{34,2},{35,3},{36,4},{37,5},{38,6},{39,7},{40,8},{41... | collective-permute-start | bytes 55304 | tf_op jit(solution)/shard_map/ppermute | solution.py:25
  224.4 8.5 %collective-permute-start.28 = (f32[32,1152]{1,0:T(8,128)S(1)}, f32[32,1152]{1,0:T(8,128)S(1)}, u32[]{:S(2)}, u32[]{:S(2)}) collective-permute-start(f32[32,1152]{1,0:T(8,128)S(1)} %constant_dynamic-slice_fusion.5), channel_id=1, source_target_pairs={{0,32},{1,33},{2,34},{3,35},{4,36},{5,37},{6,38},{7,39},{8,40},{9,... | collective-permute-start | bytes 442376 | tf_op jit(solution)/shard_map/ppermute | solution.py:38
  234.0 6.3 %collective-permute-start.29 = (f32[32,576]{1,0:T(8,128)S(1)}, f32[32,576]{1,0:T(8,128)S(1)}, u32[]{:S(2)}, u32[]{:S(2)}) collective-permute-start(f32[32,576]{1,0:T(8,128)S(1)} %constant_dynamic-slice_fusion.4), channel_id=1, source_target_pairs={{0,16},{1,17},{2,18},{3,19},{4,20},{5,21},{6,22},{7,23},{8,24},{9,... | collective-permute-start | bytes 221192 | tf_op jit(solution)/shard_map/ppermute | solution.py:38
  240.5 9.9 %collective-permute-start.30 = (f32[32,288]{1,0:T(8,128)S(1)}, f32[32,288]{1,0:T(8,128)S(1)}, u32[]{:S(2)}, u32[]{:S(2)}) collective-permute-start(f32[32,288]{1,0:T(8,128)S(1)} %constant_dynamic-slice_fusion.3), channel_id=1, source_target_pairs={{0,8},{1,9},{2,10},{3,11},{4,12},{5,13},{6,14},{7,15},{8,0},{9,1},... | collective-permute-start | bytes 110600 | tf_op jit(solution)/shard_map/ppermute | solution.py:38
  250.6 9.7 %collective-permute-start.31 = (f32[32,144]{1,0:T(8,128)S(1)}, f32[32,144]{1,0:T(8,128)S(1)}, u32[]{:S(2)}, u32[]{:S(2)}) collective-permute-start(f32[32,144]{1,0:T(8,128)S(1)} %constant_dynamic-slice_fusion.2), channel_id=1, source_target_pairs={{0,4},{1,5},{2,6},{3,7},{4,0},{5,1},{6,2},{7,3},{8,12},{9,13},{10,... | collective-permute-start | bytes 55304 | tf_op jit(solution)/shard_map/ppermute | solution.py:38
  260.4 6.5 %collective-permute-start.32 = (f32[32,72]{1,0:T(8,128)S(1)}, f32[32,72]{1,0:T(8,128)S(1)}, u32[]{:S(2)}, u32[]{:S(2)}) collective-permute-start(f32[32,72]{1,0:T(8,128)S(1)} %constant_dynamic-slice_fusion.1), channel_id=1, source_target_pairs={{0,2},{1,3},{2,0},{3,1},{4,6},{5,7},{6,4},{7,5},{8,10},{9,11},{10,... | collective-permute-start | bytes 27656 | tf_op jit(solution)/shard_map/ppermute | solution.py:38
  267.1 5.6 %collective-permute-start.33 = (f32[32,36]{1,0:T(8,128)S(1)}, f32[32,36]{1,0:T(8,128)S(1)}, u32[]{:S(2)}, u32[]{:S(2)}) collective-permute-start(f32[32,36]{1,0:T(8,128)S(1)} %constant_dynamic-slice_fusion), channel_id=1, source_target_pairs={{0,1},{1,0},{2,3},{3,2},{4,5},{5,4},{6,7},{7,6},{8,9},{9,8},{10,11... | collective-permute-start | bytes 13832 | tf_op jit(solution)/shard_map/ppermute | solution.py:38
  (14 other events, 150.1 us)
Sparse Core Ops, SparseCore 0:
  176.4 47.0 reduce-scatter.1

commit v6 on v5

--- a/solution.py
+++ b/solution.py
@@ -13,8 +13,12 @@
         down = [(j, i) for i, j in up]
         last = lax.slice_in_dim(shard, length - width, length, axis=dim)
         initial = lax.slice_in_dim(shard, 0, width, axis=dim)
-        before = lax.ppermute(last, axis, up)
-        after = lax.ppermute(initial, axis, down)
+        if width == 1:
+            before = jnp.expand_dims(lax.ppermute(jnp.squeeze(last, dim), axis, up), dim)
+            after = jnp.expand_dims(lax.ppermute(jnp.squeeze(initial, dim), axis, down), dim)
+        else:
+            before = lax.ppermute(last, axis, up)
+            after = lax.ppermute(initial, axis, down)
         shard = jnp.concatenate([before, shard, after], axis=dim)
     return shard
 

time: 282 us -> 280 us (level)
  starting transfers between devices: 138 us -> 133 us
  waiting for transfers between devices: 92.4 us -> 96.8 us
    ppermute x24, waiting for transfers between devices: 66.5 us -> 71.5 us  [exchange(): return lax.ppermute(block, axis, [(i, i ^ 1 << bit) for i in range(peers)])]
    ppermute x24, starting transfers between devices: 93.7 us -> 89.7 us  [exchange(): return lax.ppermute(block, axis, [(i, i ^ 1 << bit) for i in range(peers)])]
  transfers between devices with their start and end apart: 35 -> 35, of which waited for: 31 -> 30; matrix products, arithmetic and copies ran while one was open for 3% -> 3% of each run, Pallas kernels for 0% -> 0%
where the time goes in v6:
time: 280 us; the launch traced here: 279 us
  starting transfers between devices  133 us (48%)
  waiting for transfers between devices  96.8 us (35%)
  between operations  14.8 us (5%)
  matrix products  13.1 us (5%)
  local copies, waits for them, and re-layouts  12.5 us (4%)
  other arithmetic  8.77 us (3%)
    ppermute x24, starting transfers between devices, exchange(): return lax.ppermute(block, axis, [(i, i ^ 1 << bit) for i in range(peers)])  89.7 us
    ppermute x24, waiting for transfers between devices, exchange(): return lax.ppermute(block, axis, [(i, i ^ 1 << bit) for i in range(peers)])  71.5 us
    ppermute x4, starting transfers between devices, with_halo(): lax.ppermute(jnp.squeeze(initial, dim), axis, down)  28.4 us
    reduce_scatter x1, waiting for transfers between devices, local(): owned_cols = lax.psum_scatter(term, 'lat', scatter_dimension=0, tiled=True)  17.3 us
    ppermute x4, starting transfers between devices, with_halo(): lax.ppermute(jnp.squeeze(last, dim), axis, up)  8.93 us
    conv_general_dilated x1, matrix products, local(): lax.conv_general_dilated(merged[None], dconv.reshape(height, breadth, 1,...  7.92 us
    ppermute x2, starting transfers between devices, passed_along(): return lax.ppermute(block, axis, route)  6.05 us
  transfers between devices with their start and end apart: 35, of which 30 were waited for; matrix products, arithmetic and copies ran while one was open for 3% of the time, Pallas kernels for 0%

profile of v6, /device:TPU:6, one launch (start us, length us, event | category | flops | bytes accessed | tf_op | source)
XLA Modules:
  0.0 279.1 jit_solution(1736391243256142290)
XLA Ops:
  8.4 4.3 %collective-permute-start = (bf16[64,256]{1,0:T(8,128)(2,1)S(1)}, bf16[64,256]{1,0:T(8,128)(2,1)S(1)}, u32[]{:S(2)}, u32[]{:S(2)}) collective-permute-start(bf16[64,256]{1,0:T(8,128)(2,1)S(1)} %bitcast.155), channel_id=1, source_target_pairs={{0,1},{1,2},{2,3},{3,4},{4,5},{5,6},{6,7},{7,8},{8,9},{9,10},{10,1... | collective-permute-start | bytes 98312 | tf_op jit(solution)/shard_map/ppermute | solution.py:17
  12.7 14.1 %collective-permute-start.1 = (bf16[64,256]{1,0:T(8,128)(2,1)S(1)}, bf16[64,256]{1,0:T(8,128)(2,1)S(1)}, u32[]{:S(2)}, u32[]{:S(2)}) collective-permute-start(bf16[64,256]{1,0:T(8,128)(2,1)S(1)} %bitcast.157), channel_id=1, source_target_pairs={{1,0},{2,1},{3,2},{4,3},{5,4},{6,5},{7,6},{8,7},{9,8},{10,9},{11,1... | collective-permute-start | bytes 98312 | tf_op jit(solution)/shard_map/ppermute | solution.py:18
  31.8 3.2 %collective-permute-start.4 = (bf16[2,18,256]{2,1,0:T(8,128)(2,1)S(1)}, bf16[2,18,256]{2,1,0:T(8,128)(2,1)S(1)}, u32[]{:S(2)}, u32[]{:S(2)}) collective-permute-start(bf16[2,18,256]{2,1,0:T(8,128)(2,1)S(1)} %pad_maximum_fusion.1), channel_id=1, source_target_pairs={{32,0},{33,1},{34,2},{35,3},{36,4},{37,5},{38,6},{39,7},{40,8},{41... | collective-permute-start | bytes 55304 | tf_op jit(solution)/shard_map/ppermute | solution.py:29
  35.5 3.5 %collective-permute-done.4 = bf16[2,18,256]{2,1,0:T(8,128)(2,1)S(1)} collective-permute-done((bf16[2,18,256]{2,1,0:T(8,128)(2,1)S(1)}, bf16[2,18,256]{2,1,0:T(8,128)(2,1)S(1)}, u32[]{:S(2)}, u32[]{:S(2)}) %collective-permute-start.4) | collective-permute-done | bytes 18464 | tf_op jit(solution)/shard_map/ppermute | solution.py:29
  47.0 5.0 %collective-permute-start.6 = (f32[64]{0:T(128)S(1)}, f32[64]{0:T(128)S(1)}, u32[]{:S(2)}, u32[]{:S(2)}) collective-permute-start(f32[64]{0:T(128)S(1)} %fusion.67), channel_id=1, source_target_pairs={{0,128},{64,192},{128,0},{192,64},{256,384},{320,448},{384,256},{4... | collective-permute-start | bytes 776 | tf_op jit(solution)/shard_map/ppermute | solution.py:42
  53.5 4.0 %collective-permute-start.7 = (f32[64]{0:T(128)S(1)}, f32[64]{0:T(128)S(1)}, u32[]{:S(2)}, u32[]{:S(2)}) collective-permute-start(f32[64]{0:T(128)S(1)} %add.188), channel_id=1, source_target_pairs={{0,256},{64,320},{128,384},{192,448},{256,0},{320,64},{384,128},{4... | collective-permute-start | bytes 776 | tf_op jit(solution)/shard_map/ppermute | solution.py:42
  61.7 3.5 %collective-permute-done.8 = f32[64]{0:T(128)S(1)} collective-permute-done((f32[64]{0:T(128)S(1)}, f32[64]{0:T(128)S(1)}, u32[]{:S(2)}, u32[]{:S(2)}) %collective-permute-start.8) | collective-permute-done | bytes 288 | tf_op jit(solution)/shard_map/ppermute | solution.py:42
  67.1 4.4 %collective-permute-done.9 = f32[64]{0:T(128)S(1)} collective-permute-done((f32[64]{0:T(128)S(1)}, f32[64]{0:T(128)S(1)}, u32[]{:S(2)}, u32[]{:S(2)}) %collective-permute-start.9) | collective-permute-done | bytes 288 | tf_op jit(solution)/shard_map/ppermute | solution.py:42
  71.5 4.7 %collective-permute-start.10 = (f32[64]{0:T(128)S(1)}, f32[64]{0:T(128)S(1)}, u32[]{:S(2)}, u32[]{:S(2)}) collective-permute-start(f32[64]{0:T(128)S(1)} %add.191), channel_id=1, source_target_pairs={{0,4},{1,5},{2,6},{3,7},{4,0},{5,1},{6,2},{7,3},{8,12},{9,13},{10,... | collective-permute-start | bytes 776 | tf_op jit(solution)/shard_map/ppermute | solution.py:42
  76.3 4.6 %collective-permute-done.10 = f32[64]{0:T(128)S(1)} collective-permute-done((f32[64]{0:T(128)S(1)}, f32[64]{0:T(128)S(1)}, u32[]{:S(2)}, u32[]{:S(2)}) %collective-permute-start.10) | collective-permute-done | bytes 288 | tf_op jit(solution)/shard_map/ppermute | solution.py:42
  80.9 6.0 %collective-permute-start.11 = (f32[64]{0:T(128)S(1)}, f32[64]{0:T(128)S(1)}, u32[]{:S(2)}, u32[]{:S(2)}) collective-permute-start(f32[64]{0:T(128)S(1)} %add.192), channel_id=1, source_target_pairs={{0,8},{1,9},{2,10},{3,11},{4,12},{5,13},{6,14},{7,15},{8,0},{9,1},... | collective-permute-start | bytes 776 | tf_op jit(solution)/shard_map/ppermute | solution.py:42
  86.8 3.4 %collective-permute-done.11 = f32[64]{0:T(128)S(1)} collective-permute-done((f32[64]{0:T(128)S(1)}, f32[64]{0:T(128)S(1)}, u32[]{:S(2)}, u32[]{:S(2)}) %collective-permute-start.11) | collective-permute-done | bytes 288 | tf_op jit(solution)/shard_map/ppermute | solution.py:42
  95.6 3.8 %collective-permute-start.13 = (f32[64]{0:T(128)S(1)}, f32[64]{0:T(128)S(1)}, u32[]{:S(2)}, u32[]{:S(2)}) collective-permute-start(f32[64]{0:T(128)S(1)} %add.194), channel_id=1, source_target_pairs={{0,32},{1,33},{2,34},{3,35},{4,36},{5,37},{6,38},{7,39},{8,40},{9,... | collective-permute-start | bytes 776 | tf_op jit(solution)/shard_map/ppermute | solution.py:42
  106.9 3.9 %collective-permute-start.15 = (f32[512]{0:T(512)S(1)}, f32[512]{0:T(512)S(1)}, u32[]{:S(2)}, u32[]{:S(2)}) collective-permute-start(f32[512]{0:T(512)S(1)} %fusion.59), channel_id=1, source_target_pairs={{0,128},{64,192},{128,0},{192,64},{256,384},{320,448},{384,256},{4... | collective-permute-start | bytes 6152 | tf_op jit(solution)/shard_map/ppermute | solution.py:42
  112.4 4.0 %collective-permute-start.16 = (f32[512]{0:T(512)S(1)}, f32[512]{0:T(512)S(1)}, u32[]{:S(2)}, u32[]{:S(2)}) collective-permute-start(f32[512]{0:T(512)S(1)} %add.204), channel_id=1, source_target_pairs={{0,256},{64,320},{128,384},{192,448},{256,0},{320,64},{384,128},{4... | collective-permute-start | bytes 6152 | tf_op jit(solution)/shard_map/ppermute | solution.py:42
  120.8 3.4 %collective-permute-done.17 = f32[512]{0:T(512)S(1)} collective-permute-done((f32[512]{0:T(512)S(1)}, f32[512]{0:T(512)S(1)}, u32[]{:S(2)}, u32[]{:S(2)}) %collective-permute-start.17) | collective-permute-done | bytes 2080 | tf_op jit(solution)/shard_map/ppermute | solution.py:42
  127.2 3.4 %collective-permute-done.18 = f32[512]{0:T(512)S(1)} collective-permute-done((f32[512]{0:T(512)S(1)}, f32[512]{0:T(512)S(1)}, u32[]{:S(2)}, u32[]{:S(2)}) %collective-permute-start.18) | collective-permute-done | bytes 2080 | tf_op jit(solution)/shard_map/ppermute | solution.py:42
  130.6 6.0 %collective-permute-start.19 = (f32[512]{0:T(512)S(1)}, f32[512]{0:T(512)S(1)}, u32[]{:S(2)}, u32[]{:S(2)}) collective-permute-start(f32[512]{0:T(512)S(1)} %add.207), channel_id=1, source_target_pairs={{0,4},{1,5},{2,6},{3,7},{4,0},{5,1},{6,2},{7,3},{8,12},{9,13},{10,... | collective-permute-start | bytes 6152 | tf_op jit(solution)/shard_map/ppermute | solution.py:42
  136.6 3.4 %collective-permute-done.19 = f32[512]{0:T(512)S(1)} collective-permute-done((f32[512]{0:T(512)S(1)}, f32[512]{0:T(512)S(1)}, u32[]{:S(2)}, u32[]{:S(2)}) %collective-permute-start.19) | collective-permute-done | bytes 2080 | tf_op jit(solution)/shard_map/ppermute | solution.py:42
  140.0 6.0 %collective-permute-start.20 = (f32[512]{0:T(512)S(1)}, f32[512]{0:T(512)S(1)}, u32[]{:S(2)}, u32[]{:S(2)}) collective-permute-start(f32[512]{0:T(512)S(1)} %add.208), channel_id=1, source_target_pairs={{0,8},{1,9},{2,10},{3,11},{4,12},{5,13},{6,14},{7,15},{8,0},{9,1},... | collective-permute-start | bytes 6152 | tf_op jit(solution)/shard_map/ppermute | solution.py:42
  146.0 3.4 %collective-permute-done.20 = f32[512]{0:T(512)S(1)} collective-permute-done((f32[512]{0:T(512)S(1)}, f32[512]{0:T(512)S(1)}, u32[]{:S(2)}, u32[]{:S(2)}) %collective-permute-start.20) | collective-permute-done | bytes 2080 | tf_op jit(solution)/shard_map/ppermute | solution.py:42
  154.8 3.9 %collective-permute-start.22 = (f32[512]{0:T(512)S(1)}, f32[512]{0:T(512)S(1)}, u32[]{:S(2)}, u32[]{:S(2)}) collective-permute-start(f32[512]{0:T(512)S(1)} %add.210), channel_id=1, source_target_pairs={{0,32},{1,33},{2,34},{3,35},{4,36},{5,37},{6,38},{7,39},{8,40},{9,... | collective-permute-start | bytes 6152 | tf_op jit(solution)/shard_map/ppermute | solution.py:42
  165.0 7.9 %fusion.14 = f32[256,3,3,256]{0,3,2,1:T(8,128)} fusion(bf16[1,66,18,256]{3,2,1,0:T(8,128)(2,1)S(1)} %fusion.49, bf16[64,16,1,256]{3,1,0,2:T(8,128)(2,1)S(1)} %bitcast.136), kind=kOutput, calls=%fused_computation.19 | convolution fusion | flops 1207959552 | bytes 3491840 | tf_op jit(solution)/shard_map/conv_general_dilated | solution.py:120
  172.9 3.1 %copy.58 = f32[256,2304]{1,0:T(8,128)} copy(f32[256,2304]{0,1:T(8,128)} %bitcast.144) | data formatting | bytes 4718592 | tf_op jit(solution)/shard_map/reshape | solution.py:127
  178.2 11.7 %collective-permute-start.24 = (bf16[64,256]{1,0:T(8,128)(2,1)S(1)}, bf16[64,256]{1,0:T(8,128)(2,1)S(1)}, u32[]{:S(2)}, u32[]{:S(2)}) collective-permute-start(bf16[64,256]{1,0:T(8,128)(2,1)S(1)} %bitcast.153), channel_id=1, source_target_pairs={{1,0},{2,1},{3,2},{4,3},{5,4},{6,5},{7,6},{8,7},{9,8},{10,9},{11,1... | collective-permute-start | bytes 98312 | tf_op jit(solution)/shard_map/ppermute | solution.py:18
  204.9 17.3 %reduce-scatter.2.cloned.1.call-done = f32[32,2304]{1,0:T(8,128)} async-done(((f32[256,2304]{1,0:T(8,128)}), f32[32,2304]{1,0:T(8,128)}) %reduce-scatter.2.cloned.1.call-update) | async-done | bytes 294928 | tf_op jit(solution)/shard_map/reduce_scatter | solution.py:128
  226.0 5.7 %collective-permute-done.28 = f32[32,1152]{1,0:T(8,128)S(1)} collective-permute-done((f32[32,1152]{1,0:T(8,128)S(1)}, f32[32,1152]{1,0:T(8,128)S(1)}, u32[]{:S(2)}, u32[]{:S(2)}) %collective-permute-start.28) | collective-permute-done | bytes 147488 | tf_op jit(solution)/shard_map/ppermute | solution.py:42
  234.8 4.2 %collective-permute-done.29 = f32[32,576]{1,0:T(8,128)S(1)} collective-permute-done((f32[32,576]{1,0:T(8,128)S(1)}, f32[32,576]{1,0:T(8,128)S(1)}, u32[]{:S(2)}, u32[]{:S(2)}) %collective-permute-start.29) | collective-permute-done | bytes 73760 | tf_op jit(solution)/shard_map/ppermute | solution.py:42
  239.2 5.2 %collective-permute-start.30 = (f32[32,288]{1,0:T(8,128)S(1)}, f32[32,288]{1,0:T(8,128)S(1)}, u32[]{:S(2)}, u32[]{:S(2)}) collective-permute-start(f32[32,288]{1,0:T(8,128)S(1)} %constant_dynamic-slice_fusion.3), channel_id=1, source_target_pairs={{0,8},{1,9},{2,10},{3,11},{4,12},{5,13},{6,14},{7,15},{8,0},{9,1},... | collective-permute-start | bytes 110600 | tf_op jit(solution)/shard_map/ppermute | solution.py:42
  244.6 4.5 %collective-permute-done.30 = f32[32,288]{1,0:T(8,128)S(1)} collective-permute-done((f32[32,288]{1,0:T(8,128)S(1)}, f32[32,288]{1,0:T(8,128)S(1)}, u32[]{:S(2)}, u32[]{:S(2)}) %collective-permute-start.30) | collective-permute-done | bytes 36896 | tf_op jit(solution)/shard_map/ppermute | solution.py:42
  249.3 7.3 %collective-permute-start.31 = (f32[32,144]{1,0:T(8,128)S(1)}, f32[32,144]{1,0:T(8,128)S(1)}, u32[]{:S(2)}, u32[]{:S(2)}) collective-permute-start(f32[32,144]{1,0:T(8,128)S(1)} %constant_dynamic-slice_fusion.2), channel_id=1, source_target_pairs={{0,4},{1,5},{2,6},{3,7},{4,0},{5,1},{6,2},{7,3},{8,12},{9,13},{10,... | collective-permute-start | bytes 55304 | tf_op jit(solution)/shard_map/ppermute | solution.py:42
  259.2 4.0 %collective-permute-start.32 = (f32[32,72]{1,0:T(8,128)S(1)}, f32[32,72]{1,0:T(8,128)S(1)}, u32[]{:S(2)}, u32[]{:S(2)}) collective-permute-start(f32[32,72]{1,0:T(8,128)S(1)} %constant_dynamic-slice_fusion.1), channel_id=1, source_target_pairs={{0,2},{1,3},{2,0},{3,1},{4,6},{5,7},{6,4},{7,5},{8,10},{9,11},{10,... | collective-permute-start | bytes 27656 | tf_op jit(solution)/shard_map/ppermute | solution.py:42
  (160 shorter events, 91.6 us)
Async XLA Ops:
  7.2 215.0 %reduce-scatter.2.cloned.1.call-start = ((), (), s32[]{:S(2)}) async-start(), calls=%async_computation.1 | async-start | bytes 2654208 | tf_op jit(solution)/shard_map/reduce_scatter | solution.py:128
  8.4 18.6 %collective-permute-start = (bf16[64,256]{1,0:T(8,128)(2,1)S(1)}, bf16[64,256]{1,0:T(8,128)(2,1)S(1)}, u32[]{:S(2)}, u32[]{:S(2)}) collective-permute-start(bf16[64,256]{1,0:T(8,128)(2,1)S(1)} %bitcast.155), channel_id=1, source_target_pairs={{0,1},{1,2},{2,3},{3,4},{4,5},{5,6},{6,7},{7,8},{8,9},{9,10},{10,1... | collective-permute-start | bytes 98312 | tf_op jit(solution)/shard_map/ppermute | solution.py:17
  12.7 15.7 %collective-permute-start.1 = (bf16[64,256]{1,0:T(8,128)(2,1)S(1)}, bf16[64,256]{1,0:T(8,128)(2,1)S(1)}, u32[]{:S(2)}, u32[]{:S(2)}) collective-permute-start(bf16[64,256]{1,0:T(8,128)(2,1)S(1)} %bitcast.157), channel_id=1, source_target_pairs={{1,0},{2,1},{3,2},{4,3},{5,4},{6,5},{7,6},{8,7},{9,8},{10,9},{11,1... | collective-permute-start | bytes 98312 | tf_op jit(solution)/shard_map/ppermute | solution.py:18
  29.2 5.8 %collective-permute-start.2 = (bf16[18,256]{1,0:T(8,128)(2,1)S(1)}, bf16[18,256]{1,0:T(8,128)(2,1)S(1)}, u32[]{:S(2)}, u32[]{:S(2)}) collective-permute-start(bf16[18,256]{1,0:T(8,128)(2,1)S(1)} %bitcast.149), channel_id=1, source_target_pairs={{0,64},{64,128},{128,192},{192,256},{256,320},{320,384},{384,448},... | collective-permute-start | bytes 27656 | tf_op jit(solution)/shard_map/ppermute | solution.py:17
  31.8 7.2 %collective-permute-start.4 = (bf16[2,18,256]{2,1,0:T(8,128)(2,1)S(1)}, bf16[2,18,256]{2,1,0:T(8,128)(2,1)S(1)}, u32[]{:S(2)}, u32[]{:S(2)}) collective-permute-start(bf16[2,18,256]{2,1,0:T(8,128)(2,1)S(1)} %pad_maximum_fusion.1), channel_id=1, source_target_pairs={{32,0},{33,1},{34,2},{35,3},{36,4},{37,5},{38,6},{39,7},{40,8},{41... | collective-permute-start | bytes 55304 | tf_op jit(solution)/shard_map/ppermute | solution.py:29
  47.0 6.5 %collective-permute-start.6 = (f32[64]{0:T(128)S(1)}, f32[64]{0:T(128)S(1)}, u32[]{:S(2)}, u32[]{:S(2)}) collective-permute-start(f32[64]{0:T(128)S(1)} %fusion.67), channel_id=1, source_target_pairs={{0,128},{64,192},{128,0},{192,64},{256,384},{320,448},{384,256},{4... | collective-permute-start | bytes 776 | tf_op jit(solution)/shard_map/ppermute | solution.py:42
  53.5 6.3 %collective-permute-start.7 = (f32[64]{0:T(128)S(1)}, f32[64]{0:T(128)S(1)}, u32[]{:S(2)}, u32[]{:S(2)}) collective-permute-start(f32[64]{0:T(128)S(1)} %add.188), channel_id=1, source_target_pairs={{0,256},{64,320},{128,384},{192,448},{256,0},{320,64},{384,128},{4... | collective-permute-start | bytes 776 | tf_op jit(solution)/shard_map/ppermute | solution.py:42
  59.8 5.4 %collective-permute-start.8 = (f32[64]{0:T(128)S(1)}, f32[64]{0:T(128)S(1)}, u32[]{:S(2)}, u32[]{:S(2)}) collective-permute-start(f32[64]{0:T(128)S(1)} %add.189), channel_id=1, source_target_pairs={{0,1},{1,0},{2,3},{3,2},{4,5},{5,4},{6,7},{7,6},{8,9},{9,8},{10,11... | collective-permute-start | bytes 776 | tf_op jit(solution)/shard_map/ppermute | solution.py:42
  65.2 6.3 %collective-permute-start.9 = (f32[64]{0:T(128)S(1)}, f32[64]{0:T(128)S(1)}, u32[]{:S(2)}, u32[]{:S(2)}) collective-permute-start(f32[64]{0:T(128)S(1)} %add.190), channel_id=1, source_target_pairs={{0,2},{1,3},{2,0},{3,1},{4,6},{5,7},{6,4},{7,5},{8,10},{9,11},{10,... | collective-permute-start | bytes 776 | tf_op jit(solution)/shard_map/ppermute | solution.py:42
  71.5 9.3 %collective-permute-start.10 = (f32[64]{0:T(128)S(1)}, f32[64]{0:T(128)S(1)}, u32[]{:S(2)}, u32[]{:S(2)}) collective-permute-start(f32[64]{0:T(128)S(1)} %add.191), channel_id=1, source_target_pairs={{0,4},{1,5},{2,6},{3,7},{4,0},{5,1},{6,2},{7,3},{8,12},{9,13},{10,... | collective-permute-start | bytes 776 | tf_op jit(solution)/shard_map/ppermute | solution.py:42
  80.9 9.3 %collective-permute-start.11 = (f32[64]{0:T(128)S(1)}, f32[64]{0:T(128)S(1)}, u32[]{:S(2)}, u32[]{:S(2)}) collective-permute-start(f32[64]{0:T(128)S(1)} %add.192), channel_id=1, source_target_pairs={{0,8},{1,9},{2,10},{3,11},{4,12},{5,13},{6,14},{7,15},{8,0},{9,1},... | collective-permute-start | bytes 776 | tf_op jit(solution)/shard_map/ppermute | solution.py:42
  90.2 5.4 %collective-permute-start.12 = (f32[64]{0:T(128)S(1)}, f32[64]{0:T(128)S(1)}, u32[]{:S(2)}, u32[]{:S(2)}) collective-permute-start(f32[64]{0:T(128)S(1)} %add.193), channel_id=1, source_target_pairs={{0,16},{1,17},{2,18},{3,19},{4,20},{5,21},{6,22},{7,23},{8,24},{9,... | collective-permute-start | bytes 776 | tf_op jit(solution)/shard_map/ppermute | solution.py:42
  95.6 6.9 %collective-permute-start.13 = (f32[64]{0:T(128)S(1)}, f32[64]{0:T(128)S(1)}, u32[]{:S(2)}, u32[]{:S(2)}) collective-permute-start(f32[64]{0:T(128)S(1)} %add.194), channel_id=1, source_target_pairs={{0,32},{1,33},{2,34},{3,35},{4,36},{5,37},{6,38},{7,39},{8,40},{9,... | collective-permute-start | bytes 776 | tf_op jit(solution)/shard_map/ppermute | solution.py:42
  106.9 5.5 %collective-permute-start.15 = (f32[512]{0:T(512)S(1)}, f32[512]{0:T(512)S(1)}, u32[]{:S(2)}, u32[]{:S(2)}) collective-permute-start(f32[512]{0:T(512)S(1)} %fusion.59), channel_id=1, source_target_pairs={{0,128},{64,192},{128,0},{192,64},{256,384},{320,448},{384,256},{4... | collective-permute-start | bytes 6152 | tf_op jit(solution)/shard_map/ppermute | solution.py:42
  112.4 6.4 %collective-permute-start.16 = (f32[512]{0:T(512)S(1)}, f32[512]{0:T(512)S(1)}, u32[]{:S(2)}, u32[]{:S(2)}) collective-permute-start(f32[512]{0:T(512)S(1)} %add.204), channel_id=1, source_target_pairs={{0,256},{64,320},{128,384},{192,448},{256,0},{320,64},{384,128},{4... | collective-permute-start | bytes 6152 | tf_op jit(solution)/shard_map/ppermute | solution.py:42
  118.8 5.5 %collective-permute-start.17 = (f32[512]{0:T(512)S(1)}, f32[512]{0:T(512)S(1)}, u32[]{:S(2)}, u32[]{:S(2)}) collective-permute-start(f32[512]{0:T(512)S(1)} %add.205), channel_id=1, source_target_pairs={{0,1},{1,0},{2,3},{3,2},{4,5},{5,4},{6,7},{7,6},{8,9},{9,8},{10,11... | collective-permute-start | bytes 6152 | tf_op jit(solution)/shard_map/ppermute | solution.py:42
  124.2 6.4 %collective-permute-start.18 = (f32[512]{0:T(512)S(1)}, f32[512]{0:T(512)S(1)}, u32[]{:S(2)}, u32[]{:S(2)}) collective-permute-start(f32[512]{0:T(512)S(1)} %add.206), channel_id=1, source_target_pairs={{0,2},{1,3},{2,0},{3,1},{4,6},{5,7},{6,4},{7,5},{8,10},{9,11},{10,... | collective-permute-start | bytes 6152 | tf_op jit(solution)/shard_map/ppermute | solution.py:42
  130.6 9.4 %collective-permute-start.19 = (f32[512]{0:T(512)S(1)}, f32[512]{0:T(512)S(1)}, u32[]{:S(2)}, u32[]{:S(2)}) collective-permute-start(f32[512]{0:T(512)S(1)} %add.207), channel_id=1, source_target_pairs={{0,4},{1,5},{2,6},{3,7},{4,0},{5,1},{6,2},{7,3},{8,12},{9,13},{10,... | collective-permute-start | bytes 6152 | tf_op jit(solution)/shard_map/ppermute | solution.py:42
  140.0 9.4 %collective-permute-start.20 = (f32[512]{0:T(512)S(1)}, f32[512]{0:T(512)S(1)}, u32[]{:S(2)}, u32[]{:S(2)}) collective-permute-start(f32[512]{0:T(512)S(1)} %add.208), channel_id=1, source_target_pairs={{0,8},{1,9},{2,10},{3,11},{4,12},{5,13},{6,14},{7,15},{8,0},{9,1},... | collective-permute-start | bytes 6152 | tf_op jit(solution)/shard_map/ppermute | solution.py:42
  149.4 5.5 %collective-permute-start.21 = (f32[512]{0:T(512)S(1)}, f32[512]{0:T(512)S(1)}, u32[]{:S(2)}, u32[]{:S(2)}) collective-permute-start(f32[512]{0:T(512)S(1)} %add.209), channel_id=1, source_target_pairs={{0,16},{1,17},{2,18},{3,19},{4,20},{5,21},{6,22},{7,23},{8,24},{9,... | collective-permute-start | bytes 6152 | tf_op jit(solution)/shard_map/ppermute | solution.py:42
  154.8 7.0 %collective-permute-start.22 = (f32[512]{0:T(512)S(1)}, f32[512]{0:T(512)S(1)}, u32[]{:S(2)}, u32[]{:S(2)}) collective-permute-start(f32[512]{0:T(512)S(1)} %add.210), channel_id=1, source_target_pairs={{0,32},{1,33},{2,34},{3,35},{4,36},{5,37},{6,38},{7,39},{8,40},{9,... | collective-permute-start | bytes 6152 | tf_op jit(solution)/shard_map/ppermute | solution.py:42
  176.1 13.9 %collective-permute-start.23 = (bf16[64,256]{1,0:T(8,128)(2,1)S(1)}, bf16[64,256]{1,0:T(8,128)(2,1)S(1)}, u32[]{:S(2)}, u32[]{:S(2)}) collective-permute-start(bf16[64,256]{1,0:T(8,128)(2,1)S(1)} %bitcast.151), channel_id=1, source_target_pairs={{0,1},{1,2},{2,3},{3,4},{4,5},{5,6},{6,7},{7,8},{8,9},{9,10},{10,1... | collective-permute-start | bytes 98312 | tf_op jit(solution)/shard_map/ppermute | solution.py:17
  178.2 13.4 %collective-permute-start.24 = (bf16[64,256]{1,0:T(8,128)(2,1)S(1)}, bf16[64,256]{1,0:T(8,128)(2,1)S(1)}, u32[]{:S(2)}, u32[]{:S(2)}) collective-permute-start(bf16[64,256]{1,0:T(8,128)(2,1)S(1)} %bitcast.153), channel_id=1, source_target_pairs={{1,0},{2,1},{3,2},{4,3},{5,4},{6,5},{7,6},{8,7},{9,8},{10,9},{11,1... | collective-permute-start | bytes 98312 | tf_op jit(solution)/shard_map/ppermute | solution.py:18
  191.7 5.5 %collective-permute-start.25 = (bf16[18,256]{1,0:T(8,128)(2,1)S(1)}, bf16[18,256]{1,0:T(8,128)(2,1)S(1)}, u32[]{:S(2)}, u32[]{:S(2)}) collective-permute-start(bf16[18,256]{1,0:T(8,128)(2,1)S(1)} %bitcast.150), channel_id=1, source_target_pairs={{0,64},{64,128},{128,192},{192,256},{256,320},{320,384},{384,448},... | collective-permute-start | bytes 27656 | tf_op jit(solution)/shard_map/ppermute | solution.py:17
  193.0 5.6 %collective-permute-start.26 = (bf16[18,256]{1,0:T(8,128)(2,1)S(1)}, bf16[18,256]{1,0:T(8,128)(2,1)S(1)}, u32[]{:S(2)}, u32[]{:S(2)}) collective-permute-start(bf16[18,256]{1,0:T(8,128)(2,1)S(1)} %bitcast.148), channel_id=1, source_target_pairs={{64,0},{128,64},{192,128},{256,192},{320,256},{384,320},{448,384},... | collective-permute-start | bytes 27656 | tf_op jit(solution)/shard_map/ppermute | solution.py:18
  194.3 10.4 %collective-permute-start.27 = (bf16[2,18,256]{2,1,0:T(8,128)(2,1)S(1)}, bf16[2,18,256]{2,1,0:T(8,128)(2,1)S(1)}, u32[]{:S(2)}, u32[]{:S(2)}) collective-permute-start(bf16[2,18,256]{2,1,0:T(8,128)(2,1)S(1)} %pad_maximum_fusion.2), channel_id=1, source_target_pairs={{32,0},{33,1},{34,2},{35,3},{36,4},{37,5},{38,6},{39,7},{40,8},{41... | collective-permute-start | bytes 55304 | tf_op jit(solution)/shard_map/ppermute | solution.py:29
  223.1 8.5 %collective-permute-start.28 = (f32[32,1152]{1,0:T(8,128)S(1)}, f32[32,1152]{1,0:T(8,128)S(1)}, u32[]{:S(2)}, u32[]{:S(2)}) collective-permute-start(f32[32,1152]{1,0:T(8,128)S(1)} %constant_dynamic-slice_fusion.5), channel_id=1, source_target_pairs={{0,32},{1,33},{2,34},{3,35},{4,36},{5,37},{6,38},{7,39},{8,40},{9,... | collective-permute-start | bytes 442376 | tf_op jit(solution)/shard_map/ppermute | solution.py:42
  232.7 6.3 %collective-permute-start.29 = (f32[32,576]{1,0:T(8,128)S(1)}, f32[32,576]{1,0:T(8,128)S(1)}, u32[]{:S(2)}, u32[]{:S(2)}) collective-permute-start(f32[32,576]{1,0:T(8,128)S(1)} %constant_dynamic-slice_fusion.4), channel_id=1, source_target_pairs={{0,16},{1,17},{2,18},{3,19},{4,20},{5,21},{6,22},{7,23},{8,24},{9,... | collective-permute-start | bytes 221192 | tf_op jit(solution)/shard_map/ppermute | solution.py:42
  239.2 9.9 %collective-permute-start.30 = (f32[32,288]{1,0:T(8,128)S(1)}, f32[32,288]{1,0:T(8,128)S(1)}, u32[]{:S(2)}, u32[]{:S(2)}) collective-permute-start(f32[32,288]{1,0:T(8,128)S(1)} %constant_dynamic-slice_fusion.3), channel_id=1, source_target_pairs={{0,8},{1,9},{2,10},{3,11},{4,12},{5,13},{6,14},{7,15},{8,0},{9,1},... | collective-permute-start | bytes 110600 | tf_op jit(solution)/shard_map/ppermute | solution.py:42
  249.3 9.8 %collective-permute-start.31 = (f32[32,144]{1,0:T(8,128)S(1)}, f32[32,144]{1,0:T(8,128)S(1)}, u32[]{:S(2)}, u32[]{:S(2)}) collective-permute-start(f32[32,144]{1,0:T(8,128)S(1)} %constant_dynamic-slice_fusion.2), channel_id=1, source_target_pairs={{0,4},{1,5},{2,6},{3,7},{4,0},{5,1},{6,2},{7,3},{8,12},{9,13},{10,... | collective-permute-start | bytes 55304 | tf_op jit(solution)/shard_map/ppermute | solution.py:42
  259.2 6.5 %collective-permute-start.32 = (f32[32,72]{1,0:T(8,128)S(1)}, f32[32,72]{1,0:T(8,128)S(1)}, u32[]{:S(2)}, u32[]{:S(2)}) collective-permute-start(f32[32,72]{1,0:T(8,128)S(1)} %constant_dynamic-slice_fusion.1), channel_id=1, source_target_pairs={{0,2},{1,3},{2,0},{3,1},{4,6},{5,7},{6,4},{7,5},{8,10},{9,11},{10,... | collective-permute-start | bytes 27656 | tf_op jit(solution)/shard_map/ppermute | solution.py:42
  265.9 5.6 %collective-permute-start.33 = (f32[32,36]{1,0:T(8,128)S(1)}, f32[32,36]{1,0:T(8,128)S(1)}, u32[]{:S(2)}, u32[]{:S(2)}) collective-permute-start(f32[32,36]{1,0:T(8,128)S(1)} %constant_dynamic-slice_fusion), channel_id=1, source_target_pairs={{0,1},{1,0},{2,3},{3,2},{4,5},{5,4},{6,7},{7,6},{8,9},{9,8},{10,11... | collective-permute-start | bytes 13832 | tf_op jit(solution)/shard_map/ppermute | solution.py:42
  (14 other events, 119.3 us)
Sparse Core Ops, SparseCore 0:
  176.1 46.0 reduce-scatter.1

commit v7 on v6

--- a/solution.py
+++ b/solution.py
@@ -50,8 +50,9 @@
 
 
 def butterfly_sum(value):
-    for axis, bit in butterfly_order():
-        value = value + exchange(value, axis, bit)
+    value = jnp.sum(lax.all_gather(value, "lat"), 0)
+    for bit in range((lax.axis_size("lon") - 1).bit_length()):
+        value = value + exchange(value, "lon", bit)
     return value
 
 

time: 280 us -> 275 us (0.982)
  blocking collectives: 0 us -> 27.2 us
  starting transfers between devices: 133 us -> 115 us
  waiting for transfers between devices: 96.8 us -> 80.5 us
    ppermute x24 -> x18, starting transfers between devices: 89.7 us -> 71.7 us  [exchange(): return lax.ppermute(block, axis, [(i, i ^ 1 << bit) for i in range(peers)])]
    unnamed x0 -> x1, blocking collectives: none -> 14.5 us
    ppermute x24 -> x18, waiting for transfers between devices: 71.5 us -> 58.5 us  [exchange(): return lax.ppermute(block, axis, [(i, i ^ 1 << bit) for i in range(peers)])]
    all_gather x0 -> x1, blocking collectives: none -> 12.7 us  [butterfly_sum(): value = jnp.sum(lax.all_gather(value, 'lat'), 0)]
  transfers between devices with their start and end apart: 35 -> 29, of which waited for: 30 -> 21; matrix products, arithmetic and copies ran while one was open for 3% -> 3% of each run, Pallas kernels for 0% -> 0%
where the time goes in v7:
time: 275 us; the launch traced here: 274 us
  starting transfers between devices  115 us (42%)
  waiting for transfers between devices  80.5 us (29%)
  blocking collectives  27.2 us (10%)
  between operations  15.5 us (6%)
  local copies, waits for them, and re-layouts  13.8 us (5%)
  matrix products  13 us (5%)
  other arithmetic  8.82 us (3%)
    ppermute x18, starting transfers between devices, exchange(): return lax.ppermute(block, axis, [(i, i ^ 1 << bit) for i in range(peers)])  71.7 us
    ppermute x18, waiting for transfers between devices, exchange(): return lax.ppermute(block, axis, [(i, i ^ 1 << bit) for i in range(peers)])  58.5 us
    ppermute x4, starting transfers between devices, with_halo(): lax.ppermute(jnp.squeeze(initial, dim), axis, down)  27.9 us
    reduce_scatter x1, waiting for transfers between devices, local(): owned_cols = lax.psum_scatter(term, 'lat', scatter_dimension=0, tiled=True)  16.4 us
    unnamed x1, blocking collectives  14.5 us
    all_gather x1, blocking collectives, butterfly_sum(): value = jnp.sum(lax.all_gather(value, 'lat'), 0)  12.7 us
    ppermute x4, starting transfers between devices, with_halo(): lax.ppermute(jnp.squeeze(last, dim), axis, up)  8.99 us
    conv_general_dilated x1, matrix products, local(): lax.conv_general_dilated(merged[None], dconv.reshape(height, breadth, 1,...  7.87 us
  transfers between devices with their start and end apart: 29, of which 21 were waited for; matrix products, arithmetic and copies ran while one was open for 3% of the time, Pallas kernels for 0%

profile of v7, /device:TPU:6, one launch (start us, length us, event | category | flops | bytes accessed | tf_op | source)
XLA Modules:
  0.0 274.0 jit_solution(15195274731251387833)
XLA Ops:
  8.4 4.3 %collective-permute-start = (bf16[64,256]{1,0:T(8,128)(2,1)S(1)}, bf16[64,256]{1,0:T(8,128)(2,1)S(1)}, u32[]{:S(2)}, u32[]{:S(2)}) collective-permute-start(bf16[64,256]{1,0:T(8,128)(2,1)S(1)} %bitcast.157), channel_id=1, source_target_pairs={{0,1},{1,2},{2,3},{3,4},{4,5},{5,6},{6,7},{7,8},{8,9},{9,10},{10,1... | collective-permute-start | bytes 98312 | tf_op jit(solution)/shard_map/ppermute | solution.py:17
  12.7 14.1 %collective-permute-start.1 = (bf16[64,256]{1,0:T(8,128)(2,1)S(1)}, bf16[64,256]{1,0:T(8,128)(2,1)S(1)}, u32[]{:S(2)}, u32[]{:S(2)}) collective-permute-start(bf16[64,256]{1,0:T(8,128)(2,1)S(1)} %bitcast.159), channel_id=1, source_target_pairs={{1,0},{2,1},{3,2},{4,3},{5,4},{6,5},{7,6},{8,7},{9,8},{10,9},{11,1... | collective-permute-start | bytes 98312 | tf_op jit(solution)/shard_map/ppermute | solution.py:18
  36.0 3.7 %collective-permute-done.4 = bf16[2,18,256]{2,1,0:T(8,128)(2,1)S(1)} collective-permute-done((bf16[2,18,256]{2,1,0:T(8,128)(2,1)S(1)}, bf16[2,18,256]{2,1,0:T(8,128)(2,1)S(1)}, u32[]{:S(2)}, u32[]{:S(2)}) %collective-permute-start.4) | collective-permute-done | bytes 18464 | tf_op jit(solution)/shard_map/ppermute | solution.py:29
  44.0 14.5 %all-reduce = f32[512]{0:T(512)S(1)} all-reduce(f32[512]{0:T(512)S(1)} %maximum_dynamic-update-slice_fusion), channel_id=2, replica_groups=mesh['lat'=8,'lon'=64] {'lat'}, use_global_device_ids=true, to_apply=%add | all-reduce | flops 512 | bytes 4096
  60.5 3.5 %collective-permute-done.5 = f32[64]{0:T(128)S(1)} collective-permute-done((f32[64]{0:T(128)S(1)}, f32[64]{0:T(128)S(1)}, u32[]{:S(2)}, u32[]{:S(2)}) %collective-permute-start.5) | collective-permute-done | bytes 288 | tf_op jit(solution)/shard_map/ppermute | solution.py:42
  66.0 4.4 %collective-permute-done.6 = f32[64]{0:T(128)S(1)} collective-permute-done((f32[64]{0:T(128)S(1)}, f32[64]{0:T(128)S(1)}, u32[]{:S(2)}, u32[]{:S(2)}) %collective-permute-start.6) | collective-permute-done | bytes 288 | tf_op jit(solution)/shard_map/ppermute | solution.py:42
  70.4 5.9 %collective-permute-start.7 = (f32[64]{0:T(128)S(1)}, f32[64]{0:T(128)S(1)}, u32[]{:S(2)}, u32[]{:S(2)}) collective-permute-start(f32[64]{0:T(128)S(1)} %add.170), channel_id=1, source_target_pairs={{0,4},{1,5},{2,6},{3,7},{4,0},{5,1},{6,2},{7,3},{8,12},{9,13},{10,... | collective-permute-start | bytes 776 | tf_op jit(solution)/shard_map/ppermute | solution.py:42
  76.2 3.5 %collective-permute-done.7 = f32[64]{0:T(128)S(1)} collective-permute-done((f32[64]{0:T(128)S(1)}, f32[64]{0:T(128)S(1)}, u32[]{:S(2)}, u32[]{:S(2)}) %collective-permute-start.7) | collective-permute-done | bytes 288 | tf_op jit(solution)/shard_map/ppermute | solution.py:42
  79.7 5.3 %collective-permute-start.8 = (f32[64]{0:T(128)S(1)}, f32[64]{0:T(128)S(1)}, u32[]{:S(2)}, u32[]{:S(2)}) collective-permute-start(f32[64]{0:T(128)S(1)} %add.171), channel_id=1, source_target_pairs={{0,8},{1,9},{2,10},{3,11},{4,12},{5,13},{6,14},{7,15},{8,0},{9,1},... | collective-permute-start | bytes 776 | tf_op jit(solution)/shard_map/ppermute | solution.py:42
  85.0 4.0 %collective-permute-done.8 = f32[64]{0:T(128)S(1)} collective-permute-done((f32[64]{0:T(128)S(1)}, f32[64]{0:T(128)S(1)}, u32[]{:S(2)}, u32[]{:S(2)}) %collective-permute-start.8) | collective-permute-done | bytes 288 | tf_op jit(solution)/shard_map/ppermute | solution.py:42
  94.5 3.8 %collective-permute-start.10 = (f32[64]{0:T(128)S(1)}, f32[64]{0:T(128)S(1)}, u32[]{:S(2)}, u32[]{:S(2)}) collective-permute-start(f32[64]{0:T(128)S(1)} %add.173), channel_id=1, source_target_pairs={{0,32},{1,33},{2,34},{3,35},{4,36},{5,37},{6,38},{7,39},{8,40},{9,... | collective-permute-start | bytes 776 | tf_op jit(solution)/shard_map/ppermute | solution.py:42
  102.7 12.7 %all-gather.2 = f32[8,1,512]{2,1,0:T(1,128)S(1)} all-gather(f32[1,1,512]{2,1,0:T(1,128)S(1)} %bitcast.164), channel_id=3, replica_groups=mesh['lat'=8,'lon'=64] {'lat'}, dimensions={0}, use_global_device_ids=true | all-gather | bytes 18432 | tf_op jit(solution)/shard_map/all_gather | solution.py:53
  117.4 3.5 %collective-permute-done.11 = f32[512]{0:T(512)S(1)} collective-permute-done((f32[512]{0:T(512)S(1)}, f32[512]{0:T(512)S(1)}, u32[]{:S(2)}, u32[]{:S(2)}) %collective-permute-start.11) | collective-permute-done | bytes 2080 | tf_op jit(solution)/shard_map/ppermute | solution.py:42
  123.8 3.5 %collective-permute-done.12 = f32[512]{0:T(512)S(1)} collective-permute-done((f32[512]{0:T(512)S(1)}, f32[512]{0:T(512)S(1)}, u32[]{:S(2)}, u32[]{:S(2)}) %collective-permute-start.12) | collective-permute-done | bytes 2080 | tf_op jit(solution)/shard_map/ppermute | solution.py:42
  127.3 5.9 %collective-permute-start.13 = (f32[512]{0:T(512)S(1)}, f32[512]{0:T(512)S(1)}, u32[]{:S(2)}, u32[]{:S(2)}) collective-permute-start(f32[512]{0:T(512)S(1)} %add.183), channel_id=1, source_target_pairs={{0,4},{1,5},{2,6},{3,7},{4,0},{5,1},{6,2},{7,3},{8,12},{9,13},{10,... | collective-permute-start | bytes 6152 | tf_op jit(solution)/shard_map/ppermute | solution.py:42
  133.2 3.5 %collective-permute-done.13 = f32[512]{0:T(512)S(1)} collective-permute-done((f32[512]{0:T(512)S(1)}, f32[512]{0:T(512)S(1)}, u32[]{:S(2)}, u32[]{:S(2)}) %collective-permute-start.13) | collective-permute-done | bytes 2080 | tf_op jit(solution)/shard_map/ppermute | solution.py:42
  136.7 5.3 %collective-permute-start.14 = (f32[512]{0:T(512)S(1)}, f32[512]{0:T(512)S(1)}, u32[]{:S(2)}, u32[]{:S(2)}) collective-permute-start(f32[512]{0:T(512)S(1)} %add.184), channel_id=1, source_target_pairs={{0,8},{1,9},{2,10},{3,11},{4,12},{5,13},{6,14},{7,15},{8,0},{9,1},... | collective-permute-start | bytes 6152 | tf_op jit(solution)/shard_map/ppermute | solution.py:42
  142.0 4.1 %collective-permute-done.14 = f32[512]{0:T(512)S(1)} collective-permute-done((f32[512]{0:T(512)S(1)}, f32[512]{0:T(512)S(1)}, u32[]{:S(2)}, u32[]{:S(2)}) %collective-permute-start.14) | collective-permute-done | bytes 2080 | tf_op jit(solution)/shard_map/ppermute | solution.py:42
  151.5 3.9 %collective-permute-start.16 = (f32[512]{0:T(512)S(1)}, f32[512]{0:T(512)S(1)}, u32[]{:S(2)}, u32[]{:S(2)}) collective-permute-start(f32[512]{0:T(512)S(1)} %add.186), channel_id=1, source_target_pairs={{0,32},{1,33},{2,34},{3,35},{4,36},{5,37},{6,38},{7,39},{8,40},{9,... | collective-permute-start | bytes 6152 | tf_op jit(solution)/shard_map/ppermute | solution.py:42
  161.7 7.9 %fusion.14 = f32[256,3,3,256]{0,3,2,1:T(8,128)} fusion(bf16[1,66,18,256]{3,2,1,0:T(8,128)(2,1)S(1)} %fusion.49, bf16[64,16,1,256]{3,1,0,2:T(8,128)(2,1)S(1)} %bitcast.138), kind=kOutput, calls=%fused_computation.19 | convolution fusion | flops 1207959552 | bytes 3491840 | tf_op jit(solution)/shard_map/conv_general_dilated | solution.py:121
  169.6 3.1 %copy.100 = f32[256,2304]{1,0:T(8,128)} copy(f32[256,2304]{0,1:T(8,128)} %bitcast.146) | data formatting | bytes 4718592 | tf_op jit(solution)/shard_map/reshape | solution.py:128
  174.8 11.2 %collective-permute-start.18 = (bf16[64,256]{1,0:T(8,128)(2,1)S(1)}, bf16[64,256]{1,0:T(8,128)(2,1)S(1)}, u32[]{:S(2)}, u32[]{:S(2)}) collective-permute-start(bf16[64,256]{1,0:T(8,128)(2,1)S(1)} %bitcast.155), channel_id=1, source_target_pairs={{1,0},{2,1},{3,2},{4,3},{5,4},{6,5},{7,6},{8,7},{9,8},{10,9},{11,1... | collective-permute-start | bytes 98312 | tf_op jit(solution)/shard_map/ppermute | solution.py:18
  190.6 3.5 %collective-permute-start.21 = (bf16[2,18,256]{2,1,0:T(8,128)(2,1)S(1)}, bf16[2,18,256]{2,1,0:T(8,128)(2,1)S(1)}, u32[]{:S(2)}, u32[]{:S(2)}) collective-permute-start(bf16[2,18,256]{2,1,0:T(8,128)(2,1)S(1)} %pad_maximum_fusion.2), channel_id=1, source_target_pairs={{32,0},{33,1},{34,2},{35,3},{36,4},{37,5},{38,6},{39,7},{40,8},{41... | collective-permute-start | bytes 55304 | tf_op jit(solution)/shard_map/ppermute | solution.py:29
  200.5 16.4 %reduce-scatter.2.cloned.1.call-done = f32[32,2304]{1,0:T(8,128)} async-done(((f32[256,2304]{1,0:T(8,128)}), f32[32,2304]{1,0:T(8,128)}) %reduce-scatter.2.cloned.1.call-update) | async-done | bytes 294928 | tf_op jit(solution)/shard_map/reduce_scatter | solution.py:129
  217.8 3.3 %collective-permute-start.22 = (f32[32,1152]{1,0:T(8,128)S(1)}, f32[32,1152]{1,0:T(8,128)S(1)}, u32[]{:S(2)}, u32[]{:S(2)}) collective-permute-start(f32[32,1152]{1,0:T(8,128)S(1)} %constant_dynamic-slice_fusion.5), channel_id=1, source_target_pairs={{0,32},{1,33},{2,34},{3,35},{4,36},{5,37},{6,38},{7,39},{8,40},{9,... | collective-permute-start | bytes 442376 | tf_op jit(solution)/shard_map/ppermute | solution.py:42
  221.3 5.1 %collective-permute-done.22 = f32[32,1152]{1,0:T(8,128)S(1)} collective-permute-done((f32[32,1152]{1,0:T(8,128)S(1)}, f32[32,1152]{1,0:T(8,128)S(1)}, u32[]{:S(2)}, u32[]{:S(2)}) %collective-permute-start.22) | collective-permute-done | bytes 147488 | tf_op jit(solution)/shard_map/ppermute | solution.py:42
  230.4 3.3 %collective-permute-done.23 = f32[32,576]{1,0:T(8,128)S(1)} collective-permute-done((f32[32,576]{1,0:T(8,128)S(1)}, f32[32,576]{1,0:T(8,128)S(1)}, u32[]{:S(2)}, u32[]{:S(2)}) %collective-permute-start.23) | collective-permute-done | bytes 73760 | tf_op jit(solution)/shard_map/ppermute | solution.py:42
  233.9 6.0 %collective-permute-start.24 = (f32[32,288]{1,0:T(8,128)S(1)}, f32[32,288]{1,0:T(8,128)S(1)}, u32[]{:S(2)}, u32[]{:S(2)}) collective-permute-start(f32[32,288]{1,0:T(8,128)S(1)} %constant_dynamic-slice_fusion.3), channel_id=1, source_target_pairs={{0,8},{1,9},{2,10},{3,11},{4,12},{5,13},{6,14},{7,15},{8,0},{9,1},... | collective-permute-start | bytes 110600 | tf_op jit(solution)/shard_map/ppermute | solution.py:42
  240.0 3.8 %collective-permute-done.24 = f32[32,288]{1,0:T(8,128)S(1)} collective-permute-done((f32[32,288]{1,0:T(8,128)S(1)}, f32[32,288]{1,0:T(8,128)S(1)}, u32[]{:S(2)}, u32[]{:S(2)}) %collective-permute-start.24) | collective-permute-done | bytes 36896 | tf_op jit(solution)/shard_map/ppermute | solution.py:42
  244.0 8.1 %collective-permute-start.25 = (f32[32,144]{1,0:T(8,128)S(1)}, f32[32,144]{1,0:T(8,128)S(1)}, u32[]{:S(2)}, u32[]{:S(2)}) collective-permute-start(f32[32,144]{1,0:T(8,128)S(1)} %constant_dynamic-slice_fusion.2), channel_id=1, source_target_pairs={{0,4},{1,5},{2,6},{3,7},{4,0},{5,1},{6,2},{7,3},{8,12},{9,13},{10,... | collective-permute-start | bytes 55304 | tf_op jit(solution)/shard_map/ppermute | solution.py:42
  254.2 4.6 %collective-permute-start.26 = (f32[32,72]{1,0:T(8,128)S(1)}, f32[32,72]{1,0:T(8,128)S(1)}, u32[]{:S(2)}, u32[]{:S(2)}) collective-permute-start(f32[32,72]{1,0:T(8,128)S(1)} %constant_dynamic-slice_fusion.1), channel_id=1, source_target_pairs={{0,2},{1,3},{2,0},{3,1},{4,6},{5,7},{6,4},{7,5},{8,10},{9,11},{10,... | collective-permute-start | bytes 27656 | tf_op jit(solution)/shard_map/ppermute | solution.py:42
  260.9 3.3 %collective-permute-start.27 = (f32[32,36]{1,0:T(8,128)S(1)}, f32[32,36]{1,0:T(8,128)S(1)}, u32[]{:S(2)}, u32[]{:S(2)}) collective-permute-start(f32[32,36]{1,0:T(8,128)S(1)} %constant_dynamic-slice_fusion), channel_id=1, source_target_pairs={{0,1},{1,0},{2,3},{3,2},{4,5},{5,4},{6,7},{7,6},{8,9},{9,8},{10,11... | collective-permute-start | bytes 13832 | tf_op jit(solution)/shard_map/ppermute | solution.py:42
  (149 shorter events, 69.7 us)
Async XLA Ops:
  7.2 28.3 %copy-start = (bf16[64,16,256]{2,1,0:T(8,128)(2,1)S(1)}, bf16[64,16,256]{2,1,0:T(8,128)(2,1)}, u32[]{:S(2)}) copy-start(bf16[64,16,256]{2,1,0:T(8,128)(2,1)} %param.13) | copy-start | bytes 1572868
  7.2 209.7 %reduce-scatter.2.cloned.1.call-start = ((), (), s32[]{:S(2)}) async-start(), calls=%async_computation.1 | async-start | bytes 2654208 | tf_op jit(solution)/shard_map/reduce_scatter | solution.py:129
  8.4 20.4 %collective-permute-start = (bf16[64,256]{1,0:T(8,128)(2,1)S(1)}, bf16[64,256]{1,0:T(8,128)(2,1)S(1)}, u32[]{:S(2)}, u32[]{:S(2)}) collective-permute-start(bf16[64,256]{1,0:T(8,128)(2,1)S(1)} %bitcast.157), channel_id=1, source_target_pairs={{0,1},{1,2},{2,3},{3,4},{4,5},{5,6},{6,7},{7,8},{8,9},{9,10},{10,1... | collective-permute-start | bytes 98312 | tf_op jit(solution)/shard_map/ppermute | solution.py:17
  12.7 16.1 %collective-permute-start.1 = (bf16[64,256]{1,0:T(8,128)(2,1)S(1)}, bf16[64,256]{1,0:T(8,128)(2,1)S(1)}, u32[]{:S(2)}, u32[]{:S(2)}) collective-permute-start(bf16[64,256]{1,0:T(8,128)(2,1)S(1)} %bitcast.159), channel_id=1, source_target_pairs={{1,0},{2,1},{3,2},{4,3},{5,4},{6,5},{7,6},{8,7},{9,8},{10,9},{11,1... | collective-permute-start | bytes 98312 | tf_op jit(solution)/shard_map/ppermute | solution.py:18
  29.7 5.8 %collective-permute-start.2 = (bf16[18,256]{1,0:T(8,128)(2,1)S(1)}, bf16[18,256]{1,0:T(8,128)(2,1)S(1)}, u32[]{:S(2)}, u32[]{:S(2)}) collective-permute-start(bf16[18,256]{1,0:T(8,128)(2,1)S(1)} %bitcast.151), channel_id=1, source_target_pairs={{0,64},{64,128},{128,192},{192,256},{256,320},{320,384},{384,448},... | collective-permute-start | bytes 27656 | tf_op jit(solution)/shard_map/ppermute | solution.py:17
  31.1 4.4 %collective-permute-start.3 = (bf16[18,256]{1,0:T(8,128)(2,1)S(1)}, bf16[18,256]{1,0:T(8,128)(2,1)S(1)}, u32[]{:S(2)}, u32[]{:S(2)}) collective-permute-start(bf16[18,256]{1,0:T(8,128)(2,1)S(1)} %bitcast.149), channel_id=1, source_target_pairs={{64,0},{128,64},{192,128},{256,192},{320,256},{384,320},{448,384},... | collective-permute-start | bytes 27656 | tf_op jit(solution)/shard_map/ppermute | solution.py:18
  32.4 7.2 %collective-permute-start.4 = (bf16[2,18,256]{2,1,0:T(8,128)(2,1)S(1)}, bf16[2,18,256]{2,1,0:T(8,128)(2,1)S(1)}, u32[]{:S(2)}, u32[]{:S(2)}) collective-permute-start(bf16[2,18,256]{2,1,0:T(8,128)(2,1)S(1)} %pad_maximum_fusion.1), channel_id=1, source_target_pairs={{32,0},{33,1},{34,2},{35,3},{36,4},{37,5},{38,6},{39,7},{40,8},{41... | collective-permute-start | bytes 55304 | tf_op jit(solution)/shard_map/ppermute | solution.py:29
  58.6 5.4 %collective-permute-start.5 = (f32[64]{0:T(128)S(1)}, f32[64]{0:T(128)S(1)}, u32[]{:S(2)}, u32[]{:S(2)}) collective-permute-start(f32[64]{0:T(128)S(1)} %reduce_sum.94), channel_id=1, source_target_pairs={{0,1},{1,0},{2,3},{3,2},{4,5},{5,4},{6,7},{7,6},{8,9},{9,8},{10,11... | collective-permute-start | bytes 776 | tf_op jit(solution)/shard_map/ppermute | solution.py:42
  64.0 6.3 %collective-permute-start.6 = (f32[64]{0:T(128)S(1)}, f32[64]{0:T(128)S(1)}, u32[]{:S(2)}, u32[]{:S(2)}) collective-permute-start(f32[64]{0:T(128)S(1)} %add.169), channel_id=1, source_target_pairs={{0,2},{1,3},{2,0},{3,1},{4,6},{5,7},{6,4},{7,5},{8,10},{9,11},{10,... | collective-permute-start | bytes 776 | tf_op jit(solution)/shard_map/ppermute | solution.py:42
  70.4 9.3 %collective-permute-start.7 = (f32[64]{0:T(128)S(1)}, f32[64]{0:T(128)S(1)}, u32[]{:S(2)}, u32[]{:S(2)}) collective-permute-start(f32[64]{0:T(128)S(1)} %add.170), channel_id=1, source_target_pairs={{0,4},{1,5},{2,6},{3,7},{4,0},{5,1},{6,2},{7,3},{8,12},{9,13},{10,... | collective-permute-start | bytes 776 | tf_op jit(solution)/shard_map/ppermute | solution.py:42
  79.7 9.3 %collective-permute-start.8 = (f32[64]{0:T(128)S(1)}, f32[64]{0:T(128)S(1)}, u32[]{:S(2)}, u32[]{:S(2)}) collective-permute-start(f32[64]{0:T(128)S(1)} %add.171), channel_id=1, source_target_pairs={{0,8},{1,9},{2,10},{3,11},{4,12},{5,13},{6,14},{7,15},{8,0},{9,1},... | collective-permute-start | bytes 776 | tf_op jit(solution)/shard_map/ppermute | solution.py:42
  89.0 5.4 %collective-permute-start.9 = (f32[64]{0:T(128)S(1)}, f32[64]{0:T(128)S(1)}, u32[]{:S(2)}, u32[]{:S(2)}) collective-permute-start(f32[64]{0:T(128)S(1)} %add.172), channel_id=1, source_target_pairs={{0,16},{1,17},{2,18},{3,19},{4,20},{5,21},{6,22},{7,23},{8,24},{9,... | collective-permute-start | bytes 776 | tf_op jit(solution)/shard_map/ppermute | solution.py:42
  94.5 6.9 %collective-permute-start.10 = (f32[64]{0:T(128)S(1)}, f32[64]{0:T(128)S(1)}, u32[]{:S(2)}, u32[]{:S(2)}) collective-permute-start(f32[64]{0:T(128)S(1)} %add.173), channel_id=1, source_target_pairs={{0,32},{1,33},{2,34},{3,35},{4,36},{5,37},{6,38},{7,39},{8,40},{9,... | collective-permute-start | bytes 776 | tf_op jit(solution)/shard_map/ppermute | solution.py:42
  98.7 3.1 %copy-start.1 = (bf16[64,16,256]{2,1,0:T(8,128)(2,1)S(1)}, bf16[64,16,256]{2,1,0:T(8,128)(2,1)}, u32[]{:S(2)}) copy-start(bf16[64,16,256]{2,1,0:T(8,128)(2,1)} %param.17) | copy-start | bytes 1572868
  115.5 5.5 %collective-permute-start.11 = (f32[512]{0:T(512)S(1)}, f32[512]{0:T(512)S(1)}, u32[]{:S(2)}, u32[]{:S(2)}) collective-permute-start(f32[512]{0:T(512)S(1)} %reduce_sum.97), channel_id=1, source_target_pairs={{0,1},{1,0},{2,3},{3,2},{4,5},{5,4},{6,7},{7,6},{8,9},{9,8},{10,11... | collective-permute-start | bytes 6152 | tf_op jit(solution)/shard_map/ppermute | solution.py:42
  120.9 6.4 %collective-permute-start.12 = (f32[512]{0:T(512)S(1)}, f32[512]{0:T(512)S(1)}, u32[]{:S(2)}, u32[]{:S(2)}) collective-permute-start(f32[512]{0:T(512)S(1)} %add.182), channel_id=1, source_target_pairs={{0,2},{1,3},{2,0},{3,1},{4,6},{5,7},{6,4},{7,5},{8,10},{9,11},{10,... | collective-permute-start | bytes 6152 | tf_op jit(solution)/shard_map/ppermute | solution.py:42
  127.3 9.4 %collective-permute-start.13 = (f32[512]{0:T(512)S(1)}, f32[512]{0:T(512)S(1)}, u32[]{:S(2)}, u32[]{:S(2)}) collective-permute-start(f32[512]{0:T(512)S(1)} %add.183), channel_id=1, source_target_pairs={{0,4},{1,5},{2,6},{3,7},{4,0},{5,1},{6,2},{7,3},{8,12},{9,13},{10,... | collective-permute-start | bytes 6152 | tf_op jit(solution)/shard_map/ppermute | solution.py:42
  136.7 9.4 %collective-permute-start.14 = (f32[512]{0:T(512)S(1)}, f32[512]{0:T(512)S(1)}, u32[]{:S(2)}, u32[]{:S(2)}) collective-permute-start(f32[512]{0:T(512)S(1)} %add.184), channel_id=1, source_target_pairs={{0,8},{1,9},{2,10},{3,11},{4,12},{5,13},{6,14},{7,15},{8,0},{9,1},... | collective-permute-start | bytes 6152 | tf_op jit(solution)/shard_map/ppermute | solution.py:42
  146.1 5.5 %collective-permute-start.15 = (f32[512]{0:T(512)S(1)}, f32[512]{0:T(512)S(1)}, u32[]{:S(2)}, u32[]{:S(2)}) collective-permute-start(f32[512]{0:T(512)S(1)} %add.185), channel_id=1, source_target_pairs={{0,16},{1,17},{2,18},{3,19},{4,20},{5,21},{6,22},{7,23},{8,24},{9,... | collective-permute-start | bytes 6152 | tf_op jit(solution)/shard_map/ppermute | solution.py:42
  151.5 7.0 %collective-permute-start.16 = (f32[512]{0:T(512)S(1)}, f32[512]{0:T(512)S(1)}, u32[]{:S(2)}, u32[]{:S(2)}) collective-permute-start(f32[512]{0:T(512)S(1)} %add.186), channel_id=1, source_target_pairs={{0,32},{1,33},{2,34},{3,35},{4,36},{5,37},{6,38},{7,39},{8,40},{9,... | collective-permute-start | bytes 6152 | tf_op jit(solution)/shard_map/ppermute | solution.py:42
  172.8 13.2 %collective-permute-start.17 = (bf16[64,256]{1,0:T(8,128)(2,1)S(1)}, bf16[64,256]{1,0:T(8,128)(2,1)S(1)}, u32[]{:S(2)}, u32[]{:S(2)}) collective-permute-start(bf16[64,256]{1,0:T(8,128)(2,1)S(1)} %bitcast.153), channel_id=1, source_target_pairs={{0,1},{1,2},{2,3},{3,4},{4,5},{5,6},{6,7},{7,8},{8,9},{9,10},{10,1... | collective-permute-start | bytes 98312 | tf_op jit(solution)/shard_map/ppermute | solution.py:17
  174.8 13.2 %collective-permute-start.18 = (bf16[64,256]{1,0:T(8,128)(2,1)S(1)}, bf16[64,256]{1,0:T(8,128)(2,1)S(1)}, u32[]{:S(2)}, u32[]{:S(2)}) collective-permute-start(bf16[64,256]{1,0:T(8,128)(2,1)S(1)} %bitcast.155), channel_id=1, source_target_pairs={{1,0},{2,1},{3,2},{4,3},{5,4},{6,5},{7,6},{8,7},{9,8},{10,9},{11,1... | collective-permute-start | bytes 98312 | tf_op jit(solution)/shard_map/ppermute | solution.py:18
  188.0 6.2 %collective-permute-start.19 = (bf16[18,256]{1,0:T(8,128)(2,1)S(1)}, bf16[18,256]{1,0:T(8,128)(2,1)S(1)}, u32[]{:S(2)}, u32[]{:S(2)}) collective-permute-start(bf16[18,256]{1,0:T(8,128)(2,1)S(1)} %bitcast.152), channel_id=1, source_target_pairs={{0,64},{64,128},{128,192},{192,256},{256,320},{320,384},{384,448},... | collective-permute-start | bytes 27656 | tf_op jit(solution)/shard_map/ppermute | solution.py:17
  189.3 4.9 %collective-permute-start.20 = (bf16[18,256]{1,0:T(8,128)(2,1)S(1)}, bf16[18,256]{1,0:T(8,128)(2,1)S(1)}, u32[]{:S(2)}, u32[]{:S(2)}) collective-permute-start(bf16[18,256]{1,0:T(8,128)(2,1)S(1)} %bitcast.150), channel_id=1, source_target_pairs={{64,0},{128,64},{192,128},{256,192},{320,256},{384,320},{448,384},... | collective-permute-start | bytes 27656 | tf_op jit(solution)/shard_map/ppermute | solution.py:18
  190.6 9.7 %collective-permute-start.21 = (bf16[2,18,256]{2,1,0:T(8,128)(2,1)S(1)}, bf16[2,18,256]{2,1,0:T(8,128)(2,1)S(1)}, u32[]{:S(2)}, u32[]{:S(2)}) collective-permute-start(bf16[2,18,256]{2,1,0:T(8,128)(2,1)S(1)} %pad_maximum_fusion.2), channel_id=1, source_target_pairs={{32,0},{33,1},{34,2},{35,3},{36,4},{37,5},{38,6},{39,7},{40,8},{41... | collective-permute-start | bytes 55304 | tf_op jit(solution)/shard_map/ppermute | solution.py:29
  200.3 63.9 %copy-start.2 = (bf16[64,16,256]{2,1,0:T(8,128)(2,1)S(1)}, bf16[64,16,256]{2,1,0:T(8,128)(2,1)}, u32[]{:S(2)}) copy-start(bf16[64,16,256]{2,1,0:T(8,128)(2,1)} %param.17) | copy-start | bytes 1572868
  217.8 8.5 %collective-permute-start.22 = (f32[32,1152]{1,0:T(8,128)S(1)}, f32[32,1152]{1,0:T(8,128)S(1)}, u32[]{:S(2)}, u32[]{:S(2)}) collective-permute-start(f32[32,1152]{1,0:T(8,128)S(1)} %constant_dynamic-slice_fusion.5), channel_id=1, source_target_pairs={{0,32},{1,33},{2,34},{3,35},{4,36},{5,37},{6,38},{7,39},{8,40},{9,... | collective-permute-start | bytes 442376 | tf_op jit(solution)/shard_map/ppermute | solution.py:42
  227.4 6.3 %collective-permute-start.23 = (f32[32,576]{1,0:T(8,128)S(1)}, f32[32,576]{1,0:T(8,128)S(1)}, u32[]{:S(2)}, u32[]{:S(2)}) collective-permute-start(f32[32,576]{1,0:T(8,128)S(1)} %constant_dynamic-slice_fusion.4), channel_id=1, source_target_pairs={{0,16},{1,17},{2,18},{3,19},{4,20},{5,21},{6,22},{7,23},{8,24},{9,... | collective-permute-start | bytes 221192 | tf_op jit(solution)/shard_map/ppermute | solution.py:42
  233.9 9.9 %collective-permute-start.24 = (f32[32,288]{1,0:T(8,128)S(1)}, f32[32,288]{1,0:T(8,128)S(1)}, u32[]{:S(2)}, u32[]{:S(2)}) collective-permute-start(f32[32,288]{1,0:T(8,128)S(1)} %constant_dynamic-slice_fusion.3), channel_id=1, source_target_pairs={{0,8},{1,9},{2,10},{3,11},{4,12},{5,13},{6,14},{7,15},{8,0},{9,1},... | collective-permute-start | bytes 110600 | tf_op jit(solution)/shard_map/ppermute | solution.py:42
  244.0 10.0 %collective-permute-start.25 = (f32[32,144]{1,0:T(8,128)S(1)}, f32[32,144]{1,0:T(8,128)S(1)}, u32[]{:S(2)}, u32[]{:S(2)}) collective-permute-start(f32[32,144]{1,0:T(8,128)S(1)} %constant_dynamic-slice_fusion.2), channel_id=1, source_target_pairs={{0,4},{1,5},{2,6},{3,7},{4,0},{5,1},{6,2},{7,3},{8,12},{9,13},{10,... | collective-permute-start | bytes 55304 | tf_op jit(solution)/shard_map/ppermute | solution.py:42
  254.2 6.5 %collective-permute-start.26 = (f32[32,72]{1,0:T(8,128)S(1)}, f32[32,72]{1,0:T(8,128)S(1)}, u32[]{:S(2)}, u32[]{:S(2)}) collective-permute-start(f32[32,72]{1,0:T(8,128)S(1)} %constant_dynamic-slice_fusion.1), channel_id=1, source_target_pairs={{0,2},{1,3},{2,0},{3,1},{4,6},{5,7},{6,4},{7,5},{8,10},{9,11},{10,... | collective-permute-start | bytes 27656 | tf_op jit(solution)/shard_map/ppermute | solution.py:42
  260.9 5.6 %collective-permute-start.27 = (f32[32,36]{1,0:T(8,128)S(1)}, f32[32,36]{1,0:T(8,128)S(1)}, u32[]{:S(2)}, u32[]{:S(2)}) collective-permute-start(f32[32,36]{1,0:T(8,128)S(1)} %constant_dynamic-slice_fusion), channel_id=1, source_target_pairs={{0,1},{1,0},{2,3},{3,2},{4,5},{5,4},{6,7},{7,6},{8,9},{9,8},{10,11... | collective-permute-start | bytes 13832 | tf_op jit(solution)/shard_map/ppermute | solution.py:42
  (8 other events, 13.1 us)
Sparse Core Ops, SparseCore 0:
  172.8 44.0 reduce-scatter.1

commit v8 on v7

--- a/solution.py
+++ b/solution.py
@@ -56,8 +56,8 @@
     return value
 
 
-def lon_halving_sum(rows):
-    for bit in reversed(range((lax.axis_size("lon") - 1).bit_length())):
+def lon_halving_sum(rows, bits):
+    for bit in reversed(range(bits)):
         half = rows.shape[1] // 2
         mine = (lax.axis_index("lon") >> bit) & 1
         keep = lax.dynamic_slice_in_dim(rows, mine * half, half, axis=1)
@@ -126,7 +126,15 @@
         dimension_numbers=("CHWN", "HWIO", "CHWN"),
         preferred_element_type=jnp.float32,
     ).reshape(channels, 9 * channels)
-    owned_cols = lax.psum_scatter(term, "lat", scatter_dimension=0, tiled=True)
+    top = (lax.axis_size("lon") - 1).bit_length() - 1
+    half = term.shape[1] // 2
+    mine = (lax.axis_index("lon") >> top) & 1
+    sent = lax.psum_scatter(
+        lax.dynamic_slice_in_dim(term, (1 - mine) * half, half, axis=1), "lat", scatter_dimension=0, tiled=True
+    )
+    kept = lax.psum_scatter(
+        lax.dynamic_slice_in_dim(term, mine * half, half, axis=1), "lat", scatter_dimension=0, tiled=True
+    )
     grad_banded, grad_distant = extend(dconv)
     flipped = jnp.swapaxes(kernel[::-1, ::-1], 2, 3)
     back = conv_valid(grad_banded, flipped)
@@ -146,7 +154,7 @@
     back = back.at[0].add(jnp.where(north, upper_term, 0.0))
     back = back.at[-1].add(jnp.where(south, lower_term, 0.0))
     grad_fields = (upstream.reshape(height, breadth, channels) + back).astype(jnp.bfloat16)
-    grad_kernel = lon_halving_sum(owned_cols).T
+    grad_kernel = lon_halving_sum(kept + exchange(sent, "lon", top), top).T
     return (block_out, grad_fields, grad_kernel, grad_gain, grad_shift)
 
 

time: 275 us -> 303 us (1.10)
  waiting for transfers between devices: 80.5 us -> 109 us
    reduce_scatter x1 -> x2, waiting for transfers between devices: 16.4 us -> 50.4 us  [the longest x1 38.7 us: local(): lax.psum_scatter(lax.dynamic_slice_in_dim(term, mine * half, half, axis=1...]
    ppermute x18, waiting for transfers between devices: 58.5 us -> 53 us  [exchange(): return lax.ppermute(block, axis, [(i, i ^ 1 << bit) for i in range(peers)])]
    reshape x1 -> x0, local copies, waits for them, and re-layouts: 3.08 us -> none  [local(): term = lax.conv_general_dilated(merged[None], dconv.reshape(height, bread...]
    unnamed x30 -> x32, local copies, waits for them, and re-layouts: 4.79 us -> 7.58 us
  transfers between devices with their start and end apart: 29 -> 30, of which waited for: 21 -> 21; matrix products, arithmetic and copies ran while one was open for 3% -> 4% of each run, Pallas kernels for 0% -> 0%
where the time goes in v8:
time: 303 us; the launch traced here: 301 us
  starting transfers between devices  114 us (38%)
  waiting for transfers between devices  109 us (36%)
  blocking collectives  27.2 us (9%)
  between operations  15.5 us (5%)
  local copies, waits for them, and re-layouts  14.2 us (5%)
  matrix products  12.8 us (4%)
  other arithmetic  8.79 us (3%)
    ppermute x18, starting transfers between devices, exchange(): return lax.ppermute(block, axis, [(i, i ^ 1 << bit) for i in range(peers)])  70.7 us
    ppermute x18, waiting for transfers between devices, exchange(): return lax.ppermute(block, axis, [(i, i ^ 1 << bit) for i in range(peers)])  53 us
    reduce_scatter x1, waiting for transfers between devices, local(): lax.psum_scatter(lax.dynamic_slice_in_dim(term, mine * half, half, axis=1...  38.7 us
    ppermute x4, starting transfers between devices, with_halo(): lax.ppermute(jnp.squeeze(initial, dim), axis, down)  27.9 us
    unnamed x1, blocking collectives  14.5 us
    all_gather x1, blocking collectives, butterfly_sum(): value = jnp.sum(lax.all_gather(value, 'lat'), 0)  12.7 us
    reduce_scatter x1, waiting for transfers between devices, local(): lax.psum_scatter(lax.dynamic_slice_in_dim(term, (1 - mine) * half, half,...  11.7 us
    ppermute x4, starting transfers between devices, with_halo(): lax.ppermute(jnp.squeeze(last, dim), axis, up)  8.99 us
  transfers between devices with their start and end apart: 30, of which 21 were waited for; matrix products, arithmetic and copies ran while one was open for 4% of the time, Pallas kernels for 0%

profile of v8, /device:TPU:6, one launch (start us, length us, event | category | flops | bytes accessed | tf_op | source)
XLA Modules:
  0.0 301.5 jit_solution(11017679643391909921)
XLA Ops:
  8.4 4.3 %collective-permute-start = (bf16[64,256]{1,0:T(8,128)(2,1)S(1)}, bf16[64,256]{1,0:T(8,128)(2,1)S(1)}, u32[]{:S(2)}, u32[]{:S(2)}) collective-permute-start(bf16[64,256]{1,0:T(8,128)(2,1)S(1)} %bitcast.157), channel_id=1, source_target_pairs={{0,1},{1,2},{2,3},{3,4},{4,5},{5,6},{6,7},{7,8},{8,9},{9,10},{10,1... | collective-permute-start | bytes 98312 | tf_op jit(solution)/shard_map/ppermute | solution.py:17
  12.7 14.1 %collective-permute-start.1 = (bf16[64,256]{1,0:T(8,128)(2,1)S(1)}, bf16[64,256]{1,0:T(8,128)(2,1)S(1)}, u32[]{:S(2)}, u32[]{:S(2)}) collective-permute-start(bf16[64,256]{1,0:T(8,128)(2,1)S(1)} %bitcast.159), channel_id=1, source_target_pairs={{1,0},{2,1},{3,2},{4,3},{5,4},{6,5},{7,6},{8,7},{9,8},{10,9},{11,1... | collective-permute-start | bytes 98312 | tf_op jit(solution)/shard_map/ppermute | solution.py:18
  36.0 3.7 %collective-permute-done.4 = bf16[2,18,256]{2,1,0:T(8,128)(2,1)S(1)} collective-permute-done((bf16[2,18,256]{2,1,0:T(8,128)(2,1)S(1)}, bf16[2,18,256]{2,1,0:T(8,128)(2,1)S(1)}, u32[]{:S(2)}, u32[]{:S(2)}) %collective-permute-start.4) | collective-permute-done | bytes 18464 | tf_op jit(solution)/shard_map/ppermute | solution.py:29
  41.2 3.3 %select_reduce_fusion.1 = (f32[256]{0:T(256)S(1)}, f32[256]{0:T(256)S(1)}, f32[64,8,3,256]{3,1,2,0:T(8,128)}) fusion(pred[8,3]{0,1:T(4,128)(4,1)S(1)} %copy-done.8, bf16[3,3,256,256]{3,2,1,0:T(8,128)(2,1)S(1)} %copy-done.4, bf16[66,1,7,2,256]{4,2,3,0,1:T(8,128)(2,1)S(1)} %slice.207, bf16[66,1,8,3,256]{4,2,3,0,1:T(8,128)(2,1)S(1)} %copy.90), kind=kOutput, calls=%fused_computation.4 | convolution fusion | flops 1818353152 | bytes 4038680 | tf_op jit(solution)/shard_map/conv_general_dilated | solution.py:70
  45.1 14.5 %all-reduce = f32[512]{0:T(512)S(1)} all-reduce(f32[512]{0:T(512)S(1)} %maximum_dynamic-update-slice_fusion), channel_id=2, replica_groups=mesh['lat'=8,'lon'=64] {'lat'}, use_global_device_ids=true, to_apply=%add | all-reduce | flops 512 | bytes 4096
  61.6 3.5 %collective-permute-done.5 = f32[64]{0:T(128)S(1)} collective-permute-done((f32[64]{0:T(128)S(1)}, f32[64]{0:T(128)S(1)}, u32[]{:S(2)}, u32[]{:S(2)}) %collective-permute-start.5) | collective-permute-done | bytes 288 | tf_op jit(solution)/shard_map/ppermute | solution.py:42
  67.0 4.4 %collective-permute-done.6 = f32[64]{0:T(128)S(1)} collective-permute-done((f32[64]{0:T(128)S(1)}, f32[64]{0:T(128)S(1)}, u32[]{:S(2)}, u32[]{:S(2)}) %collective-permute-start.6) | collective-permute-done | bytes 288 | tf_op jit(solution)/shard_map/ppermute | solution.py:42
  71.4 5.9 %collective-permute-start.7 = (f32[64]{0:T(128)S(1)}, f32[64]{0:T(128)S(1)}, u32[]{:S(2)}, u32[]{:S(2)}) collective-permute-start(f32[64]{0:T(128)S(1)} %add.172), channel_id=1, source_target_pairs={{0,4},{1,5},{2,6},{3,7},{4,0},{5,1},{6,2},{7,3},{8,12},{9,13},{10,... | collective-permute-start | bytes 776 | tf_op jit(solution)/shard_map/ppermute | solution.py:42
  77.3 3.5 %collective-permute-done.7 = f32[64]{0:T(128)S(1)} collective-permute-done((f32[64]{0:T(128)S(1)}, f32[64]{0:T(128)S(1)}, u32[]{:S(2)}, u32[]{:S(2)}) %collective-permute-start.7) | collective-permute-done | bytes 288 | tf_op jit(solution)/shard_map/ppermute | solution.py:42
  80.8 5.3 %collective-permute-start.8 = (f32[64]{0:T(128)S(1)}, f32[64]{0:T(128)S(1)}, u32[]{:S(2)}, u32[]{:S(2)}) collective-permute-start(f32[64]{0:T(128)S(1)} %add.173), channel_id=1, source_target_pairs={{0,8},{1,9},{2,10},{3,11},{4,12},{5,13},{6,14},{7,15},{8,0},{9,1},... | collective-permute-start | bytes 776 | tf_op jit(solution)/shard_map/ppermute | solution.py:42
  86.1 4.0 %collective-permute-done.8 = f32[64]{0:T(128)S(1)} collective-permute-done((f32[64]{0:T(128)S(1)}, f32[64]{0:T(128)S(1)}, u32[]{:S(2)}, u32[]{:S(2)}) %collective-permute-start.8) | collective-permute-done | bytes 288 | tf_op jit(solution)/shard_map/ppermute | solution.py:42
  95.5 3.8 %collective-permute-start.10 = (f32[64]{0:T(128)S(1)}, f32[64]{0:T(128)S(1)}, u32[]{:S(2)}, u32[]{:S(2)}) collective-permute-start(f32[64]{0:T(128)S(1)} %add.175), channel_id=1, source_target_pairs={{0,32},{1,33},{2,34},{3,35},{4,36},{5,37},{6,38},{7,39},{8,40},{9,... | collective-permute-start | bytes 776 | tf_op jit(solution)/shard_map/ppermute | solution.py:42
  103.8 12.7 %all-gather.2 = f32[8,1,512]{2,1,0:T(1,128)S(1)} all-gather(f32[1,1,512]{2,1,0:T(1,128)S(1)} %bitcast.164), channel_id=3, replica_groups=mesh['lat'=8,'lon'=64] {'lat'}, dimensions={0}, use_global_device_ids=true | all-gather | bytes 18432 | tf_op jit(solution)/shard_map/all_gather | solution.py:53
  118.5 3.5 %collective-permute-done.11 = f32[512]{0:T(512)S(1)} collective-permute-done((f32[512]{0:T(512)S(1)}, f32[512]{0:T(512)S(1)}, u32[]{:S(2)}, u32[]{:S(2)}) %collective-permute-start.11) | collective-permute-done | bytes 2080 | tf_op jit(solution)/shard_map/ppermute | solution.py:42
  124.9 3.5 %collective-permute-done.12 = f32[512]{0:T(512)S(1)} collective-permute-done((f32[512]{0:T(512)S(1)}, f32[512]{0:T(512)S(1)}, u32[]{:S(2)}, u32[]{:S(2)}) %collective-permute-start.12) | collective-permute-done | bytes 2080 | tf_op jit(solution)/shard_map/ppermute | solution.py:42
  128.4 5.9 %collective-permute-start.13 = (f32[512]{0:T(512)S(1)}, f32[512]{0:T(512)S(1)}, u32[]{:S(2)}, u32[]{:S(2)}) collective-permute-start(f32[512]{0:T(512)S(1)} %add.185), channel_id=1, source_target_pairs={{0,4},{1,5},{2,6},{3,7},{4,0},{5,1},{6,2},{7,3},{8,12},{9,13},{10,... | collective-permute-start | bytes 6152 | tf_op jit(solution)/shard_map/ppermute | solution.py:42
  134.2 3.5 %collective-permute-done.13 = f32[512]{0:T(512)S(1)} collective-permute-done((f32[512]{0:T(512)S(1)}, f32[512]{0:T(512)S(1)}, u32[]{:S(2)}, u32[]{:S(2)}) %collective-permute-start.13) | collective-permute-done | bytes 2080 | tf_op jit(solution)/shard_map/ppermute | solution.py:42
  137.7 5.3 %collective-permute-start.14 = (f32[512]{0:T(512)S(1)}, f32[512]{0:T(512)S(1)}, u32[]{:S(2)}, u32[]{:S(2)}) collective-permute-start(f32[512]{0:T(512)S(1)} %add.186), channel_id=1, source_target_pairs={{0,8},{1,9},{2,10},{3,11},{4,12},{5,13},{6,14},{7,15},{8,0},{9,1},... | collective-permute-start | bytes 6152 | tf_op jit(solution)/shard_map/ppermute | solution.py:42
  143.1 4.1 %collective-permute-done.14 = f32[512]{0:T(512)S(1)} collective-permute-done((f32[512]{0:T(512)S(1)}, f32[512]{0:T(512)S(1)}, u32[]{:S(2)}, u32[]{:S(2)}) %collective-permute-start.14) | collective-permute-done | bytes 2080 | tf_op jit(solution)/shard_map/ppermute | solution.py:42
  152.6 3.9 %collective-permute-start.16 = (f32[512]{0:T(512)S(1)}, f32[512]{0:T(512)S(1)}, u32[]{:S(2)}, u32[]{:S(2)}) collective-permute-start(f32[512]{0:T(512)S(1)} %add.188), channel_id=1, source_target_pairs={{0,32},{1,33},{2,34},{3,35},{4,36},{5,37},{6,38},{7,39},{8,40},{9,... | collective-permute-start | bytes 6152 | tf_op jit(solution)/shard_map/ppermute | solution.py:42
  162.7 6.6 %fusion.14 = f32[256,3,3,256]{0,3,2,1:T(8,128)S(1)} fusion(bf16[1,66,18,256]{3,2,1,0:T(8,128)(2,1)S(1)} %fusion.49, bf16[64,16,1,256]{3,1,0,2:T(8,128)(2,1)S(1)} %bitcast.138), kind=kOutput, calls=%fused_computation.19 | convolution fusion | flops 1207959552 | bytes 3491840 | tf_op jit(solution)/shard_map/conv_general_dilated | solution.py:121
  174.5 11.2 %collective-permute-start.18 = (bf16[64,256]{1,0:T(8,128)(2,1)S(1)}, bf16[64,256]{1,0:T(8,128)(2,1)S(1)}, u32[]{:S(2)}, u32[]{:S(2)}) collective-permute-start(bf16[64,256]{1,0:T(8,128)(2,1)S(1)} %bitcast.155), channel_id=1, source_target_pairs={{1,0},{2,1},{3,2},{4,3},{5,4},{6,5},{7,6},{8,7},{9,8},{10,9},{11,1... | collective-permute-start | bytes 98312 | tf_op jit(solution)/shard_map/ppermute | solution.py:18
  190.0 3.8 %collective-permute-start.21 = (bf16[2,18,256]{2,1,0:T(8,128)(2,1)S(1)}, bf16[2,18,256]{2,1,0:T(8,128)(2,1)S(1)}, u32[]{:S(2)}, u32[]{:S(2)}) collective-permute-start(bf16[2,18,256]{2,1,0:T(8,128)(2,1)S(1)} %pad_maximum_fusion.2), channel_id=1, source_target_pairs={{32,0},{33,1},{34,2},{35,3},{36,4},{37,5},{38,6},{39,7},{40,8},{41... | collective-permute-start | bytes 55304 | tf_op jit(solution)/shard_map/ppermute | solution.py:29
  200.0 11.7 %reduce-scatter.5.cloned.1.call-done = f32[32,1152]{1,0:T(8,128)} async-done(((f32[256,1152]{1,0:T(8,128)}), f32[32,1152]{1,0:T(8,128)}) %reduce-scatter.5.cloned.1.call-update) | async-done | bytes 147472 | tf_op jit(solution)/shard_map/reduce_scatter | solution.py:132
  211.7 3.2 %collective-permute-start.22 = (f32[32,1152]{1,0:T(8,128)}, f32[32,1152]{1,0:T(8,128)S(1)}, u32[]{:S(2)}, u32[]{:S(2)}) collective-permute-start(f32[32,1152]{1,0:T(8,128)} %reduce-scatter.5.cloned.1.call-done), channel_id=1, source_target_pairs={{0,32},{1,33},{2,34},{3,35},{4,36},{5,37},{6,38},{7,39},{8,40},{9,... | collective-permute-start | bytes 442376 | tf_op jit(solution)/shard_map/ppermute | solution.py:42
  215.1 38.7 %reduce-scatter.3.cloned.1.call-done = f32[32,1152]{1,0:T(8,128)} async-done(((f32[256,1152]{1,0:T(8,128)}), f32[32,1152]{1,0:T(8,128)}) %reduce-scatter.3.cloned.1.call-update) | async-done | bytes 147472 | tf_op jit(solution)/shard_map/reduce_scatter | solution.py:135
  257.9 3.3 %collective-permute-done.23 = f32[32,576]{1,0:T(8,128)S(1)} collective-permute-done((f32[32,576]{1,0:T(8,128)S(1)}, f32[32,576]{1,0:T(8,128)S(1)}, u32[]{:S(2)}, u32[]{:S(2)}) %collective-permute-start.23) | collective-permute-done | bytes 73760 | tf_op jit(solution)/shard_map/ppermute | solution.py:42
  261.4 4.8 %collective-permute-start.24 = (f32[32,288]{1,0:T(8,128)S(1)}, f32[32,288]{1,0:T(8,128)S(1)}, u32[]{:S(2)}, u32[]{:S(2)}) collective-permute-start(f32[32,288]{1,0:T(8,128)S(1)} %constant_dynamic-slice_fusion.3), channel_id=1, source_target_pairs={{0,8},{1,9},{2,10},{3,11},{4,12},{5,13},{6,14},{7,15},{8,0},{9,1},... | collective-permute-start | bytes 110600 | tf_op jit(solution)/shard_map/ppermute | solution.py:42
  266.3 4.9 %collective-permute-done.24 = f32[32,288]{1,0:T(8,128)S(1)} collective-permute-done((f32[32,288]{1,0:T(8,128)S(1)}, f32[32,288]{1,0:T(8,128)S(1)}, u32[]{:S(2)}, u32[]{:S(2)}) %collective-permute-start.24) | collective-permute-done | bytes 36896 | tf_op jit(solution)/shard_map/ppermute | solution.py:42
  271.4 8.1 %collective-permute-start.25 = (f32[32,144]{1,0:T(8,128)S(1)}, f32[32,144]{1,0:T(8,128)S(1)}, u32[]{:S(2)}, u32[]{:S(2)}) collective-permute-start(f32[32,144]{1,0:T(8,128)S(1)} %constant_dynamic-slice_fusion.2), channel_id=1, source_target_pairs={{0,4},{1,5},{2,6},{3,7},{4,0},{5,1},{6,2},{7,3},{8,12},{9,13},{10,... | collective-permute-start | bytes 55304 | tf_op jit(solution)/shard_map/ppermute | solution.py:42
  281.6 4.6 %collective-permute-start.26 = (f32[32,72]{1,0:T(8,128)S(1)}, f32[32,72]{1,0:T(8,128)S(1)}, u32[]{:S(2)}, u32[]{:S(2)}) collective-permute-start(f32[32,72]{1,0:T(8,128)S(1)} %constant_dynamic-slice_fusion.1), channel_id=1, source_target_pairs={{0,2},{1,3},{2,0},{3,1},{4,6},{5,7},{6,4},{7,5},{8,10},{9,11},{10,... | collective-permute-start | bytes 27656 | tf_op jit(solution)/shard_map/ppermute | solution.py:42
  288.3 3.3 %collective-permute-start.27 = (f32[32,36]{1,0:T(8,128)S(1)}, f32[32,36]{1,0:T(8,128)S(1)}, u32[]{:S(2)}, u32[]{:S(2)}) collective-permute-start(f32[32,36]{1,0:T(8,128)S(1)} %constant_dynamic-slice_fusion), channel_id=1, source_target_pairs={{0,1},{1,0},{2,3},{3,2},{4,5},{5,4},{6,7},{7,6},{8,9},{9,8},{10,11... | collective-permute-start | bytes 13832 | tf_op jit(solution)/shard_map/ppermute | solution.py:42
  (153 shorter events, 69.3 us)
Async XLA Ops:
  7.2 28.3 %copy-start = (bf16[64,16,256]{2,1,0:T(8,128)(2,1)S(1)}, bf16[64,16,256]{2,1,0:T(8,128)(2,1)}, u32[]{:S(2)}) copy-start(bf16[64,16,256]{2,1,0:T(8,128)(2,1)} %param.13) | copy-start | bytes 1572868
  7.2 204.5 %reduce-scatter.5.cloned.1.call-start = ((), (), s32[]{:S(2)}) async-start(), calls=%async_computation.3 | async-start | bytes 1327104 | tf_op jit(solution)/shard_map/reduce_scatter | solution.py:132
  8.4 20.4 %collective-permute-start = (bf16[64,256]{1,0:T(8,128)(2,1)S(1)}, bf16[64,256]{1,0:T(8,128)(2,1)S(1)}, u32[]{:S(2)}, u32[]{:S(2)}) collective-permute-start(bf16[64,256]{1,0:T(8,128)(2,1)S(1)} %bitcast.157), channel_id=1, source_target_pairs={{0,1},{1,2},{2,3},{3,4},{4,5},{5,6},{6,7},{7,8},{8,9},{9,10},{10,1... | collective-permute-start | bytes 98312 | tf_op jit(solution)/shard_map/ppermute | solution.py:17
  12.7 16.1 %collective-permute-start.1 = (bf16[64,256]{1,0:T(8,128)(2,1)S(1)}, bf16[64,256]{1,0:T(8,128)(2,1)S(1)}, u32[]{:S(2)}, u32[]{:S(2)}) collective-permute-start(bf16[64,256]{1,0:T(8,128)(2,1)S(1)} %bitcast.159), channel_id=1, source_target_pairs={{1,0},{2,1},{3,2},{4,3},{5,4},{6,5},{7,6},{8,7},{9,8},{10,9},{11,1... | collective-permute-start | bytes 98312 | tf_op jit(solution)/shard_map/ppermute | solution.py:18
  29.7 5.8 %collective-permute-start.2 = (bf16[18,256]{1,0:T(8,128)(2,1)S(1)}, bf16[18,256]{1,0:T(8,128)(2,1)S(1)}, u32[]{:S(2)}, u32[]{:S(2)}) collective-permute-start(bf16[18,256]{1,0:T(8,128)(2,1)S(1)} %bitcast.151), channel_id=1, source_target_pairs={{0,64},{64,128},{128,192},{192,256},{256,320},{320,384},{384,448},... | collective-permute-start | bytes 27656 | tf_op jit(solution)/shard_map/ppermute | solution.py:17
  31.1 4.4 %collective-permute-start.3 = (bf16[18,256]{1,0:T(8,128)(2,1)S(1)}, bf16[18,256]{1,0:T(8,128)(2,1)S(1)}, u32[]{:S(2)}, u32[]{:S(2)}) collective-permute-start(bf16[18,256]{1,0:T(8,128)(2,1)S(1)} %bitcast.149), channel_id=1, source_target_pairs={{64,0},{128,64},{192,128},{256,192},{320,256},{384,320},{448,384},... | collective-permute-start | bytes 27656 | tf_op jit(solution)/shard_map/ppermute | solution.py:18
  32.4 7.2 %collective-permute-start.4 = (bf16[2,18,256]{2,1,0:T(8,128)(2,1)S(1)}, bf16[2,18,256]{2,1,0:T(8,128)(2,1)S(1)}, u32[]{:S(2)}, u32[]{:S(2)}) collective-permute-start(bf16[2,18,256]{2,1,0:T(8,128)(2,1)S(1)} %pad_maximum_fusion.1), channel_id=1, source_target_pairs={{32,0},{33,1},{34,2},{35,3},{36,4},{37,5},{38,6},{39,7},{40,8},{41... | collective-permute-start | bytes 55304 | tf_op jit(solution)/shard_map/ppermute | solution.py:29
  59.7 5.4 %collective-permute-start.5 = (f32[64]{0:T(128)S(1)}, f32[64]{0:T(128)S(1)}, u32[]{:S(2)}, u32[]{:S(2)}) collective-permute-start(f32[64]{0:T(128)S(1)} %reduce_sum.94), channel_id=1, source_target_pairs={{0,1},{1,0},{2,3},{3,2},{4,5},{5,4},{6,7},{7,6},{8,9},{9,8},{10,11... | collective-permute-start | bytes 776 | tf_op jit(solution)/shard_map/ppermute | solution.py:42
  65.1 6.3 %collective-permute-start.6 = (f32[64]{0:T(128)S(1)}, f32[64]{0:T(128)S(1)}, u32[]{:S(2)}, u32[]{:S(2)}) collective-permute-start(f32[64]{0:T(128)S(1)} %add.171), channel_id=1, source_target_pairs={{0,2},{1,3},{2,0},{3,1},{4,6},{5,7},{6,4},{7,5},{8,10},{9,11},{10,... | collective-permute-start | bytes 776 | tf_op jit(solution)/shard_map/ppermute | solution.py:42
  71.4 9.3 %collective-permute-start.7 = (f32[64]{0:T(128)S(1)}, f32[64]{0:T(128)S(1)}, u32[]{:S(2)}, u32[]{:S(2)}) collective-permute-start(f32[64]{0:T(128)S(1)} %add.172), channel_id=1, source_target_pairs={{0,4},{1,5},{2,6},{3,7},{4,0},{5,1},{6,2},{7,3},{8,12},{9,13},{10,... | collective-permute-start | bytes 776 | tf_op jit(solution)/shard_map/ppermute | solution.py:42
  80.8 9.3 %collective-permute-start.8 = (f32[64]{0:T(128)S(1)}, f32[64]{0:T(128)S(1)}, u32[]{:S(2)}, u32[]{:S(2)}) collective-permute-start(f32[64]{0:T(128)S(1)} %add.173), channel_id=1, source_target_pairs={{0,8},{1,9},{2,10},{3,11},{4,12},{5,13},{6,14},{7,15},{8,0},{9,1},... | collective-permute-start | bytes 776 | tf_op jit(solution)/shard_map/ppermute | solution.py:42
  90.1 5.4 %collective-permute-start.9 = (f32[64]{0:T(128)S(1)}, f32[64]{0:T(128)S(1)}, u32[]{:S(2)}, u32[]{:S(2)}) collective-permute-start(f32[64]{0:T(128)S(1)} %add.174), channel_id=1, source_target_pairs={{0,16},{1,17},{2,18},{3,19},{4,20},{5,21},{6,22},{7,23},{8,24},{9,... | collective-permute-start | bytes 776 | tf_op jit(solution)/shard_map/ppermute | solution.py:42
  95.5 6.9 %collective-permute-start.10 = (f32[64]{0:T(128)S(1)}, f32[64]{0:T(128)S(1)}, u32[]{:S(2)}, u32[]{:S(2)}) collective-permute-start(f32[64]{0:T(128)S(1)} %add.175), channel_id=1, source_target_pairs={{0,32},{1,33},{2,34},{3,35},{4,36},{5,37},{6,38},{7,39},{8,40},{9,... | collective-permute-start | bytes 776 | tf_op jit(solution)/shard_map/ppermute | solution.py:42
  116.5 5.5 %collective-permute-start.11 = (f32[512]{0:T(512)S(1)}, f32[512]{0:T(512)S(1)}, u32[]{:S(2)}, u32[]{:S(2)}) collective-permute-start(f32[512]{0:T(512)S(1)} %reduce_sum.97), channel_id=1, source_target_pairs={{0,1},{1,0},{2,3},{3,2},{4,5},{5,4},{6,7},{7,6},{8,9},{9,8},{10,11... | collective-permute-start | bytes 6152 | tf_op jit(solution)/shard_map/ppermute | solution.py:42
  122.0 6.4 %collective-permute-start.12 = (f32[512]{0:T(512)S(1)}, f32[512]{0:T(512)S(1)}, u32[]{:S(2)}, u32[]{:S(2)}) collective-permute-start(f32[512]{0:T(512)S(1)} %add.184), channel_id=1, source_target_pairs={{0,2},{1,3},{2,0},{3,1},{4,6},{5,7},{6,4},{7,5},{8,10},{9,11},{10,... | collective-permute-start | bytes 6152 | tf_op jit(solution)/shard_map/ppermute | solution.py:42
  128.4 9.4 %collective-permute-start.13 = (f32[512]{0:T(512)S(1)}, f32[512]{0:T(512)S(1)}, u32[]{:S(2)}, u32[]{:S(2)}) collective-permute-start(f32[512]{0:T(512)S(1)} %add.185), channel_id=1, source_target_pairs={{0,4},{1,5},{2,6},{3,7},{4,0},{5,1},{6,2},{7,3},{8,12},{9,13},{10,... | collective-permute-start | bytes 6152 | tf_op jit(solution)/shard_map/ppermute | solution.py:42
  137.7 9.4 %collective-permute-start.14 = (f32[512]{0:T(512)S(1)}, f32[512]{0:T(512)S(1)}, u32[]{:S(2)}, u32[]{:S(2)}) collective-permute-start(f32[512]{0:T(512)S(1)} %add.186), channel_id=1, source_target_pairs={{0,8},{1,9},{2,10},{3,11},{4,12},{5,13},{6,14},{7,15},{8,0},{9,1},... | collective-permute-start | bytes 6152 | tf_op jit(solution)/shard_map/ppermute | solution.py:42
  147.1 5.5 %collective-permute-start.15 = (f32[512]{0:T(512)S(1)}, f32[512]{0:T(512)S(1)}, u32[]{:S(2)}, u32[]{:S(2)}) collective-permute-start(f32[512]{0:T(512)S(1)} %add.187), channel_id=1, source_target_pairs={{0,16},{1,17},{2,18},{3,19},{4,20},{5,21},{6,22},{7,23},{8,24},{9,... | collective-permute-start | bytes 6152 | tf_op jit(solution)/shard_map/ppermute | solution.py:42
  152.6 7.0 %collective-permute-start.16 = (f32[512]{0:T(512)S(1)}, f32[512]{0:T(512)S(1)}, u32[]{:S(2)}, u32[]{:S(2)}) collective-permute-start(f32[512]{0:T(512)S(1)} %add.188), channel_id=1, source_target_pairs={{0,32},{1,33},{2,34},{3,35},{4,36},{5,37},{6,38},{7,39},{8,40},{9,... | collective-permute-start | bytes 6152 | tf_op jit(solution)/shard_map/ppermute | solution.py:42
  170.9 82.9 %reduce-scatter.3.cloned.1.call-start = ((), (), s32[]{:S(2)}) async-start(), calls=%async_computation.2 | async-start | bytes 1327104 | tf_op jit(solution)/shard_map/reduce_scatter | solution.py:135
  172.5 13.2 %collective-permute-start.17 = (bf16[64,256]{1,0:T(8,128)(2,1)S(1)}, bf16[64,256]{1,0:T(8,128)(2,1)S(1)}, u32[]{:S(2)}, u32[]{:S(2)}) collective-permute-start(bf16[64,256]{1,0:T(8,128)(2,1)S(1)} %bitcast.153), channel_id=1, source_target_pairs={{0,1},{1,2},{2,3},{3,4},{4,5},{5,6},{6,7},{7,8},{8,9},{9,10},{10,1... | collective-permute-start | bytes 98312 | tf_op jit(solution)/shard_map/ppermute | solution.py:17
  174.5 12.8 %collective-permute-start.18 = (bf16[64,256]{1,0:T(8,128)(2,1)S(1)}, bf16[64,256]{1,0:T(8,128)(2,1)S(1)}, u32[]{:S(2)}, u32[]{:S(2)}) collective-permute-start(bf16[64,256]{1,0:T(8,128)(2,1)S(1)} %bitcast.155), channel_id=1, source_target_pairs={{1,0},{2,1},{3,2},{4,3},{5,4},{6,5},{7,6},{8,7},{9,8},{10,9},{11,1... | collective-permute-start | bytes 98312 | tf_op jit(solution)/shard_map/ppermute | solution.py:18
  187.3 6.4 %collective-permute-start.19 = (bf16[18,256]{1,0:T(8,128)(2,1)S(1)}, bf16[18,256]{1,0:T(8,128)(2,1)S(1)}, u32[]{:S(2)}, u32[]{:S(2)}) collective-permute-start(bf16[18,256]{1,0:T(8,128)(2,1)S(1)} %bitcast.152), channel_id=1, source_target_pairs={{0,64},{64,128},{128,192},{192,256},{256,320},{320,384},{384,448},... | collective-permute-start | bytes 27656 | tf_op jit(solution)/shard_map/ppermute | solution.py:17
  188.6 5.1 %collective-permute-start.20 = (bf16[18,256]{1,0:T(8,128)(2,1)S(1)}, bf16[18,256]{1,0:T(8,128)(2,1)S(1)}, u32[]{:S(2)}, u32[]{:S(2)}) collective-permute-start(bf16[18,256]{1,0:T(8,128)(2,1)S(1)} %bitcast.150), channel_id=1, source_target_pairs={{64,0},{128,64},{192,128},{256,192},{320,256},{384,320},{448,384},... | collective-permute-start | bytes 27656 | tf_op jit(solution)/shard_map/ppermute | solution.py:18
  190.0 9.9 %collective-permute-start.21 = (bf16[2,18,256]{2,1,0:T(8,128)(2,1)S(1)}, bf16[2,18,256]{2,1,0:T(8,128)(2,1)S(1)}, u32[]{:S(2)}, u32[]{:S(2)}) collective-permute-start(bf16[2,18,256]{2,1,0:T(8,128)(2,1)S(1)} %pad_maximum_fusion.2), channel_id=1, source_target_pairs={{32,0},{33,1},{34,2},{35,3},{36,4},{37,5},{38,6},{39,7},{40,8},{41... | collective-permute-start | bytes 55304 | tf_op jit(solution)/shard_map/ppermute | solution.py:29
  199.8 91.8 %copy-start.2 = (bf16[64,16,256]{2,1,0:T(8,128)(2,1)S(1)}, bf16[64,16,256]{2,1,0:T(8,128)(2,1)}, u32[]{:S(2)}) copy-start(bf16[64,16,256]{2,1,0:T(8,128)(2,1)} %param.17) | copy-start | bytes 1572868
  211.7 42.1 %collective-permute-start.22 = (f32[32,1152]{1,0:T(8,128)}, f32[32,1152]{1,0:T(8,128)S(1)}, u32[]{:S(2)}, u32[]{:S(2)}) collective-permute-start(f32[32,1152]{1,0:T(8,128)} %reduce-scatter.5.cloned.1.call-done), channel_id=1, source_target_pairs={{0,32},{1,33},{2,34},{3,35},{4,36},{5,37},{6,38},{7,39},{8,40},{9,... | collective-permute-start | bytes 442376 | tf_op jit(solution)/shard_map/ppermute | solution.py:42
  254.9 6.3 %collective-permute-start.23 = (f32[32,576]{1,0:T(8,128)S(1)}, f32[32,576]{1,0:T(8,128)S(1)}, u32[]{:S(2)}, u32[]{:S(2)}) collective-permute-start(f32[32,576]{1,0:T(8,128)S(1)} %constant_dynamic-slice_fusion.4), channel_id=1, source_target_pairs={{0,16},{1,17},{2,18},{3,19},{4,20},{5,21},{6,22},{7,23},{8,24},{9,... | collective-permute-start | bytes 221192 | tf_op jit(solution)/shard_map/ppermute | solution.py:42
  261.4 9.9 %collective-permute-start.24 = (f32[32,288]{1,0:T(8,128)S(1)}, f32[32,288]{1,0:T(8,128)S(1)}, u32[]{:S(2)}, u32[]{:S(2)}) collective-permute-start(f32[32,288]{1,0:T(8,128)S(1)} %constant_dynamic-slice_fusion.3), channel_id=1, source_target_pairs={{0,8},{1,9},{2,10},{3,11},{4,12},{5,13},{6,14},{7,15},{8,0},{9,1},... | collective-permute-start | bytes 110600 | tf_op jit(solution)/shard_map/ppermute | solution.py:42
  271.4 10.1 %collective-permute-start.25 = (f32[32,144]{1,0:T(8,128)S(1)}, f32[32,144]{1,0:T(8,128)S(1)}, u32[]{:S(2)}, u32[]{:S(2)}) collective-permute-start(f32[32,144]{1,0:T(8,128)S(1)} %constant_dynamic-slice_fusion.2), channel_id=1, source_target_pairs={{0,4},{1,5},{2,6},{3,7},{4,0},{5,1},{6,2},{7,3},{8,12},{9,13},{10,... | collective-permute-start | bytes 55304 | tf_op jit(solution)/shard_map/ppermute | solution.py:42
  281.6 6.5 %collective-permute-start.26 = (f32[32,72]{1,0:T(8,128)S(1)}, f32[32,72]{1,0:T(8,128)S(1)}, u32[]{:S(2)}, u32[]{:S(2)}) collective-permute-start(f32[32,72]{1,0:T(8,128)S(1)} %constant_dynamic-slice_fusion.1), channel_id=1, source_target_pairs={{0,2},{1,3},{2,0},{3,1},{4,6},{5,7},{6,4},{7,5},{8,10},{9,11},{10,... | collective-permute-start | bytes 27656 | tf_op jit(solution)/shard_map/ppermute | solution.py:42
  288.3 5.6 %collective-permute-start.27 = (f32[32,36]{1,0:T(8,128)S(1)}, f32[32,36]{1,0:T(8,128)S(1)}, u32[]{:S(2)}, u32[]{:S(2)}) collective-permute-start(f32[32,36]{1,0:T(8,128)S(1)} %constant_dynamic-slice_fusion), channel_id=1, source_target_pairs={{0,1},{1,0},{2,3},{3,2},{4,5},{5,4},{6,7},{7,6},{8,9},{9,8},{10,11... | collective-permute-start | bytes 13832 | tf_op jit(solution)/shard_map/ppermute | solution.py:42
  (9 other events, 12.0 us)
Sparse Core Ops, SparseCore 0:
  171.0 40.5 reduce-scatter.4
  214.5 39.2 reduce-scatter.2

commit v9 on v7

--- a/solution.py
+++ b/solution.py
@@ -125,8 +125,9 @@
         "VALID",
         dimension_numbers=("CHWN", "HWIO", "CHWN"),
         preferred_element_type=jnp.float32,
-    ).reshape(channels, 9 * channels)
+    )
     owned_cols = lax.psum_scatter(term, "lat", scatter_dimension=0, tiled=True)
+    owned_cols = owned_cols.reshape(owned_cols.shape[0], 9 * channels)
     grad_banded, grad_distant = extend(dconv)
     flipped = jnp.swapaxes(kernel[::-1, ::-1], 2, 3)
     back = conv_valid(grad_banded, flipped)

time: 275 us -> 272 us (0.989)
  waiting for transfers between devices: 80.5 us -> 74.2 us
  matrix products: 13 us -> 17.9 us
    ppermute x18, waiting for transfers between devices: 58.5 us -> 52.1 us  [exchange(): return lax.ppermute(block, axis, [(i, i ^ 1 << bit) for i in range(peers)])]
    reshape x1, local copies, waits for them, and re-layouts: 3.08 us -> 0.2 us  [local(): owned_cols = owned_cols.reshape(owned_cols.shape[0], 9 * channels)]
  transfers between devices with their start and end apart: 29 -> 29, of which waited for: 21 -> 21; matrix products, arithmetic and copies ran while one was open for 3% -> 5% of each run, Pallas kernels for 0% -> 0%
where the time goes in v9:
time: 272 us; the launch traced here: 271 us
  starting transfers between devices  115 us (42%)
  waiting for transfers between devices  74.2 us (27%)
  blocking collectives  27.2 us (10%)
  matrix products  17.9 us (7%)
  between operations  15.5 us (6%)
  local copies, waits for them, and re-layouts  12.6 us (5%)
  other arithmetic  7.88 us (3%)
    ppermute x18, starting transfers between devices, exchange(): return lax.ppermute(block, axis, [(i, i ^ 1 << bit) for i in range(peers)])  72 us
    ppermute x18, waiting for transfers between devices, exchange(): return lax.ppermute(block, axis, [(i, i ^ 1 << bit) for i in range(peers)])  52.1 us
    ppermute x4, starting transfers between devices, with_halo(): lax.ppermute(jnp.squeeze(initial, dim), axis, down)  27.9 us
    reduce_scatter x1, waiting for transfers between devices, local(): owned_cols = lax.psum_scatter(term, 'lat', scatter_dimension=0, tiled=True)  16.6 us
    unnamed x1, blocking collectives  14.5 us
    all_gather x1, blocking collectives, butterfly_sum(): value = jnp.sum(lax.all_gather(value, 'lat'), 0)  12.7 us
    ppermute x4, starting transfers between devices, with_halo(): lax.ppermute(jnp.squeeze(last, dim), axis, up)  8.99 us
    conv_general_dilated x1, matrix products, local(): lax.conv_general_dilated(merged[None], dconv.reshape(height, breadth, 1,...  7.16 us
  transfers between devices with their start and end apart: 29, of which 21 were waited for; matrix products, arithmetic and copies ran while one was open for 5% of the time, Pallas kernels for 0%

profile of v9, /device:TPU:6, one launch (start us, length us, event | category | flops | bytes accessed | tf_op | source)
XLA Modules:
  0.0 270.6 jit_solution(2213887290017619807)
XLA Ops:
  8.4 4.3 %collective-permute-start = (bf16[64,256]{1,0:T(8,128)(2,1)S(1)}, bf16[64,256]{1,0:T(8,128)(2,1)S(1)}, u32[]{:S(2)}, u32[]{:S(2)}) collective-permute-start(bf16[64,256]{1,0:T(8,128)(2,1)S(1)} %bitcast.155), channel_id=1, source_target_pairs={{0,1},{1,2},{2,3},{3,4},{4,5},{5,6},{6,7},{7,8},{8,9},{9,10},{10,1... | collective-permute-start | bytes 98312 | tf_op jit(solution)/shard_map/ppermute | solution.py:17
  12.7 14.1 %collective-permute-start.1 = (bf16[64,256]{1,0:T(8,128)(2,1)S(1)}, bf16[64,256]{1,0:T(8,128)(2,1)S(1)}, u32[]{:S(2)}, u32[]{:S(2)}) collective-permute-start(bf16[64,256]{1,0:T(8,128)(2,1)S(1)} %bitcast.157), channel_id=1, source_target_pairs={{1,0},{2,1},{3,2},{4,3},{5,4},{6,5},{7,6},{8,7},{9,8},{10,9},{11,1... | collective-permute-start | bytes 98312 | tf_op jit(solution)/shard_map/ppermute | solution.py:18
  32.4 3.0 %collective-permute-start.4 = (bf16[2,18,256]{2,1,0:T(8,128)(2,1)S(1)}, bf16[2,18,256]{2,1,0:T(8,128)(2,1)S(1)}, u32[]{:S(2)}, u32[]{:S(2)}) collective-permute-start(bf16[2,18,256]{2,1,0:T(8,128)(2,1)S(1)} %pad_maximum_fusion.1), channel_id=1, source_target_pairs={{32,0},{33,1},{34,2},{35,3},{36,4},{37,5},{38,6},{39,7},{40,8},{41... | collective-permute-start | bytes 55304 | tf_op jit(solution)/shard_map/ppermute | solution.py:29
  36.0 3.7 %collective-permute-done.4 = bf16[2,18,256]{2,1,0:T(8,128)(2,1)S(1)} collective-permute-done((bf16[2,18,256]{2,1,0:T(8,128)(2,1)S(1)}, bf16[2,18,256]{2,1,0:T(8,128)(2,1)S(1)}, u32[]{:S(2)}, u32[]{:S(2)}) %collective-permute-start.4) | collective-permute-done | bytes 18464 | tf_op jit(solution)/shard_map/ppermute | solution.py:29
  41.2 3.2 %select_reduce_fusion.1 = (f32[256]{0:T(256)S(1)}, f32[256]{0:T(256)S(1)}, f32[64,8,3,256]{3,1,2,0:T(8,128)}) fusion(pred[8,3]{0,1:T(4,128)(4,1)S(1)} %copy-done.7, bf16[3,3,256,256]{3,2,1,0:T(8,128)(2,1)S(1)} %copy-done.3, bf16[66,1,7,2,256]{4,2,3,0,1:T(8,128)(2,1)S(1)} %slice.207, bf16[66,1,8,3,256]{4,2,3,0,1:T(8,128)(2,1)S(1)} %copy.85), kind=kOutput, calls=%fused_computation.4 | convolution fusion | flops 1818353152 | bytes 4038680 | tf_op jit(solution)/shard_map/conv_general_dilated | solution.py:70
  45.1 14.5 %all-reduce = f32[512]{0:T(512)S(1)} all-reduce(f32[512]{0:T(512)S(1)} %maximum_dynamic-update-slice_fusion), channel_id=2, replica_groups=mesh['lat'=8,'lon'=64] {'lat'}, use_global_device_ids=true, to_apply=%add | all-reduce | flops 512 | bytes 4096
  61.6 3.5 %collective-permute-done.5 = f32[64]{0:T(128)S(1)} collective-permute-done((f32[64]{0:T(128)S(1)}, f32[64]{0:T(128)S(1)}, u32[]{:S(2)}, u32[]{:S(2)}) %collective-permute-start.5) | collective-permute-done | bytes 288 | tf_op jit(solution)/shard_map/ppermute | solution.py:42
  67.0 4.4 %collective-permute-done.6 = f32[64]{0:T(128)S(1)} collective-permute-done((f32[64]{0:T(128)S(1)}, f32[64]{0:T(128)S(1)}, u32[]{:S(2)}, u32[]{:S(2)}) %collective-permute-start.6) | collective-permute-done | bytes 288 | tf_op jit(solution)/shard_map/ppermute | solution.py:42
  71.4 5.9 %collective-permute-start.7 = (f32[64]{0:T(128)S(1)}, f32[64]{0:T(128)S(1)}, u32[]{:S(2)}, u32[]{:S(2)}) collective-permute-start(f32[64]{0:T(128)S(1)} %add.170), channel_id=1, source_target_pairs={{0,4},{1,5},{2,6},{3,7},{4,0},{5,1},{6,2},{7,3},{8,12},{9,13},{10,... | collective-permute-start | bytes 776 | tf_op jit(solution)/shard_map/ppermute | solution.py:42
  77.3 3.5 %collective-permute-done.7 = f32[64]{0:T(128)S(1)} collective-permute-done((f32[64]{0:T(128)S(1)}, f32[64]{0:T(128)S(1)}, u32[]{:S(2)}, u32[]{:S(2)}) %collective-permute-start.7) | collective-permute-done | bytes 288 | tf_op jit(solution)/shard_map/ppermute | solution.py:42
  80.8 5.3 %collective-permute-start.8 = (f32[64]{0:T(128)S(1)}, f32[64]{0:T(128)S(1)}, u32[]{:S(2)}, u32[]{:S(2)}) collective-permute-start(f32[64]{0:T(128)S(1)} %add.171), channel_id=1, source_target_pairs={{0,8},{1,9},{2,10},{3,11},{4,12},{5,13},{6,14},{7,15},{8,0},{9,1},... | collective-permute-start | bytes 776 | tf_op jit(solution)/shard_map/ppermute | solution.py:42
  86.1 4.0 %collective-permute-done.8 = f32[64]{0:T(128)S(1)} collective-permute-done((f32[64]{0:T(128)S(1)}, f32[64]{0:T(128)S(1)}, u32[]{:S(2)}, u32[]{:S(2)}) %collective-permute-start.8) | collective-permute-done | bytes 288 | tf_op jit(solution)/shard_map/ppermute | solution.py:42
  95.5 3.8 %collective-permute-start.10 = (f32[64]{0:T(128)S(1)}, f32[64]{0:T(128)S(1)}, u32[]{:S(2)}, u32[]{:S(2)}) collective-permute-start(f32[64]{0:T(128)S(1)} %add.173), channel_id=1, source_target_pairs={{0,32},{1,33},{2,34},{3,35},{4,36},{5,37},{6,38},{7,39},{8,40},{9,... | collective-permute-start | bytes 776 | tf_op jit(solution)/shard_map/ppermute | solution.py:42
  103.8 12.7 %all-gather.2 = f32[8,1,512]{2,1,0:T(1,128)S(1)} all-gather(f32[1,1,512]{2,1,0:T(1,128)S(1)} %bitcast.162), channel_id=3, replica_groups=mesh['lat'=8,'lon'=64] {'lat'}, dimensions={0}, use_global_device_ids=true | all-gather | bytes 18432 | tf_op jit(solution)/shard_map/all_gather | solution.py:53
  118.5 3.5 %collective-permute-done.11 = f32[512]{0:T(512)S(1)} collective-permute-done((f32[512]{0:T(512)S(1)}, f32[512]{0:T(512)S(1)}, u32[]{:S(2)}, u32[]{:S(2)}) %collective-permute-start.11) | collective-permute-done | bytes 2080 | tf_op jit(solution)/shard_map/ppermute | solution.py:42
  124.8 3.5 %collective-permute-done.12 = f32[512]{0:T(512)S(1)} collective-permute-done((f32[512]{0:T(512)S(1)}, f32[512]{0:T(512)S(1)}, u32[]{:S(2)}, u32[]{:S(2)}) %collective-permute-start.12) | collective-permute-done | bytes 2080 | tf_op jit(solution)/shard_map/ppermute | solution.py:42
  128.4 5.9 %collective-permute-start.13 = (f32[512]{0:T(512)S(1)}, f32[512]{0:T(512)S(1)}, u32[]{:S(2)}, u32[]{:S(2)}) collective-permute-start(f32[512]{0:T(512)S(1)} %add.183), channel_id=1, source_target_pairs={{0,4},{1,5},{2,6},{3,7},{4,0},{5,1},{6,2},{7,3},{8,12},{9,13},{10,... | collective-permute-start | bytes 6152 | tf_op jit(solution)/shard_map/ppermute | solution.py:42
  134.2 3.5 %collective-permute-done.13 = f32[512]{0:T(512)S(1)} collective-permute-done((f32[512]{0:T(512)S(1)}, f32[512]{0:T(512)S(1)}, u32[]{:S(2)}, u32[]{:S(2)}) %collective-permute-start.13) | collective-permute-done | bytes 2080 | tf_op jit(solution)/shard_map/ppermute | solution.py:42
  137.7 5.3 %collective-permute-start.14 = (f32[512]{0:T(512)S(1)}, f32[512]{0:T(512)S(1)}, u32[]{:S(2)}, u32[]{:S(2)}) collective-permute-start(f32[512]{0:T(512)S(1)} %add.184), channel_id=1, source_target_pairs={{0,8},{1,9},{2,10},{3,11},{4,12},{5,13},{6,14},{7,15},{8,0},{9,1},... | collective-permute-start | bytes 6152 | tf_op jit(solution)/shard_map/ppermute | solution.py:42
  143.1 4.1 %collective-permute-done.14 = f32[512]{0:T(512)S(1)} collective-permute-done((f32[512]{0:T(512)S(1)}, f32[512]{0:T(512)S(1)}, u32[]{:S(2)}, u32[]{:S(2)}) %collective-permute-start.14) | collective-permute-done | bytes 2080 | tf_op jit(solution)/shard_map/ppermute | solution.py:42
  152.6 3.9 %collective-permute-start.16 = (f32[512]{0:T(512)S(1)}, f32[512]{0:T(512)S(1)}, u32[]{:S(2)}, u32[]{:S(2)}) collective-permute-start(f32[512]{0:T(512)S(1)} %add.186), channel_id=1, source_target_pairs={{0,32},{1,33},{2,34},{3,35},{4,36},{5,37},{6,38},{7,39},{8,40},{9,... | collective-permute-start | bytes 6152 | tf_op jit(solution)/shard_map/ppermute | solution.py:42
  156.5 3.0 %collective-permute-done.16 = f32[512]{0:T(512)S(1)} collective-permute-done((f32[512]{0:T(512)S(1)}, f32[512]{0:T(512)S(1)}, u32[]{:S(2)}, u32[]{:S(2)}) %collective-permute-start.16) | collective-permute-done | bytes 2080 | tf_op jit(solution)/shard_map/ppermute | solution.py:42
  162.7 7.2 %fusion.14 = f32[256,3,3,256]{3,0,2,1:T(8,128)} fusion(bf16[1,66,18,256]{3,2,1,0:T(8,128)(2,1)S(1)} %fusion.49, bf16[64,16,1,256]{3,1,0,2:T(8,128)(2,1)S(1)} %bitcast.137), kind=kOutput, calls=%fused_computation.19 | convolution fusion | flops 1207959552 | bytes 3491840 | tf_op jit(solution)/shard_map/conv_general_dilated | solution.py:121
  172.0 11.2 %collective-permute-start.18 = (bf16[64,256]{1,0:T(8,128)(2,1)S(1)}, bf16[64,256]{1,0:T(8,128)(2,1)S(1)}, u32[]{:S(2)}, u32[]{:S(2)}) collective-permute-start(bf16[64,256]{1,0:T(8,128)(2,1)S(1)} %bitcast.153), channel_id=1, source_target_pairs={{1,0},{2,1},{3,2},{4,3},{5,4},{6,5},{7,6},{8,7},{9,8},{10,9},{11,1... | collective-permute-start | bytes 98312 | tf_op jit(solution)/shard_map/ppermute | solution.py:18
  187.9 3.4 %collective-permute-start.21 = (bf16[2,18,256]{2,1,0:T(8,128)(2,1)S(1)}, bf16[2,18,256]{2,1,0:T(8,128)(2,1)S(1)}, u32[]{:S(2)}, u32[]{:S(2)}) collective-permute-start(bf16[2,18,256]{2,1,0:T(8,128)(2,1)S(1)} %pad_maximum_fusion.2), channel_id=1, source_target_pairs={{32,0},{33,1},{34,2},{35,3},{36,4},{37,5},{38,6},{39,7},{40,8},{41... | collective-permute-start | bytes 55304 | tf_op jit(solution)/shard_map/ppermute | solution.py:29
  197.5 16.6 %reduce-scatter.2.cloned.1.call-done = f32[32,3,3,256]{3,0,2,1:T(8,128)} async-done(((f32[256,3,3,256]{3,0,2,1:T(8,128)}), f32[32,3,3,256]{3,0,2,1:T(8,128)}) %reduce-scatter.2.cloned.1.call-update) | async-done | bytes 294928 | tf_op jit(solution)/shard_map/reduce_scatter | solution.py:129
  215.6 3.5 %collective-permute-start.22 = (f32[32,1152]{1,0:T(8,128)S(1)}, f32[32,1152]{1,0:T(8,128)S(1)}, u32[]{:S(2)}, u32[]{:S(2)}) collective-permute-start(f32[32,1152]{1,0:T(8,128)S(1)} %constant_dynamic-slice_fusion.5), channel_id=1, source_target_pairs={{0,32},{1,33},{2,34},{3,35},{4,36},{5,37},{6,38},{7,39},{8,40},{9,... | collective-permute-start | bytes 442376 | tf_op jit(solution)/shard_map/ppermute | solution.py:42
  220.2 4.0 %collective-permute-done.22 = f32[32,1152]{1,0:T(8,128)S(1)} collective-permute-done((f32[32,1152]{1,0:T(8,128)S(1)}, f32[32,1152]{1,0:T(8,128)S(1)}, u32[]{:S(2)}, u32[]{:S(2)}) %collective-permute-start.22) | collective-permute-done | bytes 147488 | tf_op jit(solution)/shard_map/ppermute | solution.py:42
  230.8 5.9 %collective-permute-start.24 = (f32[32,288]{1,0:T(8,128)S(1)}, f32[32,288]{1,0:T(8,128)S(1)}, u32[]{:S(2)}, u32[]{:S(2)}) collective-permute-start(f32[32,288]{1,0:T(8,128)S(1)} %constant_dynamic-slice_fusion.3), channel_id=1, source_target_pairs={{0,8},{1,9},{2,10},{3,11},{4,12},{5,13},{6,14},{7,15},{8,0},{9,1},... | collective-permute-start | bytes 110600 | tf_op jit(solution)/shard_map/ppermute | solution.py:42
  240.8 7.9 %collective-permute-start.25 = (f32[32,144]{1,0:T(8,128)S(1)}, f32[32,144]{1,0:T(8,128)S(1)}, u32[]{:S(2)}, u32[]{:S(2)}) collective-permute-start(f32[32,144]{1,0:T(8,128)S(1)} %constant_dynamic-slice_fusion.2), channel_id=1, source_target_pairs={{0,4},{1,5},{2,6},{3,7},{4,0},{5,1},{6,2},{7,3},{8,12},{9,13},{10,... | collective-permute-start | bytes 55304 | tf_op jit(solution)/shard_map/ppermute | solution.py:42
  250.8 4.6 %collective-permute-start.26 = (f32[32,72]{1,0:T(8,128)S(1)}, f32[32,72]{1,0:T(8,128)S(1)}, u32[]{:S(2)}, u32[]{:S(2)}) collective-permute-start(f32[32,72]{1,0:T(8,128)S(1)} %constant_dynamic-slice_fusion.1), channel_id=1, source_target_pairs={{0,2},{1,3},{2,0},{3,1},{4,6},{5,7},{6,4},{7,5},{8,10},{9,11},{10,... | collective-permute-start | bytes 27656 | tf_op jit(solution)/shard_map/ppermute | solution.py:42
  257.4 3.4 %collective-permute-start.27 = (f32[32,36]{1,0:T(8,128)S(1)}, f32[32,36]{1,0:T(8,128)S(1)}, u32[]{:S(2)}, u32[]{:S(2)}) collective-permute-start(f32[32,36]{1,0:T(8,128)S(1)} %constant_dynamic-slice_fusion), channel_id=1, source_target_pairs={{0,1},{1,0},{2,3},{3,2},{4,5},{5,4},{6,7},{7,6},{8,9},{9,8},{10,11... | collective-permute-start | bytes 13832 | tf_op jit(solution)/shard_map/ppermute | solution.py:42
  (146 shorter events, 68.9 us)
Async XLA Ops:
  7.2 28.3 %copy-start = (bf16[64,16,256]{2,1,0:T(8,128)(2,1)S(1)}, bf16[64,16,256]{2,1,0:T(8,128)(2,1)}, u32[]{:S(2)}) copy-start(bf16[64,16,256]{2,1,0:T(8,128)(2,1)} %param.13) | copy-start | bytes 1572868
  7.2 207.0 %reduce-scatter.2.cloned.1.call-start = ((), (), s32[]{:S(2)}) async-start(), calls=%async_computation.1 | async-start | bytes 2654208 | tf_op jit(solution)/shard_map/reduce_scatter | solution.py:129
  8.4 20.4 %collective-permute-start = (bf16[64,256]{1,0:T(8,128)(2,1)S(1)}, bf16[64,256]{1,0:T(8,128)(2,1)S(1)}, u32[]{:S(2)}, u32[]{:S(2)}) collective-permute-start(bf16[64,256]{1,0:T(8,128)(2,1)S(1)} %bitcast.155), channel_id=1, source_target_pairs={{0,1},{1,2},{2,3},{3,4},{4,5},{5,6},{6,7},{7,8},{8,9},{9,10},{10,1... | collective-permute-start | bytes 98312 | tf_op jit(solution)/shard_map/ppermute | solution.py:17
  12.7 16.1 %collective-permute-start.1 = (bf16[64,256]{1,0:T(8,128)(2,1)S(1)}, bf16[64,256]{1,0:T(8,128)(2,1)S(1)}, u32[]{:S(2)}, u32[]{:S(2)}) collective-permute-start(bf16[64,256]{1,0:T(8,128)(2,1)S(1)} %bitcast.157), channel_id=1, source_target_pairs={{1,0},{2,1},{3,2},{4,3},{5,4},{6,5},{7,6},{8,7},{9,8},{10,9},{11,1... | collective-permute-start | bytes 98312 | tf_op jit(solution)/shard_map/ppermute | solution.py:18
  29.7 5.8 %collective-permute-start.2 = (bf16[18,256]{1,0:T(8,128)(2,1)S(1)}, bf16[18,256]{1,0:T(8,128)(2,1)S(1)}, u32[]{:S(2)}, u32[]{:S(2)}) collective-permute-start(bf16[18,256]{1,0:T(8,128)(2,1)S(1)} %bitcast.149), channel_id=1, source_target_pairs={{0,64},{64,128},{128,192},{192,256},{256,320},{320,384},{384,448},... | collective-permute-start | bytes 27656 | tf_op jit(solution)/shard_map/ppermute | solution.py:17
  31.1 4.4 %collective-permute-start.3 = (bf16[18,256]{1,0:T(8,128)(2,1)S(1)}, bf16[18,256]{1,0:T(8,128)(2,1)S(1)}, u32[]{:S(2)}, u32[]{:S(2)}) collective-permute-start(bf16[18,256]{1,0:T(8,128)(2,1)S(1)} %bitcast.147), channel_id=1, source_target_pairs={{64,0},{128,64},{192,128},{256,192},{320,256},{384,320},{448,384},... | collective-permute-start | bytes 27656 | tf_op jit(solution)/shard_map/ppermute | solution.py:18
  32.4 7.2 %collective-permute-start.4 = (bf16[2,18,256]{2,1,0:T(8,128)(2,1)S(1)}, bf16[2,18,256]{2,1,0:T(8,128)(2,1)S(1)}, u32[]{:S(2)}, u32[]{:S(2)}) collective-permute-start(bf16[2,18,256]{2,1,0:T(8,128)(2,1)S(1)} %pad_maximum_fusion.1), channel_id=1, source_target_pairs={{32,0},{33,1},{34,2},{35,3},{36,4},{37,5},{38,6},{39,7},{40,8},{41... | collective-permute-start | bytes 55304 | tf_op jit(solution)/shard_map/ppermute | solution.py:29
  59.7 5.4 %collective-permute-start.5 = (f32[64]{0:T(128)S(1)}, f32[64]{0:T(128)S(1)}, u32[]{:S(2)}, u32[]{:S(2)}) collective-permute-start(f32[64]{0:T(128)S(1)} %reduce_sum.94), channel_id=1, source_target_pairs={{0,1},{1,0},{2,3},{3,2},{4,5},{5,4},{6,7},{7,6},{8,9},{9,8},{10,11... | collective-permute-start | bytes 776 | tf_op jit(solution)/shard_map/ppermute | solution.py:42
  65.1 6.3 %collective-permute-start.6 = (f32[64]{0:T(128)S(1)}, f32[64]{0:T(128)S(1)}, u32[]{:S(2)}, u32[]{:S(2)}) collective-permute-start(f32[64]{0:T(128)S(1)} %add.169), channel_id=1, source_target_pairs={{0,2},{1,3},{2,0},{3,1},{4,6},{5,7},{6,4},{7,5},{8,10},{9,11},{10,... | collective-permute-start | bytes 776 | tf_op jit(solution)/shard_map/ppermute | solution.py:42
  71.4 9.3 %collective-permute-start.7 = (f32[64]{0:T(128)S(1)}, f32[64]{0:T(128)S(1)}, u32[]{:S(2)}, u32[]{:S(2)}) collective-permute-start(f32[64]{0:T(128)S(1)} %add.170), channel_id=1, source_target_pairs={{0,4},{1,5},{2,6},{3,7},{4,0},{5,1},{6,2},{7,3},{8,12},{9,13},{10,... | collective-permute-start | bytes 776 | tf_op jit(solution)/shard_map/ppermute | solution.py:42
  80.8 9.3 %collective-permute-start.8 = (f32[64]{0:T(128)S(1)}, f32[64]{0:T(128)S(1)}, u32[]{:S(2)}, u32[]{:S(2)}) collective-permute-start(f32[64]{0:T(128)S(1)} %add.171), channel_id=1, source_target_pairs={{0,8},{1,9},{2,10},{3,11},{4,12},{5,13},{6,14},{7,15},{8,0},{9,1},... | collective-permute-start | bytes 776 | tf_op jit(solution)/shard_map/ppermute | solution.py:42
  90.1 5.4 %collective-permute-start.9 = (f32[64]{0:T(128)S(1)}, f32[64]{0:T(128)S(1)}, u32[]{:S(2)}, u32[]{:S(2)}) collective-permute-start(f32[64]{0:T(128)S(1)} %add.172), channel_id=1, source_target_pairs={{0,16},{1,17},{2,18},{3,19},{4,20},{5,21},{6,22},{7,23},{8,24},{9,... | collective-permute-start | bytes 776 | tf_op jit(solution)/shard_map/ppermute | solution.py:42
  95.5 6.9 %collective-permute-start.10 = (f32[64]{0:T(128)S(1)}, f32[64]{0:T(128)S(1)}, u32[]{:S(2)}, u32[]{:S(2)}) collective-permute-start(f32[64]{0:T(128)S(1)} %add.173), channel_id=1, source_target_pairs={{0,32},{1,33},{2,34},{3,35},{4,36},{5,37},{6,38},{7,39},{8,40},{9,... | collective-permute-start | bytes 776 | tf_op jit(solution)/shard_map/ppermute | solution.py:42
  101.2 1.7 copy-start.1
  101.2 1.7 copy-start.5
  116.5 5.5 %collective-permute-start.11 = (f32[512]{0:T(512)S(1)}, f32[512]{0:T(512)S(1)}, u32[]{:S(2)}, u32[]{:S(2)}) collective-permute-start(f32[512]{0:T(512)S(1)} %reduce_sum.97), channel_id=1, source_target_pairs={{0,1},{1,0},{2,3},{3,2},{4,5},{5,4},{6,7},{7,6},{8,9},{9,8},{10,11... | collective-permute-start | bytes 6152 | tf_op jit(solution)/shard_map/ppermute | solution.py:42
  122.0 6.4 %collective-permute-start.12 = (f32[512]{0:T(512)S(1)}, f32[512]{0:T(512)S(1)}, u32[]{:S(2)}, u32[]{:S(2)}) collective-permute-start(f32[512]{0:T(512)S(1)} %add.182), channel_id=1, source_target_pairs={{0,2},{1,3},{2,0},{3,1},{4,6},{5,7},{6,4},{7,5},{8,10},{9,11},{10,... | collective-permute-start | bytes 6152 | tf_op jit(solution)/shard_map/ppermute | solution.py:42
  128.4 9.4 %collective-permute-start.13 = (f32[512]{0:T(512)S(1)}, f32[512]{0:T(512)S(1)}, u32[]{:S(2)}, u32[]{:S(2)}) collective-permute-start(f32[512]{0:T(512)S(1)} %add.183), channel_id=1, source_target_pairs={{0,4},{1,5},{2,6},{3,7},{4,0},{5,1},{6,2},{7,3},{8,12},{9,13},{10,... | collective-permute-start | bytes 6152 | tf_op jit(solution)/shard_map/ppermute | solution.py:42
  137.7 9.4 %collective-permute-start.14 = (f32[512]{0:T(512)S(1)}, f32[512]{0:T(512)S(1)}, u32[]{:S(2)}, u32[]{:S(2)}) collective-permute-start(f32[512]{0:T(512)S(1)} %add.184), channel_id=1, source_target_pairs={{0,8},{1,9},{2,10},{3,11},{4,12},{5,13},{6,14},{7,15},{8,0},{9,1},... | collective-permute-start | bytes 6152 | tf_op jit(solution)/shard_map/ppermute | solution.py:42
  147.1 5.5 %collective-permute-start.15 = (f32[512]{0:T(512)S(1)}, f32[512]{0:T(512)S(1)}, u32[]{:S(2)}, u32[]{:S(2)}) collective-permute-start(f32[512]{0:T(512)S(1)} %add.185), channel_id=1, source_target_pairs={{0,16},{1,17},{2,18},{3,19},{4,20},{5,21},{6,22},{7,23},{8,24},{9,... | collective-permute-start | bytes 6152 | tf_op jit(solution)/shard_map/ppermute | solution.py:42
  152.6 7.0 %collective-permute-start.16 = (f32[512]{0:T(512)S(1)}, f32[512]{0:T(512)S(1)}, u32[]{:S(2)}, u32[]{:S(2)}) collective-permute-start(f32[512]{0:T(512)S(1)} %add.186), channel_id=1, source_target_pairs={{0,32},{1,33},{2,34},{3,35},{4,36},{5,37},{6,38},{7,39},{8,40},{9,... | collective-permute-start | bytes 6152 | tf_op jit(solution)/shard_map/ppermute | solution.py:42
  170.1 13.2 %collective-permute-start.17 = (bf16[64,256]{1,0:T(8,128)(2,1)S(1)}, bf16[64,256]{1,0:T(8,128)(2,1)S(1)}, u32[]{:S(2)}, u32[]{:S(2)}) collective-permute-start(bf16[64,256]{1,0:T(8,128)(2,1)S(1)} %bitcast.151), channel_id=1, source_target_pairs={{0,1},{1,2},{2,3},{3,4},{4,5},{5,6},{6,7},{7,8},{8,9},{9,10},{10,1... | collective-permute-start | bytes 98312 | tf_op jit(solution)/shard_map/ppermute | solution.py:17
  172.0 13.2 %collective-permute-start.18 = (bf16[64,256]{1,0:T(8,128)(2,1)S(1)}, bf16[64,256]{1,0:T(8,128)(2,1)S(1)}, u32[]{:S(2)}, u32[]{:S(2)}) collective-permute-start(bf16[64,256]{1,0:T(8,128)(2,1)S(1)} %bitcast.153), channel_id=1, source_target_pairs={{1,0},{2,1},{3,2},{4,3},{5,4},{6,5},{7,6},{8,7},{9,8},{10,9},{11,1... | collective-permute-start | bytes 98312 | tf_op jit(solution)/shard_map/ppermute | solution.py:18
  185.3 6.0 %collective-permute-start.19 = (bf16[18,256]{1,0:T(8,128)(2,1)S(1)}, bf16[18,256]{1,0:T(8,128)(2,1)S(1)}, u32[]{:S(2)}, u32[]{:S(2)}) collective-permute-start(bf16[18,256]{1,0:T(8,128)(2,1)S(1)} %bitcast.150), channel_id=1, source_target_pairs={{0,64},{64,128},{128,192},{192,256},{256,320},{320,384},{384,448},... | collective-permute-start | bytes 27656 | tf_op jit(solution)/shard_map/ppermute | solution.py:17
  186.6 4.7 %collective-permute-start.20 = (bf16[18,256]{1,0:T(8,128)(2,1)S(1)}, bf16[18,256]{1,0:T(8,128)(2,1)S(1)}, u32[]{:S(2)}, u32[]{:S(2)}) collective-permute-start(bf16[18,256]{1,0:T(8,128)(2,1)S(1)} %bitcast.148), channel_id=1, source_target_pairs={{64,0},{128,64},{192,128},{256,192},{320,256},{384,320},{448,384},... | collective-permute-start | bytes 27656 | tf_op jit(solution)/shard_map/ppermute | solution.py:18
  187.9 9.5 %collective-permute-start.21 = (bf16[2,18,256]{2,1,0:T(8,128)(2,1)S(1)}, bf16[2,18,256]{2,1,0:T(8,128)(2,1)S(1)}, u32[]{:S(2)}, u32[]{:S(2)}) collective-permute-start(bf16[2,18,256]{2,1,0:T(8,128)(2,1)S(1)} %pad_maximum_fusion.2), channel_id=1, source_target_pairs={{32,0},{33,1},{34,2},{35,3},{36,4},{37,5},{38,6},{39,7},{40,8},{41... | collective-permute-start | bytes 55304 | tf_op jit(solution)/shard_map/ppermute | solution.py:29
  215.6 8.5 %collective-permute-start.22 = (f32[32,1152]{1,0:T(8,128)S(1)}, f32[32,1152]{1,0:T(8,128)S(1)}, u32[]{:S(2)}, u32[]{:S(2)}) collective-permute-start(f32[32,1152]{1,0:T(8,128)S(1)} %constant_dynamic-slice_fusion.5), channel_id=1, source_target_pairs={{0,32},{1,33},{2,34},{3,35},{4,36},{5,37},{6,38},{7,39},{8,40},{9,... | collective-permute-start | bytes 442376 | tf_op jit(solution)/shard_map/ppermute | solution.py:42
  224.2 6.3 %collective-permute-start.23 = (f32[32,576]{1,0:T(8,128)S(1)}, f32[32,576]{1,0:T(8,128)S(1)}, u32[]{:S(2)}, u32[]{:S(2)}) collective-permute-start(f32[32,576]{1,0:T(8,128)S(1)} %constant_dynamic-slice_fusion.4), channel_id=1, source_target_pairs={{0,16},{1,17},{2,18},{3,19},{4,20},{5,21},{6,22},{7,23},{8,24},{9,... | collective-permute-start | bytes 221192 | tf_op jit(solution)/shard_map/ppermute | solution.py:42
  230.8 9.9 %collective-permute-start.24 = (f32[32,288]{1,0:T(8,128)S(1)}, f32[32,288]{1,0:T(8,128)S(1)}, u32[]{:S(2)}, u32[]{:S(2)}) collective-permute-start(f32[32,288]{1,0:T(8,128)S(1)} %constant_dynamic-slice_fusion.3), channel_id=1, source_target_pairs={{0,8},{1,9},{2,10},{3,11},{4,12},{5,13},{6,14},{7,15},{8,0},{9,1},... | collective-permute-start | bytes 110600 | tf_op jit(solution)/shard_map/ppermute | solution.py:42
  240.8 9.8 %collective-permute-start.25 = (f32[32,144]{1,0:T(8,128)S(1)}, f32[32,144]{1,0:T(8,128)S(1)}, u32[]{:S(2)}, u32[]{:S(2)}) collective-permute-start(f32[32,144]{1,0:T(8,128)S(1)} %constant_dynamic-slice_fusion.2), channel_id=1, source_target_pairs={{0,4},{1,5},{2,6},{3,7},{4,0},{5,1},{6,2},{7,3},{8,12},{9,13},{10,... | collective-permute-start | bytes 55304 | tf_op jit(solution)/shard_map/ppermute | solution.py:42
  250.8 6.5 %collective-permute-start.26 = (f32[32,72]{1,0:T(8,128)S(1)}, f32[32,72]{1,0:T(8,128)S(1)}, u32[]{:S(2)}, u32[]{:S(2)}) collective-permute-start(f32[32,72]{1,0:T(8,128)S(1)} %constant_dynamic-slice_fusion.1), channel_id=1, source_target_pairs={{0,2},{1,3},{2,0},{3,1},{4,6},{5,7},{6,4},{7,5},{8,10},{9,11},{10,... | collective-permute-start | bytes 27656 | tf_op jit(solution)/shard_map/ppermute | solution.py:42
  257.4 5.6 %collective-permute-start.27 = (f32[32,36]{1,0:T(8,128)S(1)}, f32[32,36]{1,0:T(8,128)S(1)}, u32[]{:S(2)}, u32[]{:S(2)}) collective-permute-start(f32[32,36]{1,0:T(8,128)S(1)} %constant_dynamic-slice_fusion), channel_id=1, source_target_pairs={{0,1},{1,0},{2,3},{3,2},{4,5},{5,4},{6,7},{7,6},{8,9},{9,8},{10,11... | collective-permute-start | bytes 13832 | tf_op jit(solution)/shard_map/ppermute | solution.py:42
  (6 other events, 7.4 us)
Sparse Core Ops, SparseCore 0:
  170.1 44.0 reduce-scatter.1

commit v10 on v7

--- a/solution.py
+++ b/solution.py
@@ -118,15 +118,19 @@
         * rstd_ch
     ).astype(jnp.bfloat16)
     dconv = dconv.reshape(height, breadth, channels)
-    term = lax.conv_general_dilated(
-        merged[None],
-        dconv.reshape(height, breadth, 1, channels),
-        (1, 1),
-        "VALID",
-        dimension_numbers=("CHWN", "HWIO", "CHWN"),
-        preferred_element_type=jnp.float32,
-    ).reshape(channels, 9 * channels)
-    owned_cols = lax.psum_scatter(term, "lat", scatter_dimension=0, tiled=True)
+    grad_rows = dconv.reshape(-1, channels)
+    taps = []
+    for tap_row in range(3):
+        for tap_col in range(3):
+            shifted = merged[:, tap_col : tap_col + breadth].reshape(-1, channels)
+            window = lax.slice_in_dim(shifted, tap_row * breadth, tap_row * breadth + height * breadth)
+            taps.append(
+                lax.dot_general(
+                    grad_rows, window, (((0,), (0,)), ((), ())), preferred_element_type=jnp.float32
+                )
+            )
+    owned_taps = lax.psum_scatter(jnp.stack(taps), "lat", scatter_dimension=1, tiled=True)
+    owned_cols = owned_taps.transpose(1, 0, 2).reshape(owned_taps.shape[1], 9 * channels)
     grad_banded, grad_distant = extend(dconv)
     flipped = jnp.swapaxes(kernel[::-1, ::-1], 2, 3)
     back = conv_valid(grad_banded, flipped)

time: 275 us -> 274 us (level)
    dot_general x0 -> x9, matrix products: none -> 9.47 us  [local(): lax.dot_general(grad_rows, window, (((0,), (0,)), ((), ())), preferred_el...]
    conv_general_dilated x1 -> x0, matrix products: 7.87 us -> none  [local(): lax.conv_general_dilated(merged[None], dconv.reshape(height, breadth, 1,...]
  transfers between devices with their start and end apart: 29 -> 29, of which waited for: 21 -> 21; matrix products, arithmetic and copies ran while one was open for 3% -> 4% of each run, Pallas kernels for 0% -> 0%
where the time goes in v10:
time: 274 us; the launch traced here: 272 us
  starting transfers between devices  115 us (42%)
  waiting for transfers between devices  79.2 us (29%)
  blocking collectives  27.2 us (10%)
  matrix products  15.7 us (6%)
  between operations  15.4 us (6%)
  local copies, waits for them, and re-layouts  11.4 us (4%)
  other arithmetic  7.9 us (3%)
    ppermute x18, starting transfers between devices, exchange(): return lax.ppermute(block, axis, [(i, i ^ 1 << bit) for i in range(peers)])  72.2 us
    ppermute x18, waiting for transfers between devices, exchange(): return lax.ppermute(block, axis, [(i, i ^ 1 << bit) for i in range(peers)])  56.4 us
    ppermute x4, starting transfers between devices, with_halo(): lax.ppermute(jnp.squeeze(initial, dim), axis, down)  27.9 us
    reduce_scatter x1, waiting for transfers between devices, local(): lax.psum_scatter(jnp.stack(taps), 'lat', scatter_dimension=1, tiled=True)  17.3 us
    unnamed x1, blocking collectives  14.5 us
    all_gather x1, blocking collectives, butterfly_sum(): value = jnp.sum(lax.all_gather(value, 'lat'), 0)  12.7 us
    dot_general x9, matrix products, local(): lax.dot_general(grad_rows, window, (((0,), (0,)), ((), ())), preferred_el...  9.47 us
    ppermute x4, starting transfers between devices, with_halo(): lax.ppermute(jnp.squeeze(last, dim), axis, up)  9 us
  transfers between devices with their start and end apart: 29, of which 21 were waited for; matrix products, arithmetic and copies ran while one was open for 4% of the time, Pallas kernels for 0%

profile of v10, /device:TPU:6, one launch (start us, length us, event | category | flops | bytes accessed | tf_op | source)
XLA Modules:
  0.0 272.5 jit_solution(17102510581659738325)
XLA Ops:
  8.4 4.3 %collective-permute-start = (bf16[64,256]{1,0:T(8,128)(2,1)S(1)}, bf16[64,256]{1,0:T(8,128)(2,1)S(1)}, u32[]{:S(2)}, u32[]{:S(2)}) collective-permute-start(bf16[64,256]{1,0:T(8,128)(2,1)S(1)} %bitcast.207), channel_id=1, source_target_pairs={{0,1},{1,2},{2,3},{3,4},{4,5},{5,6},{6,7},{7,8},{8,9},{9,10},{10,1... | collective-permute-start | bytes 98312 | tf_op jit(solution)/shard_map/ppermute | solution.py:17
  12.7 14.1 %collective-permute-start.1 = (bf16[64,256]{1,0:T(8,128)(2,1)S(1)}, bf16[64,256]{1,0:T(8,128)(2,1)S(1)}, u32[]{:S(2)}, u32[]{:S(2)}) collective-permute-start(bf16[64,256]{1,0:T(8,128)(2,1)S(1)} %bitcast.209), channel_id=1, source_target_pairs={{1,0},{2,1},{3,2},{4,3},{5,4},{6,5},{7,6},{8,7},{9,8},{10,9},{11,1... | collective-permute-start | bytes 98312 | tf_op jit(solution)/shard_map/ppermute | solution.py:18
  36.0 3.7 %collective-permute-done.4 = bf16[2,18,256]{2,1,0:T(8,128)(2,1)S(1)} collective-permute-done((bf16[2,18,256]{2,1,0:T(8,128)(2,1)S(1)}, bf16[2,18,256]{2,1,0:T(8,128)(2,1)S(1)}, u32[]{:S(2)}, u32[]{:S(2)}) %collective-permute-start.4) | collective-permute-done | bytes 18464 | tf_op jit(solution)/shard_map/ppermute | solution.py:29
  41.2 3.2 %select_reduce_fusion.1 = (f32[256]{0:T(256)S(1)}, f32[256]{0:T(256)S(1)}, f32[64,8,3,256]{3,1,2,0:T(8,128)}) fusion(pred[8,3]{0,1:T(4,128)(4,1)S(1)} %copy-done.6, bf16[3,3,256,256]{3,2,1,0:T(8,128)(2,1)S(1)} %copy-done.2, bf16[66,1,7,2,256]{4,2,3,0,1:T(8,128)(2,1)S(1)} %slice.270, bf16[66,1,8,3,256]{4,2,3,0,1:T(8,128)(2,1)S(1)} %copy.100), kind=kOutput, calls=%fused_computation.4 | convolution fusion | flops 1818353152 | bytes 4038680 | tf_op jit(solution)/shard_map/conv_general_dilated | solution.py:70
  45.0 14.5 %all-reduce = f32[512]{0:T(512)S(1)} all-reduce(f32[512]{0:T(512)S(1)} %maximum_dynamic-update-slice_fusion), channel_id=2, replica_groups=mesh['lat'=8,'lon'=64] {'lat'}, use_global_device_ids=true, to_apply=%add | all-reduce | flops 512 | bytes 4096
  61.5 3.5 %collective-permute-done.5 = f32[64]{0:T(128)S(1)} collective-permute-done((f32[64]{0:T(128)S(1)}, f32[64]{0:T(128)S(1)}, u32[]{:S(2)}, u32[]{:S(2)}) %collective-permute-start.5) | collective-permute-done | bytes 288 | tf_op jit(solution)/shard_map/ppermute | solution.py:42
  66.9 4.4 %collective-permute-done.6 = f32[64]{0:T(128)S(1)} collective-permute-done((f32[64]{0:T(128)S(1)}, f32[64]{0:T(128)S(1)}, u32[]{:S(2)}, u32[]{:S(2)}) %collective-permute-start.6) | collective-permute-done | bytes 288 | tf_op jit(solution)/shard_map/ppermute | solution.py:42
  71.4 5.9 %collective-permute-start.7 = (f32[64]{0:T(128)S(1)}, f32[64]{0:T(128)S(1)}, u32[]{:S(2)}, u32[]{:S(2)}) collective-permute-start(f32[64]{0:T(128)S(1)} %add.191), channel_id=1, source_target_pairs={{0,4},{1,5},{2,6},{3,7},{4,0},{5,1},{6,2},{7,3},{8,12},{9,13},{10,... | collective-permute-start | bytes 776 | tf_op jit(solution)/shard_map/ppermute | solution.py:42
  77.2 3.5 %collective-permute-done.7 = f32[64]{0:T(128)S(1)} collective-permute-done((f32[64]{0:T(128)S(1)}, f32[64]{0:T(128)S(1)}, u32[]{:S(2)}, u32[]{:S(2)}) %collective-permute-start.7) | collective-permute-done | bytes 288 | tf_op jit(solution)/shard_map/ppermute | solution.py:42
  80.7 5.3 %collective-permute-start.8 = (f32[64]{0:T(128)S(1)}, f32[64]{0:T(128)S(1)}, u32[]{:S(2)}, u32[]{:S(2)}) collective-permute-start(f32[64]{0:T(128)S(1)} %add.192), channel_id=1, source_target_pairs={{0,8},{1,9},{2,10},{3,11},{4,12},{5,13},{6,14},{7,15},{8,0},{9,1},... | collective-permute-start | bytes 776 | tf_op jit(solution)/shard_map/ppermute | solution.py:42
  86.0 4.0 %collective-permute-done.8 = f32[64]{0:T(128)S(1)} collective-permute-done((f32[64]{0:T(128)S(1)}, f32[64]{0:T(128)S(1)}, u32[]{:S(2)}, u32[]{:S(2)}) %collective-permute-start.8) | collective-permute-done | bytes 288 | tf_op jit(solution)/shard_map/ppermute | solution.py:42
  95.5 3.8 %collective-permute-start.10 = (f32[64]{0:T(128)S(1)}, f32[64]{0:T(128)S(1)}, u32[]{:S(2)}, u32[]{:S(2)}) collective-permute-start(f32[64]{0:T(128)S(1)} %add.194), channel_id=1, source_target_pairs={{0,32},{1,33},{2,34},{3,35},{4,36},{5,37},{6,38},{7,39},{8,40},{9,... | collective-permute-start | bytes 776 | tf_op jit(solution)/shard_map/ppermute | solution.py:42
  103.7 12.7 %all-gather.2 = f32[8,1,512]{2,1,0:T(1,128)S(1)} all-gather(f32[1,1,512]{2,1,0:T(1,128)S(1)} %bitcast.214), channel_id=3, replica_groups=mesh['lat'=8,'lon'=64] {'lat'}, dimensions={0}, use_global_device_ids=true | all-gather | bytes 18432 | tf_op jit(solution)/shard_map/all_gather | solution.py:53
  118.4 3.5 %collective-permute-done.11 = f32[512]{0:T(512)S(1)} collective-permute-done((f32[512]{0:T(512)S(1)}, f32[512]{0:T(512)S(1)}, u32[]{:S(2)}, u32[]{:S(2)}) %collective-permute-start.11) | collective-permute-done | bytes 2080 | tf_op jit(solution)/shard_map/ppermute | solution.py:42
  124.8 3.5 %collective-permute-done.12 = f32[512]{0:T(512)S(1)} collective-permute-done((f32[512]{0:T(512)S(1)}, f32[512]{0:T(512)S(1)}, u32[]{:S(2)}, u32[]{:S(2)}) %collective-permute-start.12) | collective-permute-done | bytes 2080 | tf_op jit(solution)/shard_map/ppermute | solution.py:42
  128.3 5.9 %collective-permute-start.13 = (f32[512]{0:T(512)S(1)}, f32[512]{0:T(512)S(1)}, u32[]{:S(2)}, u32[]{:S(2)}) collective-permute-start(f32[512]{0:T(512)S(1)} %add.204), channel_id=1, source_target_pairs={{0,4},{1,5},{2,6},{3,7},{4,0},{5,1},{6,2},{7,3},{8,12},{9,13},{10,... | collective-permute-start | bytes 6152 | tf_op jit(solution)/shard_map/ppermute | solution.py:42
  134.2 3.5 %collective-permute-done.13 = f32[512]{0:T(512)S(1)} collective-permute-done((f32[512]{0:T(512)S(1)}, f32[512]{0:T(512)S(1)}, u32[]{:S(2)}, u32[]{:S(2)}) %collective-permute-start.13) | collective-permute-done | bytes 2080 | tf_op jit(solution)/shard_map/ppermute | solution.py:42
  137.7 5.3 %collective-permute-start.14 = (f32[512]{0:T(512)S(1)}, f32[512]{0:T(512)S(1)}, u32[]{:S(2)}, u32[]{:S(2)}) collective-permute-start(f32[512]{0:T(512)S(1)} %add.205), channel_id=1, source_target_pairs={{0,8},{1,9},{2,10},{3,11},{4,12},{5,13},{6,14},{7,15},{8,0},{9,1},... | collective-permute-start | bytes 6152 | tf_op jit(solution)/shard_map/ppermute | solution.py:42
  143.0 4.1 %collective-permute-done.14 = f32[512]{0:T(512)S(1)} collective-permute-done((f32[512]{0:T(512)S(1)}, f32[512]{0:T(512)S(1)}, u32[]{:S(2)}, u32[]{:S(2)}) %collective-permute-start.14) | collective-permute-done | bytes 2080 | tf_op jit(solution)/shard_map/ppermute | solution.py:42
  152.5 3.8 %collective-permute-start.16 = (f32[512]{0:T(512)S(1)}, f32[512]{0:T(512)S(1)}, u32[]{:S(2)}, u32[]{:S(2)}) collective-permute-start(f32[512]{0:T(512)S(1)} %add.207), channel_id=1, source_target_pairs={{0,32},{1,33},{2,34},{3,35},{4,36},{5,37},{6,38},{7,39},{8,40},{9,... | collective-permute-start | bytes 6152 | tf_op jit(solution)/shard_map/ppermute | solution.py:42
  156.3 3.2 %collective-permute-done.16 = f32[512]{0:T(512)S(1)} collective-permute-done((f32[512]{0:T(512)S(1)}, f32[512]{0:T(512)S(1)}, u32[]{:S(2)}, u32[]{:S(2)}) %collective-permute-start.16) | collective-permute-done | bytes 2080 | tf_op jit(solution)/shard_map/ppermute | solution.py:42
  174.3 11.2 %collective-permute-start.18 = (bf16[64,256]{1,0:T(8,128)(2,1)S(1)}, bf16[64,256]{1,0:T(8,128)(2,1)S(1)}, u32[]{:S(2)}, u32[]{:S(2)}) collective-permute-start(bf16[64,256]{1,0:T(8,128)(2,1)S(1)} %bitcast.205), channel_id=1, source_target_pairs={{1,0},{2,1},{3,2},{4,3},{5,4},{6,5},{7,6},{8,7},{9,8},{10,9},{11,1... | collective-permute-start | bytes 98312 | tf_op jit(solution)/shard_map/ppermute | solution.py:18
  190.2 3.3 %collective-permute-start.21 = (bf16[2,18,256]{2,1,0:T(8,128)(2,1)S(1)}, bf16[2,18,256]{2,1,0:T(8,128)(2,1)S(1)}, u32[]{:S(2)}, u32[]{:S(2)}) collective-permute-start(bf16[2,18,256]{2,1,0:T(8,128)(2,1)S(1)} %pad_maximum_fusion.2), channel_id=1, source_target_pairs={{32,0},{33,1},{34,2},{35,3},{36,4},{37,5},{38,6},{39,7},{40,8},{41... | collective-permute-start | bytes 55304 | tf_op jit(solution)/shard_map/ppermute | solution.py:29
  199.1 17.3 %reduce-scatter.2.cloned.1.call-done = f32[9,32,256]{2,1,0:T(8,128)} async-done(((f32[9,256,256]{2,1,0:T(8,128)}), f32[9,32,256]{2,1,0:T(8,128)}) %reduce-scatter.2.cloned.1.call-update) | async-done | bytes 294928 | tf_op jit(solution)/shard_map/reduce_scatter | solution.py:132
  217.4 3.6 %collective-permute-start.22 = (f32[32,1152]{1,0:T(8,128)S(1)}, f32[32,1152]{1,0:T(8,128)S(1)}, u32[]{:S(2)}, u32[]{:S(2)}) collective-permute-start(f32[32,1152]{1,0:T(8,128)S(1)} %constant_dynamic-slice_fusion.5), channel_id=1, source_target_pairs={{0,32},{1,33},{2,34},{3,35},{4,36},{5,37},{6,38},{7,39},{8,40},{9,... | collective-permute-start | bytes 442376 | tf_op jit(solution)/shard_map/ppermute | solution.py:42
  221.1 4.8 %collective-permute-done.22 = f32[32,1152]{1,0:T(8,128)S(1)} collective-permute-done((f32[32,1152]{1,0:T(8,128)S(1)}, f32[32,1152]{1,0:T(8,128)S(1)}, u32[]{:S(2)}, u32[]{:S(2)}) %collective-permute-start.22) | collective-permute-done | bytes 147488 | tf_op jit(solution)/shard_map/ppermute | solution.py:42
  226.1 3.3 %collective-permute-start.23 = (f32[32,576]{1,0:T(8,128)S(1)}, f32[32,576]{1,0:T(8,128)S(1)}, u32[]{:S(2)}, u32[]{:S(2)}) collective-permute-start(f32[32,576]{1,0:T(8,128)S(1)} %constant_dynamic-slice_fusion.4), channel_id=1, source_target_pairs={{0,16},{1,17},{2,18},{3,19},{4,20},{5,21},{6,22},{7,23},{8,24},{9,... | collective-permute-start | bytes 221192 | tf_op jit(solution)/shard_map/ppermute | solution.py:42
  232.6 5.9 %collective-permute-start.24 = (f32[32,288]{1,0:T(8,128)S(1)}, f32[32,288]{1,0:T(8,128)S(1)}, u32[]{:S(2)}, u32[]{:S(2)}) collective-permute-start(f32[32,288]{1,0:T(8,128)S(1)} %constant_dynamic-slice_fusion.3), channel_id=1, source_target_pairs={{0,8},{1,9},{2,10},{3,11},{4,12},{5,13},{6,14},{7,15},{8,0},{9,1},... | collective-permute-start | bytes 110600 | tf_op jit(solution)/shard_map/ppermute | solution.py:42
  238.6 3.9 %collective-permute-done.24 = f32[32,288]{1,0:T(8,128)S(1)} collective-permute-done((f32[32,288]{1,0:T(8,128)S(1)}, f32[32,288]{1,0:T(8,128)S(1)}, u32[]{:S(2)}, u32[]{:S(2)}) %collective-permute-start.24) | collective-permute-done | bytes 36896 | tf_op jit(solution)/shard_map/ppermute | solution.py:42
  242.6 8.0 %collective-permute-start.25 = (f32[32,144]{1,0:T(8,128)S(1)}, f32[32,144]{1,0:T(8,128)S(1)}, u32[]{:S(2)}, u32[]{:S(2)}) collective-permute-start(f32[32,144]{1,0:T(8,128)S(1)} %constant_dynamic-slice_fusion.2), channel_id=1, source_target_pairs={{0,4},{1,5},{2,6},{3,7},{4,0},{5,1},{6,2},{7,3},{8,12},{9,13},{10,... | collective-permute-start | bytes 55304 | tf_op jit(solution)/shard_map/ppermute | solution.py:42
  252.6 4.6 %collective-permute-start.26 = (f32[32,72]{1,0:T(8,128)S(1)}, f32[32,72]{1,0:T(8,128)S(1)}, u32[]{:S(2)}, u32[]{:S(2)}) collective-permute-start(f32[32,72]{1,0:T(8,128)S(1)} %constant_dynamic-slice_fusion.1), channel_id=1, source_target_pairs={{0,2},{1,3},{2,0},{3,1},{4,6},{5,7},{6,4},{7,5},{8,10},{9,11},{10,... | collective-permute-start | bytes 27656 | tf_op jit(solution)/shard_map/ppermute | solution.py:42
  259.3 3.4 %collective-permute-start.27 = (f32[32,36]{1,0:T(8,128)S(1)}, f32[32,36]{1,0:T(8,128)S(1)}, u32[]{:S(2)}, u32[]{:S(2)}) collective-permute-start(f32[32,36]{1,0:T(8,128)S(1)} %constant_dynamic-slice_fusion), channel_id=1, source_target_pairs={{0,1},{1,0},{2,3},{3,2},{4,5},{5,4},{6,7},{7,6},{8,9},{9,8},{10,11... | collective-permute-start | bytes 13832 | tf_op jit(solution)/shard_map/ppermute | solution.py:42
  (149 shorter events, 72.4 us)
Async XLA Ops:
  7.2 28.3 %copy-start = (bf16[64,16,256]{2,1,0:T(8,128)(2,1)S(1)}, bf16[64,16,256]{2,1,0:T(8,128)(2,1)}, u32[]{:S(2)}) copy-start(bf16[64,16,256]{2,1,0:T(8,128)(2,1)} %param.13) | copy-start | bytes 1572868
  7.2 209.2 %reduce-scatter.2.cloned.1.call-start = ((), (), s32[]{:S(2)}) async-start(), calls=%async_computation.1 | async-start | bytes 2654208 | tf_op jit(solution)/shard_map/reduce_scatter | solution.py:132
  8.4 20.4 %collective-permute-start = (bf16[64,256]{1,0:T(8,128)(2,1)S(1)}, bf16[64,256]{1,0:T(8,128)(2,1)S(1)}, u32[]{:S(2)}, u32[]{:S(2)}) collective-permute-start(bf16[64,256]{1,0:T(8,128)(2,1)S(1)} %bitcast.207), channel_id=1, source_target_pairs={{0,1},{1,2},{2,3},{3,4},{4,5},{5,6},{6,7},{7,8},{8,9},{9,10},{10,1... | collective-permute-start | bytes 98312 | tf_op jit(solution)/shard_map/ppermute | solution.py:17
  12.7 16.1 %collective-permute-start.1 = (bf16[64,256]{1,0:T(8,128)(2,1)S(1)}, bf16[64,256]{1,0:T(8,128)(2,1)S(1)}, u32[]{:S(2)}, u32[]{:S(2)}) collective-permute-start(bf16[64,256]{1,0:T(8,128)(2,1)S(1)} %bitcast.209), channel_id=1, source_target_pairs={{1,0},{2,1},{3,2},{4,3},{5,4},{6,5},{7,6},{8,7},{9,8},{10,9},{11,1... | collective-permute-start | bytes 98312 | tf_op jit(solution)/shard_map/ppermute | solution.py:18
  29.7 5.8 %collective-permute-start.2 = (bf16[18,256]{1,0:T(8,128)(2,1)S(1)}, bf16[18,256]{1,0:T(8,128)(2,1)S(1)}, u32[]{:S(2)}, u32[]{:S(2)}) collective-permute-start(bf16[18,256]{1,0:T(8,128)(2,1)S(1)} %bitcast.201), channel_id=1, source_target_pairs={{0,64},{64,128},{128,192},{192,256},{256,320},{320,384},{384,448},... | collective-permute-start | bytes 27656 | tf_op jit(solution)/shard_map/ppermute | solution.py:17
  31.1 4.4 %collective-permute-start.3 = (bf16[18,256]{1,0:T(8,128)(2,1)S(1)}, bf16[18,256]{1,0:T(8,128)(2,1)S(1)}, u32[]{:S(2)}, u32[]{:S(2)}) collective-permute-start(bf16[18,256]{1,0:T(8,128)(2,1)S(1)} %bitcast.199), channel_id=1, source_target_pairs={{64,0},{128,64},{192,128},{256,192},{320,256},{384,320},{448,384},... | collective-permute-start | bytes 27656 | tf_op jit(solution)/shard_map/ppermute | solution.py:18
  32.4 7.2 %collective-permute-start.4 = (bf16[2,18,256]{2,1,0:T(8,128)(2,1)S(1)}, bf16[2,18,256]{2,1,0:T(8,128)(2,1)S(1)}, u32[]{:S(2)}, u32[]{:S(2)}) collective-permute-start(bf16[2,18,256]{2,1,0:T(8,128)(2,1)S(1)} %pad_maximum_fusion.1), channel_id=1, source_target_pairs={{32,0},{33,1},{34,2},{35,3},{36,4},{37,5},{38,6},{39,7},{40,8},{41... | collective-permute-start | bytes 55304 | tf_op jit(solution)/shard_map/ppermute | solution.py:29
  59.6 5.4 %collective-permute-start.5 = (f32[64]{0:T(128)S(1)}, f32[64]{0:T(128)S(1)}, u32[]{:S(2)}, u32[]{:S(2)}) collective-permute-start(f32[64]{0:T(128)S(1)} %reduce_sum.94), channel_id=1, source_target_pairs={{0,1},{1,0},{2,3},{3,2},{4,5},{5,4},{6,7},{7,6},{8,9},{9,8},{10,11... | collective-permute-start | bytes 776 | tf_op jit(solution)/shard_map/ppermute | solution.py:42
  65.0 6.3 %collective-permute-start.6 = (f32[64]{0:T(128)S(1)}, f32[64]{0:T(128)S(1)}, u32[]{:S(2)}, u32[]{:S(2)}) collective-permute-start(f32[64]{0:T(128)S(1)} %add.190), channel_id=1, source_target_pairs={{0,2},{1,3},{2,0},{3,1},{4,6},{5,7},{6,4},{7,5},{8,10},{9,11},{10,... | collective-permute-start | bytes 776 | tf_op jit(solution)/shard_map/ppermute | solution.py:42
  71.4 9.3 %collective-permute-start.7 = (f32[64]{0:T(128)S(1)}, f32[64]{0:T(128)S(1)}, u32[]{:S(2)}, u32[]{:S(2)}) collective-permute-start(f32[64]{0:T(128)S(1)} %add.191), channel_id=1, source_target_pairs={{0,4},{1,5},{2,6},{3,7},{4,0},{5,1},{6,2},{7,3},{8,12},{9,13},{10,... | collective-permute-start | bytes 776 | tf_op jit(solution)/shard_map/ppermute | solution.py:42
  80.7 9.3 %collective-permute-start.8 = (f32[64]{0:T(128)S(1)}, f32[64]{0:T(128)S(1)}, u32[]{:S(2)}, u32[]{:S(2)}) collective-permute-start(f32[64]{0:T(128)S(1)} %add.192), channel_id=1, source_target_pairs={{0,8},{1,9},{2,10},{3,11},{4,12},{5,13},{6,14},{7,15},{8,0},{9,1},... | collective-permute-start | bytes 776 | tf_op jit(solution)/shard_map/ppermute | solution.py:42
  90.0 5.4 %collective-permute-start.9 = (f32[64]{0:T(128)S(1)}, f32[64]{0:T(128)S(1)}, u32[]{:S(2)}, u32[]{:S(2)}) collective-permute-start(f32[64]{0:T(128)S(1)} %add.193), channel_id=1, source_target_pairs={{0,16},{1,17},{2,18},{3,19},{4,20},{5,21},{6,22},{7,23},{8,24},{9,... | collective-permute-start | bytes 776 | tf_op jit(solution)/shard_map/ppermute | solution.py:42
  95.5 6.9 %collective-permute-start.10 = (f32[64]{0:T(128)S(1)}, f32[64]{0:T(128)S(1)}, u32[]{:S(2)}, u32[]{:S(2)}) collective-permute-start(f32[64]{0:T(128)S(1)} %add.194), channel_id=1, source_target_pairs={{0,32},{1,33},{2,34},{3,35},{4,36},{5,37},{6,38},{7,39},{8,40},{9,... | collective-permute-start | bytes 776 | tf_op jit(solution)/shard_map/ppermute | solution.py:42
  101.1 1.7 copy-start.1
  101.1 1.7 copy-start.4
  116.4 5.5 %collective-permute-start.11 = (f32[512]{0:T(512)S(1)}, f32[512]{0:T(512)S(1)}, u32[]{:S(2)}, u32[]{:S(2)}) collective-permute-start(f32[512]{0:T(512)S(1)} %reduce_sum.97), channel_id=1, source_target_pairs={{0,1},{1,0},{2,3},{3,2},{4,5},{5,4},{6,7},{7,6},{8,9},{9,8},{10,11... | collective-permute-start | bytes 6152 | tf_op jit(solution)/shard_map/ppermute | solution.py:42
  121.9 6.4 %collective-permute-start.12 = (f32[512]{0:T(512)S(1)}, f32[512]{0:T(512)S(1)}, u32[]{:S(2)}, u32[]{:S(2)}) collective-permute-start(f32[512]{0:T(512)S(1)} %add.203), channel_id=1, source_target_pairs={{0,2},{1,3},{2,0},{3,1},{4,6},{5,7},{6,4},{7,5},{8,10},{9,11},{10,... | collective-permute-start | bytes 6152 | tf_op jit(solution)/shard_map/ppermute | solution.py:42
  128.3 9.4 %collective-permute-start.13 = (f32[512]{0:T(512)S(1)}, f32[512]{0:T(512)S(1)}, u32[]{:S(2)}, u32[]{:S(2)}) collective-permute-start(f32[512]{0:T(512)S(1)} %add.204), channel_id=1, source_target_pairs={{0,4},{1,5},{2,6},{3,7},{4,0},{5,1},{6,2},{7,3},{8,12},{9,13},{10,... | collective-permute-start | bytes 6152 | tf_op jit(solution)/shard_map/ppermute | solution.py:42
  137.7 9.4 %collective-permute-start.14 = (f32[512]{0:T(512)S(1)}, f32[512]{0:T(512)S(1)}, u32[]{:S(2)}, u32[]{:S(2)}) collective-permute-start(f32[512]{0:T(512)S(1)} %add.205), channel_id=1, source_target_pairs={{0,8},{1,9},{2,10},{3,11},{4,12},{5,13},{6,14},{7,15},{8,0},{9,1},... | collective-permute-start | bytes 6152 | tf_op jit(solution)/shard_map/ppermute | solution.py:42
  147.1 5.5 %collective-permute-start.15 = (f32[512]{0:T(512)S(1)}, f32[512]{0:T(512)S(1)}, u32[]{:S(2)}, u32[]{:S(2)}) collective-permute-start(f32[512]{0:T(512)S(1)} %add.206), channel_id=1, source_target_pairs={{0,16},{1,17},{2,18},{3,19},{4,20},{5,21},{6,22},{7,23},{8,24},{9,... | collective-permute-start | bytes 6152 | tf_op jit(solution)/shard_map/ppermute | solution.py:42
  152.5 7.0 %collective-permute-start.16 = (f32[512]{0:T(512)S(1)}, f32[512]{0:T(512)S(1)}, u32[]{:S(2)}, u32[]{:S(2)}) collective-permute-start(f32[512]{0:T(512)S(1)} %add.207), channel_id=1, source_target_pairs={{0,32},{1,33},{2,34},{3,35},{4,36},{5,37},{6,38},{7,39},{8,40},{9,... | collective-permute-start | bytes 6152 | tf_op jit(solution)/shard_map/ppermute | solution.py:42
  172.3 13.2 %collective-permute-start.17 = (bf16[64,256]{1,0:T(8,128)(2,1)S(1)}, bf16[64,256]{1,0:T(8,128)(2,1)S(1)}, u32[]{:S(2)}, u32[]{:S(2)}) collective-permute-start(bf16[64,256]{1,0:T(8,128)(2,1)S(1)} %bitcast.203), channel_id=1, source_target_pairs={{0,1},{1,2},{2,3},{3,4},{4,5},{5,6},{6,7},{7,8},{8,9},{9,10},{10,1... | collective-permute-start | bytes 98312 | tf_op jit(solution)/shard_map/ppermute | solution.py:17
  174.3 13.2 %collective-permute-start.18 = (bf16[64,256]{1,0:T(8,128)(2,1)S(1)}, bf16[64,256]{1,0:T(8,128)(2,1)S(1)}, u32[]{:S(2)}, u32[]{:S(2)}) collective-permute-start(bf16[64,256]{1,0:T(8,128)(2,1)S(1)} %bitcast.205), channel_id=1, source_target_pairs={{1,0},{2,1},{3,2},{4,3},{5,4},{6,5},{7,6},{8,7},{9,8},{10,9},{11,1... | collective-permute-start | bytes 98312 | tf_op jit(solution)/shard_map/ppermute | solution.py:18
  187.5 6.0 %collective-permute-start.19 = (bf16[18,256]{1,0:T(8,128)(2,1)S(1)}, bf16[18,256]{1,0:T(8,128)(2,1)S(1)}, u32[]{:S(2)}, u32[]{:S(2)}) collective-permute-start(bf16[18,256]{1,0:T(8,128)(2,1)S(1)} %bitcast.202), channel_id=1, source_target_pairs={{0,64},{64,128},{128,192},{192,256},{256,320},{320,384},{384,448},... | collective-permute-start | bytes 27656 | tf_op jit(solution)/shard_map/ppermute | solution.py:17
  188.8 4.7 %collective-permute-start.20 = (bf16[18,256]{1,0:T(8,128)(2,1)S(1)}, bf16[18,256]{1,0:T(8,128)(2,1)S(1)}, u32[]{:S(2)}, u32[]{:S(2)}) collective-permute-start(bf16[18,256]{1,0:T(8,128)(2,1)S(1)} %bitcast.200), channel_id=1, source_target_pairs={{64,0},{128,64},{192,128},{256,192},{320,256},{384,320},{448,384},... | collective-permute-start | bytes 27656 | tf_op jit(solution)/shard_map/ppermute | solution.py:18
  190.2 8.8 %collective-permute-start.21 = (bf16[2,18,256]{2,1,0:T(8,128)(2,1)S(1)}, bf16[2,18,256]{2,1,0:T(8,128)(2,1)S(1)}, u32[]{:S(2)}, u32[]{:S(2)}) collective-permute-start(bf16[2,18,256]{2,1,0:T(8,128)(2,1)S(1)} %pad_maximum_fusion.2), channel_id=1, source_target_pairs={{32,0},{33,1},{34,2},{35,3},{36,4},{37,5},{38,6},{39,7},{40,8},{41... | collective-permute-start | bytes 55304 | tf_op jit(solution)/shard_map/ppermute | solution.py:29
  217.4 8.5 %collective-permute-start.22 = (f32[32,1152]{1,0:T(8,128)S(1)}, f32[32,1152]{1,0:T(8,128)S(1)}, u32[]{:S(2)}, u32[]{:S(2)}) collective-permute-start(f32[32,1152]{1,0:T(8,128)S(1)} %constant_dynamic-slice_fusion.5), channel_id=1, source_target_pairs={{0,32},{1,33},{2,34},{3,35},{4,36},{5,37},{6,38},{7,39},{8,40},{9,... | collective-permute-start | bytes 442376 | tf_op jit(solution)/shard_map/ppermute | solution.py:42
  226.1 6.3 %collective-permute-start.23 = (f32[32,576]{1,0:T(8,128)S(1)}, f32[32,576]{1,0:T(8,128)S(1)}, u32[]{:S(2)}, u32[]{:S(2)}) collective-permute-start(f32[32,576]{1,0:T(8,128)S(1)} %constant_dynamic-slice_fusion.4), channel_id=1, source_target_pairs={{0,16},{1,17},{2,18},{3,19},{4,20},{5,21},{6,22},{7,23},{8,24},{9,... | collective-permute-start | bytes 221192 | tf_op jit(solution)/shard_map/ppermute | solution.py:42
  232.6 9.9 %collective-permute-start.24 = (f32[32,288]{1,0:T(8,128)S(1)}, f32[32,288]{1,0:T(8,128)S(1)}, u32[]{:S(2)}, u32[]{:S(2)}) collective-permute-start(f32[32,288]{1,0:T(8,128)S(1)} %constant_dynamic-slice_fusion.3), channel_id=1, source_target_pairs={{0,8},{1,9},{2,10},{3,11},{4,12},{5,13},{6,14},{7,15},{8,0},{9,1},... | collective-permute-start | bytes 110600 | tf_op jit(solution)/shard_map/ppermute | solution.py:42
  242.6 9.8 %collective-permute-start.25 = (f32[32,144]{1,0:T(8,128)S(1)}, f32[32,144]{1,0:T(8,128)S(1)}, u32[]{:S(2)}, u32[]{:S(2)}) collective-permute-start(f32[32,144]{1,0:T(8,128)S(1)} %constant_dynamic-slice_fusion.2), channel_id=1, source_target_pairs={{0,4},{1,5},{2,6},{3,7},{4,0},{5,1},{6,2},{7,3},{8,12},{9,13},{10,... | collective-permute-start | bytes 55304 | tf_op jit(solution)/shard_map/ppermute | solution.py:42
  252.6 6.5 %collective-permute-start.26 = (f32[32,72]{1,0:T(8,128)S(1)}, f32[32,72]{1,0:T(8,128)S(1)}, u32[]{:S(2)}, u32[]{:S(2)}) collective-permute-start(f32[32,72]{1,0:T(8,128)S(1)} %constant_dynamic-slice_fusion.1), channel_id=1, source_target_pairs={{0,2},{1,3},{2,0},{3,1},{4,6},{5,7},{6,4},{7,5},{8,10},{9,11},{10,... | collective-permute-start | bytes 27656 | tf_op jit(solution)/shard_map/ppermute | solution.py:42
  259.3 5.6 %collective-permute-start.27 = (f32[32,36]{1,0:T(8,128)S(1)}, f32[32,36]{1,0:T(8,128)S(1)}, u32[]{:S(2)}, u32[]{:S(2)}) collective-permute-start(f32[32,36]{1,0:T(8,128)S(1)} %constant_dynamic-slice_fusion), channel_id=1, source_target_pairs={{0,1},{1,0},{2,3},{3,2},{4,5},{5,4},{6,7},{7,6},{8,9},{9,8},{10,11... | collective-permute-start | bytes 13832 | tf_op jit(solution)/shard_map/ppermute | solution.py:42
  (4 other events, 5.5 us)
Sparse Core Ops, SparseCore 0:
  172.3 44.0 reduce-scatter.1

commit v11 on v9

--- a/solution.py
+++ b/solution.py
@@ -15,6 +15,8 @@
         initial = lax.slice_in_dim(shard, 0, width, axis=dim)
         if width == 1:
             before = jnp.expand_dims(lax.ppermute(jnp.squeeze(last, dim), axis, up), dim)
+            if wrap:
+                before, initial = lax.optimization_barrier((before, initial))
             after = jnp.expand_dims(lax.ppermute(jnp.squeeze(initial, dim), axis, down), dim)
         else:
             before = lax.ppermute(last, axis, up)

time: 272 us -> 277 us (1.018)
  waiting for transfers between devices: 74.2 us -> 101 us
  starting transfers between devices: 115 us -> 93 us
    ppermute x4, waiting for transfers between devices: 0.01 us -> 25.2 us  [with_halo(): lax.ppermute(jnp.squeeze(last, dim), axis, up)]
    ppermute x4, starting transfers between devices: 27.9 us -> 10.1 us  [with_halo(): lax.ppermute(jnp.squeeze(initial, dim), axis, down)]
    ppermute x18, starting transfers between devices: 72 us -> 67.2 us  [exchange(): return lax.ppermute(block, axis, [(i, i ^ 1 << bit) for i in range(peers)])]
    ppermute x18, waiting for transfers between devices: 52.1 us -> 56.8 us  [exchange(): return lax.ppermute(block, axis, [(i, i ^ 1 << bit) for i in range(peers)])]
    reduce_scatter x1, waiting for transfers between devices: 16.6 us -> 13.5 us  [local(): owned_cols = lax.psum_scatter(term, 'lat', scatter_dimension=0, tiled=True)]
  transfers between devices with their start and end apart: 29 -> 29, of which waited for: 21 -> 24; matrix products, arithmetic and copies ran while one was open for 5% -> 5% of each run, Pallas kernels for 0% -> 0%
where the time goes in v11:
time: 277 us; the launch traced here: 275 us
  waiting for transfers between devices  101 us (36%)
  starting transfers between devices  93 us (34%)
  blocking collectives  27.5 us (10%)
  matrix products  17.9 us (6%)
  between operations  15.4 us (6%)
  local copies, waits for them, and re-layouts  12.6 us (5%)
  other arithmetic  7.88 us (3%)
    ppermute x18, starting transfers between devices, exchange(): return lax.ppermute(block, axis, [(i, i ^ 1 << bit) for i in range(peers)])  67.2 us
    ppermute x18, waiting for transfers between devices, exchange(): return lax.ppermute(block, axis, [(i, i ^ 1 << bit) for i in range(peers)])  56.8 us
    ppermute x4, waiting for transfers between devices, with_halo(): lax.ppermute(jnp.squeeze(last, dim), axis, up)  25.2 us
    unnamed x1, blocking collectives  14.8 us
    reduce_scatter x1, waiting for transfers between devices, local(): owned_cols = lax.psum_scatter(term, 'lat', scatter_dimension=0, tiled=True)  13.5 us
    all_gather x1, blocking collectives, butterfly_sum(): value = jnp.sum(lax.all_gather(value, 'lat'), 0)  12.7 us
    ppermute x4, starting transfers between devices, with_halo(): lax.ppermute(jnp.squeeze(initial, dim), axis, down)  10.1 us
    ppermute x4, starting transfers between devices, with_halo(): lax.ppermute(jnp.squeeze(last, dim), axis, up)  8.91 us
  transfers between devices with their start and end apart: 29, of which 24 were waited for; matrix products, arithmetic and copies ran while one was open for 5% of the time, Pallas kernels for 0%

profile of v11, /device:TPU:6, one launch (start us, length us, event | category | flops | bytes accessed | tf_op | source)
XLA Modules:
  0.0 275.4 jit_solution(1286175357272468062)
XLA Ops:
  8.4 4.3 %collective-permute-start = (bf16[64,256]{1,0:T(8,128)(2,1)S(1)}, bf16[64,256]{1,0:T(8,128)(2,1)S(1)}, u32[]{:S(2)}, u32[]{:S(2)}) collective-permute-start(bf16[64,256]{1,0:T(8,128)(2,1)S(1)} %bitcast.155), channel_id=1, source_target_pairs={{0,1},{1,2},{2,3},{3,4},{4,5},{5,6},{6,7},{7,8},{8,9},{9,10},{10,1... | collective-permute-start | bytes 98312 | tf_op jit(solution)/shard_map/ppermute | solution.py:17
  12.7 14.3 %collective-permute-done = bf16[64,256]{1,0:T(8,128)(2,1)S(1)} collective-permute-done((bf16[64,256]{1,0:T(8,128)(2,1)S(1)}, bf16[64,256]{1,0:T(8,128)(2,1)S(1)}, u32[]{:S(2)}, u32[]{:S(2)}) %collective-permute-start) | collective-permute-done | bytes 32800 | tf_op jit(solution)/shard_map/ppermute | solution.py:17
  27.0 3.7 %collective-permute-start.1 = (bf16[64,256]{1,0:T(8,128)(2,1)S(1)}, bf16[64,256]{1,0:T(8,128)(2,1)S(1)}, u32[]{:S(2)}, u32[]{:S(2)}) collective-permute-start(bf16[64,256]{1,0:T(8,128)(2,1)S(1)} %bitcast.153), channel_id=1, source_target_pairs={{1,0},{2,1},{3,2},{4,3},{5,4},{6,5},{7,6},{8,7},{9,8},{10,9},{11,1... | collective-permute-start | bytes 98312 | tf_op jit(solution)/shard_map/ppermute | solution.py:20
  39.8 3.7 %collective-permute-done.4 = bf16[2,18,256]{2,1,0:T(8,128)(2,1)S(1)} collective-permute-done((bf16[2,18,256]{2,1,0:T(8,128)(2,1)S(1)}, bf16[2,18,256]{2,1,0:T(8,128)(2,1)S(1)}, u32[]{:S(2)}, u32[]{:S(2)}) %collective-permute-start.4) | collective-permute-done | bytes 18464 | tf_op jit(solution)/shard_map/ppermute | solution.py:31
  45.0 3.2 %select_reduce_fusion.1 = (f32[256]{0:T(256)S(1)}, f32[256]{0:T(256)S(1)}, f32[64,8,3,256]{3,1,2,0:T(8,128)}) fusion(pred[8,3]{0,1:T(4,128)(4,1)S(1)} %copy-done.7, bf16[3,3,256,256]{3,2,1,0:T(8,128)(2,1)S(1)} %copy-done.3, bf16[66,1,7,2,256]{4,2,3,0,1:T(8,128)(2,1)S(1)} %slice.207, bf16[66,1,8,3,256]{4,2,3,0,1:T(8,128)(2,1)S(1)} %copy.85), kind=kOutput, calls=%fused_computation.4 | convolution fusion | flops 1818353152 | bytes 4038680 | tf_op jit(solution)/shard_map/conv_general_dilated | solution.py:72
  48.9 14.8 %all-reduce = f32[512]{0:T(512)S(1)} all-reduce(f32[512]{0:T(512)S(1)} %maximum_dynamic-update-slice_fusion), channel_id=2, replica_groups=mesh['lat'=8,'lon'=64] {'lat'}, use_global_device_ids=true, to_apply=%add | all-reduce | flops 512 | bytes 4096
  65.8 3.4 %collective-permute-done.5 = f32[64]{0:T(128)S(1)} collective-permute-done((f32[64]{0:T(128)S(1)}, f32[64]{0:T(128)S(1)}, u32[]{:S(2)}, u32[]{:S(2)}) %collective-permute-start.5) | collective-permute-done | bytes 288 | tf_op jit(solution)/shard_map/ppermute | solution.py:44
  71.1 4.4 %collective-permute-done.6 = f32[64]{0:T(128)S(1)} collective-permute-done((f32[64]{0:T(128)S(1)}, f32[64]{0:T(128)S(1)}, u32[]{:S(2)}, u32[]{:S(2)}) %collective-permute-start.6) | collective-permute-done | bytes 288 | tf_op jit(solution)/shard_map/ppermute | solution.py:44
  75.5 5.7 %collective-permute-start.7 = (f32[64]{0:T(128)S(1)}, f32[64]{0:T(128)S(1)}, u32[]{:S(2)}, u32[]{:S(2)}) collective-permute-start(f32[64]{0:T(128)S(1)} %add.170), channel_id=1, source_target_pairs={{0,4},{1,5},{2,6},{3,7},{4,0},{5,1},{6,2},{7,3},{8,12},{9,13},{10,... | collective-permute-start | bytes 776 | tf_op jit(solution)/shard_map/ppermute | solution.py:44
  81.2 3.7 %collective-permute-done.7 = f32[64]{0:T(128)S(1)} collective-permute-done((f32[64]{0:T(128)S(1)}, f32[64]{0:T(128)S(1)}, u32[]{:S(2)}, u32[]{:S(2)}) %collective-permute-start.7) | collective-permute-done | bytes 288 | tf_op jit(solution)/shard_map/ppermute | solution.py:44
  84.8 5.1 %collective-permute-start.8 = (f32[64]{0:T(128)S(1)}, f32[64]{0:T(128)S(1)}, u32[]{:S(2)}, u32[]{:S(2)}) collective-permute-start(f32[64]{0:T(128)S(1)} %add.171), channel_id=1, source_target_pairs={{0,8},{1,9},{2,10},{3,11},{4,12},{5,13},{6,14},{7,15},{8,0},{9,1},... | collective-permute-start | bytes 776 | tf_op jit(solution)/shard_map/ppermute | solution.py:44
  89.9 4.2 %collective-permute-done.8 = f32[64]{0:T(128)S(1)} collective-permute-done((f32[64]{0:T(128)S(1)}, f32[64]{0:T(128)S(1)}, u32[]{:S(2)}, u32[]{:S(2)}) %collective-permute-start.8) | collective-permute-done | bytes 288 | tf_op jit(solution)/shard_map/ppermute | solution.py:44
  99.6 3.8 %collective-permute-start.10 = (f32[64]{0:T(128)S(1)}, f32[64]{0:T(128)S(1)}, u32[]{:S(2)}, u32[]{:S(2)}) collective-permute-start(f32[64]{0:T(128)S(1)} %add.173), channel_id=1, source_target_pairs={{0,32},{1,33},{2,34},{3,35},{4,36},{5,37},{6,38},{7,39},{8,40},{9,... | collective-permute-start | bytes 776 | tf_op jit(solution)/shard_map/ppermute | solution.py:44
  107.8 12.7 %all-gather.2 = f32[8,1,512]{2,1,0:T(1,128)S(1)} all-gather(f32[1,1,512]{2,1,0:T(1,128)S(1)} %bitcast.160), channel_id=3, replica_groups=mesh['lat'=8,'lon'=64] {'lat'}, dimensions={0}, use_global_device_ids=true | all-gather | bytes 18432 | tf_op jit(solution)/shard_map/all_gather | solution.py:55
  122.6 3.4 %collective-permute-done.11 = f32[512]{0:T(512)S(1)} collective-permute-done((f32[512]{0:T(512)S(1)}, f32[512]{0:T(512)S(1)}, u32[]{:S(2)}, u32[]{:S(2)}) %collective-permute-start.11) | collective-permute-done | bytes 2080 | tf_op jit(solution)/shard_map/ppermute | solution.py:44
  128.7 3.7 %collective-permute-done.12 = f32[512]{0:T(512)S(1)} collective-permute-done((f32[512]{0:T(512)S(1)}, f32[512]{0:T(512)S(1)}, u32[]{:S(2)}, u32[]{:S(2)}) %collective-permute-start.12) | collective-permute-done | bytes 2080 | tf_op jit(solution)/shard_map/ppermute | solution.py:44
  132.4 5.7 %collective-permute-start.13 = (f32[512]{0:T(512)S(1)}, f32[512]{0:T(512)S(1)}, u32[]{:S(2)}, u32[]{:S(2)}) collective-permute-start(f32[512]{0:T(512)S(1)} %add.183), channel_id=1, source_target_pairs={{0,4},{1,5},{2,6},{3,7},{4,0},{5,1},{6,2},{7,3},{8,12},{9,13},{10,... | collective-permute-start | bytes 6152 | tf_op jit(solution)/shard_map/ppermute | solution.py:44
  138.1 3.7 %collective-permute-done.13 = f32[512]{0:T(512)S(1)} collective-permute-done((f32[512]{0:T(512)S(1)}, f32[512]{0:T(512)S(1)}, u32[]{:S(2)}, u32[]{:S(2)}) %collective-permute-start.13) | collective-permute-done | bytes 2080 | tf_op jit(solution)/shard_map/ppermute | solution.py:44
  141.8 5.1 %collective-permute-start.14 = (f32[512]{0:T(512)S(1)}, f32[512]{0:T(512)S(1)}, u32[]{:S(2)}, u32[]{:S(2)}) collective-permute-start(f32[512]{0:T(512)S(1)} %add.184), channel_id=1, source_target_pairs={{0,8},{1,9},{2,10},{3,11},{4,12},{5,13},{6,14},{7,15},{8,0},{9,1},... | collective-permute-start | bytes 6152 | tf_op jit(solution)/shard_map/ppermute | solution.py:44
  146.9 4.3 %collective-permute-done.14 = f32[512]{0:T(512)S(1)} collective-permute-done((f32[512]{0:T(512)S(1)}, f32[512]{0:T(512)S(1)}, u32[]{:S(2)}, u32[]{:S(2)}) %collective-permute-start.14) | collective-permute-done | bytes 2080 | tf_op jit(solution)/shard_map/ppermute | solution.py:44
  156.7 3.9 %collective-permute-start.16 = (f32[512]{0:T(512)S(1)}, f32[512]{0:T(512)S(1)}, u32[]{:S(2)}, u32[]{:S(2)}) collective-permute-start(f32[512]{0:T(512)S(1)} %add.186), channel_id=1, source_target_pairs={{0,32},{1,33},{2,34},{3,35},{4,36},{5,37},{6,38},{7,39},{8,40},{9,... | collective-permute-start | bytes 6152 | tf_op jit(solution)/shard_map/ppermute | solution.py:44
  166.8 7.2 %fusion.14 = f32[256,3,3,256]{3,0,2,1:T(8,128)} fusion(bf16[1,66,18,256]{3,2,1,0:T(8,128)(2,1)S(1)} %fusion.49, bf16[64,16,1,256]{3,1,0,2:T(8,128)(2,1)S(1)} %bitcast.135), kind=kOutput, calls=%fused_computation.19 | convolution fusion | flops 1207959552 | bytes 3491840 | tf_op jit(solution)/shard_map/conv_general_dilated | solution.py:123
  176.2 10.9 %collective-permute-done.17 = bf16[64,256]{1,0:T(8,128)(2,1)S(1)} collective-permute-done((bf16[64,256]{1,0:T(8,128)(2,1)S(1)}, bf16[64,256]{1,0:T(8,128)(2,1)S(1)}, u32[]{:S(2)}, u32[]{:S(2)}) %collective-permute-start.17) | collective-permute-done | bytes 32800 | tf_op jit(solution)/shard_map/ppermute | solution.py:17
  187.1 3.9 %collective-permute-start.18 = (bf16[64,256]{1,0:T(8,128)(2,1)S(1)}, bf16[64,256]{1,0:T(8,128)(2,1)S(1)}, u32[]{:S(2)}, u32[]{:S(2)}) collective-permute-start(bf16[64,256]{1,0:T(8,128)(2,1)S(1)} %bitcast.150), channel_id=1, source_target_pairs={{1,0},{2,1},{3,2},{4,3},{5,4},{6,5},{7,6},{8,7},{9,8},{10,9},{11,1... | collective-permute-start | bytes 98312 | tf_op jit(solution)/shard_map/ppermute | solution.py:20
  195.6 3.8 %collective-permute-start.21 = (bf16[2,18,256]{2,1,0:T(8,128)(2,1)S(1)}, bf16[2,18,256]{2,1,0:T(8,128)(2,1)S(1)}, u32[]{:S(2)}, u32[]{:S(2)}) collective-permute-start(bf16[2,18,256]{2,1,0:T(8,128)(2,1)S(1)} %pad_maximum_fusion.2), channel_id=1, source_target_pairs={{32,0},{33,1},{34,2},{35,3},{36,4},{37,5},{38,6},{39,7},{40,8},{41... | collective-permute-start | bytes 55304 | tf_op jit(solution)/shard_map/ppermute | solution.py:31
  205.6 13.5 %reduce-scatter.2.cloned.1.call-done = f32[32,3,3,256]{3,0,2,1:T(8,128)} async-done(((f32[256,3,3,256]{3,0,2,1:T(8,128)}), f32[32,3,3,256]{3,0,2,1:T(8,128)}) %reduce-scatter.2.cloned.1.call-update) | async-done | bytes 294928 | tf_op jit(solution)/shard_map/reduce_scatter | solution.py:131
  220.5 3.1 %collective-permute-start.22 = (f32[32,1152]{1,0:T(8,128)S(1)}, f32[32,1152]{1,0:T(8,128)S(1)}, u32[]{:S(2)}, u32[]{:S(2)}) collective-permute-start(f32[32,1152]{1,0:T(8,128)S(1)} %constant_dynamic-slice_fusion.5), channel_id=1, source_target_pairs={{0,32},{1,33},{2,34},{3,35},{4,36},{5,37},{6,38},{7,39},{8,40},{9,... | collective-permute-start | bytes 442376 | tf_op jit(solution)/shard_map/ppermute | solution.py:44
  224.6 4.4 %collective-permute-done.22 = f32[32,1152]{1,0:T(8,128)S(1)} collective-permute-done((f32[32,1152]{1,0:T(8,128)S(1)}, f32[32,1152]{1,0:T(8,128)S(1)}, u32[]{:S(2)}, u32[]{:S(2)}) %collective-permute-start.22) | collective-permute-done | bytes 147488 | tf_op jit(solution)/shard_map/ppermute | solution.py:44
  235.7 5.4 %collective-permute-start.24 = (f32[32,288]{1,0:T(8,128)S(1)}, f32[32,288]{1,0:T(8,128)S(1)}, u32[]{:S(2)}, u32[]{:S(2)}) collective-permute-start(f32[32,288]{1,0:T(8,128)S(1)} %constant_dynamic-slice_fusion.3), channel_id=1, source_target_pairs={{0,8},{1,9},{2,10},{3,11},{4,12},{5,13},{6,14},{7,15},{8,0},{9,1},... | collective-permute-start | bytes 110600 | tf_op jit(solution)/shard_map/ppermute | solution.py:44
  242.1 3.4 %collective-permute-done.24 = f32[32,288]{1,0:T(8,128)S(1)} collective-permute-done((f32[32,288]{1,0:T(8,128)S(1)}, f32[32,288]{1,0:T(8,128)S(1)}, u32[]{:S(2)}, u32[]{:S(2)}) %collective-permute-start.24) | collective-permute-done | bytes 36896 | tf_op jit(solution)/shard_map/ppermute | solution.py:44
  245.7 7.0 %collective-permute-start.25 = (f32[32,144]{1,0:T(8,128)S(1)}, f32[32,144]{1,0:T(8,128)S(1)}, u32[]{:S(2)}, u32[]{:S(2)}) collective-permute-start(f32[32,144]{1,0:T(8,128)S(1)} %constant_dynamic-slice_fusion.2), channel_id=1, source_target_pairs={{0,4},{1,5},{2,6},{3,7},{4,0},{5,1},{6,2},{7,3},{8,12},{9,13},{10,... | collective-permute-start | bytes 55304 | tf_op jit(solution)/shard_map/ppermute | solution.py:44
  255.6 3.6 %collective-permute-start.26 = (f32[32,72]{1,0:T(8,128)S(1)}, f32[32,72]{1,0:T(8,128)S(1)}, u32[]{:S(2)}, u32[]{:S(2)}) collective-permute-start(f32[32,72]{1,0:T(8,128)S(1)} %constant_dynamic-slice_fusion.1), channel_id=1, source_target_pairs={{0,2},{1,3},{2,0},{3,1},{4,6},{5,7},{6,4},{7,5},{8,10},{9,11},{10,... | collective-permute-start | bytes 27656 | tf_op jit(solution)/shard_map/ppermute | solution.py:44
  (146 shorter events, 77.3 us)
Async XLA Ops:
  7.2 32.1 %copy-start = (bf16[64,16,256]{2,1,0:T(8,128)(2,1)S(1)}, bf16[64,16,256]{2,1,0:T(8,128)(2,1)}, u32[]{:S(2)}) copy-start(bf16[64,16,256]{2,1,0:T(8,128)(2,1)} %param.13) | copy-start | bytes 1572868
  7.2 211.9 %reduce-scatter.2.cloned.1.call-start = ((), (), s32[]{:S(2)}) async-start(), calls=%async_computation.1 | async-start | bytes 2654208 | tf_op jit(solution)/shard_map/reduce_scatter | solution.py:131
  8.4 18.6 %collective-permute-start = (bf16[64,256]{1,0:T(8,128)(2,1)S(1)}, bf16[64,256]{1,0:T(8,128)(2,1)S(1)}, u32[]{:S(2)}, u32[]{:S(2)}) collective-permute-start(bf16[64,256]{1,0:T(8,128)(2,1)S(1)} %bitcast.155), channel_id=1, source_target_pairs={{0,1},{1,2},{2,3},{3,4},{4,5},{5,6},{6,7},{7,8},{8,9},{9,10},{10,1... | collective-permute-start | bytes 98312 | tf_op jit(solution)/shard_map/ppermute | solution.py:17
  27.0 5.8 %collective-permute-start.1 = (bf16[64,256]{1,0:T(8,128)(2,1)S(1)}, bf16[64,256]{1,0:T(8,128)(2,1)S(1)}, u32[]{:S(2)}, u32[]{:S(2)}) collective-permute-start(bf16[64,256]{1,0:T(8,128)(2,1)S(1)} %bitcast.153), channel_id=1, source_target_pairs={{1,0},{2,1},{3,2},{4,3},{5,4},{6,5},{7,6},{8,7},{9,8},{10,9},{11,1... | collective-permute-start | bytes 98312 | tf_op jit(solution)/shard_map/ppermute | solution.py:20
  33.6 5.6 %collective-permute-start.2 = (bf16[18,256]{1,0:T(8,128)(2,1)S(1)}, bf16[18,256]{1,0:T(8,128)(2,1)S(1)}, u32[]{:S(2)}, u32[]{:S(2)}) collective-permute-start(bf16[18,256]{1,0:T(8,128)(2,1)S(1)} %bitcast.147), channel_id=1, source_target_pairs={{0,64},{64,128},{128,192},{192,256},{256,320},{320,384},{384,448},... | collective-permute-start | bytes 27656 | tf_op jit(solution)/shard_map/ppermute | solution.py:17
  34.9 4.4 %collective-permute-start.3 = (bf16[18,256]{1,0:T(8,128)(2,1)S(1)}, bf16[18,256]{1,0:T(8,128)(2,1)S(1)}, u32[]{:S(2)}, u32[]{:S(2)}) collective-permute-start(bf16[18,256]{1,0:T(8,128)(2,1)S(1)} %bitcast.145), channel_id=1, source_target_pairs={{64,0},{128,64},{192,128},{256,192},{320,256},{384,320},{448,384},... | collective-permute-start | bytes 27656 | tf_op jit(solution)/shard_map/ppermute | solution.py:20
  36.2 7.2 %collective-permute-start.4 = (bf16[2,18,256]{2,1,0:T(8,128)(2,1)S(1)}, bf16[2,18,256]{2,1,0:T(8,128)(2,1)S(1)}, u32[]{:S(2)}, u32[]{:S(2)}) collective-permute-start(bf16[2,18,256]{2,1,0:T(8,128)(2,1)S(1)} %pad_maximum_fusion.1), channel_id=1, source_target_pairs={{32,0},{33,1},{34,2},{35,3},{36,4},{37,5},{38,6},{39,7},{40,8},{41... | collective-permute-start | bytes 55304 | tf_op jit(solution)/shard_map/ppermute | solution.py:31
  63.7 5.4 %collective-permute-start.5 = (f32[64]{0:T(128)S(1)}, f32[64]{0:T(128)S(1)}, u32[]{:S(2)}, u32[]{:S(2)}) collective-permute-start(f32[64]{0:T(128)S(1)} %reduce_sum.94), channel_id=1, source_target_pairs={{0,1},{1,0},{2,3},{3,2},{4,5},{5,4},{6,7},{7,6},{8,9},{9,8},{10,11... | collective-permute-start | bytes 776 | tf_op jit(solution)/shard_map/ppermute | solution.py:44
  69.2 6.3 %collective-permute-start.6 = (f32[64]{0:T(128)S(1)}, f32[64]{0:T(128)S(1)}, u32[]{:S(2)}, u32[]{:S(2)}) collective-permute-start(f32[64]{0:T(128)S(1)} %add.169), channel_id=1, source_target_pairs={{0,2},{1,3},{2,0},{3,1},{4,6},{5,7},{6,4},{7,5},{8,10},{9,11},{10,... | collective-permute-start | bytes 776 | tf_op jit(solution)/shard_map/ppermute | solution.py:44
  75.5 9.3 %collective-permute-start.7 = (f32[64]{0:T(128)S(1)}, f32[64]{0:T(128)S(1)}, u32[]{:S(2)}, u32[]{:S(2)}) collective-permute-start(f32[64]{0:T(128)S(1)} %add.170), channel_id=1, source_target_pairs={{0,4},{1,5},{2,6},{3,7},{4,0},{5,1},{6,2},{7,3},{8,12},{9,13},{10,... | collective-permute-start | bytes 776 | tf_op jit(solution)/shard_map/ppermute | solution.py:44
  84.8 9.3 %collective-permute-start.8 = (f32[64]{0:T(128)S(1)}, f32[64]{0:T(128)S(1)}, u32[]{:S(2)}, u32[]{:S(2)}) collective-permute-start(f32[64]{0:T(128)S(1)} %add.171), channel_id=1, source_target_pairs={{0,8},{1,9},{2,10},{3,11},{4,12},{5,13},{6,14},{7,15},{8,0},{9,1},... | collective-permute-start | bytes 776 | tf_op jit(solution)/shard_map/ppermute | solution.py:44
  94.2 5.4 %collective-permute-start.9 = (f32[64]{0:T(128)S(1)}, f32[64]{0:T(128)S(1)}, u32[]{:S(2)}, u32[]{:S(2)}) collective-permute-start(f32[64]{0:T(128)S(1)} %add.172), channel_id=1, source_target_pairs={{0,16},{1,17},{2,18},{3,19},{4,20},{5,21},{6,22},{7,23},{8,24},{9,... | collective-permute-start | bytes 776 | tf_op jit(solution)/shard_map/ppermute | solution.py:44
  99.6 6.9 %collective-permute-start.10 = (f32[64]{0:T(128)S(1)}, f32[64]{0:T(128)S(1)}, u32[]{:S(2)}, u32[]{:S(2)}) collective-permute-start(f32[64]{0:T(128)S(1)} %add.173), channel_id=1, source_target_pairs={{0,32},{1,33},{2,34},{3,35},{4,36},{5,37},{6,38},{7,39},{8,40},{9,... | collective-permute-start | bytes 776 | tf_op jit(solution)/shard_map/ppermute | solution.py:44
  105.3 1.7 copy-start.1
  105.3 1.7 copy-start.5
  120.6 5.5 %collective-permute-start.11 = (f32[512]{0:T(512)S(1)}, f32[512]{0:T(512)S(1)}, u32[]{:S(2)}, u32[]{:S(2)}) collective-permute-start(f32[512]{0:T(512)S(1)} %reduce_sum.97), channel_id=1, source_target_pairs={{0,1},{1,0},{2,3},{3,2},{4,5},{5,4},{6,7},{7,6},{8,9},{9,8},{10,11... | collective-permute-start | bytes 6152 | tf_op jit(solution)/shard_map/ppermute | solution.py:44
  126.1 6.4 %collective-permute-start.12 = (f32[512]{0:T(512)S(1)}, f32[512]{0:T(512)S(1)}, u32[]{:S(2)}, u32[]{:S(2)}) collective-permute-start(f32[512]{0:T(512)S(1)} %add.182), channel_id=1, source_target_pairs={{0,2},{1,3},{2,0},{3,1},{4,6},{5,7},{6,4},{7,5},{8,10},{9,11},{10,... | collective-permute-start | bytes 6152 | tf_op jit(solution)/shard_map/ppermute | solution.py:44
  132.4 9.4 %collective-permute-start.13 = (f32[512]{0:T(512)S(1)}, f32[512]{0:T(512)S(1)}, u32[]{:S(2)}, u32[]{:S(2)}) collective-permute-start(f32[512]{0:T(512)S(1)} %add.183), channel_id=1, source_target_pairs={{0,4},{1,5},{2,6},{3,7},{4,0},{5,1},{6,2},{7,3},{8,12},{9,13},{10,... | collective-permute-start | bytes 6152 | tf_op jit(solution)/shard_map/ppermute | solution.py:44
  141.8 9.4 %collective-permute-start.14 = (f32[512]{0:T(512)S(1)}, f32[512]{0:T(512)S(1)}, u32[]{:S(2)}, u32[]{:S(2)}) collective-permute-start(f32[512]{0:T(512)S(1)} %add.184), channel_id=1, source_target_pairs={{0,8},{1,9},{2,10},{3,11},{4,12},{5,13},{6,14},{7,15},{8,0},{9,1},... | collective-permute-start | bytes 6152 | tf_op jit(solution)/shard_map/ppermute | solution.py:44
  151.2 5.5 %collective-permute-start.15 = (f32[512]{0:T(512)S(1)}, f32[512]{0:T(512)S(1)}, u32[]{:S(2)}, u32[]{:S(2)}) collective-permute-start(f32[512]{0:T(512)S(1)} %add.185), channel_id=1, source_target_pairs={{0,16},{1,17},{2,18},{3,19},{4,20},{5,21},{6,22},{7,23},{8,24},{9,... | collective-permute-start | bytes 6152 | tf_op jit(solution)/shard_map/ppermute | solution.py:44
  156.7 7.0 %collective-permute-start.16 = (f32[512]{0:T(512)S(1)}, f32[512]{0:T(512)S(1)}, u32[]{:S(2)}, u32[]{:S(2)}) collective-permute-start(f32[512]{0:T(512)S(1)} %add.186), channel_id=1, source_target_pairs={{0,32},{1,33},{2,34},{3,35},{4,36},{5,37},{6,38},{7,39},{8,40},{9,... | collective-permute-start | bytes 6152 | tf_op jit(solution)/shard_map/ppermute | solution.py:44
  174.1 13.0 %collective-permute-start.17 = (bf16[64,256]{1,0:T(8,128)(2,1)S(1)}, bf16[64,256]{1,0:T(8,128)(2,1)S(1)}, u32[]{:S(2)}, u32[]{:S(2)}) collective-permute-start(bf16[64,256]{1,0:T(8,128)(2,1)S(1)} %bitcast.156), channel_id=1, source_target_pairs={{0,1},{1,2},{2,3},{3,4},{4,5},{5,6},{6,7},{7,8},{8,9},{9,10},{10,1... | collective-permute-start | bytes 98312 | tf_op jit(solution)/shard_map/ppermute | solution.py:17
  187.1 5.8 %collective-permute-start.18 = (bf16[64,256]{1,0:T(8,128)(2,1)S(1)}, bf16[64,256]{1,0:T(8,128)(2,1)S(1)}, u32[]{:S(2)}, u32[]{:S(2)}) collective-permute-start(bf16[64,256]{1,0:T(8,128)(2,1)S(1)} %bitcast.150), channel_id=1, source_target_pairs={{1,0},{2,1},{3,2},{4,3},{5,4},{6,5},{7,6},{8,7},{9,8},{10,9},{11,1... | collective-permute-start | bytes 98312 | tf_op jit(solution)/shard_map/ppermute | solution.py:20
  193.0 6.4 %collective-permute-start.19 = (bf16[18,256]{1,0:T(8,128)(2,1)S(1)}, bf16[18,256]{1,0:T(8,128)(2,1)S(1)}, u32[]{:S(2)}, u32[]{:S(2)}) collective-permute-start(bf16[18,256]{1,0:T(8,128)(2,1)S(1)} %bitcast.148), channel_id=1, source_target_pairs={{0,64},{64,128},{128,192},{192,256},{256,320},{320,384},{384,448},... | collective-permute-start | bytes 27656 | tf_op jit(solution)/shard_map/ppermute | solution.py:17
  194.3 5.1 %collective-permute-start.20 = (bf16[18,256]{1,0:T(8,128)(2,1)S(1)}, bf16[18,256]{1,0:T(8,128)(2,1)S(1)}, u32[]{:S(2)}, u32[]{:S(2)}) collective-permute-start(bf16[18,256]{1,0:T(8,128)(2,1)S(1)} %bitcast.146), channel_id=1, source_target_pairs={{64,0},{128,64},{192,128},{256,192},{320,256},{384,320},{448,384},... | collective-permute-start | bytes 27656 | tf_op jit(solution)/shard_map/ppermute | solution.py:20
  195.6 9.8 %collective-permute-start.21 = (bf16[2,18,256]{2,1,0:T(8,128)(2,1)S(1)}, bf16[2,18,256]{2,1,0:T(8,128)(2,1)S(1)}, u32[]{:S(2)}, u32[]{:S(2)}) collective-permute-start(bf16[2,18,256]{2,1,0:T(8,128)(2,1)S(1)} %pad_maximum_fusion.2), channel_id=1, source_target_pairs={{32,0},{33,1},{34,2},{35,3},{36,4},{37,5},{38,6},{39,7},{40,8},{41... | collective-permute-start | bytes 55304 | tf_op jit(solution)/shard_map/ppermute | solution.py:31
  220.5 8.5 %collective-permute-start.22 = (f32[32,1152]{1,0:T(8,128)S(1)}, f32[32,1152]{1,0:T(8,128)S(1)}, u32[]{:S(2)}, u32[]{:S(2)}) collective-permute-start(f32[32,1152]{1,0:T(8,128)S(1)} %constant_dynamic-slice_fusion.5), channel_id=1, source_target_pairs={{0,32},{1,33},{2,34},{3,35},{4,36},{5,37},{6,38},{7,39},{8,40},{9,... | collective-permute-start | bytes 442376 | tf_op jit(solution)/shard_map/ppermute | solution.py:44
  229.1 6.3 %collective-permute-start.23 = (f32[32,576]{1,0:T(8,128)S(1)}, f32[32,576]{1,0:T(8,128)S(1)}, u32[]{:S(2)}, u32[]{:S(2)}) collective-permute-start(f32[32,576]{1,0:T(8,128)S(1)} %constant_dynamic-slice_fusion.4), channel_id=1, source_target_pairs={{0,16},{1,17},{2,18},{3,19},{4,20},{5,21},{6,22},{7,23},{8,24},{9,... | collective-permute-start | bytes 221192 | tf_op jit(solution)/shard_map/ppermute | solution.py:44
  235.7 9.9 %collective-permute-start.24 = (f32[32,288]{1,0:T(8,128)S(1)}, f32[32,288]{1,0:T(8,128)S(1)}, u32[]{:S(2)}, u32[]{:S(2)}) collective-permute-start(f32[32,288]{1,0:T(8,128)S(1)} %constant_dynamic-slice_fusion.3), channel_id=1, source_target_pairs={{0,8},{1,9},{2,10},{3,11},{4,12},{5,13},{6,14},{7,15},{8,0},{9,1},... | collective-permute-start | bytes 110600 | tf_op jit(solution)/shard_map/ppermute | solution.py:44
  245.7 9.7 %collective-permute-start.25 = (f32[32,144]{1,0:T(8,128)S(1)}, f32[32,144]{1,0:T(8,128)S(1)}, u32[]{:S(2)}, u32[]{:S(2)}) collective-permute-start(f32[32,144]{1,0:T(8,128)S(1)} %constant_dynamic-slice_fusion.2), channel_id=1, source_target_pairs={{0,4},{1,5},{2,6},{3,7},{4,0},{5,1},{6,2},{7,3},{8,12},{9,13},{10,... | collective-permute-start | bytes 55304 | tf_op jit(solution)/shard_map/ppermute | solution.py:44
  255.6 6.5 %collective-permute-start.26 = (f32[32,72]{1,0:T(8,128)S(1)}, f32[32,72]{1,0:T(8,128)S(1)}, u32[]{:S(2)}, u32[]{:S(2)}) collective-permute-start(f32[32,72]{1,0:T(8,128)S(1)} %constant_dynamic-slice_fusion.1), channel_id=1, source_target_pairs={{0,2},{1,3},{2,0},{3,1},{4,6},{5,7},{6,4},{7,5},{8,10},{9,11},{10,... | collective-permute-start | bytes 27656 | tf_op jit(solution)/shard_map/ppermute | solution.py:44
  262.3 5.6 %collective-permute-start.27 = (f32[32,36]{1,0:T(8,128)S(1)}, f32[32,36]{1,0:T(8,128)S(1)}, u32[]{:S(2)}, u32[]{:S(2)}) collective-permute-start(f32[32,36]{1,0:T(8,128)S(1)} %constant_dynamic-slice_fusion), channel_id=1, source_target_pairs={{0,1},{1,0},{2,3},{3,2},{4,5},{5,4},{6,7},{7,6},{8,9},{9,8},{10,11... | collective-permute-start | bytes 13832 | tf_op jit(solution)/shard_map/ppermute | solution.py:44
  (6 other events, 7.4 us)
Sparse Core Ops, SparseCore 0:
  174.1 44.9 reduce-scatter.1

commit v12 on v9

--- a/solution.py
+++ b/solution.py
@@ -89,7 +89,7 @@
     local_stats = jnp.concatenate(
         [jnp.sum(conv_out, 0).reshape(G, -1).sum(1), jnp.sum(conv_out * conv_out, 0).reshape(G, -1).sum(1)]
     )
-    stats = butterfly_sum(local_stats)
+    stats = butterfly_sum(jnp.pad(local_stats, (0, 2 * channels - 2 * G)))[: 2 * G]
     mean = stats[:G] / count
     var = stats[G:] / count - mean * mean
     rstd = lax.rsqrt(var + 1e-05)

time: 272 us -> 271 us (level)
    unnamed x1 -> x0, blocking collectives: 14.5 us -> none
    all_gather x1 -> x2, blocking collectives: 12.7 us -> 26.8 us  [butterfly_sum(): value = jnp.sum(lax.all_gather(value, 'lat'), 0)]
  transfers between devices with their start and end apart: 29 -> 29, of which waited for: 21 -> 23; matrix products, arithmetic and copies ran while one was open for 5% -> 5% of each run, Pallas kernels for 0% -> 0%
where the time goes in v12:
time: 271 us; the launch traced here: 270 us
  starting transfers between devices  116 us (43%)
  waiting for transfers between devices  75.8 us (28%)
  blocking collectives  26.8 us (10%)
  matrix products  17.9 us (7%)
  between operations  14.8 us (5%)
  local copies, waits for them, and re-layouts  11.2 us (4%)
  other arithmetic  7.79 us (3%)
    ppermute x18, starting transfers between devices, exchange(): return lax.ppermute(block, axis, [(i, i ^ 1 << bit) for i in range(peers)])  72.2 us
    ppermute x18, waiting for transfers between devices, exchange(): return lax.ppermute(block, axis, [(i, i ^ 1 << bit) for i in range(peers)])  52.3 us
    ppermute x4, starting transfers between devices, with_halo(): lax.ppermute(jnp.squeeze(initial, dim), axis, down)  28.2 us
    all_gather x2, blocking collectives, butterfly_sum(): value = jnp.sum(lax.all_gather(value, 'lat'), 0)  26.8 us
    reduce_scatter x1, waiting for transfers between devices, local(): owned_cols = lax.psum_scatter(term, 'lat', scatter_dimension=0, tiled=True)  16.5 us
    ppermute x4, starting transfers between devices, with_halo(): lax.ppermute(jnp.squeeze(last, dim), axis, up)  8.78 us
    conv_general_dilated x1, matrix products, local(): lax.conv_general_dilated(merged[None], dconv.reshape(height, breadth, 1,...  7.17 us
    ppermute x2, starting transfers between devices, passed_along(): return lax.ppermute(block, axis, route)  6.52 us
  transfers between devices with their start and end apart: 29, of which 23 were waited for; matrix products, arithmetic and copies ran while one was open for 5% of the time, Pallas kernels for 0%

profile of v12, /device:TPU:6, one launch (start us, length us, event | category | flops | bytes accessed | tf_op | source)
XLA Modules:
  0.0 270.1 jit_solution(16858224228879902246)
XLA Ops:
  8.4 4.3 %collective-permute-start = (bf16[64,256]{1,0:T(8,128)(2,1)S(1)}, bf16[64,256]{1,0:T(8,128)(2,1)S(1)}, u32[]{:S(2)}, u32[]{:S(2)}) collective-permute-start(bf16[64,256]{1,0:T(8,128)(2,1)S(1)} %bitcast.155), channel_id=1, source_target_pairs={{0,1},{1,2},{2,3},{3,4},{4,5},{5,6},{6,7},{7,8},{8,9},{9,10},{10,1... | collective-permute-start | bytes 98312 | tf_op jit(solution)/shard_map/ppermute | solution.py:17
  12.7 14.1 %collective-permute-start.1 = (bf16[64,256]{1,0:T(8,128)(2,1)S(1)}, bf16[64,256]{1,0:T(8,128)(2,1)S(1)}, u32[]{:S(2)}, u32[]{:S(2)}) collective-permute-start(bf16[64,256]{1,0:T(8,128)(2,1)S(1)} %bitcast.157), channel_id=1, source_target_pairs={{1,0},{2,1},{3,2},{4,3},{5,4},{6,5},{7,6},{8,7},{9,8},{10,9},{11,1... | collective-permute-start | bytes 98312 | tf_op jit(solution)/shard_map/ppermute | solution.py:18
  31.8 3.2 %collective-permute-start.4 = (bf16[2,18,256]{2,1,0:T(8,128)(2,1)S(1)}, bf16[2,18,256]{2,1,0:T(8,128)(2,1)S(1)}, u32[]{:S(2)}, u32[]{:S(2)}) collective-permute-start(bf16[2,18,256]{2,1,0:T(8,128)(2,1)S(1)} %pad_maximum_fusion.1), channel_id=1, source_target_pairs={{32,0},{33,1},{34,2},{35,3},{36,4},{37,5},{38,6},{39,7},{40,8},{41... | collective-permute-start | bytes 55304 | tf_op jit(solution)/shard_map/ppermute | solution.py:29
  35.5 3.5 %collective-permute-done.4 = bf16[2,18,256]{2,1,0:T(8,128)(2,1)S(1)} collective-permute-done((bf16[2,18,256]{2,1,0:T(8,128)(2,1)S(1)}, bf16[2,18,256]{2,1,0:T(8,128)(2,1)S(1)}, u32[]{:S(2)}, u32[]{:S(2)}) %collective-permute-start.4) | collective-permute-done | bytes 18464 | tf_op jit(solution)/shard_map/ppermute | solution.py:29
  40.6 3.2 %select_reduce_fusion.1 = (f32[256]{0:T(256)S(1)}, f32[256]{0:T(256)S(1)}, f32[64,8,3,256]{3,1,2,0:T(8,128)}) fusion(pred[8,3]{0,1:T(4,128)(4,1)S(1)} %copy-done.7, bf16[3,3,256,256]{3,2,1,0:T(8,128)(2,1)S(1)} %copy-done.3, bf16[66,1,7,2,256]{4,2,3,0,1:T(8,128)(2,1)S(1)} %slice.210, bf16[66,1,8,3,256]{4,2,3,0,1:T(8,128)(2,1)S(1)} %copy.64), kind=kOutput, calls=%fused_computation.4 | convolution fusion | flops 1818353152 | bytes 4038680 | tf_op jit(solution)/shard_map/conv_general_dilated | solution.py:70
  44.3 14.1 %all-gather.2 = f32[8,1,512]{2,1,0:T(1,128)S(1)} all-gather(f32[1,1,512]{2,1,0:T(1,128)S(1)} %bitcast.162), channel_id=2, replica_groups=mesh['lat'=8,'lon'=64] {'lat'}, dimensions={0}, use_global_device_ids=true | all-gather | bytes 18432 | tf_op jit(solution)/shard_map/all_gather | solution.py:53
  60.4 3.6 %collective-permute-done.5 = f32[512]{0:T(512)S(1)} collective-permute-done((f32[512]{0:T(512)S(1)}, f32[512]{0:T(512)S(1)}, u32[]{:S(2)}, u32[]{:S(2)}) %collective-permute-start.5) | collective-permute-done | bytes 2080 | tf_op jit(solution)/shard_map/ppermute | solution.py:42
  65.9 4.4 %collective-permute-done.6 = f32[512]{0:T(512)S(1)} collective-permute-done((f32[512]{0:T(512)S(1)}, f32[512]{0:T(512)S(1)}, u32[]{:S(2)}, u32[]{:S(2)}) %collective-permute-start.6) | collective-permute-done | bytes 2080 | tf_op jit(solution)/shard_map/ppermute | solution.py:42
  70.3 5.5 %collective-permute-start.7 = (f32[512]{0:T(512)S(1)}, f32[512]{0:T(512)S(1)}, u32[]{:S(2)}, u32[]{:S(2)}) collective-permute-start(f32[512]{0:T(512)S(1)} %add.172), channel_id=1, source_target_pairs={{0,4},{1,5},{2,6},{3,7},{4,0},{5,1},{6,2},{7,3},{8,12},{9,13},{10,... | collective-permute-start | bytes 6152 | tf_op jit(solution)/shard_map/ppermute | solution.py:42
  75.9 3.8 %collective-permute-done.7 = f32[512]{0:T(512)S(1)} collective-permute-done((f32[512]{0:T(512)S(1)}, f32[512]{0:T(512)S(1)}, u32[]{:S(2)}, u32[]{:S(2)}) %collective-permute-start.7) | collective-permute-done | bytes 2080 | tf_op jit(solution)/shard_map/ppermute | solution.py:42
  79.7 5.6 %collective-permute-start.8 = (f32[512]{0:T(512)S(1)}, f32[512]{0:T(512)S(1)}, u32[]{:S(2)}, u32[]{:S(2)}) collective-permute-start(f32[512]{0:T(512)S(1)} %add.173), channel_id=1, source_target_pairs={{0,8},{1,9},{2,10},{3,11},{4,12},{5,13},{6,14},{7,15},{8,0},{9,1},... | collective-permute-start | bytes 6152 | tf_op jit(solution)/shard_map/ppermute | solution.py:42
  85.4 3.8 %collective-permute-done.8 = f32[512]{0:T(512)S(1)} collective-permute-done((f32[512]{0:T(512)S(1)}, f32[512]{0:T(512)S(1)}, u32[]{:S(2)}, u32[]{:S(2)}) %collective-permute-start.8) | collective-permute-done | bytes 2080 | tf_op jit(solution)/shard_map/ppermute | solution.py:42
  94.6 3.8 %collective-permute-start.10 = (f32[512]{0:T(512)S(1)}, f32[512]{0:T(512)S(1)}, u32[]{:S(2)}, u32[]{:S(2)}) collective-permute-start(f32[512]{0:T(512)S(1)} %add.175), channel_id=1, source_target_pairs={{0,32},{1,33},{2,34},{3,35},{4,36},{5,37},{6,38},{7,39},{8,40},{9,... | collective-permute-start | bytes 6152 | tf_op jit(solution)/shard_map/ppermute | solution.py:42
  102.9 12.7 %all-gather.3 = f32[8,1,512]{2,1,0:T(1,128)S(1)} all-gather(f32[1,1,512]{2,1,0:T(1,128)S(1)} %bitcast.163), channel_id=3, replica_groups=mesh['lat'=8,'lon'=64] {'lat'}, dimensions={0}, use_global_device_ids=true | all-gather | bytes 18432 | tf_op jit(solution)/shard_map/all_gather | solution.py:53
  117.5 3.6 %collective-permute-done.11 = f32[512]{0:T(512)S(1)} collective-permute-done((f32[512]{0:T(512)S(1)}, f32[512]{0:T(512)S(1)}, u32[]{:S(2)}, u32[]{:S(2)}) %collective-permute-start.11) | collective-permute-done | bytes 2080 | tf_op jit(solution)/shard_map/ppermute | solution.py:42
  123.7 3.8 %collective-permute-done.12 = f32[512]{0:T(512)S(1)} collective-permute-done((f32[512]{0:T(512)S(1)}, f32[512]{0:T(512)S(1)}, u32[]{:S(2)}, u32[]{:S(2)}) %collective-permute-start.12) | collective-permute-done | bytes 2080 | tf_op jit(solution)/shard_map/ppermute | solution.py:42
  127.5 5.6 %collective-permute-start.13 = (f32[512]{0:T(512)S(1)}, f32[512]{0:T(512)S(1)}, u32[]{:S(2)}, u32[]{:S(2)}) collective-permute-start(f32[512]{0:T(512)S(1)} %add.185), channel_id=1, source_target_pairs={{0,4},{1,5},{2,6},{3,7},{4,0},{5,1},{6,2},{7,3},{8,12},{9,13},{10,... | collective-permute-start | bytes 6152 | tf_op jit(solution)/shard_map/ppermute | solution.py:42
  133.1 3.7 %collective-permute-done.13 = f32[512]{0:T(512)S(1)} collective-permute-done((f32[512]{0:T(512)S(1)}, f32[512]{0:T(512)S(1)}, u32[]{:S(2)}, u32[]{:S(2)}) %collective-permute-start.13) | collective-permute-done | bytes 2080 | tf_op jit(solution)/shard_map/ppermute | solution.py:42
  136.8 5.6 %collective-permute-start.14 = (f32[512]{0:T(512)S(1)}, f32[512]{0:T(512)S(1)}, u32[]{:S(2)}, u32[]{:S(2)}) collective-permute-start(f32[512]{0:T(512)S(1)} %add.186), channel_id=1, source_target_pairs={{0,8},{1,9},{2,10},{3,11},{4,12},{5,13},{6,14},{7,15},{8,0},{9,1},... | collective-permute-start | bytes 6152 | tf_op jit(solution)/shard_map/ppermute | solution.py:42
  142.5 3.7 %collective-permute-done.14 = f32[512]{0:T(512)S(1)} collective-permute-done((f32[512]{0:T(512)S(1)}, f32[512]{0:T(512)S(1)}, u32[]{:S(2)}, u32[]{:S(2)}) %collective-permute-start.14) | collective-permute-done | bytes 2080 | tf_op jit(solution)/shard_map/ppermute | solution.py:42
  151.7 3.9 %collective-permute-start.16 = (f32[512]{0:T(512)S(1)}, f32[512]{0:T(512)S(1)}, u32[]{:S(2)}, u32[]{:S(2)}) collective-permute-start(f32[512]{0:T(512)S(1)} %add.188), channel_id=1, source_target_pairs={{0,32},{1,33},{2,34},{3,35},{4,36},{5,37},{6,38},{7,39},{8,40},{9,... | collective-permute-start | bytes 6152 | tf_op jit(solution)/shard_map/ppermute | solution.py:42
  155.6 3.0 %collective-permute-done.16 = f32[512]{0:T(512)S(1)} collective-permute-done((f32[512]{0:T(512)S(1)}, f32[512]{0:T(512)S(1)}, u32[]{:S(2)}, u32[]{:S(2)}) %collective-permute-start.16) | collective-permute-done | bytes 2080 | tf_op jit(solution)/shard_map/ppermute | solution.py:42
  161.8 7.2 %fusion.14 = f32[256,3,3,256]{3,0,2,1:T(8,128)} fusion(bf16[1,66,18,256]{3,2,1,0:T(8,128)(2,1)S(1)} %fusion.49, bf16[64,16,1,256]{3,1,0,2:T(8,128)(2,1)S(1)} %bitcast.137), kind=kOutput, calls=%fused_computation.19 | convolution fusion | flops 1207959552 | bytes 3491840 | tf_op jit(solution)/shard_map/conv_general_dilated | solution.py:121
  171.1 11.5 %collective-permute-start.18 = (bf16[64,256]{1,0:T(8,128)(2,1)S(1)}, bf16[64,256]{1,0:T(8,128)(2,1)S(1)}, u32[]{:S(2)}, u32[]{:S(2)}) collective-permute-start(bf16[64,256]{1,0:T(8,128)(2,1)S(1)} %bitcast.153), channel_id=1, source_target_pairs={{1,0},{2,1},{3,2},{4,3},{5,4},{6,5},{7,6},{8,7},{9,8},{10,9},{11,1... | collective-permute-start | bytes 98312 | tf_op jit(solution)/shard_map/ppermute | solution.py:18
  187.3 3.4 %collective-permute-start.21 = (bf16[2,18,256]{2,1,0:T(8,128)(2,1)S(1)}, bf16[2,18,256]{2,1,0:T(8,128)(2,1)S(1)}, u32[]{:S(2)}, u32[]{:S(2)}) collective-permute-start(bf16[2,18,256]{2,1,0:T(8,128)(2,1)S(1)} %pad_maximum_fusion.2), channel_id=1, source_target_pairs={{32,0},{33,1},{34,2},{35,3},{36,4},{37,5},{38,6},{39,7},{40,8},{41... | collective-permute-start | bytes 55304 | tf_op jit(solution)/shard_map/ppermute | solution.py:29
  196.9 16.5 %reduce-scatter.2.cloned.1.call-done = f32[32,3,3,256]{3,0,2,1:T(8,128)} async-done(((f32[256,3,3,256]{3,0,2,1:T(8,128)}), f32[32,3,3,256]{3,0,2,1:T(8,128)}) %reduce-scatter.2.cloned.1.call-update) | async-done | bytes 294928 | tf_op jit(solution)/shard_map/reduce_scatter | solution.py:129
  214.9 3.7 %collective-permute-start.22 = (f32[32,1152]{1,0:T(8,128)S(1)}, f32[32,1152]{1,0:T(8,128)S(1)}, u32[]{:S(2)}, u32[]{:S(2)}) collective-permute-start(f32[32,1152]{1,0:T(8,128)S(1)} %constant_dynamic-slice_fusion.5), channel_id=1, source_target_pairs={{0,32},{1,33},{2,34},{3,35},{4,36},{5,37},{6,38},{7,39},{8,40},{9,... | collective-permute-start | bytes 442376 | tf_op jit(solution)/shard_map/ppermute | solution.py:42
  219.6 3.8 %collective-permute-done.22 = f32[32,1152]{1,0:T(8,128)S(1)} collective-permute-done((f32[32,1152]{1,0:T(8,128)S(1)}, f32[32,1152]{1,0:T(8,128)S(1)}, u32[]{:S(2)}, u32[]{:S(2)}) %collective-permute-start.22) | collective-permute-done | bytes 147488 | tf_op jit(solution)/shard_map/ppermute | solution.py:42
  230.1 6.0 %collective-permute-start.24 = (f32[32,288]{1,0:T(8,128)S(1)}, f32[32,288]{1,0:T(8,128)S(1)}, u32[]{:S(2)}, u32[]{:S(2)}) collective-permute-start(f32[32,288]{1,0:T(8,128)S(1)} %constant_dynamic-slice_fusion.3), channel_id=1, source_target_pairs={{0,8},{1,9},{2,10},{3,11},{4,12},{5,13},{6,14},{7,15},{8,0},{9,1},... | collective-permute-start | bytes 110600 | tf_op jit(solution)/shard_map/ppermute | solution.py:42
  240.1 8.1 %collective-permute-start.25 = (f32[32,144]{1,0:T(8,128)S(1)}, f32[32,144]{1,0:T(8,128)S(1)}, u32[]{:S(2)}, u32[]{:S(2)}) collective-permute-start(f32[32,144]{1,0:T(8,128)S(1)} %constant_dynamic-slice_fusion.2), channel_id=1, source_target_pairs={{0,4},{1,5},{2,6},{3,7},{4,0},{5,1},{6,2},{7,3},{8,12},{9,13},{10,... | collective-permute-start | bytes 55304 | tf_op jit(solution)/shard_map/ppermute | solution.py:42
  250.3 4.6 %collective-permute-start.26 = (f32[32,72]{1,0:T(8,128)S(1)}, f32[32,72]{1,0:T(8,128)S(1)}, u32[]{:S(2)}, u32[]{:S(2)}) collective-permute-start(f32[32,72]{1,0:T(8,128)S(1)} %constant_dynamic-slice_fusion.1), channel_id=1, source_target_pairs={{0,2},{1,3},{2,0},{3,1},{4,6},{5,7},{6,4},{7,5},{8,10},{9,11},{10,... | collective-permute-start | bytes 27656 | tf_op jit(solution)/shard_map/ppermute | solution.py:42
  257.0 3.4 %collective-permute-start.27 = (f32[32,36]{1,0:T(8,128)S(1)}, f32[32,36]{1,0:T(8,128)S(1)}, u32[]{:S(2)}, u32[]{:S(2)}) collective-permute-start(f32[32,36]{1,0:T(8,128)S(1)} %constant_dynamic-slice_fusion), channel_id=1, source_target_pairs={{0,1},{1,0},{2,3},{3,2},{4,5},{5,4},{6,7},{7,6},{8,9},{9,8},{10,11... | collective-permute-start | bytes 13832 | tf_op jit(solution)/shard_map/ppermute | solution.py:42
  (143 shorter events, 68.4 us)
Async XLA Ops:
  7.2 27.9 %copy-start = (bf16[64,16,256]{2,1,0:T(8,128)(2,1)S(1)}, bf16[64,16,256]{2,1,0:T(8,128)(2,1)}, u32[]{:S(2)}) copy-start(bf16[64,16,256]{2,1,0:T(8,128)(2,1)} %param.13) | copy-start | bytes 1572868
  7.2 206.3 %reduce-scatter.2.cloned.1.call-start = ((), (), s32[]{:S(2)}) async-start(), calls=%async_computation.1 | async-start | bytes 2654208 | tf_op jit(solution)/shard_map/reduce_scatter | solution.py:129
  8.4 18.6 %collective-permute-start = (bf16[64,256]{1,0:T(8,128)(2,1)S(1)}, bf16[64,256]{1,0:T(8,128)(2,1)S(1)}, u32[]{:S(2)}, u32[]{:S(2)}) collective-permute-start(bf16[64,256]{1,0:T(8,128)(2,1)S(1)} %bitcast.155), channel_id=1, source_target_pairs={{0,1},{1,2},{2,3},{3,4},{4,5},{5,6},{6,7},{7,8},{8,9},{9,10},{10,1... | collective-permute-start | bytes 98312 | tf_op jit(solution)/shard_map/ppermute | solution.py:17
  12.7 15.7 %collective-permute-start.1 = (bf16[64,256]{1,0:T(8,128)(2,1)S(1)}, bf16[64,256]{1,0:T(8,128)(2,1)S(1)}, u32[]{:S(2)}, u32[]{:S(2)}) collective-permute-start(bf16[64,256]{1,0:T(8,128)(2,1)S(1)} %bitcast.157), channel_id=1, source_target_pairs={{1,0},{2,1},{3,2},{4,3},{5,4},{6,5},{7,6},{8,7},{9,8},{10,9},{11,1... | collective-permute-start | bytes 98312 | tf_op jit(solution)/shard_map/ppermute | solution.py:18
  29.2 5.8 %collective-permute-start.2 = (bf16[18,256]{1,0:T(8,128)(2,1)S(1)}, bf16[18,256]{1,0:T(8,128)(2,1)S(1)}, u32[]{:S(2)}, u32[]{:S(2)}) collective-permute-start(bf16[18,256]{1,0:T(8,128)(2,1)S(1)} %bitcast.149), channel_id=1, source_target_pairs={{0,64},{64,128},{128,192},{192,256},{256,320},{320,384},{384,448},... | collective-permute-start | bytes 27656 | tf_op jit(solution)/shard_map/ppermute | solution.py:17
  30.5 4.5 %collective-permute-start.3 = (bf16[18,256]{1,0:T(8,128)(2,1)S(1)}, bf16[18,256]{1,0:T(8,128)(2,1)S(1)}, u32[]{:S(2)}, u32[]{:S(2)}) collective-permute-start(bf16[18,256]{1,0:T(8,128)(2,1)S(1)} %bitcast.147), channel_id=1, source_target_pairs={{64,0},{128,64},{192,128},{256,192},{320,256},{384,320},{448,384},... | collective-permute-start | bytes 27656 | tf_op jit(solution)/shard_map/ppermute | solution.py:18
  31.8 7.2 %collective-permute-start.4 = (bf16[2,18,256]{2,1,0:T(8,128)(2,1)S(1)}, bf16[2,18,256]{2,1,0:T(8,128)(2,1)S(1)}, u32[]{:S(2)}, u32[]{:S(2)}) collective-permute-start(bf16[2,18,256]{2,1,0:T(8,128)(2,1)S(1)} %pad_maximum_fusion.1), channel_id=1, source_target_pairs={{32,0},{33,1},{34,2},{35,3},{36,4},{37,5},{38,6},{39,7},{40,8},{41... | collective-permute-start | bytes 55304 | tf_op jit(solution)/shard_map/ppermute | solution.py:29
  58.5 5.5 %collective-permute-start.5 = (f32[512]{0:T(512)S(1)}, f32[512]{0:T(512)S(1)}, u32[]{:S(2)}, u32[]{:S(2)}) collective-permute-start(f32[512]{0:T(512)S(1)} %reduce_sum.94), channel_id=1, source_target_pairs={{0,1},{1,0},{2,3},{3,2},{4,5},{5,4},{6,7},{7,6},{8,9},{9,8},{10,11... | collective-permute-start | bytes 6152 | tf_op jit(solution)/shard_map/ppermute | solution.py:42
  64.0 6.4 %collective-permute-start.6 = (f32[512]{0:T(512)S(1)}, f32[512]{0:T(512)S(1)}, u32[]{:S(2)}, u32[]{:S(2)}) collective-permute-start(f32[512]{0:T(512)S(1)} %add.171), channel_id=1, source_target_pairs={{0,2},{1,3},{2,0},{3,1},{4,6},{5,7},{6,4},{7,5},{8,10},{9,11},{10,... | collective-permute-start | bytes 6152 | tf_op jit(solution)/shard_map/ppermute | solution.py:42
  70.3 9.4 %collective-permute-start.7 = (f32[512]{0:T(512)S(1)}, f32[512]{0:T(512)S(1)}, u32[]{:S(2)}, u32[]{:S(2)}) collective-permute-start(f32[512]{0:T(512)S(1)} %add.172), channel_id=1, source_target_pairs={{0,4},{1,5},{2,6},{3,7},{4,0},{5,1},{6,2},{7,3},{8,12},{9,13},{10,... | collective-permute-start | bytes 6152 | tf_op jit(solution)/shard_map/ppermute | solution.py:42
  79.7 9.4 %collective-permute-start.8 = (f32[512]{0:T(512)S(1)}, f32[512]{0:T(512)S(1)}, u32[]{:S(2)}, u32[]{:S(2)}) collective-permute-start(f32[512]{0:T(512)S(1)} %add.173), channel_id=1, source_target_pairs={{0,8},{1,9},{2,10},{3,11},{4,12},{5,13},{6,14},{7,15},{8,0},{9,1},... | collective-permute-start | bytes 6152 | tf_op jit(solution)/shard_map/ppermute | solution.py:42
  89.1 5.5 %collective-permute-start.9 = (f32[512]{0:T(512)S(1)}, f32[512]{0:T(512)S(1)}, u32[]{:S(2)}, u32[]{:S(2)}) collective-permute-start(f32[512]{0:T(512)S(1)} %add.174), channel_id=1, source_target_pairs={{0,16},{1,17},{2,18},{3,19},{4,20},{5,21},{6,22},{7,23},{8,24},{9,... | collective-permute-start | bytes 6152 | tf_op jit(solution)/shard_map/ppermute | solution.py:42
  94.6 7.0 %collective-permute-start.10 = (f32[512]{0:T(512)S(1)}, f32[512]{0:T(512)S(1)}, u32[]{:S(2)}, u32[]{:S(2)}) collective-permute-start(f32[512]{0:T(512)S(1)} %add.175), channel_id=1, source_target_pairs={{0,32},{1,33},{2,34},{3,35},{4,36},{5,37},{6,38},{7,39},{8,40},{9,... | collective-permute-start | bytes 6152 | tf_op jit(solution)/shard_map/ppermute | solution.py:42
  100.3 1.7 copy-start.1
  100.3 1.7 copy-start.5
  115.6 5.5 %collective-permute-start.11 = (f32[512]{0:T(512)S(1)}, f32[512]{0:T(512)S(1)}, u32[]{:S(2)}, u32[]{:S(2)}) collective-permute-start(f32[512]{0:T(512)S(1)} %reduce_sum.97), channel_id=1, source_target_pairs={{0,1},{1,0},{2,3},{3,2},{4,5},{5,4},{6,7},{7,6},{8,9},{9,8},{10,11... | collective-permute-start | bytes 6152 | tf_op jit(solution)/shard_map/ppermute | solution.py:42
  121.1 6.4 %collective-permute-start.12 = (f32[512]{0:T(512)S(1)}, f32[512]{0:T(512)S(1)}, u32[]{:S(2)}, u32[]{:S(2)}) collective-permute-start(f32[512]{0:T(512)S(1)} %add.184), channel_id=1, source_target_pairs={{0,2},{1,3},{2,0},{3,1},{4,6},{5,7},{6,4},{7,5},{8,10},{9,11},{10,... | collective-permute-start | bytes 6152 | tf_op jit(solution)/shard_map/ppermute | solution.py:42
  127.5 9.4 %collective-permute-start.13 = (f32[512]{0:T(512)S(1)}, f32[512]{0:T(512)S(1)}, u32[]{:S(2)}, u32[]{:S(2)}) collective-permute-start(f32[512]{0:T(512)S(1)} %add.185), channel_id=1, source_target_pairs={{0,4},{1,5},{2,6},{3,7},{4,0},{5,1},{6,2},{7,3},{8,12},{9,13},{10,... | collective-permute-start | bytes 6152 | tf_op jit(solution)/shard_map/ppermute | solution.py:42
  136.8 9.4 %collective-permute-start.14 = (f32[512]{0:T(512)S(1)}, f32[512]{0:T(512)S(1)}, u32[]{:S(2)}, u32[]{:S(2)}) collective-permute-start(f32[512]{0:T(512)S(1)} %add.186), channel_id=1, source_target_pairs={{0,8},{1,9},{2,10},{3,11},{4,12},{5,13},{6,14},{7,15},{8,0},{9,1},... | collective-permute-start | bytes 6152 | tf_op jit(solution)/shard_map/ppermute | solution.py:42
  146.2 5.5 %collective-permute-start.15 = (f32[512]{0:T(512)S(1)}, f32[512]{0:T(512)S(1)}, u32[]{:S(2)}, u32[]{:S(2)}) collective-permute-start(f32[512]{0:T(512)S(1)} %add.187), channel_id=1, source_target_pairs={{0,16},{1,17},{2,18},{3,19},{4,20},{5,21},{6,22},{7,23},{8,24},{9,... | collective-permute-start | bytes 6152 | tf_op jit(solution)/shard_map/ppermute | solution.py:42
  151.7 7.0 %collective-permute-start.16 = (f32[512]{0:T(512)S(1)}, f32[512]{0:T(512)S(1)}, u32[]{:S(2)}, u32[]{:S(2)}) collective-permute-start(f32[512]{0:T(512)S(1)} %add.188), channel_id=1, source_target_pairs={{0,32},{1,33},{2,34},{3,35},{4,36},{5,37},{6,38},{7,39},{8,40},{9,... | collective-permute-start | bytes 6152 | tf_op jit(solution)/shard_map/ppermute | solution.py:42
  169.2 13.5 %collective-permute-start.17 = (bf16[64,256]{1,0:T(8,128)(2,1)S(1)}, bf16[64,256]{1,0:T(8,128)(2,1)S(1)}, u32[]{:S(2)}, u32[]{:S(2)}) collective-permute-start(bf16[64,256]{1,0:T(8,128)(2,1)S(1)} %bitcast.151), channel_id=1, source_target_pairs={{0,1},{1,2},{2,3},{3,4},{4,5},{5,6},{6,7},{7,8},{8,9},{9,10},{10,1... | collective-permute-start | bytes 98312 | tf_op jit(solution)/shard_map/ppermute | solution.py:17
  171.1 13.5 %collective-permute-start.18 = (bf16[64,256]{1,0:T(8,128)(2,1)S(1)}, bf16[64,256]{1,0:T(8,128)(2,1)S(1)}, u32[]{:S(2)}, u32[]{:S(2)}) collective-permute-start(bf16[64,256]{1,0:T(8,128)(2,1)S(1)} %bitcast.153), channel_id=1, source_target_pairs={{1,0},{2,1},{3,2},{4,3},{5,4},{6,5},{7,6},{8,7},{9,8},{10,9},{11,1... | collective-permute-start | bytes 98312 | tf_op jit(solution)/shard_map/ppermute | solution.py:18
  184.7 6.0 %collective-permute-start.19 = (bf16[18,256]{1,0:T(8,128)(2,1)S(1)}, bf16[18,256]{1,0:T(8,128)(2,1)S(1)}, u32[]{:S(2)}, u32[]{:S(2)}) collective-permute-start(bf16[18,256]{1,0:T(8,128)(2,1)S(1)} %bitcast.150), channel_id=1, source_target_pairs={{0,64},{64,128},{128,192},{192,256},{256,320},{320,384},{384,448},... | collective-permute-start | bytes 27656 | tf_op jit(solution)/shard_map/ppermute | solution.py:17
  186.0 4.7 %collective-permute-start.20 = (bf16[18,256]{1,0:T(8,128)(2,1)S(1)}, bf16[18,256]{1,0:T(8,128)(2,1)S(1)}, u32[]{:S(2)}, u32[]{:S(2)}) collective-permute-start(bf16[18,256]{1,0:T(8,128)(2,1)S(1)} %bitcast.148), channel_id=1, source_target_pairs={{64,0},{128,64},{192,128},{256,192},{320,256},{384,320},{448,384},... | collective-permute-start | bytes 27656 | tf_op jit(solution)/shard_map/ppermute | solution.py:18
  187.3 9.5 %collective-permute-start.21 = (bf16[2,18,256]{2,1,0:T(8,128)(2,1)S(1)}, bf16[2,18,256]{2,1,0:T(8,128)(2,1)S(1)}, u32[]{:S(2)}, u32[]{:S(2)}) collective-permute-start(bf16[2,18,256]{2,1,0:T(8,128)(2,1)S(1)} %pad_maximum_fusion.2), channel_id=1, source_target_pairs={{32,0},{33,1},{34,2},{35,3},{36,4},{37,5},{38,6},{39,7},{40,8},{41... | collective-permute-start | bytes 55304 | tf_op jit(solution)/shard_map/ppermute | solution.py:29
  214.9 8.5 %collective-permute-start.22 = (f32[32,1152]{1,0:T(8,128)S(1)}, f32[32,1152]{1,0:T(8,128)S(1)}, u32[]{:S(2)}, u32[]{:S(2)}) collective-permute-start(f32[32,1152]{1,0:T(8,128)S(1)} %constant_dynamic-slice_fusion.5), channel_id=1, source_target_pairs={{0,32},{1,33},{2,34},{3,35},{4,36},{5,37},{6,38},{7,39},{8,40},{9,... | collective-permute-start | bytes 442376 | tf_op jit(solution)/shard_map/ppermute | solution.py:42
  223.5 6.3 %collective-permute-start.23 = (f32[32,576]{1,0:T(8,128)S(1)}, f32[32,576]{1,0:T(8,128)S(1)}, u32[]{:S(2)}, u32[]{:S(2)}) collective-permute-start(f32[32,576]{1,0:T(8,128)S(1)} %constant_dynamic-slice_fusion.4), channel_id=1, source_target_pairs={{0,16},{1,17},{2,18},{3,19},{4,20},{5,21},{6,22},{7,23},{8,24},{9,... | collective-permute-start | bytes 221192 | tf_op jit(solution)/shard_map/ppermute | solution.py:42
  230.1 9.9 %collective-permute-start.24 = (f32[32,288]{1,0:T(8,128)S(1)}, f32[32,288]{1,0:T(8,128)S(1)}, u32[]{:S(2)}, u32[]{:S(2)}) collective-permute-start(f32[32,288]{1,0:T(8,128)S(1)} %constant_dynamic-slice_fusion.3), channel_id=1, source_target_pairs={{0,8},{1,9},{2,10},{3,11},{4,12},{5,13},{6,14},{7,15},{8,0},{9,1},... | collective-permute-start | bytes 110600 | tf_op jit(solution)/shard_map/ppermute | solution.py:42
  240.1 10.0 %collective-permute-start.25 = (f32[32,144]{1,0:T(8,128)S(1)}, f32[32,144]{1,0:T(8,128)S(1)}, u32[]{:S(2)}, u32[]{:S(2)}) collective-permute-start(f32[32,144]{1,0:T(8,128)S(1)} %constant_dynamic-slice_fusion.2), channel_id=1, source_target_pairs={{0,4},{1,5},{2,6},{3,7},{4,0},{5,1},{6,2},{7,3},{8,12},{9,13},{10,... | collective-permute-start | bytes 55304 | tf_op jit(solution)/shard_map/ppermute | solution.py:42
  250.3 6.5 %collective-permute-start.26 = (f32[32,72]{1,0:T(8,128)S(1)}, f32[32,72]{1,0:T(8,128)S(1)}, u32[]{:S(2)}, u32[]{:S(2)}) collective-permute-start(f32[32,72]{1,0:T(8,128)S(1)} %constant_dynamic-slice_fusion.1), channel_id=1, source_target_pairs={{0,2},{1,3},{2,0},{3,1},{4,6},{5,7},{6,4},{7,5},{8,10},{9,11},{10,... | collective-permute-start | bytes 27656 | tf_op jit(solution)/shard_map/ppermute | solution.py:42
  257.0 5.6 %collective-permute-start.27 = (f32[32,36]{1,0:T(8,128)S(1)}, f32[32,36]{1,0:T(8,128)S(1)}, u32[]{:S(2)}, u32[]{:S(2)}) collective-permute-start(f32[32,36]{1,0:T(8,128)S(1)} %constant_dynamic-slice_fusion), channel_id=1, source_target_pairs={{0,1},{1,0},{2,3},{3,2},{4,5},{5,4},{6,7},{7,6},{8,9},{9,8},{10,11... | collective-permute-start | bytes 13832 | tf_op jit(solution)/shard_map/ppermute | solution.py:42
  (6 other events, 7.4 us)
Sparse Core Ops, SparseCore 0:
  169.2 44.2 reduce-scatter.1
